TPU v7x, 32 devices: a whole 2x2x4 slice. The times are simulated.
32 devices in a mesh: groups: 2 (over x), wide: 16 (over z, y, core).
Axes of the slice: x: 2, y: 2, z: 4, core: 2. Of those that a mesh axis runs over, the one named last changes fastest.
Arguments:
- query_act: bfloat16 [4096, 2048], P(('groups', 'wide')), parts along dimension 0, may hold values from -6 to 6
- query_grad: bfloat16 [4096, 4096], P(('groups', 'wide')), parts along dimension 0, may hold values from -6 to 6
- query_positions: int32 [4096], P(('groups', 'wide')), parts along dimension 0, may hold values from 0 to 4095
- act_basis: bfloat16 [2048, 1024], P(None, 'wide'), may hold values from -0.125 to 0.125
- grad_basis: bfloat16 [4096, 2048], P(None, 'wide'), may hold values from -0.09375 to 0.09375
- eig_values: bfloat16 [1024, 2048], P('wide'), may hold values from 0.05 to 50, as said below
- damping_index: int32 [12], P('groups'), parts along dimension 0, may hold values from 0 to 8
- train_act_rot: bfloat16 [1024, 6144], P(None, 'wide'), may hold values from -6 to 6
- train_grad_rot: bfloat16 [2048, 6144], P(None, 'wide'), may hold values from -6 to 6
- train_positions: int32 [6144], P('wide'), may hold values from 0 to 4095
Outputs:
- influences: float32 [12, 6144], P('groups', 'wide'), parts along dimension 0
There are 2 independent parts, one for each index of `groups`. A program takes and returns all parts, laid end to end along the dimension named above; an argument that names none is the same for every part. Nothing has to cross between parts.
Inputs may be any that keep to these rules, and one draw needn't show every extreme that they name: `eig_values`: positive corrected eigenvalues.
All inputs are finite; a program needn't handle non-finite values.
Results may differ from a plain program's by a relative error of at most 0.0059.
Values may be sent and summed in bfloat16 or wider, within the bound.
No kernel may reach another device: no remote copies, remote signals or barrier semaphores. Data moves between devices by JAX's collectives and lax.ppermute only.
A program may use at most 128 MiB of HBM per device.

v0:
```python
import math

import jax
import jax.numpy as jnp
from jax import lax
from jax.sharding import PartitionSpec as P

EIG_IN = 1024
EIG_OUT = 2048
PROMPT = 1024


def score_rows(grad_rows, eig_rows, dampings, train_act_rot, train_grad_rot):
    acts_rows = train_act_rot.astype(jnp.float32)
    grad_wide = grad_rows.astype(jnp.float32)
    eig_wide = eig_rows.astype(jnp.float32)
    results = []
    for damping in range(dampings.shape[0]):
        precond = (grad_wide / (eig_wide + dampings[damping])).astype(jnp.bfloat16)
        projected = jnp.dot(precond, train_grad_rot, preferred_element_type=jnp.float32)
        results.append(jnp.sum(projected * acts_rows, axis=0))
    return jnp.stack(results)


def shards(
    query_act,
    query_grad,
    query_positions,
    act_basis,
    grad_basis,
    eig_values,
    damping_index,
    train_act_rot,
    train_grad_rot,
    train_positions,
):
    act_full = jnp.dot(
        query_act,
        lax.all_gather(act_basis, "wide", axis=1, tiled=True),
        preferred_element_type=jnp.float32,
    )
    grad_full = jnp.dot(
        query_grad,
        lax.all_gather(grad_basis, "wide", axis=1, tiled=True),
        preferred_element_type=jnp.float32,
    )
    act_rot = act_full.astype(jnp.bfloat16)
    grad_rot = grad_full.astype(jnp.bfloat16)
    query_weight = jnp.where(query_positions >= PROMPT, 1.0, 0.0).astype(jnp.bfloat16)
    grad_kept = grad_rot * query_weight[:, None]
    eig_total = lax.psum(jnp.sum(eig_values.astype(jnp.float32)), "wide")
    mean_eig = eig_total / (EIG_IN * EIG_OUT)
    dampings = mean_eig * jnp.exp2(damping_index.astype(jnp.float32) - 4.0)
    partial_whole = lax.dot_general(
        act_rot, grad_kept, (((0,), (0,)), ((), ())), preferred_element_type=jnp.float32
    )
    query_gradient = lax.psum(partial_whole, "wide").astype(jnp.bfloat16)
    totals = score_rows(
        query_gradient,
        lax.all_gather(eig_values, "wide", axis=0, tiled=True),
        dampings,
        train_act_rot,
        train_grad_rot,
    )
    query_count = query_act.shape[0] * lax.axis_size("wide")
    factor = mean_eig * (1.0 / math.sqrt(float(query_count) * EIG_IN * EIG_OUT))
    train_weight = jnp.where(train_positions >= PROMPT, 1.0, 0.0).astype(jnp.float32)
    return totals * factor * train_weight[None, :]


def solution(mesh):
    in_specs = (
        P(("groups", "wide"), None),
        P(("groups", "wide"), None),
        P(("groups", "wide")),
        P(None, "wide"),
        P(None, "wide"),
        P("wide", None),
        P("groups"),
        P(None, "wide"),
        P(None, "wide"),
        P("wide"),
    )
    out_specs = P("groups", "wide")
    return jax.shard_map(shards, mesh=mesh, in_specs=in_specs, out_specs=out_specs, check_vma=False)
```

profile of v0, /device:TPU:0, one launch (start us, length us, event | category | flops | bytes accessed | tf_op | source)
XLA Modules:
  0.0 426.5 jit_solution(4725387925321449047)
XLA Ops:
  6.5 0.0 copy-start
  6.5 0.0 all-gather.6.cloned.1.call-start
  6.5 0.7 all-gather.6.cloned.1.call-update
  7.3 0.0 all-gather.4.cloned.1.call-start
  7.3 0.7 all-gather.4.cloned.1.call-update
  8.0 0.0 all-gather.8.cloned.1.call-start
  8.1 0.7 all-gather.8.cloned.1.call-update
  8.7 1.7 convert_reduce_fusion
  10.4 0.7 fusion.38
  11.1 0.7 compare_select_fusion
  11.8 0.0 copy-start.1
  11.8 130.8 %all-gather.6.cloned.1.call-done = bf16[4096,2048]{1,0:T(8,128)(2,1)} async-done(((bf16[4096,128]{1,0:T(8,128)(2,1)}), bf16[4096,2048]{1,0:T(8,128)(2,1)}) %all-gather.6.cloned.1.call-update) | async-done | bytes 16777232 | tf_op jit(solution)/shard_map/all_gather | solution.py:44
  142.6 8.4 %fusion.18 = bf16[128,2048]{1,0:T(8,128)(2,1)S(1)} fusion(bf16[128,4096]{1,0:T(8,128)(2,1)} %param.11, bf16[4096,2048]{1,0:T(8,128)(2,1)} %all-gather.6.cloned.1.call-done, bf16[128]{0:T(256)(128)(2,1)S(1)} %fusion.38), kind=kOutput, calls=%fused_computation.31 | convolution fusion | flops 2148007936 | bytes 18350336 | tf_op jit(solution)/shard_map/dot_general | solution.py:42
  151.0 42.5 %all-gather.4.cloned.1.call-done = bf16[2048,1024]{0,1:T(8,128)(2,1)} async-done(((bf16[2048,64]{0,1:T(8,128)(2,1)}), bf16[2048,1024]{0,1:T(8,128)(2,1)}) %all-gather.4.cloned.1.call-update) | async-done | bytes 4194320 | tf_op jit(solution)/shard_map/all_gather | solution.py:39
  193.5 0.0 copy-done.1
  193.5 8.1 %fusion.37 = f32[1024,2048]{1,0:T(8,128)} fusion(bf16[128,2048]{1,0:T(8,128)(2,1)S(1)} %fusion.18, bf16[128,2048]{1,0:T(8,128)(2,1)S(1)} %copy-done.1, bf16[2048,1024]{0,1:T(8,128)(2,1)} %all-gather.4.cloned.1.call-done), kind=kOutput, calls=%fused_computation.39 | convolution fusion | flops 1073872896 | bytes 13631488 | tf_op jit(solution)/shard_map/dot_general | solution.py:54
  201.6 0.0 copy-start.5
  201.6 0.0 copy-start.4
  201.6 193.2 %all-reduce.2 = (bf16[1024,2048]{1,0:T(8,128)(2,1)}, f32[]{:T(128)}) all-reduce(f32[1024,2048]{1,0:T(8,128)} %fusion.37, f32[]{:T(128)} %convert_reduce_fusion), channel_id=1, replica_groups=mesh['groups'=2,'wide'=16] {'wide'}, use_global_device_ids=true, to_apply=%region_0.1 | all-reduce | flops 2097153 | bytes 12582920 | tf_op jit(solution)/shard_map/psum | solution.py:57
  395.5 0.0 copy-done.5
  395.5 0.7 fusion.39
  396.2 0.0 all-gather.8.cloned.1.call-done
  396.2 0.0 copy-done
  396.2 0.0 copy-done.4
  396.2 0.0 copy-start.2
  396.2 0.0 copy-start.3
  396.2 7.0 %fusion.24 = f32[384]{0:T(512)S(1)} fusion(bf16[1024,384]{1,0:T(8,128)(2,1)S(1)} %copy-done.4, bf16[2048,384]{1,0:T(8,128)(2,1)S(1)} %copy-done, bf16[1024,2048]{1,0:T(8,128)(2,1)} %get-tuple-element.5, bf16[1024,2048]{1,0:T(8,128)(2,1)} %all-gather.8.cloned.1.call-done, f32[]{:T(128)} %bitcast.5), kind=kOutput, calls=%fused_computation.37 | convolution fusion | flops 1622277760 | bytes 10749444 | tf_op jit(solution)/shard_map/dot_general | solution.py:20
  403.2 0.0 copy-done.2
  403.2 0.0 copy-done.3
  403.2 3.0 fusion.23
  406.2 3.1 fusion.22
  409.3 3.0 fusion.21
  412.3 3.3 fusion.20
  415.7 3.0 fusion.19
  419.4 0.6 multiply_multiply_fusion
  (8 shorter events, 0.1 us)
Async XLA Ops:
  6.5 389.7 %copy-start = (bf16[2048,384]{1,0:T(8,128)(2,1)S(1)}, bf16[2048,384]{1,0:T(8,128)(2,1)}, u32[]{:S(2)}) copy-start(bf16[2048,384]{1,0:T(8,128)(2,1)} %param.18) | copy-start | bytes 4718596
  6.5 136.1 %all-gather.6.cloned.1.call-start = ((), (), s32[]{:S(2)}) async-start(), calls=%async_computation.1 | async-start | bytes 17825792 | tf_op jit(solution)/shard_map/all_gather | solution.py:44
  7.3 186.3 %all-gather.4.cloned.1.call-start = ((), (), s32[]{:S(2)}) async-start(), calls=%async_computation | async-start | bytes 4456448 | tf_op jit(solution)/shard_map/all_gather | solution.py:39
  8.0 388.2 %all-gather.8.cloned.1.call-start = ((), (), s32[]{:S(2)}) async-start(), calls=%async_computation.2 | async-start | bytes 4456448 | tf_op jit(solution)/shard_map/all_gather | solution.py:60
  11.8 181.8 %copy-start.1 = (bf16[128,2048]{1,0:T(8,128)(2,1)S(1)}, bf16[128,2048]{1,0:T(8,128)(2,1)}, u32[]{:S(2)}) copy-start(bf16[128,2048]{1,0:T(8,128)(2,1)} %param.10) | copy-start | bytes 1572868
  201.6 193.8 %copy-start.5 = (s32[6]{0:T(128)S(1)}, s32[6]{0:T(128)}, u32[]{:S(2)}) copy-start(s32[6]{0:T(128)} %param.16) | copy-start | bytes 76
  201.6 194.6 %copy-start.4 = (bf16[1024,384]{1,0:T(8,128)(2,1)S(1)}, bf16[1024,384]{1,0:T(8,128)(2,1)}, u32[]{:S(2)}) copy-start(bf16[1024,384]{1,0:T(8,128)(2,1)} %param.17) | copy-start | bytes 2359300
  396.2 7.0 %copy-start.2 = (bf16[1024,2048]{1,0:T(8,128)(2,1)S(1)}, bf16[1024,2048]{1,0:T(8,128)(2,1)}, u32[]{:S(2)}) copy-start(bf16[1024,2048]{1,0:T(8,128)(2,1)} %all-gather.8.cloned.1.call-done) | copy-start | bytes 12582916
  396.2 7.0 %copy-start.3 = (bf16[1024,2048]{1,0:T(8,128)(2,1)S(1)}, bf16[1024,2048]{1,0:T(8,128)(2,1)}, u32[]{:S(2)}) copy-start(bf16[1024,2048]{1,0:T(8,128)(2,1)} %get-tuple-element.5) | copy-start | bytes 12582916
Sparse Core Ops, SparseCore 0:
  9.5 133.0 all-gather.5
  144.7 48.7 all-gather.3
  195.7 67.8 all-gather.7
where the time goes:
time: 429 us; the launch traced here: 427 us
  blocking collectives  193 us (45%)
  waiting for transfers between devices  175 us (41%)
  matrix products  38.9 us (9%)
  between operations  14.5 us (3%)
    psum x1, blocking collectives, shards(): query_gradient = lax.psum(partial_whole, 'wide').astype(jnp.bfloat16)  193 us
    all_gather x1, waiting for transfers between devices, shards(): lax.all_gather(grad_basis, 'wide', axis=1, tiled=True)  131 us
    all_gather x1, waiting for transfers between devices, shards(): lax.all_gather(act_basis, 'wide', axis=1, tiled=True)  42.5 us
    dot_general x6, matrix products, score_rows(): jnp.dot(precond, train_grad_rot, preferred_element_type=jnp.float32)  22.4 us
  transfers between devices with their start and end apart: 3, of which 2 were waited for; matrix products, arithmetic and copies ran while one was open for 5% of the time, Pallas kernels for 0%

commit v1 on v0

v1 whole, which is shorter than its diff:
```python
import math

import jax
import jax.numpy as jnp
from jax import lax
from jax.sharding import Mesh
from jax.sharding import PartitionSpec as P

PROMPT = 1024
WIDE = ("wa", "wb")


def score_rows(grad_rows, eig_rows, dampings, train_act_rot, train_grad_rot):
    acts_rows = train_act_rot.astype(jnp.float32)
    grad_wide = grad_rows.astype(jnp.float32)
    eig_wide = eig_rows.astype(jnp.float32)
    results = []
    for damping in range(dampings.shape[0]):
        precond = (grad_wide / (eig_wide + dampings[damping])).astype(jnp.bfloat16)
        projected = jnp.dot(precond, train_grad_rot, preferred_element_type=jnp.float32)
        results.append(jnp.sum(projected * acts_rows, axis=0))
    return jnp.stack(results)


def shards(
    query_act,
    query_grad,
    query_positions,
    act_basis,
    grad_basis,
    eig_values,
    damping_index,
    train_act_rot,
    train_grad_rot,
    train_positions,
):
    act_tokens = lax.all_gather(query_act, "wa", axis=0, tiled=True)
    grad_tokens = lax.all_gather(query_grad, "wa", axis=0, tiled=True)
    positions = lax.all_gather(query_positions, "wa", axis=0, tiled=True)
    act_cols = lax.all_gather(act_basis, "wb", axis=1, tiled=True)
    grad_cols = lax.all_gather(grad_basis, "wb", axis=1, tiled=True)
    act_rot = jnp.dot(act_tokens, act_cols, preferred_element_type=jnp.float32).astype(jnp.bfloat16)
    grad_rot = jnp.dot(grad_tokens, grad_cols, preferred_element_type=jnp.float32).astype(jnp.bfloat16)
    query_weight = jnp.where(positions >= PROMPT, 1.0, 0.0).astype(jnp.bfloat16)
    grad_kept = grad_rot * query_weight[:, None]
    grad_all = lax.all_gather(grad_kept, "wa", axis=1, tiled=True)
    partial_rows = lax.dot_general(
        act_rot, grad_all, (((0,), (0,)), ((), ())), preferred_element_type=jnp.float32
    )
    gradient_rows = lax.psum_scatter(partial_rows, "wb", scatter_dimension=0, tiled=True)
    query_gradient = lax.all_gather(gradient_rows.astype(jnp.bfloat16), WIDE, axis=0, tiled=True)
    eig_full = lax.all_gather(eig_values, WIDE, axis=0, tiled=True)
    eig_in, eig_out = eig_full.shape
    mean_eig = jnp.sum(eig_full.astype(jnp.float32)) / (eig_in * eig_out)
    dampings = mean_eig * jnp.exp2(damping_index.astype(jnp.float32) - 4.0)
    totals = score_rows(query_gradient, eig_full, dampings, train_act_rot, train_grad_rot)
    query_count = query_act.shape[0] * lax.axis_size(WIDE)
    factor = mean_eig * (1.0 / math.sqrt(float(query_count) * eig_in * eig_out))
    train_weight = jnp.where(train_positions >= PROMPT, 1.0, 0.0).astype(jnp.float32)
    return totals * factor * train_weight[None, :]


def split_wide(size):
    wb = 1
    while wb * wb < size and size % (wb * 2) == 0:
        wb *= 2
    return size // wb, wb


def solution(mesh):
    groups, wide = mesh.devices.shape
    wa, wb = split_wide(wide)
    grid = Mesh(mesh.devices.reshape(groups, wa, wb), ("groups",) + WIDE)
    tokens = ("groups",) + WIDE
    in_specs = (
        P(tokens, None),
        P(tokens, None),
        P(tokens),
        P(None, WIDE),
        P(None, WIDE),
        P(WIDE, None),
        P("groups"),
        P(None, WIDE),
        P(None, WIDE),
        P(WIDE),
    )
    out_specs = P("groups", WIDE)
    return jax.shard_map(shards, mesh=grid, in_specs=in_specs, out_specs=out_specs, check_vma=False)
```

time: 429 us -> 380 us (0.89)
  blocking collectives: 193 us -> 12.7 us
  waiting for transfers between devices: 175 us -> 307 us
    psum x1 -> x0, blocking collectives: 193 us -> none  [shards(): query_gradient = lax.psum(partial_whole, 'wide').astype(jnp.bfloat16)]
    all_gather x3 -> x7, waiting for transfers between devices: 173 us -> 275 us  [the longest x1 70.3 us: shards(): grad_tokens = lax.all_gather(query_grad, 'wa', axis=0, tiled=True)]
    reduce_scatter x0 -> x1, waiting for transfers between devices: none -> 29.5 us  [shards(): lax.psum_scatter(partial_rows, 'wb', scatter_dimension=0, tiled=True)]
    all_gather x0 -> x1, blocking collectives: none -> 12.7 us  [shards(): positions = lax.all_gather(query_positions, 'wa', axis=0, tiled=True)]
  transfers between devices with their start and end apart: 3 -> 8, of which waited for: 2 -> 8; matrix products, arithmetic and copies ran while one was open for 5% -> 4% of each run, Pallas kernels for 0% -> 0%
where the time goes in v1:
time: 380 us
  waiting for transfers between devices  307 us (81%)
  matrix products  35 us (9%)
  between operations  16.4 us (4%)
  blocking collectives  12.7 us (3%)
  other arithmetic  7.38 us (2%)
    all_gather x1, waiting for transfers between devices, shards(): grad_tokens = lax.all_gather(query_grad, 'wa', axis=0, tiled=True)  70.3 us
    all_gather x1, waiting for transfers between devices, shards(): act_tokens = lax.all_gather(query_act, 'wa', axis=0, tiled=True)  47.4 us
    all_gather x1, waiting for transfers between devices, shards(): grad_all = lax.all_gather(grad_kept, 'wa', axis=1, tiled=True)  46.1 us
    all_gather x1, waiting for transfers between devices, shards(): lax.all_gather(gradient_rows.astype(jnp.bfloat16), WIDE, axis=0, tiled=True)  44.3 us
    all_gather x1, waiting for transfers between devices, shards(): grad_cols = lax.all_gather(grad_basis, 'wb', axis=1, tiled=True)  35.1 us
    reduce_scatter x1, waiting for transfers between devices, shards(): lax.psum_scatter(partial_rows, 'wb', scatter_dimension=0, tiled=True)  29.5 us
    dot_general x6, matrix products, score_rows(): jnp.dot(precond, train_grad_rot, preferred_element_type=jnp.float32)  22.1 us
    all_gather x1, waiting for transfers between devices, shards(): eig_full = lax.all_gather(eig_values, WIDE, axis=0, tiled=True)  19.8 us
  transfers between devices with their start and end apart: 8, of which 8 were waited for; matrix products, arithmetic and copies ran while one was open for 4% of the time, Pallas kernels for 0%

profile of v1, /device:TPU:0, one launch (start us, length us, event | category | flops | bytes accessed | tf_op | source)
XLA Modules:
  0.0 380.1 jit_solution(15575969760906076702)
XLA Ops:
  7.4 0.0 copy-start
  7.4 0.0 all-gather.13.cloned.1.call-start
  7.4 0.7 all-gather.13.cloned.1.call-update
  8.1 0.0 all-gather.15.cloned.1.call-start
  8.1 0.7 all-gather.15.cloned.1.call-update
  8.8 0.0 all-gather.11.cloned.1.call-start
  8.9 0.7 all-gather.11.cloned.1.call-update
  9.6 0.0 all-gather.9.cloned.1.call-start
  9.6 0.5 all-gather.9.cloned.1.call-update
  10.2 0.0 all-gather.17.cloned.1.call-start
  10.2 12.7 %all-gather = s32[4,1,128]{2,1,0:T(1,128)S(1)} all-gather(s32[1,1,128]{2,1,0:T(1,128)} %bitcast.20), channel_id=1, replica_groups=mesh['groups'=2,'wa'=4,'wb'=4] {'wa'}, dimensions={0}, use_global_device_ids=true | all-gather | bytes 2560 | tf_op jit(solution)/shard_map/all_gather | solution.py:39
  22.9 70.3 %all-gather.13.cloned.1.call-done = bf16[512,4096]{1,0:T(8,128)(2,1)} async-done(((bf16[128,4096]{1,0:T(8,128)(2,1)}), bf16[512,4096]{1,0:T(8,128)(2,1)}) %all-gather.13.cloned.1.call-update) | async-done | bytes 4194320 | tf_op jit(solution)/shard_map/all_gather | solution.py:38
  93.3 35.1 %all-gather.15.cloned.1.call-done = bf16[4096,512]{1,0:T(8,128)(2,1)} async-done(((bf16[4096,128]{1,0:T(8,128)(2,1)}), bf16[4096,512]{1,0:T(8,128)(2,1)}) %all-gather.15.cloned.1.call-update) | async-done | bytes 4194320 | tf_op jit(solution)/shard_map/all_gather | solution.py:41
  128.4 6.6 %fusion.36 = bf16[512,512]{1,0:T(8,128)(2,1)} fusion(bf16[512,4096]{1,0:T(8,128)(2,1)} %all-gather.13.cloned.1.call-done, bf16[4096,512]{1,0:T(8,128)(2,1)} %all-gather.15.cloned.1.call-done, bf16[512]{0:T(512)(128)(2,1)S(1)} %bitcast.19), kind=kOutput, calls=%fused_computation.38 | convolution fusion | flops 2148007936 | bytes 8913920 | tf_op jit(solution)/shard_map/dot_general | solution.py:43
  135.0 0.0 all-gather.17.cloned.1.call-update
  135.0 0.0 copy-start.2
  135.0 0.0 reduce-scatter.2.cloned.1.call-start
  135.1 11.7 %all-gather.11.cloned.1.call-done = bf16[2048,256]{0,1:T(8,128)(2,1)} async-done(((bf16[2048,64]{0,1:T(8,128)(2,1)}), bf16[2048,256]{0,1:T(8,128)(2,1)}) %all-gather.11.cloned.1.call-update) | async-done | bytes 1048592 | tf_op jit(solution)/shard_map/all_gather | solution.py:40
  146.7 47.4 %all-gather.9.cloned.1.call-done = bf16[512,2048]{1,0:T(8,128)(2,1)} async-done(((bf16[128,2048]{1,0:T(8,128)(2,1)}), bf16[512,2048]{1,0:T(8,128)(2,1)}) %all-gather.9.cloned.1.call-update) | async-done | bytes 2097168 | tf_op jit(solution)/shard_map/all_gather | solution.py:37
  194.1 46.1 %all-gather.17.cloned.1.call-done = bf16[512,2048]{1,0:T(8,128)(2,1)} async-done(((bf16[512,512]{1,0:T(8,128)(2,1)}), bf16[512,2048]{1,0:T(8,128)(2,1)}) %all-gather.17.cloned.1.call-update) | async-done | bytes 2097168 | tf_op jit(solution)/shard_map/all_gather | solution.py:46
  240.2 6.3 %fusion.37 = f32[256,2048]{1,0:T(8,128)} fusion(bf16[512,2048]{1,0:T(8,128)(2,1)} %all-gather.17.cloned.1.call-done, bf16[512,2048]{1,0:T(8,128)(2,1)} %all-gather.9.cloned.1.call-done, bf16[2048,256]{0,1:T(8,128)(2,1)} %all-gather.11.cloned.1.call-done), kind=kOutput, calls=%fused_computation.40 | convolution fusion | flops 1073872896 | bytes 7340032 | tf_op jit(solution)/shard_map/dot_general | solution.py:47
  246.5 0.0 copy-start.5
  246.5 0.0 copy-start.4
  246.5 0.0 reduce-scatter.2.cloned.1.call-update
  246.6 0.0 all-gather.21.cloned.1.call-start
  246.6 0.5 all-gather.21.cloned.1.call-update
  247.1 0.2 all-gather.19.cloned.1.call-start
  247.4 29.5 %reduce-scatter.2.cloned.1.call-done = f32[64,2048]{1,0:T(8,128)} async-done(((f32[256,2048]{1,0:T(8,128)}), f32[64,2048]{1,0:T(8,128)}) %reduce-scatter.2.cloned.1.call-update) | async-done | bytes 524304 | tf_op jit(solution)/shard_map/reduce_scatter | solution.py:50
  276.9 1.8 convert_element_type.46
  278.7 0.0 all-gather.19.cloned.1.call-update
  278.7 0.0 copy-done.2
  278.7 19.8 %all-gather.21.cloned.1.call-done = bf16[1024,2048]{1,0:T(8,128)(2,1)} async-done(((bf16[64,2048]{1,0:T(8,128)(2,1)}), bf16[1024,2048]{1,0:T(8,128)(2,1)}) %all-gather.21.cloned.1.call-update) | async-done | bytes 4194320 | tf_op jit(solution)/shard_map/all_gather | solution.py:52
  298.6 4.9 %convert_reduce_fusion = f32[]{:T(128)} fusion(bf16[1024,2048]{1,0:T(8,128)(2,1)} %all-gather.21.cloned.1.call-done), kind=kLoop, calls=%fused_computation.6 | loop fusion | flops 4194303 | bytes 4194308 | tf_op jit(solution)/shard_map/reduce_sum | solution.py:54
  304.8 0.0 copy-done.5
  304.8 0.7 fusion.40
  305.5 44.3 %all-gather.19.cloned.1.call-done = bf16[1024,2048]{1,0:T(8,128)(2,1)} async-done(((bf16[64,2048]{1,0:T(8,128)(2,1)}), bf16[1024,2048]{1,0:T(8,128)(2,1)}) %all-gather.19.cloned.1.call-update) | async-done | bytes 4194320 | tf_op jit(solution)/shard_map/all_gather | solution.py:51
  349.8 0.0 copy-done
  349.8 0.0 copy-done.4
  349.8 0.0 copy-start.1
  349.8 0.0 copy-start.3
  349.8 6.9 %fusion.18 = f32[384]{0:T(512)S(1)} fusion(bf16[1024,384]{1,0:T(8,128)(2,1)S(1)} %copy-done.4, bf16[2048,384]{1,0:T(8,128)(2,1)S(1)} %copy-done, bf16[1024,2048]{1,0:T(8,128)(2,1)} %all-gather.19.cloned.1.call-done, bf16[1024,2048]{1,0:T(8,128)(2,1)} %all-gather.21.cloned.1.call-done, f32[]{:T(128)} %bitcast.1), kind=kOutput, calls=%fused_computation.31 | convolution fusion | flops 1622277760 | bytes 10749444 | tf_op jit(solution)/shard_map/dot_general | solution.py:20
  356.7 0.0 copy-done.1
  356.7 0.0 copy-done.3
  356.7 3.0 fusion.19
  359.8 2.9 fusion.20
  362.7 3.0 fusion.21
  365.8 3.2 fusion.22
  369.0 3.0 fusion.23
  372.1 0.6 multiply_multiply_fusion
  (10 shorter events, 0.1 us)
Async XLA Ops:
  7.4 342.5 %copy-start = (bf16[2048,384]{1,0:T(8,128)(2,1)S(1)}, bf16[2048,384]{1,0:T(8,128)(2,1)}, u32[]{:S(2)}) copy-start(bf16[2048,384]{1,0:T(8,128)(2,1)} %param.18) | copy-start | bytes 4718596
  7.4 85.9 %all-gather.13.cloned.1.call-start = ((), (), s32[]{:S(2)}) async-start(), calls=%async_computation.3 | async-start | bytes 5242880 | tf_op jit(solution)/shard_map/all_gather | solution.py:38
  8.1 120.3 %all-gather.15.cloned.1.call-start = ((), (), s32[]{:S(2)}) async-start(), calls=%async_computation.4 | async-start | bytes 5242880 | tf_op jit(solution)/shard_map/all_gather | solution.py:41
  8.8 137.9 %all-gather.11.cloned.1.call-start = ((), (), s32[]{:S(2)}) async-start(), calls=%async_computation.2 | async-start | bytes 1310720 | tf_op jit(solution)/shard_map/all_gather | solution.py:40
  9.6 184.5 %all-gather.9.cloned.1.call-start = ((), (), s32[]{:S(2)}) async-start(), calls=%async_computation.1 | async-start | bytes 2621440 | tf_op jit(solution)/shard_map/all_gather | solution.py:37
  10.2 230.1 %all-gather.17.cloned.1.call-start = ((), (), s32[]{:S(2)}) async-start(), calls=%async_computation.5 | async-start | bytes 2621440 | tf_op jit(solution)/shard_map/all_gather | solution.py:46
  135.0 143.7 %copy-start.2 = (s32[384]{0:T(512)S(1)}, s32[384]{0:T(512)}, u32[]{:S(2)}) copy-start(s32[384]{0:T(512)} %param.19) | copy-start | bytes 4612
  135.0 141.9 %reduce-scatter.2.cloned.1.call-start = ((), (), s32[]{:S(2)}) async-start(), calls=%async_computation.6 | async-start | bytes 2621440 | tf_op jit(solution)/shard_map/reduce_scatter | solution.py:50
  246.5 58.3 %copy-start.5 = (s32[6]{0:T(128)S(1)}, s32[6]{0:T(128)}, u32[]{:S(2)}) copy-start(s32[6]{0:T(128)} %param.16) | copy-start | bytes 76
  246.5 103.3 %copy-start.4 = (bf16[1024,384]{1,0:T(8,128)(2,1)S(1)}, bf16[1024,384]{1,0:T(8,128)(2,1)}, u32[]{:S(2)}) copy-start(bf16[1024,384]{1,0:T(8,128)(2,1)} %param.17) | copy-start | bytes 2359300
  246.6 52.0 %all-gather.21.cloned.1.call-start = ((), (), s32[]{:S(2)}) async-start(), calls=%async_computation.8 | async-start | bytes 4456448 | tf_op jit(solution)/shard_map/all_gather | solution.py:52
  247.1 102.7 %all-gather.19.cloned.1.call-start = ((), (), s32[]{:S(2)}) async-start(), calls=%async_computation.7 | async-start | bytes 4456448 | tf_op jit(solution)/shard_map/all_gather | solution.py:51
  349.8 6.9 %copy-start.1 = (bf16[1024,2048]{1,0:T(8,128)(2,1)S(1)}, bf16[1024,2048]{1,0:T(8,128)(2,1)}, u32[]{:S(2)}) copy-start(bf16[1024,2048]{1,0:T(8,128)(2,1)} %all-gather.21.cloned.1.call-done) | copy-start | bytes 12582916
  349.8 6.9 %copy-start.3 = (bf16[1024,2048]{1,0:T(8,128)(2,1)S(1)}, bf16[1024,2048]{1,0:T(8,128)(2,1)}, u32[]{:S(2)}) copy-start(bf16[1024,2048]{1,0:T(8,128)(2,1)} %all-gather.19.cloned.1.call-done) | copy-start | bytes 12582916
Sparse Core Ops, SparseCore 0:
  9.8 83.4 all-gather.12
  94.8 33.5 all-gather.14
  130.0 16.7 all-gather.10
  148.1 45.9 all-gather.8
  195.5 44.6 all-gather.16
  246.7 30.1 reduce-scatter.1
Sparse Core Ops, SparseCore 1:
  249.2 49.3 all-gather.20
  300.8 48.9 all-gather.18

commit v2 on v1

--- a/solution.py
+++ b/solution.py
@@ -34,20 +34,23 @@
     train_grad_rot,
     train_positions,
 ):
-    act_tokens = lax.all_gather(query_act, "wa", axis=0, tiled=True)
-    grad_tokens = lax.all_gather(query_grad, "wa", axis=0, tiled=True)
-    positions = lax.all_gather(query_positions, "wa", axis=0, tiled=True)
-    act_cols = lax.all_gather(act_basis, "wb", axis=1, tiled=True)
-    grad_cols = lax.all_gather(grad_basis, "wb", axis=1, tiled=True)
+    act_tokens = lax.all_gather(query_act, "wb", axis=0, tiled=True)
+    grad_tokens = lax.all_gather(query_grad, "wb", axis=0, tiled=True)
+    positions = lax.all_gather(query_positions, "wb", axis=0, tiled=True)
+    act_cols = lax.all_gather(act_basis, "wa", axis=1, tiled=True)
+    grad_cols = lax.all_gather(grad_basis, "wa", axis=1, tiled=True)
     act_rot = jnp.dot(act_tokens, act_cols, preferred_element_type=jnp.float32).astype(jnp.bfloat16)
     grad_rot = jnp.dot(grad_tokens, grad_cols, preferred_element_type=jnp.float32).astype(jnp.bfloat16)
     query_weight = jnp.where(positions >= PROMPT, 1.0, 0.0).astype(jnp.bfloat16)
     grad_kept = grad_rot * query_weight[:, None]
-    grad_all = lax.all_gather(grad_kept, "wa", axis=1, tiled=True)
+    grad_all = lax.all_gather(grad_kept, "wb", axis=1, tiled=True)
     partial_rows = lax.dot_general(
         act_rot, grad_all, (((0,), (0,)), ((), ())), preferred_element_type=jnp.float32
     )
-    gradient_rows = lax.psum_scatter(partial_rows, "wb", scatter_dimension=0, tiled=True)
+    gradient_rows = lax.psum_scatter(partial_rows, "wa", scatter_dimension=0, tiled=True)
+    na, nb = lax.axis_size("wa"), lax.axis_size("wb")
+    rows = gradient_rows.shape[0]
+    gradient_rows = gradient_rows.reshape(rows, nb, na, -1).transpose(0, 2, 1, 3).reshape(rows, -1)
     query_gradient = lax.all_gather(gradient_rows.astype(jnp.bfloat16), WIDE, axis=0, tiled=True)
     eig_full = lax.all_gather(eig_values, WIDE, axis=0, tiled=True)
     eig_in, eig_out = eig_full.shape

time: 380 us -> 373 us (0.982)
  blocking collectives: 12.7 us -> 6.18 us
    all_gather x5, waiting for transfers between devices: 211 us -> 181 us  [the longest x1 82.2 us: shards(): grad_cols = lax.all_gather(grad_basis, 'wa', axis=1, tiled=True)]
    reduce_scatter x1, waiting for transfers between devices: 29.5 us -> 49.2 us  [shards(): lax.psum_scatter(partial_rows, 'wa', scatter_dimension=0, tiled=True)]
    all_gather x1, waiting for transfers between devices: 19.8 us -> 27.9 us  [shards(): eig_full = lax.all_gather(eig_values, WIDE, axis=0, tiled=True)]
    all_gather x1, blocking collectives: 12.7 us -> 6.18 us  [shards(): positions = lax.all_gather(query_positions, 'wb', axis=0, tiled=True)]
where the time goes in v2:
time: 373 us; the launch traced here: 372 us
  waiting for transfers between devices  306 us (82%)
  matrix products  35 us (9%)
  between operations  16.4 us (4%)
  other arithmetic  6.66 us (2%)
  blocking collectives  6.18 us (2%)
    all_gather x1, waiting for transfers between devices, shards(): grad_cols = lax.all_gather(grad_basis, 'wa', axis=1, tiled=True)  82.2 us
    reduce_scatter x1, waiting for transfers between devices, shards(): lax.psum_scatter(partial_rows, 'wa', scatter_dimension=0, tiled=True)  49.2 us
    all_gather x1, waiting for transfers between devices, shards(): lax.all_gather(gradient_rows.astype(jnp.bfloat16), WIDE, axis=0, tiled=True)  44.3 us
    all_gather x1, waiting for transfers between devices, shards(): grad_tokens = lax.all_gather(query_grad, 'wb', axis=0, tiled=True)  30.6 us
    all_gather x1, waiting for transfers between devices, shards(): eig_full = lax.all_gather(eig_values, WIDE, axis=0, tiled=True)  27.9 us
    all_gather x1, waiting for transfers between devices, shards(): grad_all = lax.all_gather(grad_kept, 'wb', axis=1, tiled=True)  24 us
    all_gather x1, waiting for transfers between devices, shards(): act_tokens = lax.all_gather(query_act, 'wb', axis=0, tiled=True)  23.5 us
    dot_general x6, matrix products, score_rows(): jnp.dot(precond, train_grad_rot, preferred_element_type=jnp.float32)  22.1 us
  transfers between devices with their start and end apart: 8, of which 8 were waited for; matrix products, arithmetic and copies ran while one was open for 4% of the time, Pallas kernels for 0%

profile of v2, /device:TPU:0, one launch (start us, length us, event | category | flops | bytes accessed | tf_op | source)
XLA Modules:
  0.0 372.5 jit_solution(13856204677504271308)
XLA Ops:
  7.4 0.0 copy-start
  7.4 0.0 all-gather.13.cloned.1.call-start
  7.4 0.7 all-gather.13.cloned.1.call-update
  8.1 0.0 all-gather.15.cloned.1.call-start
  8.1 0.7 all-gather.15.cloned.1.call-update
  8.8 0.0 all-gather.11.cloned.1.call-start
  8.9 0.7 all-gather.11.cloned.1.call-update
  9.6 0.0 all-gather.9.cloned.1.call-start
  9.6 0.5 all-gather.9.cloned.1.call-update
  10.2 0.0 all-gather.17.cloned.1.call-start
  10.2 6.2 %all-gather = s32[4,1,128]{2,1,0:T(1,128)S(1)} all-gather(s32[1,1,128]{2,1,0:T(1,128)} %bitcast.22), channel_id=1, replica_groups=mesh['groups'=2,'wa'=4,'wb'=4] {'wb'}, dimensions={0}, use_global_device_ids=true | all-gather | bytes 2560 | tf_op jit(solution)/shard_map/all_gather | solution.py:39
  16.4 30.6 %all-gather.13.cloned.1.call-done = bf16[512,4096]{1,0:T(8,128)(2,1)} async-done(((bf16[128,4096]{1,0:T(8,128)(2,1)}), bf16[512,4096]{1,0:T(8,128)(2,1)}) %all-gather.13.cloned.1.call-update) | async-done | bytes 4194320 | tf_op jit(solution)/shard_map/all_gather | solution.py:38
  47.0 82.2 %all-gather.15.cloned.1.call-done = bf16[4096,512]{1,0:T(8,128)(2,1)} async-done(((bf16[4096,128]{1,0:T(8,128)(2,1)}), bf16[4096,512]{1,0:T(8,128)(2,1)}) %all-gather.15.cloned.1.call-update) | async-done | bytes 4194320 | tf_op jit(solution)/shard_map/all_gather | solution.py:41
  129.1 6.6 %fusion.36 = bf16[512,512]{1,0:T(8,128)(2,1)} fusion(bf16[512,4096]{1,0:T(8,128)(2,1)} %all-gather.13.cloned.1.call-done, bf16[4096,512]{1,0:T(8,128)(2,1)} %all-gather.15.cloned.1.call-done, bf16[512]{0:T(512)(128)(2,1)S(1)} %bitcast.21), kind=kOutput, calls=%fused_computation.38 | convolution fusion | flops 2148007936 | bytes 8913920 | tf_op jit(solution)/shard_map/dot_general | solution.py:43
  135.7 0.0 all-gather.17.cloned.1.call-update
  135.7 0.0 reduce-scatter.2.cloned.1.call-start
  135.8 21.1 %all-gather.11.cloned.1.call-done = bf16[2048,256]{0,1:T(8,128)(2,1)} async-done(((bf16[2048,64]{0,1:T(8,128)(2,1)}), bf16[2048,256]{0,1:T(8,128)(2,1)}) %all-gather.11.cloned.1.call-update) | async-done | bytes 1048592 | tf_op jit(solution)/shard_map/all_gather | solution.py:40
  156.8 23.5 %all-gather.9.cloned.1.call-done = bf16[512,2048]{1,0:T(8,128)(2,1)} async-done(((bf16[128,2048]{1,0:T(8,128)(2,1)}), bf16[512,2048]{1,0:T(8,128)(2,1)}) %all-gather.9.cloned.1.call-update) | async-done | bytes 2097168 | tf_op jit(solution)/shard_map/all_gather | solution.py:37
  180.4 24.0 %all-gather.17.cloned.1.call-done = bf16[512,2048]{1,0:T(8,128)(2,1)} async-done(((bf16[512,512]{1,0:T(8,128)(2,1)}), bf16[512,2048]{1,0:T(8,128)(2,1)}) %all-gather.17.cloned.1.call-update) | async-done | bytes 2097168 | tf_op jit(solution)/shard_map/all_gather | solution.py:46
  204.4 6.3 %fusion.37 = f32[256,2048]{1,0:T(8,128)} fusion(bf16[512,2048]{1,0:T(8,128)(2,1)} %all-gather.17.cloned.1.call-done, bf16[512,2048]{1,0:T(8,128)(2,1)} %all-gather.9.cloned.1.call-done, bf16[2048,256]{0,1:T(8,128)(2,1)} %all-gather.11.cloned.1.call-done), kind=kOutput, calls=%fused_computation.40 | convolution fusion | flops 1073872896 | bytes 7340032 | tf_op jit(solution)/shard_map/dot_general | solution.py:47
  210.7 0.0 copy-start.2
  210.7 0.0 copy-start.5
  210.7 0.0 copy-start.4
  210.7 0.0 reduce-scatter.2.cloned.1.call-update
  210.8 0.0 all-gather.21.cloned.1.call-start
  210.8 0.5 all-gather.21.cloned.1.call-update
  211.3 0.2 all-gather.19.cloned.1.call-start
  211.6 49.2 %reduce-scatter.2.cloned.1.call-done = f32[64,2048]{1,0:T(8,128)} async-done(((f32[256,2048]{1,0:T(8,128)}), f32[64,2048]{1,0:T(8,128)}) %reduce-scatter.2.cloned.1.call-update) | async-done | bytes 524304 | tf_op jit(solution)/shard_map/reduce_scatter | solution.py:50
  260.7 1.1 convert_element_type.55
  261.8 0.2 convert_element_type.56
  262.0 0.1 copy.13
  262.1 0.9 convert_element_type.58
  263.0 0.0 all-gather.19.cloned.1.call-update
  263.0 0.0 copy-done.2
  263.0 27.9 %all-gather.21.cloned.1.call-done = bf16[1024,2048]{1,0:T(8,128)(2,1)} async-done(((bf16[64,2048]{1,0:T(8,128)(2,1)}), bf16[1024,2048]{1,0:T(8,128)(2,1)}) %all-gather.21.cloned.1.call-update) | async-done | bytes 4194320 | tf_op jit(solution)/shard_map/all_gather | solution.py:55
  290.9 4.9 %convert_reduce_fusion = f32[]{:T(128)} fusion(bf16[1024,2048]{1,0:T(8,128)(2,1)} %all-gather.21.cloned.1.call-done), kind=kLoop, calls=%fused_computation.6 | loop fusion | flops 4194303 | bytes 4194308 | tf_op jit(solution)/shard_map/reduce_sum | solution.py:57
  297.2 0.0 copy-done.5
  297.2 0.7 fusion.40
  297.9 44.3 %all-gather.19.cloned.1.call-done = bf16[1024,2048]{1,0:T(8,128)(2,1)} async-done(((bf16[64,2048]{1,0:T(8,128)(2,1)}), bf16[1024,2048]{1,0:T(8,128)(2,1)}) %all-gather.19.cloned.1.call-update) | async-done | bytes 4194320 | tf_op jit(solution)/shard_map/all_gather | solution.py:54
  342.2 0.0 copy-done
  342.2 0.0 copy-done.4
  342.2 0.0 copy-start.1
  342.2 0.0 copy-start.3
  342.2 6.9 %fusion.18 = f32[384]{0:T(512)S(1)} fusion(bf16[1024,384]{1,0:T(8,128)(2,1)S(1)} %copy-done.4, bf16[2048,384]{1,0:T(8,128)(2,1)S(1)} %copy-done, bf16[1024,2048]{1,0:T(8,128)(2,1)} %all-gather.19.cloned.1.call-done, bf16[1024,2048]{1,0:T(8,128)(2,1)} %all-gather.21.cloned.1.call-done, f32[]{:T(128)} %bitcast.2), kind=kOutput, calls=%fused_computation.31 | convolution fusion | flops 1622277760 | bytes 10749444 | tf_op jit(solution)/shard_map/dot_general | solution.py:20
  349.1 0.0 copy-done.1
  349.1 0.0 copy-done.3
  349.1 3.0 fusion.19
  352.1 2.9 fusion.20
  355.1 3.0 fusion.21
  358.1 3.2 fusion.22
  361.4 3.0 fusion.23
  364.4 0.6 multiply_multiply_fusion
  (10 shorter events, 0.1 us)
Async XLA Ops:
  7.4 334.8 %copy-start = (bf16[2048,384]{1,0:T(8,128)(2,1)S(1)}, bf16[2048,384]{1,0:T(8,128)(2,1)}, u32[]{:S(2)}) copy-start(bf16[2048,384]{1,0:T(8,128)(2,1)} %param.18) | copy-start | bytes 4718596
  7.4 39.6 %all-gather.13.cloned.1.call-start = ((), (), s32[]{:S(2)}) async-start(), calls=%async_computation.3 | async-start | bytes 5242880 | tf_op jit(solution)/shard_map/all_gather | solution.py:38
  8.1 121.0 %all-gather.15.cloned.1.call-start = ((), (), s32[]{:S(2)}) async-start(), calls=%async_computation.4 | async-start | bytes 5242880 | tf_op jit(solution)/shard_map/all_gather | solution.py:41
  8.8 148.0 %all-gather.11.cloned.1.call-start = ((), (), s32[]{:S(2)}) async-start(), calls=%async_computation.2 | async-start | bytes 1310720 | tf_op jit(solution)/shard_map/all_gather | solution.py:40
  9.6 170.8 %all-gather.9.cloned.1.call-start = ((), (), s32[]{:S(2)}) async-start(), calls=%async_computation.1 | async-start | bytes 2621440 | tf_op jit(solution)/shard_map/all_gather | solution.py:37
  10.2 194.3 %all-gather.17.cloned.1.call-start = ((), (), s32[]{:S(2)}) async-start(), calls=%async_computation.5 | async-start | bytes 2621440 | tf_op jit(solution)/shard_map/all_gather | solution.py:46
  135.7 125.0 %reduce-scatter.2.cloned.1.call-start = ((), (), s32[]{:S(2)}) async-start(), calls=%async_computation.6 | async-start | bytes 2621440 | tf_op jit(solution)/shard_map/reduce_scatter | solution.py:50
  210.7 52.3 %copy-start.2 = (s32[384]{0:T(512)S(1)}, s32[384]{0:T(512)}, u32[]{:S(2)}) copy-start(s32[384]{0:T(512)} %param.19) | copy-start | bytes 4612
  210.7 86.4 %copy-start.5 = (s32[6]{0:T(128)S(1)}, s32[6]{0:T(128)}, u32[]{:S(2)}) copy-start(s32[6]{0:T(128)} %param.16) | copy-start | bytes 76
  210.7 131.5 %copy-start.4 = (bf16[1024,384]{1,0:T(8,128)(2,1)S(1)}, bf16[1024,384]{1,0:T(8,128)(2,1)}, u32[]{:S(2)}) copy-start(bf16[1024,384]{1,0:T(8,128)(2,1)} %param.17) | copy-start | bytes 2359300
  210.8 80.2 %all-gather.21.cloned.1.call-start = ((), (), s32[]{:S(2)}) async-start(), calls=%async_computation.8 | async-start | bytes 4456448 | tf_op jit(solution)/shard_map/all_gather | solution.py:55
  211.3 130.8 %all-gather.19.cloned.1.call-start = ((), (), s32[]{:S(2)}) async-start(), calls=%async_computation.7 | async-start | bytes 4456448 | tf_op jit(solution)/shard_map/all_gather | solution.py:54
  342.2 6.9 %copy-start.1 = (bf16[1024,2048]{1,0:T(8,128)(2,1)S(1)}, bf16[1024,2048]{1,0:T(8,128)(2,1)}, u32[]{:S(2)}) copy-start(bf16[1024,2048]{1,0:T(8,128)(2,1)} %all-gather.21.cloned.1.call-done) | copy-start | bytes 12582916
  342.2 6.9 %copy-start.3 = (bf16[1024,2048]{1,0:T(8,128)(2,1)S(1)}, bf16[1024,2048]{1,0:T(8,128)(2,1)}, u32[]{:S(2)}) copy-start(bf16[1024,2048]{1,0:T(8,128)(2,1)} %all-gather.19.cloned.1.call-done) | copy-start | bytes 12582916
Sparse Core Ops, SparseCore 0:
  9.8 37.1 all-gather.12
  48.5 80.5 all-gather.14
  130.7 26.1 all-gather.10
  158.3 22.0 all-gather.8
  181.8 22.5 all-gather.16
  210.9 49.8 reduce-scatter.1
Sparse Core Ops, SparseCore 1:
  213.4 77.5 all-gather.20
  293.2 48.9 all-gather.18

commit v3 on v2

--- a/solution.py
+++ b/solution.py
@@ -22,6 +22,21 @@
     return jnp.stack(results)
 
 
+def ring_gather(x, axis):
+    n = lax.axis_size(axis)
+    parts = [x]
+    for shift in range(1, n):
+        parts.append(lax.ppermute(x, axis, perm=[(i, (i + shift) % n) for i in range(n)]))
+    return jnp.stack(parts)
+
+
+def natural_order(stacked, axis):
+    n = stacked.shape[0]
+    reverse = stacked[::-1]
+    doubled = jnp.concatenate([reverse, reverse], axis=0)
+    return lax.dynamic_slice_in_dim(doubled, n - 1 - lax.axis_index(axis), n, axis=0)
+
+
 def shards(
     query_act,
     query_grad,
@@ -34,21 +49,29 @@
     train_grad_rot,
     train_positions,
 ):
-    act_tokens = lax.all_gather(query_act, "wb", axis=0, tiled=True)
-    grad_tokens = lax.all_gather(query_grad, "wb", axis=0, tiled=True)
-    positions = lax.all_gather(query_positions, "wb", axis=0, tiled=True)
+    nb = lax.axis_size("wb")
+    act_tokens = ring_gather(query_act, "wb")
+    grad_tokens = ring_gather(query_grad, "wb")
+    positions = ring_gather(query_positions, "wb")
     act_cols = lax.all_gather(act_basis, "wa", axis=1, tiled=True)
     grad_cols = lax.all_gather(grad_basis, "wa", axis=1, tiled=True)
-    act_rot = jnp.dot(act_tokens, act_cols, preferred_element_type=jnp.float32).astype(jnp.bfloat16)
-    grad_rot = jnp.dot(grad_tokens, grad_cols, preferred_element_type=jnp.float32).astype(jnp.bfloat16)
-    query_weight = jnp.where(positions >= PROMPT, 1.0, 0.0).astype(jnp.bfloat16)
+    count = query_act.shape[0]
+    act_rot = jnp.dot(
+        act_tokens.reshape(nb * count, -1), act_cols, preferred_element_type=jnp.float32
+    ).astype(jnp.bfloat16)
+    grad_rot = jnp.dot(
+        grad_tokens.reshape(nb * count, -1), grad_cols, preferred_element_type=jnp.float32
+    ).astype(jnp.bfloat16)
+    query_weight = jnp.where(positions.reshape(-1) >= PROMPT, 1.0, 0.0).astype(jnp.bfloat16)
     grad_kept = grad_rot * query_weight[:, None]
+    act_rot = natural_order(act_rot.reshape(nb, count, -1), "wb").reshape(nb * count, -1)
+    grad_kept = natural_order(grad_kept.reshape(nb, count, -1), "wb").reshape(nb * count, -1)
     grad_all = lax.all_gather(grad_kept, "wb", axis=1, tiled=True)
     partial_rows = lax.dot_general(
         act_rot, grad_all, (((0,), (0,)), ((), ())), preferred_element_type=jnp.float32
     )
     gradient_rows = lax.psum_scatter(partial_rows, "wa", scatter_dimension=0, tiled=True)
-    na, nb = lax.axis_size("wa"), lax.axis_size("wb")
+    na = lax.axis_size("wa")
     rows = gradient_rows.shape[0]
     gradient_rows = gradient_rows.reshape(rows, nb, na, -1).transpose(0, 2, 1, 3).reshape(rows, -1)
     query_gradient = lax.all_gather(gradient_rows.astype(jnp.bfloat16), WIDE, axis=0, tiled=True)

time: 373 us -> 310 us (0.83)
  waiting for transfers between devices: 306 us -> 235 us
  starting transfers between devices: 0.46 us -> 8.37 us
  other arithmetic: 6.66 us -> 13.6 us
  blocking collectives: 6.18 us -> 0 us
    ppermute x0 -> x9, waiting for transfers between devices: none -> 67.6 us  [ring_gather(): lax.ppermute(x, axis, perm=[(i, (i + shift) % n) for i in range(n)])]
    all_gather x2 -> x0, waiting for transfers between devices: 54.1 us -> none  [the longest x1 30.6 us: shards(): grad_tokens = lax.all_gather(query_grad, 'wb', axis=0, tiled=True)]
    all_gather x1, waiting for transfers between devices: 82.2 us -> 29.5 us  [shards(): grad_cols = lax.all_gather(grad_basis, 'wa', axis=1, tiled=True)]
    all_gather x1, waiting for transfers between devices: 21.1 us -> 0.01 us  [shards(): act_cols = lax.all_gather(act_basis, 'wa', axis=1, tiled=True)]
    all_gather x1, waiting for transfers between devices: 24 us -> 15.5 us  [shards(): grad_all = lax.all_gather(grad_kept, 'wb', axis=1, tiled=True)]
    ppermute x0 -> x9, starting transfers between devices: none -> 7.98 us  [ring_gather(): lax.ppermute(x, axis, perm=[(i, (i + shift) % n) for i in range(n)])]
    all_gather x1 -> x0, blocking collectives: 6.18 us -> none  [shards(): positions = lax.all_gather(query_positions, 'wb', axis=0, tiled=True)]
    another operation x0 -> x2, other arithmetic: none -> 5.2 us  [ring_gather(): return jnp.stack(parts)]
  transfers between devices with their start and end apart: 8 -> 15, of which waited for: 8 -> 10; matrix products, arithmetic and copies ran while one was open for 4% -> 8% of each run, Pallas kernels for 0% -> 0%
where the time goes in v3:
time: 310 us
  waiting for transfers between devices  235 us (76%)
  matrix products  34.4 us (11%)
  between operations  16.1 us (5%)
  other arithmetic  13.6 us (4%)
  starting transfers between devices  8.37 us (3%)
    ppermute x9, waiting for transfers between devices, ring_gather(): lax.ppermute(x, axis, perm=[(i, (i + shift) % n) for i in range(n)])  67.6 us
    reduce_scatter x1, waiting for transfers between devices, shards(): lax.psum_scatter(partial_rows, 'wa', scatter_dimension=0, tiled=True)  49.2 us
    all_gather x1, waiting for transfers between devices, shards(): lax.all_gather(gradient_rows.astype(jnp.bfloat16), WIDE, axis=0, tiled=True)  44.3 us
    all_gather x1, waiting for transfers between devices, shards(): grad_cols = lax.all_gather(grad_basis, 'wa', axis=1, tiled=True)  29.5 us
    all_gather x1, waiting for transfers between devices, shards(): eig_full = lax.all_gather(eig_values, WIDE, axis=0, tiled=True)  27.9 us
    dot_general x6, matrix products, score_rows(): jnp.dot(precond, train_grad_rot, preferred_element_type=jnp.float32)  22.2 us
    all_gather x1, waiting for transfers between devices, shards(): grad_all = lax.all_gather(grad_kept, 'wb', axis=1, tiled=True)  15.5 us
    ppermute x9, starting transfers between devices, ring_gather(): lax.ppermute(x, axis, perm=[(i, (i + shift) % n) for i in range(n)])  7.98 us
  transfers between devices with their start and end apart: 15, of which 10 were waited for; matrix products, arithmetic and copies ran while one was open for 8% of the time, Pallas kernels for 0%

profile of v3, /device:TPU:0, one launch (start us, length us, event | category | flops | bytes accessed | tf_op | source)
XLA Modules:
  0.0 309.7 jit_solution(2564485937278151794)
XLA Ops:
  7.4 0.0 copy-start
  7.4 0.0 all-gather.8.cloned.1.call-start
  7.4 0.7 all-gather.8.cloned.1.call-update
  8.1 0.0 all-gather.6.cloned.1.call-start
  8.1 2.5 collective-permute-start.5
  10.6 0.0 collective-permute-start.3
  10.6 1.1 collective-permute-start.4
  11.7 0.0 all-gather.6.cloned.1.call-update
  11.7 0.0 all-gather.10.cloned.1.call-start
  11.7 0.8 collective-permute-start.6
  12.6 0.6 collective-permute-start.7
  13.2 44.6 %collective-permute-done.6 = s32[128]{0:T(128)S(1)} collective-permute-done((s32[128]{0:T(128)}, s32[128]{0:T(128)S(1)}, u32[]{:S(2)}, u32[]{:S(2)}) %collective-permute-start.6) | collective-permute-done | bytes 544 | tf_op jit(solution)/shard_map/ppermute | solution.py:29
  57.8 0.0 collective-permute-start.8
  57.8 0.0 collective-permute-done.7
  57.8 1.4 collective-permute-done.8
  59.3 0.7 fusion.39
  59.9 0.0 collective-permute-done.5
  59.9 0.0 collective-permute-done.3
  59.9 0.0 collective-permute-done.4
  60.0 3.6 %pad_maximum_fusion = bf16[4,128,4096]{2,1,0:T(8,128)(2,1)} fusion(bf16[1,128,4096]{2,1,0:T(8,128)(2,1)S(1)} %bitcast.45, bf16[1,128,4096]{2,1,0:T(8,128)(2,1)} %bitcast.9, bf16[1,128,4096]{2,1,0:T(8,128)(2,1)} %bitcast.8, bf16[1,128,4096]{2,1,0:T(8,128)(2,1)} %bitcast.44), kind=kLoop, calls=%fused_computation.19 | loop fusion | flops 6291456 | bytes 8388608 | tf_op jit(solution)/shard_map/stack | solution.py:30
  63.6 29.5 %all-gather.8.cloned.1.call-done = bf16[4096,512]{1,0:T(8,128)(2,1)} async-done(((bf16[4096,128]{1,0:T(8,128)(2,1)}), bf16[4096,512]{1,0:T(8,128)(2,1)}) %all-gather.8.cloned.1.call-update) | async-done | bytes 4194320 | tf_op jit(solution)/shard_map/all_gather | solution.py:57
  93.1 5.8 %fusion.36 = bf16[512,512]{1,0:T(8,128)(2,1)S(1)} fusion(bf16[512,4096]{1,0:T(8,128)(2,1)} %bitcast.39, bf16[4096,512]{1,0:T(8,128)(2,1)} %all-gather.8.cloned.1.call-done, bf16[512]{0:T(512)(128)(2,1)S(1)} %fusion.39), kind=kOutput, calls=%fused_computation.40 | convolution fusion | flops 2148007936 | bytes 8913920 | tf_op jit(solution)/shard_map/dot_general | solution.py:62
  98.9 1.0 fusion.37
  99.9 0.0 all-gather.10.cloned.1.call-update
  100.0 0.0 reduce-scatter.2.cloned.1.call-start
  100.0 0.0 copy-done.2
  100.0 0.1 collective-permute-start
  100.1 1.5 collective-permute-start.1
  101.6 1.4 collective-permute-start.2
  103.0 10.7 %collective-permute-done = bf16[128,2048]{1,0:T(8,128)(2,1)S(1)} collective-permute-done((bf16[128,2048]{1,0:T(8,128)(2,1)S(1)}, bf16[128,2048]{1,0:T(8,128)(2,1)S(1)}, u32[]{:S(2)}, u32[]{:S(2)}) %collective-permute-start) | collective-permute-done | bytes 524320 | tf_op jit(solution)/shard_map/ppermute | solution.py:29
  113.7 1.2 collective-permute-done.1
  114.9 9.6 %collective-permute-done.2 = bf16[128,2048]{1,0:T(8,128)(2,1)S(1)} collective-permute-done((bf16[128,2048]{1,0:T(8,128)(2,1)S(1)}, bf16[128,2048]{1,0:T(8,128)(2,1)S(1)}, u32[]{:S(2)}, u32[]{:S(2)}) %collective-permute-start.2) | collective-permute-done | bytes 524320 | tf_op jit(solution)/shard_map/ppermute | solution.py:29
  124.5 1.6 pad_maximum_fusion.1
  126.1 2.7 convolution_convert_fusion.1
  128.8 0.1 fusion.38
  128.9 15.5 %all-gather.10.cloned.1.call-done = bf16[512,2048]{1,0:T(8,128)(2,1)} async-done(((bf16[512,512]{1,0:T(8,128)(2,1)}), bf16[512,2048]{1,0:T(8,128)(2,1)}) %all-gather.10.cloned.1.call-update) | async-done | bytes 2097168 | tf_op jit(solution)/shard_map/all_gather | solution.py:69
  144.5 3.7 %fusion.41 = f32[256,2048]{1,0:T(8,128)} fusion(bf16[512,256]{1,0:T(8,128)(2,1)S(1)} %bitcast.42, bf16[512,2048]{1,0:T(8,128)(2,1)} %all-gather.10.cloned.1.call-done), kind=kOutput, calls=%fused_computation.55 | convolution fusion | flops 536870912 | bytes 4456448 | tf_op jit(solution)/shard_map/dot_general | solution.py:70
  148.1 0.0 reduce-scatter.2.cloned.1.call-update
  148.1 0.0 all-gather.14.cloned.1.call-start
  148.2 0.5 all-gather.14.cloned.1.call-update
  148.7 0.2 all-gather.12.cloned.1.call-start
  149.0 49.2 %reduce-scatter.2.cloned.1.call-done = f32[64,2048]{1,0:T(8,128)} async-done(((f32[256,2048]{1,0:T(8,128)}), f32[64,2048]{1,0:T(8,128)}) %reduce-scatter.2.cloned.1.call-update) | async-done | bytes 524304 | tf_op jit(solution)/shard_map/reduce_scatter | solution.py:73
  198.1 1.1 convert_element_type.63
  199.2 0.2 convert_element_type.64
  199.4 0.1 copy.11
  199.5 0.9 convert_element_type.66
  200.4 0.0 all-gather.12.cloned.1.call-update
  200.4 0.0 copy-done.3
  200.4 27.9 %all-gather.14.cloned.1.call-done = bf16[1024,2048]{1,0:T(8,128)(2,1)} async-done(((bf16[64,2048]{1,0:T(8,128)(2,1)}), bf16[1024,2048]{1,0:T(8,128)(2,1)}) %all-gather.14.cloned.1.call-update) | async-done | bytes 4194320 | tf_op jit(solution)/shard_map/all_gather | solution.py:78
  228.3 4.9 %convert_reduce_fusion = f32[]{:T(128)} fusion(bf16[1024,2048]{1,0:T(8,128)(2,1)} %all-gather.14.cloned.1.call-done), kind=kLoop, calls=%fused_computation.6 | loop fusion | flops 4194303 | bytes 4194308 | tf_op jit(solution)/shard_map/reduce_sum | solution.py:80
  234.5 0.0 copy-done.6
  234.6 0.7 fusion.40
  235.2 44.3 %all-gather.12.cloned.1.call-done = bf16[1024,2048]{1,0:T(8,128)(2,1)} async-done(((bf16[64,2048]{1,0:T(8,128)(2,1)}), bf16[1024,2048]{1,0:T(8,128)(2,1)}) %all-gather.12.cloned.1.call-update) | async-done | bytes 4194320 | tf_op jit(solution)/shard_map/all_gather | solution.py:77
  279.6 0.0 copy-done
  279.6 0.0 copy-done.5
  279.6 7.0 %fusion.19 = f32[384]{0:T(512)S(1)} fusion(bf16[1024,384]{1,0:T(8,128)(2,1)S(1)} %copy-done.5, bf16[2048,384]{1,0:T(8,128)(2,1)S(1)} %copy-done, bf16[1024,2048]{1,0:T(8,128)(2,1)} %all-gather.12.cloned.1.call-done, bf16[1024,2048]{1,0:T(8,128)(2,1)} %all-gather.14.cloned.1.call-done, f32[]{:T(128)} %bitcast.21), kind=kOutput, calls=%fused_computation.34 | convolution fusion | flops 1622277760 | bytes 10749444 | tf_op jit(solution)/shard_map/dot_general | solution.py:20
  286.6 0.0 copy-done.1
  286.6 0.0 copy-done.4
  286.6 3.1 fusion.20
  289.7 3.0 fusion.21
  292.7 3.0 fusion.22
  295.7 3.3 %fusion.23 = f32[384]{0:T(512)S(1)} fusion(bf16[1024,384]{1,0:T(8,128)(2,1)S(1)} %copy-done.5, bf16[2048,384]{1,0:T(8,128)(2,1)S(1)} %copy-done, bf16[1024,2048]{1,0:T(8,128)(2,1)S(1)} %copy-done.4, bf16[1024,2048]{1,0:T(8,128)(2,1)S(1)} %copy-done.1, f32[]{:T(128)} %bitcast.25), kind=kOutput, calls=%fused_computation.38 | convolution fusion | flops 1622277760 | bytes 10749444 | tf_op jit(solution)/shard_map/dot_general | solution.py:20
  299.0 2.9 fusion.18
  301.9 0.6 multiply_multiply_fusion
  (18 shorter events, 0.1 us)
Async XLA Ops:
  7.4 272.2 %copy-start = (bf16[2048,384]{1,0:T(8,128)(2,1)S(1)}, bf16[2048,384]{1,0:T(8,128)(2,1)}, u32[]{:S(2)}) copy-start(bf16[2048,384]{1,0:T(8,128)(2,1)} %param.18) | copy-start | bytes 4718596
  7.4 85.7 %all-gather.8.cloned.1.call-start = ((), (), s32[]{:S(2)}) async-start(), calls=%async_computation.2 | async-start | bytes 5242880 | tf_op jit(solution)/shard_map/all_gather | solution.py:57
  8.1 118.0 %all-gather.6.cloned.1.call-start = ((), (), s32[]{:S(2)}) async-start(), calls=%async_computation.1 | async-start | bytes 1310720 | tf_op jit(solution)/shard_map/all_gather | solution.py:56
  8.1 51.8 %collective-permute-start.5 = (bf16[128,4096]{1,0:T(8,128)(2,1)}, bf16[128,4096]{1,0:T(8,128)(2,1)S(1)}, u32[]{:S(2)}, u32[]{:S(2)}) collective-permute-start(bf16[128,4096]{1,0:T(8,128)(2,1)} %param.11), channel_id=1, source_target_pairs={{0,3},{1,0},{2,1},{3,2},{4,7},{5,4},{6,5},{7,6},{8,11},{9,8},{10,9... | collective-permute-start | bytes 3145736 | tf_op jit(solution)/shard_map/ppermute | solution.py:29
  10.6 49.3 %collective-permute-start.3 = (bf16[128,4096]{1,0:T(8,128)(2,1)}, bf16[128,4096]{1,0:T(8,128)(2,1)}, u32[]{:S(2)}, u32[]{:S(2)}) collective-permute-start(bf16[128,4096]{1,0:T(8,128)(2,1)} %param.11), channel_id=1, source_target_pairs={{0,1},{1,2},{2,3},{3,0},{4,5},{5,6},{6,7},{7,4},{8,9},{9,10},{10,1... | collective-permute-start | bytes 3145736 | tf_op jit(solution)/shard_map/ppermute | solution.py:29
  10.6 49.4 %collective-permute-start.4 = (bf16[128,4096]{1,0:T(8,128)(2,1)}, bf16[128,4096]{1,0:T(8,128)(2,1)}, u32[]{:S(2)}, u32[]{:S(2)}) collective-permute-start(bf16[128,4096]{1,0:T(8,128)(2,1)} %param.11), channel_id=1, source_target_pairs={{0,2},{1,3},{2,0},{3,1},{4,6},{5,7},{6,4},{7,5},{8,10},{9,11},{10,... | collective-permute-start | bytes 3145736 | tf_op jit(solution)/shard_map/ppermute | solution.py:29
  11.7 132.8 %all-gather.10.cloned.1.call-start = ((), (), s32[]{:S(2)}) async-start(), calls=%async_computation.3 | async-start | bytes 2621440 | tf_op jit(solution)/shard_map/all_gather | solution.py:69
  11.7 46.1 %collective-permute-start.6 = (s32[128]{0:T(128)}, s32[128]{0:T(128)S(1)}, u32[]{:S(2)}, u32[]{:S(2)}) collective-permute-start(s32[128]{0:T(128)} %param.12), channel_id=1, source_target_pairs={{0,1},{1,2},{2,3},{3,0},{4,5},{5,6},{6,7},{7,4},{8,9},{9,10},{10,1... | collective-permute-start | bytes 1544 | tf_op jit(solution)/shard_map/ppermute | solution.py:29
  12.6 45.3 %collective-permute-start.7 = (s32[128]{0:T(128)}, s32[128]{0:T(128)S(1)}, u32[]{:S(2)}, u32[]{:S(2)}) collective-permute-start(s32[128]{0:T(128)} %param.12), channel_id=1, source_target_pairs={{0,2},{1,3},{2,0},{3,1},{4,6},{5,7},{6,4},{7,5},{8,10},{9,11},{10,... | collective-permute-start | bytes 1544 | tf_op jit(solution)/shard_map/ppermute | solution.py:29
  57.8 1.4 collective-permute-start.8
  93.1 7.0 %copy-start.2 = (bf16[128,2048]{1,0:T(8,128)(2,1)S(1)}, bf16[128,2048]{1,0:T(8,128)(2,1)}, u32[]{:S(2)}) copy-start(bf16[128,2048]{1,0:T(8,128)(2,1)} %param.10) | copy-start | bytes 1572868
  100.0 98.2 %reduce-scatter.2.cloned.1.call-start = ((), (), s32[]{:S(2)}) async-start(), calls=%async_computation.4 | async-start | bytes 2621440 | tf_op jit(solution)/shard_map/reduce_scatter | solution.py:73
  100.0 13.7 %collective-permute-start = (bf16[128,2048]{1,0:T(8,128)(2,1)S(1)}, bf16[128,2048]{1,0:T(8,128)(2,1)S(1)}, u32[]{:S(2)}, u32[]{:S(2)}) collective-permute-start(bf16[128,2048]{1,0:T(8,128)(2,1)S(1)} %copy-done.2), channel_id=1, source_target_pairs={{0,1},{1,2},{2,3},{3,0},{4,5},{5,6},{6,7},{7,4},{8,9},{9,10},{10,1... | collective-permute-start | bytes 1572872 | tf_op jit(solution)/shard_map/ppermute | solution.py:29
  100.1 14.8 %collective-permute-start.1 = (bf16[128,2048]{1,0:T(8,128)(2,1)S(1)}, bf16[128,2048]{1,0:T(8,128)(2,1)S(1)}, u32[]{:S(2)}, u32[]{:S(2)}) collective-permute-start(bf16[128,2048]{1,0:T(8,128)(2,1)S(1)} %copy-done.2), channel_id=1, source_target_pairs={{0,2},{1,3},{2,0},{3,1},{4,6},{5,7},{6,4},{7,5},{8,10},{9,11},{10,... | collective-permute-start | bytes 1572872 | tf_op jit(solution)/shard_map/ppermute | solution.py:29
  101.6 22.9 %collective-permute-start.2 = (bf16[128,2048]{1,0:T(8,128)(2,1)S(1)}, bf16[128,2048]{1,0:T(8,128)(2,1)S(1)}, u32[]{:S(2)}, u32[]{:S(2)}) collective-permute-start(bf16[128,2048]{1,0:T(8,128)(2,1)S(1)} %copy-done.2), channel_id=1, source_target_pairs={{0,3},{1,0},{2,1},{3,2},{4,7},{5,4},{6,5},{7,6},{8,11},{9,8},{10,9... | collective-permute-start | bytes 1572872 | tf_op jit(solution)/shard_map/ppermute | solution.py:29
  144.5 56.0 %copy-start.3 = (s32[384]{0:T(512)S(1)}, s32[384]{0:T(512)}, u32[]{:S(2)}) copy-start(s32[384]{0:T(512)} %param.19) | copy-start | bytes 4612
  148.1 86.4 %copy-start.6 = (s32[6]{0:T(128)S(1)}, s32[6]{0:T(128)}, u32[]{:S(2)}) copy-start(s32[6]{0:T(128)} %param.16) | copy-start | bytes 76
  148.1 131.5 %copy-start.5 = (bf16[1024,384]{1,0:T(8,128)(2,1)S(1)}, bf16[1024,384]{1,0:T(8,128)(2,1)}, u32[]{:S(2)}) copy-start(bf16[1024,384]{1,0:T(8,128)(2,1)} %param.17) | copy-start | bytes 2359300
  148.1 80.2 %all-gather.14.cloned.1.call-start = ((), (), s32[]{:S(2)}) async-start(), calls=%async_computation.6 | async-start | bytes 4456448 | tf_op jit(solution)/shard_map/all_gather | solution.py:78
  148.7 130.8 %all-gather.12.cloned.1.call-start = ((), (), s32[]{:S(2)}) async-start(), calls=%async_computation.5 | async-start | bytes 4456448 | tf_op jit(solution)/shard_map/all_gather | solution.py:77
  279.6 7.0 %copy-start.1 = (bf16[1024,2048]{1,0:T(8,128)(2,1)S(1)}, bf16[1024,2048]{1,0:T(8,128)(2,1)}, u32[]{:S(2)}) copy-start(bf16[1024,2048]{1,0:T(8,128)(2,1)} %all-gather.14.cloned.1.call-done) | copy-start | bytes 12582916
  279.6 7.0 %copy-start.4 = (bf16[1024,2048]{1,0:T(8,128)(2,1)S(1)}, bf16[1024,2048]{1,0:T(8,128)(2,1)}, u32[]{:S(2)}) copy-start(bf16[1024,2048]{1,0:T(8,128)(2,1)} %all-gather.12.cloned.1.call-done) | copy-start | bytes 12582916
Sparse Core Ops, SparseCore 0:
  9.8 83.2 all-gather.7
  94.6 26.0 all-gather.5
  122.3 22.0 all-gather.9
  148.3 49.8 reduce-scatter.1
Sparse Core Ops, SparseCore 1:
  150.8 77.5 all-gather.13
  230.6 48.9 all-gather.11

commit v4 on v3

--- a/solution.py
+++ b/solution.py
@@ -7,7 +7,9 @@
 from jax.sharding import PartitionSpec as P
 
 PROMPT = 1024
-WIDE = ("wa", "wb")
+WIDE = ("wa", "wy", "wc")
+TOKENS = ("wy", "wc")
+LINKS = ("wa", "wy")
 
 
 def score_rows(grad_rows, eig_rows, dampings, train_act_rot, train_grad_rot):
@@ -49,10 +51,10 @@
     train_grad_rot,
     train_positions,
 ):
-    nb = lax.axis_size("wb")
-    act_tokens = ring_gather(query_act, "wb")
-    grad_tokens = ring_gather(query_grad, "wb")
-    positions = ring_gather(query_positions, "wb")
+    nb = lax.axis_size(TOKENS)
+    act_tokens = ring_gather(query_act, TOKENS)
+    grad_tokens = ring_gather(query_grad, TOKENS)
+    positions = ring_gather(query_positions, TOKENS)
     act_cols = lax.all_gather(act_basis, "wa", axis=1, tiled=True)
     grad_cols = lax.all_gather(grad_basis, "wa", axis=1, tiled=True)
     count = query_act.shape[0]
@@ -64,9 +66,9 @@
     ).astype(jnp.bfloat16)
     query_weight = jnp.where(positions.reshape(-1) >= PROMPT, 1.0, 0.0).astype(jnp.bfloat16)
     grad_kept = grad_rot * query_weight[:, None]
-    act_rot = natural_order(act_rot.reshape(nb, count, -1), "wb").reshape(nb * count, -1)
-    grad_kept = natural_order(grad_kept.reshape(nb, count, -1), "wb").reshape(nb * count, -1)
-    grad_all = lax.all_gather(grad_kept, "wb", axis=1, tiled=True)
+    act_rot = natural_order(act_rot.reshape(nb, count, -1), TOKENS).reshape(nb * count, -1)
+    grad_kept = natural_order(grad_kept.reshape(nb, count, -1), TOKENS).reshape(nb * count, -1)
+    grad_all = lax.all_gather(grad_kept, TOKENS, axis=1, tiled=True)
     partial_rows = lax.dot_general(
         act_rot, grad_all, (((0,), (0,)), ((), ())), preferred_element_type=jnp.float32
     )
@@ -74,12 +76,24 @@
     na = lax.axis_size("wa")
     rows = gradient_rows.shape[0]
     gradient_rows = gradient_rows.reshape(rows, nb, na, -1).transpose(0, 2, 1, 3).reshape(rows, -1)
-    query_gradient = lax.all_gather(gradient_rows.astype(jnp.bfloat16), WIDE, axis=0, tiled=True)
-    eig_full = lax.all_gather(eig_values, WIDE, axis=0, tiled=True)
+    query_gradient = lax.all_gather(
+        lax.all_gather(gradient_rows.astype(jnp.bfloat16), LINKS, axis=0, tiled=True),
+        "wc", axis=0, tiled=True,
+    )
+    eig_full = lax.all_gather(
+        lax.all_gather(eig_values, LINKS, axis=0, tiled=True), "wc", axis=0, tiled=True
+    )
     eig_in, eig_out = eig_full.shape
     mean_eig = jnp.sum(eig_full.astype(jnp.float32)) / (eig_in * eig_out)
     dampings = mean_eig * jnp.exp2(damping_index.astype(jnp.float32) - 4.0)
-    totals = score_rows(query_gradient, eig_full, dampings, train_act_rot, train_grad_rot)
+    cores = lax.axis_size("wc")
+    block = eig_values.shape[0]
+    acts_order = (
+        train_act_rot.reshape(eig_in // (cores * block), cores, block, -1)
+        .transpose(1, 0, 2, 3)
+        .reshape(eig_in, -1)
+    )
+    totals = score_rows(query_gradient, eig_full, dampings, acts_order, train_grad_rot)
     query_count = query_act.shape[0] * lax.axis_size(WIDE)
     factor = mean_eig * (1.0 / math.sqrt(float(query_count) * eig_in * eig_out))
     train_weight = jnp.where(train_positions >= PROMPT, 1.0, 0.0).astype(jnp.float32)
@@ -96,7 +110,8 @@
 def solution(mesh):
     groups, wide = mesh.devices.shape
     wa, wb = split_wide(wide)
-    grid = Mesh(mesh.devices.reshape(groups, wa, wb), ("groups",) + WIDE)
+    wc = 2 if wb % 2 == 0 else 1
+    grid = Mesh(mesh.devices.reshape(groups, wa, wb // wc, wc), ("groups",) + WIDE)
     tokens = ("groups",) + WIDE
     in_specs = (
         P(tokens, None),

time: 310 us -> 338 us (1.090)
  waiting for transfers between devices: 235 us -> 261 us
    all_gather x3 -> x5, waiting for transfers between devices: 87.7 us -> 113 us  [the longest x1 49.7 us: shards(): lax.all_gather(gradient_rows.astype(jnp.bfloat16), LINKS, axis=0, tiled=T...]
  transfers between devices with their start and end apart: 15 -> 17, of which waited for: 10 -> 12; matrix products, arithmetic and copies ran while one was open for 8% -> 7% of each run, Pallas kernels for 0% -> 0%
where the time goes in v4:
time: 338 us; the launch traced here: 337 us
  waiting for transfers between devices  261 us (77%)
  matrix products  34.3 us (10%)
  between operations  16.4 us (5%)
  other arithmetic  13.6 us (4%)
  starting transfers between devices  8.45 us (2%)
    ppermute x9, waiting for transfers between devices, ring_gather(): lax.ppermute(x, axis, perm=[(i, (i + shift) % n) for i in range(n)])  67.6 us
    all_gather x1, waiting for transfers between devices, shards(): lax.all_gather(gradient_rows.astype(jnp.bfloat16), LINKS, axis=0, tiled=T...  49.7 us
    reduce_scatter x1, waiting for transfers between devices, shards(): lax.psum_scatter(partial_rows, 'wa', scatter_dimension=0, tiled=True)  49.3 us
    all_gather x1, waiting for transfers between devices, shards(): grad_cols = lax.all_gather(grad_basis, 'wa', axis=1, tiled=True)  29.5 us
    all_gather x1, waiting for transfers between devices, shards(): lax.all_gather(eig_values, LINKS, axis=0, tiled=True)  26.6 us
    dot_general x6, matrix products, score_rows(): jnp.dot(precond, train_grad_rot, preferred_element_type=jnp.float32)  22.2 us
    all_gather x1, waiting for transfers between devices, shards(): grad_all = lax.all_gather(grad_kept, TOKENS, axis=1, tiled=True)  15.5 us
    all_gather x1, waiting for transfers between devices, shards(): lax.all_gather(lax.all_gather(eig_values, LINKS, axis=0, tiled=True), 'wc...  12.2 us
  transfers between devices with their start and end apart: 17, of which 12 were waited for; matrix products, arithmetic and copies ran while one was open for 7% of the time, Pallas kernels for 0%

profile of v4, /device:TPU:0, one launch (start us, length us, event | category | flops | bytes accessed | tf_op | source)
XLA Modules:
  0.0 337.2 jit_solution(14879517503798340455)
XLA Ops:
  7.4 0.0 copy-start
  7.4 0.7 all-gather.10.cloned.1.call-update
  8.1 0.0 all-gather.8.cloned.1.call-start
  8.1 2.5 collective-permute-start.5
  10.6 0.0 collective-permute-start.3
  10.6 1.1 collective-permute-start.4
  11.7 0.0 all-gather.8.cloned.1.call-update
  11.7 0.0 all-gather.12.cloned.1.call-start
  11.7 0.8 collective-permute-start.6
  12.6 0.6 collective-permute-start.7
  13.2 44.6 %collective-permute-done.6 = s32[128]{0:T(128)S(1)} collective-permute-done((s32[128]{0:T(128)}, s32[128]{0:T(128)S(1)}, u32[]{:S(2)}, u32[]{:S(2)}) %collective-permute-start.6) | collective-permute-done | bytes 544 | tf_op jit(solution)/shard_map/ppermute | solution.py:31
  57.8 0.0 collective-permute-start.8
  57.8 0.0 collective-permute-done.7
  57.8 1.4 collective-permute-done.8
  59.3 0.7 fusion.39
  59.9 0.0 collective-permute-done.5
  59.9 0.0 collective-permute-done.3
  59.9 0.0 collective-permute-done.4
  60.0 3.6 %pad_maximum_fusion = bf16[4,128,4096]{2,1,0:T(8,128)(2,1)} fusion(bf16[1,128,4096]{2,1,0:T(8,128)(2,1)S(1)} %bitcast.68, bf16[1,128,4096]{2,1,0:T(8,128)(2,1)} %bitcast.9, bf16[1,128,4096]{2,1,0:T(8,128)(2,1)} %bitcast.8, bf16[1,128,4096]{2,1,0:T(8,128)(2,1)} %bitcast.67), kind=kLoop, calls=%fused_computation.19 | loop fusion | flops 6291456 | bytes 8388608 | tf_op jit(solution)/shard_map/stack | solution.py:32
  63.6 29.5 %all-gather.10.cloned.1.call-done = bf16[4096,512]{1,0:T(8,128)(2,1)} async-done(((bf16[4096,128]{1,0:T(8,128)(2,1)}), bf16[4096,512]{1,0:T(8,128)(2,1)}) %all-gather.10.cloned.1.call-update) | async-done | bytes 4194320 | tf_op jit(solution)/shard_map/all_gather | solution.py:59
  93.1 5.8 %fusion.36 = bf16[512,512]{1,0:T(8,128)(2,1)S(1)} fusion(bf16[512,4096]{1,0:T(8,128)(2,1)} %bitcast.62, bf16[4096,512]{1,0:T(8,128)(2,1)} %all-gather.10.cloned.1.call-done, bf16[512]{0:T(512)(128)(2,1)S(1)} %fusion.39), kind=kOutput, calls=%fused_computation.40 | convolution fusion | flops 2148007936 | bytes 8913920 | tf_op jit(solution)/shard_map/dot_general | solution.py:64
  98.9 1.0 fusion.37
  99.9 0.0 all-gather.12.cloned.1.call-update
  100.0 0.0 reduce-scatter.2.cloned.1.call-start
  100.0 0.1 collective-permute-start
  100.1 1.5 collective-permute-start.1
  101.6 1.4 collective-permute-start.2
  103.0 10.7 %collective-permute-done = bf16[128,2048]{1,0:T(8,128)(2,1)S(1)} collective-permute-done((bf16[128,2048]{1,0:T(8,128)(2,1)S(1)}, bf16[128,2048]{1,0:T(8,128)(2,1)S(1)}, u32[]{:S(2)}, u32[]{:S(2)}) %collective-permute-start) | collective-permute-done | bytes 524320 | tf_op jit(solution)/shard_map/ppermute | solution.py:31
  113.7 1.2 collective-permute-done.1
  114.9 9.6 %collective-permute-done.2 = bf16[128,2048]{1,0:T(8,128)(2,1)S(1)} collective-permute-done((bf16[128,2048]{1,0:T(8,128)(2,1)S(1)}, bf16[128,2048]{1,0:T(8,128)(2,1)S(1)}, u32[]{:S(2)}, u32[]{:S(2)}) %collective-permute-start.2) | collective-permute-done | bytes 524320 | tf_op jit(solution)/shard_map/ppermute | solution.py:31
  124.5 1.6 pad_maximum_fusion.1
  126.1 2.7 convolution_convert_fusion.1
  128.8 0.1 fusion.38
  129.0 15.5 %all-gather.12.cloned.1.call-done = bf16[512,2048]{1,0:T(8,128)(2,1)} async-done(((bf16[512,512]{1,0:T(8,128)(2,1)}), bf16[512,2048]{1,0:T(8,128)(2,1)}) %all-gather.12.cloned.1.call-update) | async-done | bytes 2097168 | tf_op jit(solution)/shard_map/all_gather | solution.py:71
  144.5 3.7 %fusion.41 = f32[256,2048]{1,0:T(8,128)} fusion(bf16[512,256]{1,0:T(8,128)(2,1)S(1)} %bitcast.65, bf16[512,2048]{1,0:T(8,128)(2,1)} %all-gather.12.cloned.1.call-done), kind=kOutput, calls=%fused_computation.55 | convolution fusion | flops 536870912 | bytes 4456448 | tf_op jit(solution)/shard_map/dot_general | solution.py:72
  148.1 0.0 reduce-scatter.2.cloned.1.call-update
  148.1 0.0 all-gather.18.cloned.1.call-start
  148.2 0.5 all-gather.18.cloned.1.call-update
  148.7 0.0 all-gather.14.cloned.1.call-start
  148.8 49.3 %reduce-scatter.2.cloned.1.call-done = f32[64,2048]{1,0:T(8,128)} async-done(((f32[256,2048]{1,0:T(8,128)}), f32[64,2048]{1,0:T(8,128)}) %reduce-scatter.2.cloned.1.call-update) | async-done | bytes 524304 | tf_op jit(solution)/shard_map/reduce_scatter | solution.py:75
  198.1 1.1 convert_element_type.72
  199.2 0.0 copy-start.3
  199.2 0.2 convert_element_type.73
  199.4 0.1 copy.11
  199.5 0.9 convert_element_type.75
  200.4 0.0 all-gather.14.cloned.1.call-update
  200.4 0.0 all-gather.20.cloned.1.call-start
  200.4 26.6 %all-gather.18.cloned.1.call-done = bf16[512,2048]{1,0:T(8,128)(2,1)} async-done(((bf16[64,2048]{1,0:T(8,128)(2,1)}), bf16[512,2048]{1,0:T(8,128)(2,1)}) %all-gather.18.cloned.1.call-update) | async-done | bytes 2097168 | tf_op jit(solution)/shard_map/all_gather | solution.py:84
  227.0 0.0 all-gather.20.cloned.1.call-update
  227.0 0.2 all-gather.16.cloned.1.call-start
  227.3 49.7 %all-gather.14.cloned.1.call-done = bf16[512,2048]{1,0:T(8,128)(2,1)} async-done(((bf16[64,2048]{1,0:T(8,128)(2,1)}), bf16[512,2048]{1,0:T(8,128)(2,1)}) %all-gather.14.cloned.1.call-update) | async-done | bytes 2097168 | tf_op jit(solution)/shard_map/all_gather | solution.py:80
  277.0 0.0 all-gather.16.cloned.1.call-update
  277.0 1.3 copy.12
  278.3 12.2 %all-gather.20.cloned.1.call-done = bf16[1024,2048]{1,0:T(8,128)(2,1)} async-done(((bf16[512,2048]{1,0:T(8,128)(2,1)}), bf16[1024,2048]{1,0:T(8,128)(2,1)}) %all-gather.20.cloned.1.call-update) | async-done | bytes 4194320 | tf_op jit(solution)/shard_map/all_gather | solution.py:83
  290.5 4.9 %convert_reduce_fusion = f32[]{:T(128)} fusion(bf16[1024,2048]{1,0:T(8,128)(2,1)} %all-gather.20.cloned.1.call-done), kind=kLoop, calls=%fused_computation.6 | loop fusion | flops 4194303 | bytes 4194308 | tf_op jit(solution)/shard_map/reduce_sum | solution.py:87
  296.8 0.7 fusion.40
  297.5 9.5 %all-gather.16.cloned.1.call-done = bf16[1024,2048]{1,0:T(8,128)(2,1)} async-done(((bf16[512,2048]{1,0:T(8,128)(2,1)}), bf16[1024,2048]{1,0:T(8,128)(2,1)}) %all-gather.16.cloned.1.call-update) | async-done | bytes 4194320 | tf_op jit(solution)/shard_map/all_gather | solution.py:79
  307.0 7.0 %fusion.23 = f32[384]{0:T(512)S(1)} fusion(f32[8,2,64,384]{3,2,0,1:T(8,128)S(1)} %copy.12, bf16[2048,384]{1,0:T(8,128)(2,1)S(1)} %copy-done, bf16[1024,2048]{1,0:T(8,128)(2,1)} %all-gather.16.cloned.1.call-done, bf16[1024,2048]{1,0:T(8,128)(2,1)} %all-gather.20.cloned.1.call-done, f32[]{:T(128)} %bitcast.29), kind=kOutput, calls=%fused_computation.38 | convolution fusion | flops 1621884544 | bytes 11535876 | tf_op jit(solution)/shard_map/dot_general | solution.py:22
  314.0 3.0 fusion.22
  317.0 3.0 fusion.21
  320.1 3.0 fusion.20
  323.0 3.2 fusion.19
  326.2 3.0 fusion.18
  329.2 0.6 multiply_multiply_fusion
  (23 shorter events, 0.1 us)
Async XLA Ops:
  7.4 299.6 %copy-start = (bf16[2048,384]{1,0:T(8,128)(2,1)S(1)}, bf16[2048,384]{1,0:T(8,128)(2,1)}, u32[]{:S(2)}) copy-start(bf16[2048,384]{1,0:T(8,128)(2,1)} %param.18) | copy-start | bytes 4718596
  7.4 85.7 %all-gather.10.cloned.1.call-start = ((), (), s32[]{:S(2)}) async-start(), calls=%async_computation.2 | async-start | bytes 5242880 | tf_op jit(solution)/shard_map/all_gather | solution.py:59
  8.1 118.0 %all-gather.8.cloned.1.call-start = ((), (), s32[]{:S(2)}) async-start(), calls=%async_computation.1 | async-start | bytes 1310720 | tf_op jit(solution)/shard_map/all_gather | solution.py:58
  8.1 51.8 %collective-permute-start.5 = (bf16[128,4096]{1,0:T(8,128)(2,1)}, bf16[128,4096]{1,0:T(8,128)(2,1)S(1)}, u32[]{:S(2)}, u32[]{:S(2)}) collective-permute-start(bf16[128,4096]{1,0:T(8,128)(2,1)} %param.11), channel_id=1, source_target_pairs={{0,3},{1,0},{2,1},{3,2},{4,7},{5,4},{6,5},{7,6},{8,11},{9,8},{10,9... | collective-permute-start | bytes 3145736 | tf_op jit(solution)/shard_map/ppermute | solution.py:31
  10.6 49.3 %collective-permute-start.3 = (bf16[128,4096]{1,0:T(8,128)(2,1)}, bf16[128,4096]{1,0:T(8,128)(2,1)}, u32[]{:S(2)}, u32[]{:S(2)}) collective-permute-start(bf16[128,4096]{1,0:T(8,128)(2,1)} %param.11), channel_id=1, source_target_pairs={{0,1},{1,2},{2,3},{3,0},{4,5},{5,6},{6,7},{7,4},{8,9},{9,10},{10,1... | collective-permute-start | bytes 3145736 | tf_op jit(solution)/shard_map/ppermute | solution.py:31
  10.6 49.4 %collective-permute-start.4 = (bf16[128,4096]{1,0:T(8,128)(2,1)}, bf16[128,4096]{1,0:T(8,128)(2,1)}, u32[]{:S(2)}, u32[]{:S(2)}) collective-permute-start(bf16[128,4096]{1,0:T(8,128)(2,1)} %param.11), channel_id=1, source_target_pairs={{0,2},{1,3},{2,0},{3,1},{4,6},{5,7},{6,4},{7,5},{8,10},{9,11},{10,... | collective-permute-start | bytes 3145736 | tf_op jit(solution)/shard_map/ppermute | solution.py:31
  11.7 132.8 %all-gather.12.cloned.1.call-start = ((), (), s32[]{:S(2)}) async-start(), calls=%async_computation.3 | async-start | bytes 2621440 | tf_op jit(solution)/shard_map/all_gather | solution.py:71
  11.7 46.1 %collective-permute-start.6 = (s32[128]{0:T(128)}, s32[128]{0:T(128)S(1)}, u32[]{:S(2)}, u32[]{:S(2)}) collective-permute-start(s32[128]{0:T(128)} %param.12), channel_id=1, source_target_pairs={{0,1},{1,2},{2,3},{3,0},{4,5},{5,6},{6,7},{7,4},{8,9},{9,10},{10,1... | collective-permute-start | bytes 1544 | tf_op jit(solution)/shard_map/ppermute | solution.py:31
  12.6 45.3 %collective-permute-start.7 = (s32[128]{0:T(128)}, s32[128]{0:T(128)S(1)}, u32[]{:S(2)}, u32[]{:S(2)}) collective-permute-start(s32[128]{0:T(128)} %param.12), channel_id=1, source_target_pairs={{0,2},{1,3},{2,0},{3,1},{4,6},{5,7},{6,4},{7,5},{8,10},{9,11},{10,... | collective-permute-start | bytes 1544 | tf_op jit(solution)/shard_map/ppermute | solution.py:31
  57.8 1.4 collective-permute-start.8
  93.1 7.0 %copy-start.2 = (bf16[128,2048]{1,0:T(8,128)(2,1)S(1)}, bf16[128,2048]{1,0:T(8,128)(2,1)}, u32[]{:S(2)}) copy-start(bf16[128,2048]{1,0:T(8,128)(2,1)} %param.10) | copy-start | bytes 1572868
  100.0 98.1 %reduce-scatter.2.cloned.1.call-start = ((), (), s32[]{:S(2)}) async-start(), calls=%async_computation.4 | async-start | bytes 2621440 | tf_op jit(solution)/shard_map/reduce_scatter | solution.py:75
  100.0 13.7 %collective-permute-start = (bf16[128,2048]{1,0:T(8,128)(2,1)S(1)}, bf16[128,2048]{1,0:T(8,128)(2,1)S(1)}, u32[]{:S(2)}, u32[]{:S(2)}) collective-permute-start(bf16[128,2048]{1,0:T(8,128)(2,1)S(1)} %copy-done.2), channel_id=1, source_target_pairs={{0,1},{1,2},{2,3},{3,0},{4,5},{5,6},{6,7},{7,4},{8,9},{9,10},{10,1... | collective-permute-start | bytes 1572872 | tf_op jit(solution)/shard_map/ppermute | solution.py:31
  100.1 14.8 %collective-permute-start.1 = (bf16[128,2048]{1,0:T(8,128)(2,1)S(1)}, bf16[128,2048]{1,0:T(8,128)(2,1)S(1)}, u32[]{:S(2)}, u32[]{:S(2)}) collective-permute-start(bf16[128,2048]{1,0:T(8,128)(2,1)S(1)} %copy-done.2), channel_id=1, source_target_pairs={{0,2},{1,3},{2,0},{3,1},{4,6},{5,7},{6,4},{7,5},{8,10},{9,11},{10,... | collective-permute-start | bytes 1572872 | tf_op jit(solution)/shard_map/ppermute | solution.py:31
  101.6 22.9 %collective-permute-start.2 = (bf16[128,2048]{1,0:T(8,128)(2,1)S(1)}, bf16[128,2048]{1,0:T(8,128)(2,1)S(1)}, u32[]{:S(2)}, u32[]{:S(2)}) collective-permute-start(bf16[128,2048]{1,0:T(8,128)(2,1)S(1)} %copy-done.2), channel_id=1, source_target_pairs={{0,3},{1,0},{2,1},{3,2},{4,7},{5,4},{6,5},{7,6},{8,11},{9,8},{10,9... | collective-permute-start | bytes 1572872 | tf_op jit(solution)/shard_map/ppermute | solution.py:31
  148.1 78.9 %all-gather.18.cloned.1.call-start = ((), (), s32[]{:S(2)}) async-start(), calls=%async_computation.7 | async-start | bytes 2359296 | tf_op jit(solution)/shard_map/all_gather | solution.py:84
  148.7 128.3 %all-gather.14.cloned.1.call-start = ((), (), s32[]{:S(2)}) async-start(), calls=%async_computation.5 | async-start | bytes 2359296 | tf_op jit(solution)/shard_map/all_gather | solution.py:80
  199.2 79.1 %copy-start.3 = (s32[384]{0:T(512)S(1)}, s32[384]{0:T(512)}, u32[]{:S(2)}) copy-start(s32[384]{0:T(512)} %param.19) | copy-start | bytes 4612
  200.4 90.1 %all-gather.20.cloned.1.call-start = ((), (), s32[]{:S(2)}) async-start(), calls=%async_computation.8 | async-start | bytes 6291456 | tf_op jit(solution)/shard_map/all_gather | solution.py:83
  227.0 79.9 %all-gather.16.cloned.1.call-start = ((), (), s32[]{:S(2)}) async-start(), calls=%async_computation.6 | async-start | bytes 6291456 | tf_op jit(solution)/shard_map/all_gather | solution.py:79
  277.0 19.8 %copy-start.5 = (s32[6]{0:T(128)S(1)}, s32[6]{0:T(128)}, u32[]{:S(2)}) copy-start(s32[6]{0:T(128)} %param.16) | copy-start | bytes 76
  306.9 7.0 %copy-start.1 = (bf16[1024,2048]{1,0:T(8,128)(2,1)S(1)}, bf16[1024,2048]{1,0:T(8,128)(2,1)}, u32[]{:S(2)}) copy-start(bf16[1024,2048]{1,0:T(8,128)(2,1)} %all-gather.20.cloned.1.call-done) | copy-start | bytes 12582916
  306.9 7.0 %copy-start.4 = (bf16[1024,2048]{1,0:T(8,128)(2,1)S(1)}, bf16[1024,2048]{1,0:T(8,128)(2,1)}, u32[]{:S(2)}) copy-start(bf16[1024,2048]{1,0:T(8,128)(2,1)} %all-gather.16.cloned.1.call-done) | copy-start | bytes 12582916
Sparse Core Ops, SparseCore 0:
  9.8 83.2 all-gather.9
  94.6 26.0 all-gather.7
  122.3 22.0 all-gather.11
  148.2 49.8 reduce-scatter.1
Sparse Core Ops, SparseCore 1:
  150.7 76.2 all-gather.17
  229.2 47.7 all-gather.13
  278.5 12.0 all-gather.19
  292.2 14.7 all-gather.15

commit v5 on v3

--- a/solution.py
+++ b/solution.py
@@ -75,8 +75,13 @@
     rows = gradient_rows.shape[0]
     gradient_rows = gradient_rows.reshape(rows, nb, na, -1).transpose(0, 2, 1, 3).reshape(rows, -1)
     query_gradient = lax.all_gather(gradient_rows.astype(jnp.bfloat16), WIDE, axis=0, tiled=True)
-    eig_full = lax.all_gather(eig_values, WIDE, axis=0, tiled=True)
-    eig_in, eig_out = eig_full.shape
+    group_count = lax.axis_size("groups")
+    eig_in, eig_out = eig_values.shape[0] * lax.axis_size(WIDE), eig_values.shape[1]
+    width = eig_out // group_count
+    my_cols = lax.dynamic_slice_in_dim(eig_values, lax.axis_index("groups") * width, width, axis=1)
+    eig_part = lax.all_gather(my_cols, WIDE, axis=0, tiled=True)
+    eig_parts = natural_order(ring_gather(eig_part, "groups"), "groups")
+    eig_full = eig_parts.transpose(1, 0, 2).reshape(eig_in, eig_out)
     mean_eig = jnp.sum(eig_full.astype(jnp.float32)) / (eig_in * eig_out)
     dampings = mean_eig * jnp.exp2(damping_index.astype(jnp.float32) - 4.0)
     totals = score_rows(query_gradient, eig_full, dampings, train_act_rot, train_grad_rot)

time: 310 us -> 396 us (1.28)
  local copies, waits for them, and re-layouts: 1.99 us -> 66.2 us
  other arithmetic: 13.6 us -> 42.2 us
  waiting for transfers between devices: 235 us -> 225 us
    add x0 -> x6, local copies, waits for them, and re-layouts: none -> 55 us  [score_rows(): precond = (grad_wide / (eig_wide + dampings[damping])).astype(jnp.bfloat16)]
    ppermute x9 -> x10, waiting for transfers between devices: 67.6 us -> 114 us  [ring_gather(): lax.ppermute(x, axis, perm=[(i, (i + shift) % n) for i in range(n)])]
    all_gather x1, waiting for transfers between devices: 44.3 us -> 0.03 us  [shards(): lax.all_gather(gradient_rows.astype(jnp.bfloat16), WIDE, axis=0, tiled=True)]
    add x0 -> x1, other arithmetic: none -> 22.2 us  [score_rows(): precond = (grad_wide / (eig_wide + dampings[damping])).astype(jnp.bfloat16)]
    all_gather x1, waiting for transfers between devices: 27.9 us -> 19.7 us  [shards(): eig_part = lax.all_gather(my_cols, WIDE, axis=0, tiled=True)]
    another operation x2 -> x3, other arithmetic: 5.2 us -> 9.87 us  [ring_gather(): return jnp.stack(parts)]
    rev x2 -> x3, local copies, waits for them, and re-layouts: 0.05 us -> 4.68 us  [natural_order(): reverse = stacked[::-1]]
    ppermute x9 -> x10, starting transfers between devices: 7.98 us -> 9.45 us  [ring_gather(): lax.ppermute(x, axis, perm=[(i, (i + shift) % n) for i in range(n)])]
  transfers between devices with their start and end apart: 15 -> 16, of which waited for: 10 -> 10; matrix products, arithmetic and copies ran while one was open for 8% -> 29% of each run, Pallas kernels for 0% -> 0%
where the time goes in v5:
time: 396 us; the launch traced here: 395 us
  waiting for transfers between devices  225 us (57%)
  local copies, waits for them, and re-layouts  66.2 us (17%)
  other arithmetic  42.2 us (11%)
  matrix products  35 us (9%)
  between operations  16.3 us (4%)
  starting transfers between devices  9.84 us (2%)
    ppermute x10, waiting for transfers between devices, ring_gather(): lax.ppermute(x, axis, perm=[(i, (i + shift) % n) for i in range(n)])  114 us
    add x6, local copies, waits for them, and re-layouts, score_rows(): precond = (grad_wide / (eig_wide + dampings[damping])).astype(jnp.bfloat16)  55 us
    reduce_scatter x1, waiting for transfers between devices, shards(): lax.psum_scatter(partial_rows, 'wa', scatter_dimension=0, tiled=True)  46 us
    all_gather x1, waiting for transfers between devices, shards(): grad_cols = lax.all_gather(grad_basis, 'wa', axis=1, tiled=True)  29.4 us
    dot_general x6, matrix products, score_rows(): jnp.dot(precond, train_grad_rot, preferred_element_type=jnp.float32)  22.8 us
    add x1, other arithmetic, score_rows(): precond = (grad_wide / (eig_wide + dampings[damping])).astype(jnp.bfloat16)  22.2 us
    all_gather x1, waiting for transfers between devices, shards(): eig_part = lax.all_gather(my_cols, WIDE, axis=0, tiled=True)  19.7 us
    all_gather x1, waiting for transfers between devices, shards(): grad_all = lax.all_gather(grad_kept, 'wb', axis=1, tiled=True)  15.5 us
  transfers between devices with their start and end apart: 16, of which 10 were waited for; matrix products, arithmetic and copies ran while one was open for 29% of the time, Pallas kernels for 0%

profile of v5, /device:TPU:0, one launch (start us, length us, event | category | flops | bytes accessed | tf_op | source)
XLA Modules:
  0.0 394.6 jit_solution(8400888529108427020)
XLA Ops:
  7.4 0.7 all-gather.8.cloned.1.call-update
  8.1 0.0 all-gather.6.cloned.1.call-start
  8.1 2.5 collective-permute-start.5
  10.6 1.1 collective-permute-start.4
  11.7 0.0 all-gather.6.cloned.1.call-update
  11.7 0.0 all-gather.10.cloned.1.call-start
  11.7 0.8 collective-permute-start.6
  12.6 0.6 collective-permute-start.7
  13.2 44.6 %collective-permute-done.6 = s32[128]{0:T(128)S(1)} collective-permute-done((s32[128]{0:T(128)}, s32[128]{0:T(128)S(1)}, u32[]{:S(2)}, u32[]{:S(2)}) %collective-permute-start.6) | collective-permute-done | bytes 544 | tf_op jit(solution)/shard_map/ppermute | solution.py:29
  57.8 1.4 collective-permute-done.8
  59.3 0.7 fusion.40
  60.0 3.7 pad_maximum_fusion
  63.7 29.4 %all-gather.8.cloned.1.call-done = bf16[4096,512]{1,0:T(8,128)(2,1)} async-done(((bf16[4096,128]{1,0:T(8,128)(2,1)}), bf16[4096,512]{1,0:T(8,128)(2,1)}) %all-gather.8.cloned.1.call-update) | async-done | bytes 4194320 | tf_op jit(solution)/shard_map/all_gather | solution.py:57
  93.1 5.8 %fusion.37 = bf16[512,512]{1,0:T(8,128)(2,1)S(1)} fusion(bf16[512,4096]{1,0:T(8,128)(2,1)} %bitcast.76, bf16[4096,512]{1,0:T(8,128)(2,1)} %all-gather.8.cloned.1.call-done, bf16[512]{0:T(512)(128)(2,1)S(1)} %fusion.40), kind=kOutput, calls=%fused_computation.44 | convolution fusion | flops 2148007936 | bytes 8913920 | tf_op jit(solution)/shard_map/dot_general | solution.py:62
  98.9 1.0 fusion.38
  100.0 0.0 all-gather.10.cloned.1.call-update
  100.0 0.0 reduce-scatter.2.cloned.1.call-start
  100.0 0.1 collective-permute-start
  100.1 1.5 collective-permute-start.1
  101.6 1.4 collective-permute-start.2
  103.0 10.7 %collective-permute-done = bf16[128,2048]{1,0:T(8,128)(2,1)S(1)} collective-permute-done((bf16[128,2048]{1,0:T(8,128)(2,1)S(1)}, bf16[128,2048]{1,0:T(8,128)(2,1)S(1)}, u32[]{:S(2)}, u32[]{:S(2)}) %collective-permute-start) | collective-permute-done | bytes 524320 | tf_op jit(solution)/shard_map/ppermute | solution.py:29
  113.7 1.2 collective-permute-done.1
  114.9 9.6 %collective-permute-done.2 = bf16[128,2048]{1,0:T(8,128)(2,1)S(1)} collective-permute-done((bf16[128,2048]{1,0:T(8,128)(2,1)S(1)}, bf16[128,2048]{1,0:T(8,128)(2,1)S(1)}, u32[]{:S(2)}, u32[]{:S(2)}) %collective-permute-start.2) | collective-permute-done | bytes 524320 | tf_op jit(solution)/shard_map/ppermute | solution.py:29
  124.5 1.6 pad_maximum_fusion.2
  126.1 2.7 convolution_convert_fusion.1
  128.8 0.0 copy-start.2
  128.8 0.1 fusion.39
  129.0 15.5 %all-gather.10.cloned.1.call-done = bf16[512,2048]{1,0:T(8,128)(2,1)} async-done(((bf16[512,512]{1,0:T(8,128)(2,1)}), bf16[512,2048]{1,0:T(8,128)(2,1)}) %all-gather.10.cloned.1.call-update) | async-done | bytes 2097168 | tf_op jit(solution)/shard_map/all_gather | solution.py:69
  144.5 3.6 fusion.43
  148.1 0.0 reduce-scatter.2.cloned.1.call-update
  148.1 0.0 all-gather.14.cloned.1.call-start
  148.2 0.7 constant_dynamic-slice_fusion
  148.8 0.0 all-gather.14.cloned.1.call-update
  148.9 0.2 all-gather.12.cloned.1.call-start
  149.1 46.0 %reduce-scatter.2.cloned.1.call-done = f32[64,2048]{1,0:T(8,128)} async-done(((f32[256,2048]{1,0:T(8,128)}), f32[64,2048]{1,0:T(8,128)}) %reduce-scatter.2.cloned.1.call-update) | async-done | bytes 524304 | tf_op jit(solution)/shard_map/reduce_scatter | solution.py:73
  195.1 1.1 convert_element_type.67
  196.2 0.2 convert_element_type.68
  196.3 0.1 copy.29
  196.4 0.9 convert_element_type.70
  197.3 0.0 all-gather.12.cloned.1.call-update
  197.4 19.7 %all-gather.14.cloned.1.call-done = bf16[1024,1024]{1,0:T(8,128)(2,1)} async-done(((bf16[64,1024]{1,0:T(8,128)(2,1)}), bf16[1024,1024]{1,0:T(8,128)(2,1)}) %all-gather.14.cloned.1.call-update) | async-done | bytes 2097168 | tf_op jit(solution)/shard_map/all_gather | solution.py:82
  217.1 3.9 %copy.20 = bf16[1024,1024]{0,1:T(8,128)(2,1)} copy(bf16[1024,1024]{1,0:T(8,128)(2,1)} %all-gather.14.cloned.1.call-done) | data formatting | bytes 4194304 | tf_op jit(solution)/shard_map/all_gather | solution.py:82
  221.0 1.5 collective-permute-start.9
  222.5 0.6 compare_select_fusion
  223.1 46.1 %collective-permute-done.9 = bf16[1024,1024]{0,1:T(8,128)(2,1)} collective-permute-done((bf16[1024,1024]{0,1:T(8,128)(2,1)}, bf16[1024,1024]{0,1:T(8,128)(2,1)}, u32[]{:S(2)}, u32[]{:S(2)}) %collective-permute-start.9) | collective-permute-done | bytes 2097184 | tf_op jit(solution)/shard_map/ppermute | solution.py:29
  269.2 4.6 %pad_maximum_fusion.1 = bf16[2,1024,1024]{1,2,0:T(8,128)(2,1)} fusion(bf16[1,1024,1024]{1,2,0:T(8,128)(2,1)} %bitcast.21, bf16[1,1024,1024]{1,2,0:T(8,128)(2,1)} %bitcast.75), kind=kLoop, calls=%fused_computation.23 | loop fusion | flops 2097152 | bytes 8388608 | tf_op jit(solution)/shard_map/stack | solution.py:30
  273.7 4.6 %rev.11 = bf16[2,1024,1024]{1,2,0:T(8,128)(2,1)} reverse(bf16[2,1024,1024]{1,2,0:T(8,128)(2,1)} %pad_maximum_fusion.1), dimensions={0} | reverse | bytes 8388608 | tf_op jit(solution)/shard_map/rev | solution.py:35
  278.4 6.1 %convert_reduce_fusion = (f32[]{:T(128)}, bf16[2,1024,1024]{1,2,0:T(8,128)(2,1)}) fusion(s32[]{:T(128)S(6)} %select_n.26, bf16[2,1024,1024]{1,2,0:T(8,128)(2,1)} %rev.11), kind=kLoop, calls=%fused_computation.6 | loop fusion | flops 6291455 | bytes 8388616 | tf_op jit(solution)/shard_map/reduce_sum | solution.py:85
  285.1 0.7 fusion.42
  285.8 22.2 %convert_add_fusion = (f32[2,1024,1024]{1,2,0:T(8,128)}, f32[2,1024,1024]{1,2,0:T(8,128)}, f32[2,1024,1024]{1,2,0:T(8,128)}, f32[2,1024,1024]{1,2,0:T(8,128)}, f...) fusion(bf16[2,1024,1024]{1,2,0:T(8,128)(2,1)} %get-tuple-element.6, f32[]{:T(128)} %bitcast.37, f32[]{:T(128)} %bitcast.25, ...), kind=kLoop, calls=%fused_computation | loop fusion | flops 14680064 | bytes 54525976 | tf_op jit(solution)/shard_map/add | solution.py:19
  308.0 9.2 %copy.23 = f32[1024,2048]{1,0:T(8,128)} copy(f32[1024,2048]{0,1:T(8,128)} %bitcast.66) | data formatting | bytes 16777216 | tf_op jit(solution)/shard_map/add | solution.py:19
  317.1 9.2 %copy.24 = f32[1024,2048]{1,0:T(8,128)} copy(f32[1024,2048]{0,1:T(8,128)} %bitcast.65) | data formatting | bytes 16777216 | tf_op jit(solution)/shard_map/add | solution.py:19
  326.3 9.2 %copy.25 = f32[1024,2048]{1,0:T(8,128)} copy(f32[1024,2048]{0,1:T(8,128)} %bitcast.64) | data formatting | bytes 16777216 | tf_op jit(solution)/shard_map/add | solution.py:19
  335.5 9.1 %copy.26 = f32[1024,2048]{1,0:T(8,128)} copy(f32[1024,2048]{0,1:T(8,128)} %bitcast.63) | data formatting | bytes 16777216 | tf_op jit(solution)/shard_map/add | solution.py:19
  344.6 9.2 %copy.27 = f32[1024,2048]{1,0:T(8,128)} copy(f32[1024,2048]{0,1:T(8,128)} %bitcast.62) | data formatting | bytes 16777216 | tf_op jit(solution)/shard_map/add | solution.py:19
  353.8 9.2 %copy.22 = f32[1024,2048]{1,0:T(8,128)} copy(f32[1024,2048]{0,1:T(8,128)} %bitcast.61) | data formatting | bytes 16777216 | tf_op jit(solution)/shard_map/add | solution.py:19
  363.6 0.0 all-gather.12.cloned.1.call-done
  363.7 7.1 %fusion.20 = f32[384]{0:T(512)S(1)} fusion(bf16[1024,384]{1,0:T(8,128)(2,1)S(1)} %copy-done.6, bf16[2048,384]{1,0:T(8,128)(2,1)S(1)} %copy-done, f32[1024,2048]{1,0:T(8,128)} %copy.23, bf16[1024,2048]{1,0:T(8,128)(2,1)} %all-gather.12.cloned.1.call-done), kind=kOutput, calls=%fused_computation.38 | convolution fusion | flops 1618083456 | bytes 14943744 | tf_op jit(solution)/shard_map/dot_general | solution.py:20
  370.8 5.9 %fusion.21 = f32[384]{0:T(512)S(1)} fusion(bf16[1024,384]{1,0:T(8,128)(2,1)S(1)} %copy-done.6, bf16[2048,384]{1,0:T(8,128)(2,1)S(1)} %copy-done, f32[1024,2048]{1,0:T(8,128)} %copy.24, bf16[1024,2048]{1,0:T(8,128)(2,1)S(1)} %copy-done.5), kind=kOutput, calls=%fused_computation.39 | convolution fusion | flops 1618083456 | bytes 14943744 | tf_op jit(solution)/shard_map/dot_general | solution.py:20
  376.8 2.4 fusion.22
  379.3 2.5 fusion.23
  381.8 2.5 fusion.24
  384.3 2.5 fusion.19
  386.9 0.6 multiply_multiply_fusion
  (53 shorter events, 0.2 us)
Async XLA Ops:
  7.4 356.3 %copy-start = (bf16[2048,384]{1,0:T(8,128)(2,1)S(1)}, bf16[2048,384]{1,0:T(8,128)(2,1)}, u32[]{:S(2)}) copy-start(bf16[2048,384]{1,0:T(8,128)(2,1)} %param.18) | copy-start | bytes 4718596
  7.4 85.7 %all-gather.8.cloned.1.call-start = ((), (), s32[]{:S(2)}) async-start(), calls=%async_computation.2 | async-start | bytes 5242880 | tf_op jit(solution)/shard_map/all_gather | solution.py:57
  8.1 118.0 %all-gather.6.cloned.1.call-start = ((), (), s32[]{:S(2)}) async-start(), calls=%async_computation.1 | async-start | bytes 1310720 | tf_op jit(solution)/shard_map/all_gather | solution.py:56
  8.1 51.8 %collective-permute-start.5 = (bf16[128,4096]{1,0:T(8,128)(2,1)}, bf16[128,4096]{1,0:T(8,128)(2,1)S(1)}, u32[]{:S(2)}, u32[]{:S(2)}) collective-permute-start(bf16[128,4096]{1,0:T(8,128)(2,1)} %param.11), channel_id=1, source_target_pairs={{0,3},{1,0},{2,1},{3,2},{4,7},{5,4},{6,5},{7,6},{8,11},{9,8},{10,9... | collective-permute-start | bytes 3145736 | tf_op jit(solution)/shard_map/ppermute | solution.py:29
  10.6 49.3 %collective-permute-start.3 = (bf16[128,4096]{1,0:T(8,128)(2,1)}, bf16[128,4096]{1,0:T(8,128)(2,1)}, u32[]{:S(2)}, u32[]{:S(2)}) collective-permute-start(bf16[128,4096]{1,0:T(8,128)(2,1)} %param.11), channel_id=1, source_target_pairs={{0,1},{1,2},{2,3},{3,0},{4,5},{5,6},{6,7},{7,4},{8,9},{9,10},{10,1... | collective-permute-start | bytes 3145736 | tf_op jit(solution)/shard_map/ppermute | solution.py:29
  10.6 49.4 %collective-permute-start.4 = (bf16[128,4096]{1,0:T(8,128)(2,1)}, bf16[128,4096]{1,0:T(8,128)(2,1)}, u32[]{:S(2)}, u32[]{:S(2)}) collective-permute-start(bf16[128,4096]{1,0:T(8,128)(2,1)} %param.11), channel_id=1, source_target_pairs={{0,2},{1,3},{2,0},{3,1},{4,6},{5,7},{6,4},{7,5},{8,10},{9,11},{10,... | collective-permute-start | bytes 3145736 | tf_op jit(solution)/shard_map/ppermute | solution.py:29
  11.7 132.8 %all-gather.10.cloned.1.call-start = ((), (), s32[]{:S(2)}) async-start(), calls=%async_computation.3 | async-start | bytes 2621440 | tf_op jit(solution)/shard_map/all_gather | solution.py:69
  11.7 46.1 %collective-permute-start.6 = (s32[128]{0:T(128)}, s32[128]{0:T(128)S(1)}, u32[]{:S(2)}, u32[]{:S(2)}) collective-permute-start(s32[128]{0:T(128)} %param.12), channel_id=1, source_target_pairs={{0,1},{1,2},{2,3},{3,0},{4,5},{5,6},{6,7},{7,4},{8,9},{9,10},{10,1... | collective-permute-start | bytes 1544 | tf_op jit(solution)/shard_map/ppermute | solution.py:29
  12.6 45.3 %collective-permute-start.7 = (s32[128]{0:T(128)}, s32[128]{0:T(128)S(1)}, u32[]{:S(2)}, u32[]{:S(2)}) collective-permute-start(s32[128]{0:T(128)} %param.12), channel_id=1, source_target_pairs={{0,2},{1,3},{2,0},{3,1},{4,6},{5,7},{6,4},{7,5},{8,10},{9,11},{10,... | collective-permute-start | bytes 1544 | tf_op jit(solution)/shard_map/ppermute | solution.py:29
  57.8 1.4 collective-permute-start.8
  93.1 7.0 %copy-start.1 = (bf16[128,2048]{1,0:T(8,128)(2,1)S(1)}, bf16[128,2048]{1,0:T(8,128)(2,1)}, u32[]{:S(2)}) copy-start(bf16[128,2048]{1,0:T(8,128)(2,1)} %param.10) | copy-start | bytes 1572868
  100.0 95.1 %reduce-scatter.2.cloned.1.call-start = ((), (), s32[]{:S(2)}) async-start(), calls=%async_computation.4 | async-start | bytes 2621440 | tf_op jit(solution)/shard_map/reduce_scatter | solution.py:73
  100.0 13.7 %collective-permute-start = (bf16[128,2048]{1,0:T(8,128)(2,1)S(1)}, bf16[128,2048]{1,0:T(8,128)(2,1)S(1)}, u32[]{:S(2)}, u32[]{:S(2)}) collective-permute-start(bf16[128,2048]{1,0:T(8,128)(2,1)S(1)} %copy-done.1), channel_id=1, source_target_pairs={{0,1},{1,2},{2,3},{3,0},{4,5},{5,6},{6,7},{7,4},{8,9},{9,10},{10,1... | collective-permute-start | bytes 1572872 | tf_op jit(solution)/shard_map/ppermute | solution.py:29
  100.1 14.8 %collective-permute-start.1 = (bf16[128,2048]{1,0:T(8,128)(2,1)S(1)}, bf16[128,2048]{1,0:T(8,128)(2,1)S(1)}, u32[]{:S(2)}, u32[]{:S(2)}) collective-permute-start(bf16[128,2048]{1,0:T(8,128)(2,1)S(1)} %copy-done.1), channel_id=1, source_target_pairs={{0,2},{1,3},{2,0},{3,1},{4,6},{5,7},{6,4},{7,5},{8,10},{9,11},{10,... | collective-permute-start | bytes 1572872 | tf_op jit(solution)/shard_map/ppermute | solution.py:29
  101.6 22.9 %collective-permute-start.2 = (bf16[128,2048]{1,0:T(8,128)(2,1)S(1)}, bf16[128,2048]{1,0:T(8,128)(2,1)S(1)}, u32[]{:S(2)}, u32[]{:S(2)}) collective-permute-start(bf16[128,2048]{1,0:T(8,128)(2,1)S(1)} %copy-done.1), channel_id=1, source_target_pairs={{0,3},{1,0},{2,1},{3,2},{4,7},{5,4},{6,5},{7,6},{8,11},{9,8},{10,9... | collective-permute-start | bytes 1572872 | tf_op jit(solution)/shard_map/ppermute | solution.py:29
  128.8 19.4 %copy-start.2 = (bf16[64,2048]{1,0:T(8,128)(2,1)S(1)}, bf16[64,2048]{1,0:T(8,128)(2,1)}, u32[]{:S(2)}) copy-start(bf16[64,2048]{1,0:T(8,128)(2,1)} %param.15) | copy-start | bytes 786436
  148.1 74.4 %copy-start.4 = (s32[384]{0:T(512)S(1)}, s32[384]{0:T(512)}, u32[]{:S(2)}) copy-start(s32[384]{0:T(512)} %param.19) | copy-start | bytes 4612
  148.1 69.0 %all-gather.14.cloned.1.call-start = ((), (), s32[]{:S(2)}) async-start(), calls=%async_computation.6 | async-start | bytes 2228224 | tf_op jit(solution)/shard_map/all_gather | solution.py:82
  148.9 214.8 %all-gather.12.cloned.1.call-start = ((), (), s32[]{:S(2)}) async-start(), calls=%async_computation.5 | async-start | bytes 4456448 | tf_op jit(solution)/shard_map/all_gather | solution.py:77
  221.0 48.1 %collective-permute-start.9 = (bf16[1024,1024]{0,1:T(8,128)(2,1)}, bf16[1024,1024]{0,1:T(8,128)(2,1)}, u32[]{:S(2)}, u32[]{:S(2)}) collective-permute-start(bf16[1024,1024]{0,1:T(8,128)(2,1)} %copy.20), channel_id=1, source_target_pairs={{0,16},{16,0},{1,17},{17,1},{2,18},{18,2},{3,19},{19,3},{4,20},{20... | collective-permute-start | bytes 6291464 | tf_op jit(solution)/shard_map/ppermute | solution.py:29
  278.4 6.7 %copy-start.7 = (s32[6]{0:T(128)S(1)}, s32[6]{0:T(128)}, u32[]{:S(2)}) copy-start(s32[6]{0:T(128)} %param.16) | copy-start | bytes 76
  353.8 9.9 %copy-start.6 = (bf16[1024,384]{1,0:T(8,128)(2,1)S(1)}, bf16[1024,384]{1,0:T(8,128)(2,1)}, u32[]{:S(2)}) copy-start(bf16[1024,384]{1,0:T(8,128)(2,1)} %param.17) | copy-start | bytes 2359300
  363.7 7.1 %copy-start.5 = (bf16[1024,2048]{1,0:T(8,128)(2,1)S(1)}, bf16[1024,2048]{1,0:T(8,128)(2,1)}, u32[]{:S(2)}) copy-start(bf16[1024,2048]{1,0:T(8,128)(2,1)} %all-gather.12.cloned.1.call-done) | copy-start | bytes 12582916
  363.7 13.1 %slice-start.6 = ((s8[8388608]{0:T(1024)(128)(4,1)}), s8[4194304]{0:T(1024)(128)(4,1)S(1)}, s32[]{:S(2)}) async-start(s8[8388608]{0:T(1024)(128)(4,1)} %bitcast.73), calls=%async_computation.13 | async-start | bytes 8388608
  370.8 5.9 %slice-start.7 = ((s8[8388608]{0:T(1024)(128)(4,1)}), s8[4194304]{0:T(1024)(128)(4,1)S(1)}, s32[]{:S(2)}) async-start(s8[8388608]{0:T(1024)(128)(4,1)} %bitcast.73), calls=%async_computation.14 | async-start | bytes 8388608
  370.8 8.4 %slice-start.4 = ((s8[8388608]{0:T(1024)(128)(4,1)}), s8[4194304]{0:T(1024)(128)(4,1)S(1)}, s32[]{:S(2)}) async-start(s8[8388608]{0:T(1024)(128)(4,1)} %bitcast.71), calls=%async_computation.11 | async-start | bytes 8388608
  376.8 2.5 slice-start.5
  376.8 5.0 %slice-start.2 = ((s8[8388608]{0:T(1024)(128)(4,1)}), s8[4194304]{0:T(1024)(128)(4,1)S(1)}, s32[]{:S(2)}) async-start(s8[8388608]{0:T(1024)(128)(4,1)} %bitcast.69), calls=%async_computation.9 | async-start | bytes 8388608
  379.2 2.6 slice-start.3
  379.3 5.0 %slice-start = ((s8[8388608]{0:T(1024)(128)(4,1)}), s8[4194304]{0:T(1024)(128)(4,1)S(1)}, s32[]{:S(2)}) async-start(s8[8388608]{0:T(1024)(128)(4,1)} %bitcast.67), calls=%async_computation.7 | async-start | bytes 8388608
  381.8 2.5 slice-start.1
  384.3 2.5 copy-start.3
Sparse Core Ops, SparseCore 0:
  9.8 83.2 all-gather.7
  94.6 26.0 all-gather.5
  122.3 22.0 all-gather.9
  148.2 46.8 reduce-scatter.1
Sparse Core Ops, SparseCore 1:
  150.8 66.3 all-gather.13
  219.4 49.0 all-gather.11

commit v6 on v3

--- a/solution.py
+++ b/solution.py
@@ -66,20 +66,28 @@
     grad_kept = grad_rot * query_weight[:, None]
     act_rot = natural_order(act_rot.reshape(nb, count, -1), "wb").reshape(nb * count, -1)
     grad_kept = natural_order(grad_kept.reshape(nb, count, -1), "wb").reshape(nb * count, -1)
-    grad_all = lax.all_gather(grad_kept, "wb", axis=1, tiled=True)
+    grad_all = jnp.concatenate(list(ring_gather(grad_kept, "wb")), axis=1)
     partial_rows = lax.dot_general(
         act_rot, grad_all, (((0,), (0,)), ((), ())), preferred_element_type=jnp.float32
     )
     gradient_rows = lax.psum_scatter(partial_rows, "wa", scatter_dimension=0, tiled=True)
     na = lax.axis_size("wa")
     rows = gradient_rows.shape[0]
-    gradient_rows = gradient_rows.reshape(rows, nb, na, -1).transpose(0, 2, 1, 3).reshape(rows, -1)
-    query_gradient = lax.all_gather(gradient_rows.astype(jnp.bfloat16), WIDE, axis=0, tiled=True)
-    eig_full = lax.all_gather(eig_values, WIDE, axis=0, tiled=True)
-    eig_in, eig_out = eig_full.shape
+    by_shift = gradient_rows.reshape(rows, nb, na, -1).transpose(1, 0, 2, 3)
+    gradient_rows = natural_order(by_shift, "wb").transpose(1, 2, 0, 3).reshape(rows, -1)
+    query_gradient = ring_gather(gradient_rows.astype(jnp.bfloat16), WIDE)
+    eig_full = ring_gather(eig_values, WIDE)
+    blocks, block, eig_out = eig_full.shape
+    eig_in = blocks * block
+    query_gradient = query_gradient.reshape(eig_in, eig_out)
+    eig_full = eig_full.reshape(eig_in, eig_out)
+    acts_blocks = train_act_rot.reshape(blocks, block, -1)
+    doubled = jnp.concatenate([acts_blocks, acts_blocks], axis=0)
+    acts_order = lax.dynamic_slice_in_dim(doubled, lax.axis_index(WIDE) + 1, blocks, axis=0)[::-1]
+    acts_order = acts_order.reshape(eig_in, -1)
     mean_eig = jnp.sum(eig_full.astype(jnp.float32)) / (eig_in * eig_out)
     dampings = mean_eig * jnp.exp2(damping_index.astype(jnp.float32) - 4.0)
-    totals = score_rows(query_gradient, eig_full, dampings, train_act_rot, train_grad_rot)
+    totals = score_rows(query_gradient, eig_full, dampings, acts_order, train_grad_rot)
     query_count = query_act.shape[0] * lax.axis_size(WIDE)
     factor = mean_eig * (1.0 / math.sqrt(float(query_count) * eig_in * eig_out))
     train_weight = jnp.where(train_positions >= PROMPT, 1.0, 0.0).astype(jnp.float32)

time: 310 us -> 401 us (1.29)
  starting transfers between devices: 8.37 us -> 150 us
  waiting for transfers between devices: 235 us -> 161 us
  local copies, waits for them, and re-layouts: 1.99 us -> 19.2 us
  other arithmetic: 13.6 us -> 28.4 us
  matrix products: 34.4 us -> 26 us
    ppermute x9 -> x42, starting transfers between devices: 7.98 us -> 150 us  [ring_gather(): lax.ppermute(x, axis, perm=[(i, (i + shift) % n) for i in range(n)])]
    all_gather x3 -> x0, waiting for transfers between devices: 87.7 us -> none  [the longest x1 44.3 us: shards(): lax.all_gather(gradient_rows.astype(jnp.bfloat16), WIDE, axis=0, tiled=True)]
    ppermute x9 -> x42, waiting for transfers between devices: 67.6 us -> 134 us  [ring_gather(): lax.ppermute(x, axis, perm=[(i, (i + shift) % n) for i in range(n)])]
    reduce_scatter x1, waiting for transfers between devices: 49.2 us -> 12.5 us  [shards(): lax.psum_scatter(partial_rows, 'wa', scatter_dimension=0, tiled=True)]
    all_gather x1, waiting for transfers between devices: 29.5 us -> 0.01 us  [shards(): grad_cols = lax.all_gather(grad_basis, 'wa', axis=1, tiled=True)]
    unnamed x14 -> x46, local copies, waits for them, and re-layouts: 0.03 us -> 15 us
    all_gather x1, waiting for transfers between devices: 0.01 us -> 13.4 us  [shards(): act_cols = lax.all_gather(act_basis, 'wa', axis=1, tiled=True)]
    convert_element_type x1 -> x2, other arithmetic: 1.07 us -> 14 us  [the longest x1 13.7 us: score_rows(): precond = (grad_wide / (eig_wide + dampings[damping])).astype(jnp.bfloat16)]
  transfers between devices with their start and end apart: 15 -> 45, of which waited for: 10 -> 16; matrix products, arithmetic and copies ran while one was open for 8% -> 11% of each run, Pallas kernels for 0% -> 0%
where the time goes in v6:
time: 401 us; the launch traced here: 400 us
  waiting for transfers between devices  161 us (40%)
  starting transfers between devices  150 us (37%)
  other arithmetic  28.4 us (7%)
  matrix products  26 us (6%)
  local copies, waits for them, and re-layouts  19.2 us (5%)
  between operations  14.9 us (4%)
    ppermute x42, starting transfers between devices, ring_gather(): lax.ppermute(x, axis, perm=[(i, (i + shift) % n) for i in range(n)])  150 us
    ppermute x42, waiting for transfers between devices, ring_gather(): lax.ppermute(x, axis, perm=[(i, (i + shift) % n) for i in range(n)])  134 us
    unnamed x46, local copies, waits for them, and re-layouts  15 us
    dot_general x6, matrix products, score_rows(): jnp.dot(precond, train_grad_rot, preferred_element_type=jnp.float32)  14 us
    convert_element_type x1, other arithmetic, score_rows(): precond = (grad_wide / (eig_wide + dampings[damping])).astype(jnp.bfloat16)  13.7 us
    all_gather x1, waiting for transfers between devices, shards(): act_cols = lax.all_gather(act_basis, 'wa', axis=1, tiled=True)  13.4 us
    reduce_scatter x1, waiting for transfers between devices, shards(): lax.psum_scatter(partial_rows, 'wa', scatter_dimension=0, tiled=True)  12.5 us
  transfers between devices with their start and end apart: 45, of which 16 were waited for; matrix products, arithmetic and copies ran while one was open for 11% of the time, Pallas kernels for 0%

profile of v6, /device:TPU:0, one launch (start us, length us, event | category | flops | bytes accessed | tf_op | source)
XLA Modules:
  0.0 400.1 jit_solution(1746566638788257781)
XLA Ops:
  7.8 2.6 collective-permute-start.7
  10.4 1.4 collective-permute-start.8
  12.4 1.7 bitcast_dynamic-update-slice_fusion.15
  14.7 1.5 fusion.21
  16.2 1.0 rev.15
  17.5 2.3 collective-permute-start.4
  19.9 0.8 collective-permute-done.27
  20.7 1.4 collective-permute-start.29
  22.1 1.7 bitcast_dynamic-update-slice_fusion.14
  23.8 39.8 %collective-permute-done.28 = bf16[64,2048]{1,0:T(8,128)(2,1)S(1)} collective-permute-done((bf16[64,2048]{1,0:T(8,128)(2,1)}, bf16[64,2048]{1,0:T(8,128)(2,1)S(1)}, u32[]{:S(2)}, u32[]{:S(2)}) %collective-permute-start.28) | collective-permute-done | bytes 262176 | tf_op jit(solution)/shard_map/ppermute | solution.py:29
  63.6 1.6 collective-permute-start.30
  65.9 3.3 collective-permute-done.29
  69.2 3.5 collective-permute-start.31
  73.4 5.3 %collective-permute-done.30 = bf16[64,2048]{1,0:T(8,128)(2,1)S(1)} collective-permute-done((bf16[64,2048]{1,0:T(8,128)(2,1)}, bf16[64,2048]{1,0:T(8,128)(2,1)S(1)}, u32[]{:S(2)}, u32[]{:S(2)}) %collective-permute-start.30) | collective-permute-done | bytes 262176 | tf_op jit(solution)/shard_map/ppermute | solution.py:29
  78.7 1.6 collective-permute-start.32
  81.1 31.5 %collective-permute-done.31 = bf16[64,2048]{1,0:T(8,128)(2,1)S(1)} collective-permute-done((bf16[64,2048]{1,0:T(8,128)(2,1)}, bf16[64,2048]{1,0:T(8,128)(2,1)S(1)}, u32[]{:S(2)}, u32[]{:S(2)}) %collective-permute-start.31) | collective-permute-done | bytes 262176 | tf_op jit(solution)/shard_map/ppermute | solution.py:29
  112.6 9.4 %collective-permute-start.33 = (bf16[64,2048]{1,0:T(8,128)(2,1)}, bf16[64,2048]{1,0:T(8,128)(2,1)S(1)}, u32[]{:S(2)}, u32[]{:S(2)}) collective-permute-start(bf16[64,2048]{1,0:T(8,128)(2,1)} %param.15), channel_id=1, source_target_pairs={{0,7},{1,8},{2,9},{3,10},{4,11},{5,12},{6,13},{7,14},{8,15},{9,0},... | collective-permute-start | bytes 786440 | tf_op jit(solution)/shard_map/ppermute | solution.py:29
  122.7 3.8 collective-permute-done.32
  126.4 2.2 collective-permute-start
  129.3 10.7 %collective-permute-start.1 = (bf16[128,2048]{1,0:T(8,128)(2,1)}, bf16[128,2048]{1,0:T(8,128)(2,1)}, u32[]{:S(2)}, u32[]{:S(2)}) collective-permute-start(bf16[128,2048]{1,0:T(8,128)(2,1)} %param.10), channel_id=1, source_target_pairs={{0,2},{1,3},{2,0},{3,1},{4,6},{5,7},{6,4},{7,5},{8,10},{9,11},{10,... | collective-permute-start | bytes 1572872 | tf_op jit(solution)/shard_map/ppermute | solution.py:29
  140.0 0.7 bitcast_dynamic-update-slice_fusion.8
  140.9 2.7 collective-permute-start.35
  143.5 3.3 pad_maximum_fusion
  146.9 6.0 %fusion.20 = bf16[512,512]{1,0:T(8,128)(2,1)S(1)} fusion(bf16[512,4096]{1,0:T(8,128)(2,1)} %bitcast.123, bf16[4096,512]{1,0:T(8,128)(2,1)} %all-gather.5.cloned.1.call-done, bf16[512]{0:T(512)(128)(2,1)S(1)} %fusion.27), kind=kOutput, calls=%fused_computation.44 | convolution fusion | flops 2148007936 | bytes 8913920 | tf_op jit(solution)/shard_map/dot_general | solution.py:62
  153.2 1.3 collective-permute-done.1
  154.5 1.6 collective-permute-done.2
  156.0 8.5 %collective-permute-start.9 = (bf16[512,512]{1,0:T(8,128)(2,1)S(1)}, bf16[512,512]{1,0:T(8,128)(2,1)}, u32[]{:S(2)}, u32[]{:S(2)}) collective-permute-start(bf16[512,512]{1,0:T(8,128)(2,1)S(1)} %bitcast.139), channel_id=1, source_target_pairs={{0,1},{1,2},{2,3},{3,0},{4,5},{5,6},{6,7},{7,4},{8,9},{9,10},{10,1... | collective-permute-start | bytes 1572872 | tf_op jit(solution)/shard_map/ppermute | solution.py:29
  164.5 3.0 pad_maximum_fusion.1
  167.5 13.4 %all-gather.3.cloned.1.call-done = bf16[2048,256]{0,1:T(8,128)(2,1)} async-done(((bf16[2048,64]{0,1:T(8,128)(2,1)}), bf16[2048,256]{0,1:T(8,128)(2,1)}) %all-gather.3.cloned.1.call-update) | async-done | bytes 1048592 | tf_op jit(solution)/shard_map/all_gather | solution.py:56
  180.9 2.6 convolution_convert_fusion.1
  183.7 0.9 collective-permute-start.37
  184.7 3.7 collective-permute-start.38
  188.4 3.4 fusion.6
  192.0 1.7 bitcast_dynamic-update-slice_fusion.7
  193.6 2.8 collective-permute-start.40
  196.5 1.7 bitcast_dynamic-update-slice_fusion.6
  198.2 32.3 %collective-permute-start.41 = (bf16[64,2048]{1,0:T(8,128)(2,1)S(1)}, bf16[64,2048]{1,0:T(8,128)(2,1)S(1)}, u32[]{:S(2)}, u32[]{:S(2)}) collective-permute-start(bf16[64,2048]{1,0:T(8,128)(2,1)S(1)} %copy-done.5), channel_id=1, source_target_pairs={{0,15},{1,0},{2,1},{3,2},{4,3},{5,4},{6,5},{7,6},{8,7},{9,8},{10,9... | collective-permute-start | bytes 786440 | tf_op jit(solution)/shard_map/ppermute | solution.py:29
  232.7 0.8 bitcast_dynamic-update-slice_fusion.2
  233.5 0.7 bitcast_dynamic-update-slice_fusion.1
  234.2 6.0 %collective-permute-done.41 = bf16[64,2048]{1,0:T(8,128)(2,1)S(1)} collective-permute-done((bf16[64,2048]{1,0:T(8,128)(2,1)S(1)}, bf16[64,2048]{1,0:T(8,128)(2,1)S(1)}, u32[]{:S(2)}, u32[]{:S(2)}) %collective-permute-start.41) | collective-permute-done | bytes 262176 | tf_op jit(solution)/shard_map/ppermute | solution.py:29
  241.0 4.9 %convert_reduce_fusion = f32[]{:T(128)} fusion(bf16[16,64,2048]{2,1,0:T(8,128)(2,1)} %bitcast_dynamic-update-slice_fusion), kind=kLoop, calls=%fused_computation.6 | loop fusion | flops 4194303 | bytes 4194308 | tf_op jit(solution)/shard_map/reduce_sum | solution.py:88
  246.6 12.5 %reduce-scatter.2.cloned.1.call-done = f32[64,2048]{1,0:T(8,128)} async-done(((f32[256,2048]{1,0:T(8,128)}), f32[64,2048]{1,0:T(8,128)}) %reduce-scatter.2.cloned.1.call-update) | async-done | bytes 524304 | tf_op jit(solution)/shard_map/reduce_scatter | solution.py:73
  259.1 1.1 reshape.86
  262.6 3.4 collective-permute-start.14
  266.0 5.0 %collective-permute-start.15 = (bf16[64,2048]{1,0:T(8,128)(2,1)S(1)}, bf16[64,2048]{1,0:T(8,128)(2,1)S(1)}, u32[]{:S(2)}, u32[]{:S(2)}) collective-permute-start(bf16[64,2048]{1,0:T(8,128)(2,1)S(1)} %convert_element_type.98), channel_id=1, source_target_pairs={{0,4},{1,5},{2,6},{3,7},{4,8},{5,9},{6,10},{7,11},{8,12},{9,13},{1... | collective-permute-start | bytes 786440 | tf_op jit(solution)/shard_map/ppermute | solution.py:29
  271.2 4.3 %collective-permute-done.13 = bf16[64,2048]{1,0:T(8,128)(2,1)S(1)} collective-permute-done((bf16[64,2048]{1,0:T(8,128)(2,1)S(1)}, bf16[64,2048]{1,0:T(8,128)(2,1)S(1)}, u32[]{:S(2)}, u32[]{:S(2)}) %collective-permute-start.13) | collective-permute-done | bytes 262176 | tf_op jit(solution)/shard_map/ppermute | solution.py:29
  275.5 2.5 collective-permute-start.18
  278.0 1.3 collective-permute-start.19
  279.3 5.0 %collective-permute-start.20 = (bf16[64,2048]{1,0:T(8,128)(2,1)S(1)}, bf16[64,2048]{1,0:T(8,128)(2,1)S(1)}, u32[]{:S(2)}, u32[]{:S(2)}) collective-permute-start(bf16[64,2048]{1,0:T(8,128)(2,1)S(1)} %convert_element_type.98), channel_id=1, source_target_pairs={{0,9},{1,10},{2,11},{3,12},{4,13},{5,14},{6,15},{7,0},{8,1},{9,2},... | collective-permute-start | bytes 786440 | tf_op jit(solution)/shard_map/ppermute | solution.py:29
  284.3 30.9 %collective-permute-done.16 = bf16[64,2048]{1,0:T(8,128)(2,1)S(1)} collective-permute-done((bf16[64,2048]{1,0:T(8,128)(2,1)S(1)}, bf16[64,2048]{1,0:T(8,128)(2,1)S(1)}, u32[]{:S(2)}, u32[]{:S(2)}) %collective-permute-start.16) | collective-permute-done | bytes 262176 | tf_op jit(solution)/shard_map/ppermute | solution.py:29
  315.4 13.9 %collective-permute-start.22 = (bf16[64,2048]{1,0:T(8,128)(2,1)S(1)}, bf16[64,2048]{1,0:T(8,128)(2,1)S(1)}, u32[]{:S(2)}, u32[]{:S(2)}) collective-permute-start(bf16[64,2048]{1,0:T(8,128)(2,1)S(1)} %convert_element_type.98), channel_id=1, source_target_pairs={{0,11},{1,12},{2,13},{3,14},{4,15},{5,0},{6,1},{7,2},{8,3},{9,4},{... | collective-permute-start | bytes 786440 | tf_op jit(solution)/shard_map/ppermute | solution.py:29
  329.2 7.3 %collective-permute-start.23 = (bf16[64,2048]{1,0:T(8,128)(2,1)S(1)}, bf16[64,2048]{1,0:T(8,128)(2,1)S(1)}, u32[]{:S(2)}, u32[]{:S(2)}) collective-permute-start(bf16[64,2048]{1,0:T(8,128)(2,1)S(1)} %convert_element_type.98), channel_id=1, source_target_pairs={{0,12},{1,13},{2,14},{3,15},{4,0},{5,1},{6,2},{7,3},{8,4},{9,5},{1... | collective-permute-start | bytes 786440 | tf_op jit(solution)/shard_map/ppermute | solution.py:29
  336.6 10.4 %collective-permute-start.24 = (bf16[64,2048]{1,0:T(8,128)(2,1)S(1)}, bf16[64,2048]{1,0:T(8,128)(2,1)S(1)}, u32[]{:S(2)}, u32[]{:S(2)}) collective-permute-start(bf16[64,2048]{1,0:T(8,128)(2,1)S(1)} %convert_element_type.98), channel_id=1, source_target_pairs={{0,13},{1,14},{2,15},{3,0},{4,1},{5,2},{6,3},{7,4},{8,5},{9,6},{10... | collective-permute-start | bytes 786440 | tf_op jit(solution)/shard_map/ppermute | solution.py:29
  347.0 6.2 %collective-permute-start.25 = (bf16[64,2048]{1,0:T(8,128)(2,1)S(1)}, bf16[64,2048]{1,0:T(8,128)(2,1)S(1)}, u32[]{:S(2)}, u32[]{:S(2)}) collective-permute-start(bf16[64,2048]{1,0:T(8,128)(2,1)S(1)} %convert_element_type.98), channel_id=1, source_target_pairs={{0,14},{1,15},{2,0},{3,1},{4,2},{5,3},{6,4},{7,5},{8,6},{9,7},{10,... | collective-permute-start | bytes 786440 | tf_op jit(solution)/shard_map/ppermute | solution.py:29
  353.2 6.0 %collective-permute-start.26 = (bf16[64,2048]{1,0:T(8,128)(2,1)S(1)}, bf16[64,2048]{1,0:T(8,128)(2,1)S(1)}, u32[]{:S(2)}, u32[]{:S(2)}) collective-permute-start(bf16[64,2048]{1,0:T(8,128)(2,1)S(1)} %convert_element_type.98), channel_id=1, source_target_pairs={{0,15},{1,0},{2,1},{3,2},{4,3},{5,4},{6,5},{7,6},{8,7},{9,8},{10,9... | collective-permute-start | bytes 786440 | tf_op jit(solution)/shard_map/ppermute | solution.py:29
  359.3 2.2 collective-permute-done.25
  361.5 3.5 collective-permute-done.26
  365.1 13.7 %fusion.5 = (bf16[16,64,2048]{2,1,0:T(8,128)(2,1)S(1)}, bf16[16,64,2048]{2,1,0:T(8,128)(2,1)S(1)}, bf16[16,64,2048]{2,1,0:T(8,128)(2,1)S(1)}, bf16[16,64,2048]{2...) fusion(bf16[16,64,2048]{2,1,0:T(8,128)(2,1)S(1)} %bitcast_dynamic-update-slice_fusion.16, ...), kind=kLoop, calls=%fused_computation.18 | loop fusion | flops 41943040 | bytes 33554456 | tf_op jit(solution)/shard_map/convert_element_type | solution.py:19
  378.8 2.3 fusion.19
  381.1 2.3 fusion.18
  383.5 2.3 fusion.17
  385.8 2.3 fusion.16
  388.2 2.3 fusion.15
  390.5 2.3 fusion.14
  (114 shorter events, 13.0 us)
Async XLA Ops:
  6.5 372.2 %copy-start = (bf16[2048,384]{1,0:T(8,128)(2,1)S(1)}, bf16[2048,384]{1,0:T(8,128)(2,1)}, u32[]{:S(2)}) copy-start(bf16[2048,384]{1,0:T(8,128)(2,1)} %param.18) | copy-start | bytes 4718596
  6.5 13.4 %copy-start.6 = (s32[128]{0:T(128)S(1)}, s32[128]{0:T(128)}, u32[]{:S(2)}) copy-start(s32[128]{0:T(128)} %param.12) | copy-start | bytes 1540
  6.5 10.6 %copy-start.2 = (bf16[128,4096]{1,0:T(8,128)(2,1)S(1)}, bf16[128,4096]{1,0:T(8,128)(2,1)}, u32[]{:S(2)}) copy-start(bf16[128,4096]{1,0:T(8,128)(2,1)} %param.11) | copy-start | bytes 3145732
  6.5 140.3 %all-gather.5.cloned.1.call-start = ((), (), s32[]{:S(2)}) async-start(), calls=%async_computation.2 | async-start | bytes 5242880 | tf_op jit(solution)/shard_map/all_gather | solution.py:57
  7.3 173.6 %all-gather.3.cloned.1.call-start = ((), (), s32[]{:S(2)}) async-start(), calls=%async_computation.1 | async-start | bytes 1310720 | tf_op jit(solution)/shard_map/all_gather | solution.py:56
  7.3 9.9 %collective-permute-start.6 = (s32[128]{0:T(128)}, s32[128]{0:T(128)S(1)}, u32[]{:S(2)}, u32[]{:S(2)}) collective-permute-start(s32[128]{0:T(128)} %param.12), channel_id=1, source_target_pairs={{0,1},{1,2},{2,3},{3,0},{4,5},{5,6},{6,7},{7,4},{8,9},{9,10},{10,1... | collective-permute-start | bytes 1544 | tf_op jit(solution)/shard_map/ppermute | solution.py:29
  7.8 9.7 %collective-permute-start.7 = (s32[128]{0:T(128)}, s32[128]{0:T(128)S(1)}, u32[]{:S(2)}, u32[]{:S(2)}) collective-permute-start(s32[128]{0:T(128)} %param.12), channel_id=1, source_target_pairs={{0,2},{1,3},{2,0},{3,1},{4,6},{5,7},{6,4},{7,5},{8,10},{9,11},{10,... | collective-permute-start | bytes 1544 | tf_op jit(solution)/shard_map/ppermute | solution.py:29
  10.4 9.5 %collective-permute-start.8 = (s32[128]{0:T(128)}, s32[128]{0:T(128)S(1)}, u32[]{:S(2)}, u32[]{:S(2)}) collective-permute-start(s32[128]{0:T(128)} %param.12), channel_id=1, source_target_pairs={{0,3},{1,0},{2,1},{3,2},{4,7},{5,4},{6,5},{7,6},{8,11},{9,8},{10,9... | collective-permute-start | bytes 1544 | tf_op jit(solution)/shard_map/ppermute | solution.py:29
  11.8 129.0 %collective-permute-start.5 = (bf16[128,4096]{1,0:T(8,128)(2,1)}, bf16[128,4096]{1,0:T(8,128)(2,1)}, u32[]{:S(2)}, u32[]{:S(2)}) collective-permute-start(bf16[128,4096]{1,0:T(8,128)(2,1)} %param.11), channel_id=1, source_target_pairs={{0,3},{1,0},{2,1},{3,2},{4,7},{5,4},{6,5},{7,6},{8,11},{9,8},{10,9... | collective-permute-start | bytes 3145736 | tf_op jit(solution)/shard_map/ppermute | solution.py:29
  11.8 8.9 %collective-permute-start.27 = (bf16[64,2048]{1,0:T(8,128)(2,1)}, bf16[64,2048]{1,0:T(8,128)(2,1)}, u32[]{:S(2)}, u32[]{:S(2)}) collective-permute-start(bf16[64,2048]{1,0:T(8,128)(2,1)} %param.15), channel_id=1, source_target_pairs={{0,1},{1,2},{2,3},{3,4},{4,5},{5,6},{6,7},{7,8},{8,9},{9,10},{10,1... | collective-permute-start | bytes 786440 | tf_op jit(solution)/shard_map/ppermute | solution.py:29
  12.3 246.8 %reduce-scatter.2.cloned.1.call-start = ((), (), s32[]{:S(2)}) async-start(), calls=%async_computation.3 | async-start | bytes 2621440 | tf_op jit(solution)/shard_map/reduce_scatter | solution.py:73
  17.2 123.6 %collective-permute-start.3 = (bf16[128,4096]{1,0:T(8,128)(2,1)S(1)}, bf16[128,4096]{1,0:T(8,128)(2,1)S(1)}, u32[]{:S(2)}, u32[]{:S(2)}) collective-permute-start(bf16[128,4096]{1,0:T(8,128)(2,1)S(1)} %copy-done.2), channel_id=1, source_target_pairs={{0,1},{1,2},{2,3},{3,0},{4,5},{5,6},{6,7},{7,4},{8,9},{9,10},{10,1... | collective-permute-start | bytes 3145736 | tf_op jit(solution)/shard_map/ppermute | solution.py:29
  17.5 123.3 %collective-permute-start.4 = (bf16[128,4096]{1,0:T(8,128)(2,1)S(1)}, bf16[128,4096]{1,0:T(8,128)(2,1)S(1)}, u32[]{:S(2)}, u32[]{:S(2)}) collective-permute-start(bf16[128,4096]{1,0:T(8,128)(2,1)S(1)} %copy-done.2), channel_id=1, source_target_pairs={{0,2},{1,3},{2,0},{3,1},{4,6},{5,7},{6,4},{7,5},{8,10},{9,11},{10,... | collective-permute-start | bytes 3145736 | tf_op jit(solution)/shard_map/ppermute | solution.py:29
  19.9 43.8 %collective-permute-start.28 = (bf16[64,2048]{1,0:T(8,128)(2,1)}, bf16[64,2048]{1,0:T(8,128)(2,1)S(1)}, u32[]{:S(2)}, u32[]{:S(2)}) collective-permute-start(bf16[64,2048]{1,0:T(8,128)(2,1)} %param.15), channel_id=1, source_target_pairs={{0,2},{1,3},{2,4},{3,5},{4,6},{5,7},{6,8},{7,9},{8,10},{9,11},{10,... | collective-permute-start | bytes 786440 | tf_op jit(solution)/shard_map/ppermute | solution.py:29
  20.7 48.5 %collective-permute-start.29 = (bf16[64,2048]{1,0:T(8,128)(2,1)}, bf16[64,2048]{1,0:T(8,128)(2,1)S(1)}, u32[]{:S(2)}, u32[]{:S(2)}) collective-permute-start(bf16[64,2048]{1,0:T(8,128)(2,1)} %param.15), channel_id=1, source_target_pairs={{0,3},{1,4},{2,5},{3,6},{4,7},{5,8},{6,9},{7,10},{8,11},{9,12},{10... | collective-permute-start | bytes 786440 | tf_op jit(solution)/shard_map/ppermute | solution.py:29
  63.6 15.1 %collective-permute-start.30 = (bf16[64,2048]{1,0:T(8,128)(2,1)}, bf16[64,2048]{1,0:T(8,128)(2,1)S(1)}, u32[]{:S(2)}, u32[]{:S(2)}) collective-permute-start(bf16[64,2048]{1,0:T(8,128)(2,1)} %param.15), channel_id=1, source_target_pairs={{0,4},{1,5},{2,6},{3,7},{4,8},{5,9},{6,10},{7,11},{8,12},{9,13},{1... | collective-permute-start | bytes 786440 | tf_op jit(solution)/shard_map/ppermute | solution.py:29
  69.2 43.3 %collective-permute-start.31 = (bf16[64,2048]{1,0:T(8,128)(2,1)}, bf16[64,2048]{1,0:T(8,128)(2,1)S(1)}, u32[]{:S(2)}, u32[]{:S(2)}) collective-permute-start(bf16[64,2048]{1,0:T(8,128)(2,1)} %param.15), channel_id=1, source_target_pairs={{0,5},{1,6},{2,7},{3,8},{4,9},{5,10},{6,11},{7,12},{8,13},{9,14},{... | collective-permute-start | bytes 786440 | tf_op jit(solution)/shard_map/ppermute | solution.py:29
  78.7 47.7 %collective-permute-start.32 = (bf16[64,2048]{1,0:T(8,128)(2,1)}, bf16[64,2048]{1,0:T(8,128)(2,1)S(1)}, u32[]{:S(2)}, u32[]{:S(2)}) collective-permute-start(bf16[64,2048]{1,0:T(8,128)(2,1)} %param.15), channel_id=1, source_target_pairs={{0,6},{1,7},{2,8},{3,9},{4,10},{5,11},{6,12},{7,13},{8,14},{9,15},... | collective-permute-start | bytes 786440 | tf_op jit(solution)/shard_map/ppermute | solution.py:29
  112.6 16.8 %collective-permute-start.33 = (bf16[64,2048]{1,0:T(8,128)(2,1)}, bf16[64,2048]{1,0:T(8,128)(2,1)S(1)}, u32[]{:S(2)}, u32[]{:S(2)}) collective-permute-start(bf16[64,2048]{1,0:T(8,128)(2,1)} %param.15), channel_id=1, source_target_pairs={{0,7},{1,8},{2,9},{3,10},{4,11},{5,12},{6,13},{7,14},{8,15},{9,0},... | collective-permute-start | bytes 786440 | tf_op jit(solution)/shard_map/ppermute | solution.py:29
  126.4 26.6 %collective-permute-start = (bf16[128,2048]{1,0:T(8,128)(2,1)}, bf16[128,2048]{1,0:T(8,128)(2,1)}, u32[]{:S(2)}, u32[]{:S(2)}) collective-permute-start(bf16[128,2048]{1,0:T(8,128)(2,1)} %param.10), channel_id=1, source_target_pairs={{0,1},{1,2},{2,3},{3,0},{4,5},{5,6},{6,7},{7,4},{8,9},{9,10},{10,1... | collective-permute-start | bytes 1572872 | tf_op jit(solution)/shard_map/ppermute | solution.py:29
  129.3 25.1 %collective-permute-start.1 = (bf16[128,2048]{1,0:T(8,128)(2,1)}, bf16[128,2048]{1,0:T(8,128)(2,1)}, u32[]{:S(2)}, u32[]{:S(2)}) collective-permute-start(bf16[128,2048]{1,0:T(8,128)(2,1)} %param.10), channel_id=1, source_target_pairs={{0,2},{1,3},{2,0},{3,1},{4,6},{5,7},{6,4},{7,5},{8,10},{9,11},{10,... | collective-permute-start | bytes 1572872 | tf_op jit(solution)/shard_map/ppermute | solution.py:29
  140.8 15.3 %collective-permute-start.2 = (bf16[128,2048]{1,0:T(8,128)(2,1)}, bf16[128,2048]{1,0:T(8,128)(2,1)}, u32[]{:S(2)}, u32[]{:S(2)}) collective-permute-start(bf16[128,2048]{1,0:T(8,128)(2,1)} %param.10), channel_id=1, source_target_pairs={{0,3},{1,0},{2,1},{3,2},{4,7},{5,4},{6,5},{7,6},{8,11},{9,8},{10,9... | collective-permute-start | bytes 1572872 | tf_op jit(solution)/shard_map/ppermute | solution.py:29
  140.8 51.1 %collective-permute-start.34 = (bf16[64,2048]{1,0:T(8,128)(2,1)}, bf16[64,2048]{1,0:T(8,128)(2,1)}, u32[]{:S(2)}, u32[]{:S(2)}) collective-permute-start(bf16[64,2048]{1,0:T(8,128)(2,1)} %param.15), channel_id=1, source_target_pairs={{0,8},{1,9},{2,10},{3,11},{4,12},{5,13},{6,14},{7,15},{8,0},{9,1},... | collective-permute-start | bytes 786440 | tf_op jit(solution)/shard_map/ppermute | solution.py:29
  140.9 52.8 %collective-permute-start.35 = (bf16[64,2048]{1,0:T(8,128)(2,1)}, bf16[64,2048]{1,0:T(8,128)(2,1)}, u32[]{:S(2)}, u32[]{:S(2)}) collective-permute-start(bf16[64,2048]{1,0:T(8,128)(2,1)} %param.15), channel_id=1, source_target_pairs={{0,9},{1,10},{2,11},{3,12},{4,13},{5,14},{6,15},{7,0},{8,1},{9,2},... | collective-permute-start | bytes 786440 | tf_op jit(solution)/shard_map/ppermute | solution.py:29
  146.9 17.7 %copy-start.4 = (bf16[128,2048]{1,0:T(8,128)(2,1)S(1)}, bf16[128,2048]{1,0:T(8,128)(2,1)}, u32[]{:S(2)}) copy-start(bf16[128,2048]{1,0:T(8,128)(2,1)} %param.10) | copy-start | bytes 1572868
  153.1 30.6 %collective-permute-start.10 = (bf16[512,512]{1,0:T(8,128)(2,1)S(1)}, bf16[512,512]{1,0:T(8,128)(2,1)}, u32[]{:S(2)}, u32[]{:S(2)}) collective-permute-start(bf16[512,512]{1,0:T(8,128)(2,1)S(1)} %bitcast.137), channel_id=1, source_target_pairs={{0,2},{1,3},{2,0},{3,1},{4,6},{5,7},{6,4},{7,5},{8,10},{9,11},{10,... | collective-permute-start | bytes 1572872 | tf_op jit(solution)/shard_map/ppermute | solution.py:29
  154.5 29.3 %collective-permute-start.11 = (bf16[512,512]{1,0:T(8,128)(2,1)S(1)}, bf16[512,512]{1,0:T(8,128)(2,1)}, u32[]{:S(2)}, u32[]{:S(2)}) collective-permute-start(bf16[512,512]{1,0:T(8,128)(2,1)S(1)} %bitcast.138), channel_id=1, source_target_pairs={{0,3},{1,0},{2,1},{3,2},{4,7},{5,4},{6,5},{7,6},{8,11},{9,8},{10,9... | collective-permute-start | bytes 1572872 | tf_op jit(solution)/shard_map/ppermute | solution.py:29
  156.0 28.6 %collective-permute-start.9 = (bf16[512,512]{1,0:T(8,128)(2,1)S(1)}, bf16[512,512]{1,0:T(8,128)(2,1)}, u32[]{:S(2)}, u32[]{:S(2)}) collective-permute-start(bf16[512,512]{1,0:T(8,128)(2,1)S(1)} %bitcast.139), channel_id=1, source_target_pairs={{0,1},{1,2},{2,3},{3,0},{4,5},{5,6},{6,7},{7,4},{8,9},{9,10},{10,1... | collective-permute-start | bytes 1572872 | tf_op jit(solution)/shard_map/ppermute | solution.py:29
  164.5 19.1 %copy-start.5 = (bf16[64,2048]{1,0:T(8,128)(2,1)S(1)}, bf16[64,2048]{1,0:T(8,128)(2,1)}, u32[]{:S(2)}) copy-start(bf16[64,2048]{1,0:T(8,128)(2,1)} %param.15) | copy-start | bytes 786436
  183.7 14.5 %collective-permute-start.36 = (bf16[64,2048]{1,0:T(8,128)(2,1)S(1)}, bf16[64,2048]{1,0:T(8,128)(2,1)S(1)}, u32[]{:S(2)}, u32[]{:S(2)}) collective-permute-start(bf16[64,2048]{1,0:T(8,128)(2,1)S(1)} %copy-done.5), channel_id=1, source_target_pairs={{0,10},{1,11},{2,12},{3,13},{4,14},{5,15},{6,0},{7,1},{8,2},{9,3},... | collective-permute-start | bytes 786440 | tf_op jit(solution)/shard_map/ppermute | solution.py:29
  183.7 47.5 %collective-permute-start.37 = (bf16[64,2048]{1,0:T(8,128)(2,1)S(1)}, bf16[64,2048]{1,0:T(8,128)(2,1)S(1)}, u32[]{:S(2)}, u32[]{:S(2)}) collective-permute-start(bf16[64,2048]{1,0:T(8,128)(2,1)S(1)} %copy-done.5), channel_id=1, source_target_pairs={{0,11},{1,12},{2,13},{3,14},{4,15},{5,0},{6,1},{7,2},{8,3},{9,4},{... | collective-permute-start | bytes 786440 | tf_op jit(solution)/shard_map/ppermute | solution.py:29
  184.7 47.3 %collective-permute-start.38 = (bf16[64,2048]{1,0:T(8,128)(2,1)S(1)}, bf16[64,2048]{1,0:T(8,128)(2,1)S(1)}, u32[]{:S(2)}, u32[]{:S(2)}) collective-permute-start(bf16[64,2048]{1,0:T(8,128)(2,1)S(1)} %copy-done.5), channel_id=1, source_target_pairs={{0,12},{1,13},{2,14},{3,15},{4,0},{5,1},{6,2},{7,3},{8,4},{9,5},{1... | collective-permute-start | bytes 786440 | tf_op jit(solution)/shard_map/ppermute | solution.py:29
  191.9 54.7 %copy-start.7 = (s32[6]{0:T(128)S(1)}, s32[6]{0:T(128)}, u32[]{:S(2)}) copy-start(s32[6]{0:T(128)} %param.16) | copy-start | bytes 76
  191.9 40.8 %collective-permute-start.39 = (bf16[64,2048]{1,0:T(8,128)(2,1)S(1)}, bf16[64,2048]{1,0:T(8,128)(2,1)S(1)}, u32[]{:S(2)}, u32[]{:S(2)}) collective-permute-start(bf16[64,2048]{1,0:T(8,128)(2,1)S(1)} %copy-done.5), channel_id=1, source_target_pairs={{0,13},{1,14},{2,15},{3,0},{4,1},{5,2},{6,3},{7,4},{8,5},{9,6},{10... | collective-permute-start | bytes 786440 | tf_op jit(solution)/shard_map/ppermute | solution.py:29
  193.6 39.9 %collective-permute-start.40 = (bf16[64,2048]{1,0:T(8,128)(2,1)S(1)}, bf16[64,2048]{1,0:T(8,128)(2,1)S(1)}, u32[]{:S(2)}, u32[]{:S(2)}) collective-permute-start(bf16[64,2048]{1,0:T(8,128)(2,1)S(1)} %copy-done.5), channel_id=1, source_target_pairs={{0,14},{1,15},{2,0},{3,1},{4,2},{5,3},{6,4},{7,5},{8,6},{9,7},{10,... | collective-permute-start | bytes 786440 | tf_op jit(solution)/shard_map/ppermute | solution.py:29
  198.2 42.0 %collective-permute-start.41 = (bf16[64,2048]{1,0:T(8,128)(2,1)S(1)}, bf16[64,2048]{1,0:T(8,128)(2,1)S(1)}, u32[]{:S(2)}, u32[]{:S(2)}) collective-permute-start(bf16[64,2048]{1,0:T(8,128)(2,1)S(1)} %copy-done.5), channel_id=1, source_target_pairs={{0,15},{1,0},{2,1},{3,2},{4,3},{5,4},{6,5},{7,6},{8,7},{9,8},{10,9... | collective-permute-start | bytes 786440 | tf_op jit(solution)/shard_map/ppermute | solution.py:29
  261.0 10.1 %collective-permute-start.12 = (bf16[64,2048]{1,0:T(8,128)(2,1)S(1)}, bf16[64,2048]{1,0:T(8,128)(2,1)S(1)}, u32[]{:S(2)}, u32[]{:S(2)}) collective-permute-start(bf16[64,2048]{1,0:T(8,128)(2,1)S(1)} %convert_element_type.98), channel_id=1, source_target_pairs={{0,1},{1,2},{2,3},{3,4},{4,5},{5,6},{6,7},{7,8},{8,9},{9,10},{10,1... | collective-permute-start | bytes 786440 | tf_op jit(solution)/shard_map/ppermute | solution.py:29
  262.5 102.5 %copy-start.1 = (bf16[16,64,2048]{2,1,0:T(8,128)(2,1)S(1)}, bf16[16,64,2048]{2,1,0:T(8,128)(2,1)}, u32[]{:S(2)}) copy-start(bf16[16,64,2048]{2,1,0:T(8,128)(2,1)} %bitcast_dynamic-update-slice_fusion) | copy-start | bytes 12582916
  262.5 12.9 %collective-permute-start.13 = (bf16[64,2048]{1,0:T(8,128)(2,1)S(1)}, bf16[64,2048]{1,0:T(8,128)(2,1)S(1)}, u32[]{:S(2)}, u32[]{:S(2)}) collective-permute-start(bf16[64,2048]{1,0:T(8,128)(2,1)S(1)} %convert_element_type.98), channel_id=1, source_target_pairs={{0,2},{1,3},{2,4},{3,5},{4,6},{5,7},{6,8},{7,9},{8,10},{9,11},{10,... | collective-permute-start | bytes 786440 | tf_op jit(solution)/shard_map/ppermute | solution.py:29
  262.6 15.4 %collective-permute-start.14 = (bf16[64,2048]{1,0:T(8,128)(2,1)S(1)}, bf16[64,2048]{1,0:T(8,128)(2,1)S(1)}, u32[]{:S(2)}, u32[]{:S(2)}) collective-permute-start(bf16[64,2048]{1,0:T(8,128)(2,1)S(1)} %convert_element_type.98), channel_id=1, source_target_pairs={{0,3},{1,4},{2,5},{3,6},{4,7},{5,8},{6,9},{7,10},{8,11},{9,12},{10... | collective-permute-start | bytes 786440 | tf_op jit(solution)/shard_map/ppermute | solution.py:29
  266.0 13.3 %collective-permute-start.15 = (bf16[64,2048]{1,0:T(8,128)(2,1)S(1)}, bf16[64,2048]{1,0:T(8,128)(2,1)S(1)}, u32[]{:S(2)}, u32[]{:S(2)}) collective-permute-start(bf16[64,2048]{1,0:T(8,128)(2,1)S(1)} %convert_element_type.98), channel_id=1, source_target_pairs={{0,4},{1,5},{2,6},{3,7},{4,8},{5,9},{6,10},{7,11},{8,12},{9,13},{1... | collective-permute-start | bytes 786440 | tf_op jit(solution)/shard_map/ppermute | solution.py:29
  271.1 44.2 %collective-permute-start.16 = (bf16[64,2048]{1,0:T(8,128)(2,1)S(1)}, bf16[64,2048]{1,0:T(8,128)(2,1)S(1)}, u32[]{:S(2)}, u32[]{:S(2)}) collective-permute-start(bf16[64,2048]{1,0:T(8,128)(2,1)S(1)} %convert_element_type.98), channel_id=1, source_target_pairs={{0,5},{1,6},{2,7},{3,8},{4,9},{5,10},{6,11},{7,12},{8,13},{9,14},{... | collective-permute-start | bytes 786440 | tf_op jit(solution)/shard_map/ppermute | solution.py:29
  271.1 44.3 %collective-permute-start.17 = (bf16[64,2048]{1,0:T(8,128)(2,1)S(1)}, bf16[64,2048]{1,0:T(8,128)(2,1)S(1)}, u32[]{:S(2)}, u32[]{:S(2)}) collective-permute-start(bf16[64,2048]{1,0:T(8,128)(2,1)S(1)} %convert_element_type.98), channel_id=1, source_target_pairs={{0,6},{1,7},{2,8},{3,9},{4,10},{5,11},{6,12},{7,13},{8,14},{9,15},... | collective-permute-start | bytes 786440 | tf_op jit(solution)/shard_map/ppermute | solution.py:29
  275.5 53.8 %collective-permute-start.18 = (bf16[64,2048]{1,0:T(8,128)(2,1)S(1)}, bf16[64,2048]{1,0:T(8,128)(2,1)S(1)}, u32[]{:S(2)}, u32[]{:S(2)}) collective-permute-start(bf16[64,2048]{1,0:T(8,128)(2,1)S(1)} %convert_element_type.98), channel_id=1, source_target_pairs={{0,7},{1,8},{2,9},{3,10},{4,11},{5,12},{6,13},{7,14},{8,15},{9,0},... | collective-permute-start | bytes 786440 | tf_op jit(solution)/shard_map/ppermute | solution.py:29
  278.0 58.6 %collective-permute-start.19 = (bf16[64,2048]{1,0:T(8,128)(2,1)S(1)}, bf16[64,2048]{1,0:T(8,128)(2,1)S(1)}, u32[]{:S(2)}, u32[]{:S(2)}) collective-permute-start(bf16[64,2048]{1,0:T(8,128)(2,1)S(1)} %convert_element_type.98), channel_id=1, source_target_pairs={{0,8},{1,9},{2,10},{3,11},{4,12},{5,13},{6,14},{7,15},{8,0},{9,1},... | collective-permute-start | bytes 786440 | tf_op jit(solution)/shard_map/ppermute | solution.py:29
  279.3 67.7 %collective-permute-start.20 = (bf16[64,2048]{1,0:T(8,128)(2,1)S(1)}, bf16[64,2048]{1,0:T(8,128)(2,1)S(1)}, u32[]{:S(2)}, u32[]{:S(2)}) collective-permute-start(bf16[64,2048]{1,0:T(8,128)(2,1)S(1)} %convert_element_type.98), channel_id=1, source_target_pairs={{0,9},{1,10},{2,11},{3,12},{4,13},{5,14},{6,15},{7,0},{8,1},{9,2},... | collective-permute-start | bytes 786440 | tf_op jit(solution)/shard_map/ppermute | solution.py:29
  315.2 37.9 %collective-permute-start.21 = (bf16[64,2048]{1,0:T(8,128)(2,1)S(1)}, bf16[64,2048]{1,0:T(8,128)(2,1)S(1)}, u32[]{:S(2)}, u32[]{:S(2)}) collective-permute-start(bf16[64,2048]{1,0:T(8,128)(2,1)S(1)} %convert_element_type.98), channel_id=1, source_target_pairs={{0,10},{1,11},{2,12},{3,13},{4,14},{5,15},{6,0},{7,1},{8,2},{9,3},... | collective-permute-start | bytes 786440 | tf_op jit(solution)/shard_map/ppermute | solution.py:29
  315.4 43.8 %collective-permute-start.22 = (bf16[64,2048]{1,0:T(8,128)(2,1)S(1)}, bf16[64,2048]{1,0:T(8,128)(2,1)S(1)}, u32[]{:S(2)}, u32[]{:S(2)}) collective-permute-start(bf16[64,2048]{1,0:T(8,128)(2,1)S(1)} %convert_element_type.98), channel_id=1, source_target_pairs={{0,11},{1,12},{2,13},{3,14},{4,15},{5,0},{6,1},{7,2},{8,3},{9,4},{... | collective-permute-start | bytes 786440 | tf_op jit(solution)/shard_map/ppermute | solution.py:29
  329.2 30.0 %collective-permute-start.23 = (bf16[64,2048]{1,0:T(8,128)(2,1)S(1)}, bf16[64,2048]{1,0:T(8,128)(2,1)S(1)}, u32[]{:S(2)}, u32[]{:S(2)}) collective-permute-start(bf16[64,2048]{1,0:T(8,128)(2,1)S(1)} %convert_element_type.98), channel_id=1, source_target_pairs={{0,12},{1,13},{2,14},{3,15},{4,0},{5,1},{6,2},{7,3},{8,4},{9,5},{1... | collective-permute-start | bytes 786440 | tf_op jit(solution)/shard_map/ppermute | solution.py:29
  336.6 22.7 %collective-permute-start.24 = (bf16[64,2048]{1,0:T(8,128)(2,1)S(1)}, bf16[64,2048]{1,0:T(8,128)(2,1)S(1)}, u32[]{:S(2)}, u32[]{:S(2)}) collective-permute-start(bf16[64,2048]{1,0:T(8,128)(2,1)S(1)} %convert_element_type.98), channel_id=1, source_target_pairs={{0,13},{1,14},{2,15},{3,0},{4,1},{5,2},{6,3},{7,4},{8,5},{9,6},{10... | collective-permute-start | bytes 786440 | tf_op jit(solution)/shard_map/ppermute | solution.py:29
  347.0 14.5 %collective-permute-start.25 = (bf16[64,2048]{1,0:T(8,128)(2,1)S(1)}, bf16[64,2048]{1,0:T(8,128)(2,1)S(1)}, u32[]{:S(2)}, u32[]{:S(2)}) collective-permute-start(bf16[64,2048]{1,0:T(8,128)(2,1)S(1)} %convert_element_type.98), channel_id=1, source_target_pairs={{0,14},{1,15},{2,0},{3,1},{4,2},{5,3},{6,4},{7,5},{8,6},{9,7},{10,... | collective-permute-start | bytes 786440 | tf_op jit(solution)/shard_map/ppermute | solution.py:29
  353.2 11.8 %collective-permute-start.26 = (bf16[64,2048]{1,0:T(8,128)(2,1)S(1)}, bf16[64,2048]{1,0:T(8,128)(2,1)S(1)}, u32[]{:S(2)}, u32[]{:S(2)}) collective-permute-start(bf16[64,2048]{1,0:T(8,128)(2,1)S(1)} %convert_element_type.98), channel_id=1, source_target_pairs={{0,15},{1,0},{2,1},{3,2},{4,3},{5,4},{6,5},{7,6},{8,7},{9,8},{10,9... | collective-permute-start | bytes 786440 | tf_op jit(solution)/shard_map/ppermute | solution.py:29
  365.1 13.7 %copy-start.3 = (bf16[16,64,384]{2,1,0:T(8,128)(2,1)S(1)}, bf16[16,64,384]{2,1,0:T(8,128)(2,1)}, u32[]{:S(2)}) copy-start(bf16[16,64,384]{2,1,0:T(8,128)(2,1)} %rev.15) | copy-start | bytes 2359300
Sparse Core Ops, SparseCore 0:
  8.9 107.1 all-gather.4
  117.7 63.1 all-gather.2
  192.0 67.0 reduce-scatter.1

commit v7 on v3

--- a/solution.py
+++ b/solution.py
@@ -74,17 +74,37 @@
     na = lax.axis_size("wa")
     rows = gradient_rows.shape[0]
     gradient_rows = gradient_rows.reshape(rows, nb, na, -1).transpose(0, 2, 1, 3).reshape(rows, -1)
-    query_gradient = lax.all_gather(gradient_rows.astype(jnp.bfloat16), WIDE, axis=0, tiled=True)
-    eig_full = lax.all_gather(eig_values, WIDE, axis=0, tiled=True)
-    eig_in, eig_out = eig_full.shape
-    mean_eig = jnp.sum(eig_full.astype(jnp.float32)) / (eig_in * eig_out)
+    eig_in = eig_values.shape[0] * lax.axis_size(WIDE)
+    eig_out = eig_values.shape[1]
+    eig_total = lax.psum(jnp.sum(eig_values.astype(jnp.float32)), WIDE)
+    mean_eig = eig_total / (eig_in * eig_out)
     dampings = mean_eig * jnp.exp2(damping_index.astype(jnp.float32) - 4.0)
-    totals = score_rows(query_gradient, eig_full, dampings, train_act_rot, train_grad_rot)
+    payload = jnp.concatenate([gradient_rows.astype(jnp.bfloat16), eig_values], axis=1)
+    rows_held = lax.all_gather(payload, "wa", axis=0, tiled=True)
+    gradient_held, eig_held = rows_held[:, :eig_out], rows_held[:, eig_out:]
+    grads_near = ring_gather(train_grad_rot, "wb")
+    me = lax.axis_index("wb")
+    act_blocks = train_act_rot.reshape(na, nb, -1, train_act_rot.shape[1])
+    acts_near = [act_blocks[:, me]]
+    for shift in range(1, nb):
+        outgoing = lax.dynamic_index_in_dim(act_blocks, (me + shift) % nb, axis=1, keepdims=False)
+        acts_near.append(lax.ppermute(outgoing, "wb", perm=[(i, (i + shift) % nb) for i in range(nb)]))
+    acts_near = jnp.stack(acts_near).reshape(nb, na * act_blocks.shape[2], -1).astype(jnp.float32)
+    grad_wide = gradient_held.astype(jnp.float32)
+    eig_wide = eig_held.astype(jnp.float32)
+    results = []
+    for damping in range(dampings.shape[0]):
+        precond = (grad_wide / (eig_wide + dampings[damping])).astype(jnp.bfloat16)
+        projected = jnp.einsum("ij,sjt->sit", precond, grads_near, preferred_element_type=jnp.float32)
+        results.append(jnp.sum(projected * acts_near, axis=1))
+    partial = jnp.stack(results, axis=1)
+    totals = partial[0]
+    for shift in range(1, nb):
+        totals = totals + lax.ppermute(partial[shift], "wb", perm=[(i, (i - shift) % nb) for i in range(nb)])
     query_count = query_act.shape[0] * lax.axis_size(WIDE)
     factor = mean_eig * (1.0 / math.sqrt(float(query_count) * eig_in * eig_out))
     train_weight = jnp.where(train_positions >= PROMPT, 1.0, 0.0).astype(jnp.float32)
     return totals * factor * train_weight[None, :]
-
 
 def split_wide(size):
     wb = 1

time: 310 us -> 341 us (1.10)
  blocking collectives: 0 us -> 93.9 us
  waiting for transfers between devices: 235 us -> 164 us
  starting transfers between devices: 8.37 us -> 16 us
  matrix products: 34.4 us -> 40.9 us
  other arithmetic: 13.6 us -> 8.64 us
    psum x0 -> x1, blocking collectives: none -> 93.9 us  [shards(): eig_total = lax.psum(jnp.sum(eig_values.astype(jnp.float32)), WIDE)]
    all_gather x2 -> x1, waiting for transfers between devices: 72.2 us -> 0.02 us  [shards(): rows_held = lax.all_gather(payload, 'wa', axis=0, tiled=True)]
    dot_general x6, matrix products: 22.2 us -> 29.5 us  [shards(): jnp.einsum('ij,sjt->sit', precond, grads_near, preferred_element_type=jnp...]
    ppermute x0 -> x6, waiting for transfers between devices: none -> 5.75 us  [the longest x3 4.41 us: shards(): lax.ppermute(outgoing, 'wb', perm=[(i, (i + shift) % nb) for i in range(n...]
    reduce_scatter x1, waiting for transfers between devices: 49.2 us -> 43.9 us  [shards(): lax.psum_scatter(partial_rows, 'wa', scatter_dimension=0, tiled=True)]
    ppermute x0 -> x6, starting transfers between devices: none -> 4.92 us  [the longest x3 3.1 us: shards(): lax.ppermute(outgoing, 'wb', perm=[(i, (i + shift) % nb) for i in range(n...]
    reduce_sum x1, other arithmetic: 4.95 us -> 0.73 us  [shards(): eig_total = lax.psum(jnp.sum(eig_values.astype(jnp.float32)), WIDE)]
    ppermute x9 -> x12, starting transfers between devices: 7.98 us -> 10.9 us  [ring_gather(): lax.ppermute(x, axis, perm=[(i, (i + shift) % n) for i in range(n)])]
  transfers between devices with their start and end apart: 15 -> 23, of which waited for: 10 -> 10; matrix products, arithmetic and copies ran while one was open for 8% -> 4% of each run, Pallas kernels for 0% -> 0%
where the time goes in v7:
time: 341 us; the launch traced here: 340 us
  waiting for transfers between devices  164 us (48%)
  blocking collectives  93.9 us (28%)
  matrix products  40.9 us (12%)
  starting transfers between devices  16 us (5%)
  between operations  14.8 us (4%)
  other arithmetic  8.64 us (3%)
    psum x1, blocking collectives, shards(): eig_total = lax.psum(jnp.sum(eig_values.astype(jnp.float32)), WIDE)  93.9 us
    ppermute x12, waiting for transfers between devices, ring_gather(): lax.ppermute(x, axis, perm=[(i, (i + shift) % n) for i in range(n)])  68.7 us
    reduce_scatter x1, waiting for transfers between devices, shards(): lax.psum_scatter(partial_rows, 'wa', scatter_dimension=0, tiled=True)  43.9 us
    dot_general x6, matrix products, shards(): jnp.einsum('ij,sjt->sit', precond, grads_near, preferred_element_type=jnp...  29.5 us
    all_gather x1, waiting for transfers between devices, shards(): grad_cols = lax.all_gather(grad_basis, 'wa', axis=1, tiled=True)  28.7 us
    all_gather x1, waiting for transfers between devices, shards(): grad_all = lax.all_gather(grad_kept, 'wb', axis=1, tiled=True)  16.4 us
    ppermute x12, starting transfers between devices, ring_gather(): lax.ppermute(x, axis, perm=[(i, (i + shift) % n) for i in range(n)])  10.9 us
  transfers between devices with their start and end apart: 23, of which 10 were waited for; matrix products, arithmetic and copies ran while one was open for 4% of the time, Pallas kernels for 0%

profile of v7, /device:TPU:0, one launch (start us, length us, event | category | flops | bytes accessed | tf_op | source)
XLA Modules:
  0.0 339.8 jit_solution(2628064255703927935)
XLA Ops:
  6.5 0.7 all-gather.7.cloned.1.call-update
  7.3 0.0 all-gather.5.cloned.1.call-start
  7.3 2.5 collective-permute-start.8
  9.8 0.6 collective-permute-start.7
  10.4 0.2 collective-permute-start.6
  10.6 0.0 all-gather.5.cloned.1.call-update
  10.6 0.0 all-gather.9.cloned.1.call-start
  10.6 1.6 collective-permute-start.11
  12.3 1.4 collective-permute-start.10
  13.7 42.3 %collective-permute-done.11 = s32[128]{0:T(128)S(1)} collective-permute-done((s32[128]{0:T(128)}, s32[128]{0:T(128)S(1)}, u32[]{:S(2)}, u32[]{:S(2)}) %collective-permute-start.11) | collective-permute-done | bytes 544 | tf_op jit(solution)/shard_map/ppermute | solution.py:29
  56.0 1.1 collective-permute-start.9
  57.0 2.5 collective-permute-done.9
  59.5 0.7 fusion.44
  60.2 3.3 pad_maximum_fusion.1
  63.5 28.7 %all-gather.7.cloned.1.call-done = bf16[4096,512]{1,0:T(8,128)(2,1)} async-done(((bf16[4096,128]{1,0:T(8,128)(2,1)}), bf16[4096,512]{1,0:T(8,128)(2,1)}) %all-gather.7.cloned.1.call-update) | async-done | bytes 4194320 | tf_op jit(solution)/shard_map/all_gather | solution.py:57
  92.2 5.8 %fusion.12 = bf16[512,512]{1,0:T(8,128)(2,1)S(1)} fusion(bf16[512,4096]{1,0:T(8,128)(2,1)} %bitcast.98, bf16[4096,512]{1,0:T(8,128)(2,1)} %all-gather.7.cloned.1.call-done, bf16[512]{0:T(512)(128)(2,1)S(1)} %fusion.44), kind=kOutput, calls=%fused_computation.34 | convolution fusion | flops 2148007936 | bytes 8913920 | tf_op jit(solution)/shard_map/dot_general | solution.py:62
  98.1 1.0 fusion.25
  99.1 0.0 all-gather.9.cloned.1.call-update
  99.1 0.0 reduce-scatter.2.cloned.1.call-start
  99.2 1.2 collective-permute-start.5
  100.4 0.5 collective-permute-start.4
  100.8 0.1 collective-permute-start.3
  100.9 11.7 %collective-permute-done.5 = bf16[128,2048]{1,0:T(8,128)(2,1)S(1)} collective-permute-done((bf16[128,2048]{1,0:T(8,128)(2,1)S(1)}, bf16[128,2048]{1,0:T(8,128)(2,1)S(1)}, u32[]{:S(2)}, u32[]{:S(2)}) %collective-permute-start.5) | collective-permute-done | bytes 524320 | tf_op jit(solution)/shard_map/ppermute | solution.py:29
  112.7 12.1 %collective-permute-done.4 = bf16[128,2048]{1,0:T(8,128)(2,1)S(1)} collective-permute-done((bf16[128,2048]{1,0:T(8,128)(2,1)S(1)}, bf16[128,2048]{1,0:T(8,128)(2,1)S(1)}, u32[]{:S(2)}, u32[]{:S(2)}) %collective-permute-start.4) | collective-permute-done | bytes 524320 | tf_op jit(solution)/shard_map/ppermute | solution.py:29
  124.8 0.3 pad_maximum_fusion.2
  125.1 0.0 all-gather.5.cloned.1.call-done
  125.1 2.0 convolution_convert_fusion.1
  127.1 0.1 fusion.38
  127.2 16.4 %all-gather.9.cloned.1.call-done = bf16[512,2048]{1,0:T(8,128)(2,1)} async-done(((bf16[512,512]{1,0:T(8,128)(2,1)}), bf16[512,2048]{1,0:T(8,128)(2,1)}) %all-gather.9.cloned.1.call-update) | async-done | bytes 2097168 | tf_op jit(solution)/shard_map/all_gather | solution.py:69
  143.6 3.6 %fusion.46 = f32[256,2048]{1,0:T(8,128)} fusion(bf16[512,256]{1,0:T(8,128)(2,1)S(1)} %bitcast.101, bf16[512,2048]{1,0:T(8,128)(2,1)} %all-gather.9.cloned.1.call-done), kind=kOutput, calls=%fused_computation.82 | convolution fusion | flops 536870912 | bytes 4456448 | tf_op jit(solution)/shard_map/dot_general | solution.py:70
  147.3 0.0 reduce-scatter.2.cloned.1.call-update
  147.3 0.0 all-gather.11.cloned.1.call-start
  147.4 43.9 %reduce-scatter.2.cloned.1.call-done = f32[64,2048]{1,0:T(8,128)} async-done(((f32[256,2048]{1,0:T(8,128)}), f32[64,2048]{1,0:T(8,128)}) %reduce-scatter.2.cloned.1.call-update) | async-done | bytes 524304 | tf_op jit(solution)/shard_map/reduce_scatter | solution.py:73
  191.3 1.1 convert_element_type.65
  192.4 0.2 convert_element_type.66
  192.6 0.1 copy.11
  192.7 0.2 convert_element_type.68
  192.9 0.8 pad_maximum_fusion.4
  193.7 0.0 all-gather.11.cloned.1.call-update
  193.7 0.8 collective-permute-start.2
  194.6 0.8 collective-permute-start.1
  195.4 0.2 collective-permute-start
  195.5 0.1 constant_dynamic-slice_fusion
  195.6 1.6 collective-permute-start.14
  197.2 0.7 convert_reduce_fusion
  198.0 1.2 collective-permute-start.13
  199.2 93.9 %psum.7 = f32[]{:T(128)} all-reduce(f32[]{:T(128)} %convert_reduce_fusion), channel_id=1, replica_groups=mesh['groups'=2,'wa'=4,'wb'=4] {'wa','wb'}, use_global_device_ids=true, to_apply=%region_2.3 | all-reduce | flops 1 | bytes 8 | tf_op jit(solution)/shard_map/psum | solution.py:79
  293.7 0.2 collective-permute-start.12
  294.0 0.6 fusion.45
  294.7 4.4 %collective-permute-done.12 = bf16[4,64,384]{2,1,0:T(8,128)(2,1)S(1)} collective-permute-done((bf16[4,64,384]{2,1,0:T(8,128)(2,1)S(1)}, bf16[4,64,384]{2,1,0:T(8,128)(2,1)S(1)}, u32[]{:S(2)}, u32[]{:S(2)}) %collective-permute-start.12) | collective-permute-done | bytes 196640 | tf_op jit(solution)/shard_map/ppermute | solution.py:91
  299.1 0.0 all-gather.11.cloned.1.call-done
  299.1 5.5 %fusion.6 = f32[4,384]{1,0:T(4,128)S(1)} fusion(f32[]{:T(128)} %bitcast.24, bf16[256,4096]{1,0:T(8,128)(2,1)} %all-gather.11.cloned.1.call-done, bf16[1,256,384]{2,1,0:T(8,128)(2,1)S(1)} %bitcast.130, bf16[1,256,384]{2,1,0:T(8,128)(2,1)S(1)} %bitcast.136, bf16[1,256,384]{2,1,0:T(8,128)(2,1)S(1)} %bitcast.142, bf16[1,256,384]{2,1,0:T(8,128)(2,1)S(1)} %bitcast.114, ...), kind=kOutput, calls=%fused_computation.27 | convolution fusion | flops 1640757760 | bytes 9181188 | tf_op jit(solution)/shard_map/ij,sjt->sit/dot_general | solution.py:98
  304.7 4.8 %fusion.7 = f32[4,384]{1,0:T(4,128)S(1)} fusion(f32[]{:T(128)} %bitcast.35, bf16[256,4096]{1,0:T(8,128)(2,1)S(1)} %copy-done.4, bf16[1,256,384]{2,1,0:T(8,128)(2,1)S(1)} %bitcast.131, bf16[1,256,384]{2,1,0:T(8,128)(2,1)S(1)} %bitcast.137, bf16[1,256,384]{2,1,0:T(8,128)(2,1)S(1)} %bitcast.143, bf16[1,256,384]{2,1,0:T(8,128)(2,1)S(1)} %bitcast.115, ...), kind=kOutput, calls=%fused_computation.28 | convolution fusion | flops 1640757760 | bytes 9181188 | tf_op jit(solution)/shard_map/ij,sjt->sit/dot_general | solution.py:98
  309.5 4.8 %fusion.8 = f32[4,384]{1,0:T(4,128)S(1)} fusion(f32[]{:T(128)} %bitcast.38, bf16[256,4096]{1,0:T(8,128)(2,1)S(1)} %copy-done.4, bf16[1,256,384]{2,1,0:T(8,128)(2,1)S(1)} %bitcast.132, bf16[1,256,384]{2,1,0:T(8,128)(2,1)S(1)} %bitcast.138, bf16[1,256,384]{2,1,0:T(8,128)(2,1)S(1)} %bitcast.144, bf16[1,256,384]{2,1,0:T(8,128)(2,1)S(1)} %bitcast.116, ...), kind=kOutput, calls=%fused_computation.29 | convolution fusion | flops 1640757760 | bytes 9181188 | tf_op jit(solution)/shard_map/ij,sjt->sit/dot_general | solution.py:98
  314.3 4.8 %fusion.9 = f32[4,384]{1,0:T(4,128)S(1)} fusion(f32[]{:T(128)} %bitcast.41, bf16[256,4096]{1,0:T(8,128)(2,1)S(1)} %copy-done.4, bf16[1,256,384]{2,1,0:T(8,128)(2,1)S(1)} %bitcast.133, bf16[1,256,384]{2,1,0:T(8,128)(2,1)S(1)} %bitcast.139, bf16[1,256,384]{2,1,0:T(8,128)(2,1)S(1)} %bitcast.145, bf16[1,256,384]{2,1,0:T(8,128)(2,1)S(1)} %bitcast.117, ...), kind=kOutput, calls=%fused_computation.30 | convolution fusion | flops 1640757760 | bytes 9181188 | tf_op jit(solution)/shard_map/ij,sjt->sit/dot_general | solution.py:98
  319.1 4.8 %fusion.10 = f32[4,384]{1,0:T(4,128)S(1)} fusion(f32[]{:T(128)} %bitcast.44, bf16[256,4096]{1,0:T(8,128)(2,1)S(1)} %copy-done.4, bf16[1,256,384]{2,1,0:T(8,128)(2,1)S(1)} %bitcast.134, bf16[1,256,384]{2,1,0:T(8,128)(2,1)S(1)} %bitcast.140, bf16[1,256,384]{2,1,0:T(8,128)(2,1)S(1)} %bitcast.146, bf16[1,256,384]{2,1,0:T(8,128)(2,1)S(1)} %bitcast.118, ...), kind=kOutput, calls=%fused_computation.31 | convolution fusion | flops 1640757760 | bytes 9181188 | tf_op jit(solution)/shard_map/ij,sjt->sit/dot_general | solution.py:98
  323.9 4.8 %fusion.11 = f32[4,384]{1,0:T(4,128)S(1)} fusion(f32[]{:T(128)} %bitcast.47, bf16[256,4096]{1,0:T(8,128)(2,1)S(1)} %copy-done.4, bf16[1,256,384]{2,1,0:T(8,128)(2,1)S(1)} %bitcast.135, bf16[1,256,384]{2,1,0:T(8,128)(2,1)S(1)} %bitcast.141, bf16[1,256,384]{2,1,0:T(8,128)(2,1)S(1)} %bitcast.147, bf16[1,256,384]{2,1,0:T(8,128)(2,1)S(1)} %bitcast.119, ...), kind=kOutput, calls=%fused_computation.32 | convolution fusion | flops 1640757760 | bytes 9181188 | tf_op jit(solution)/shard_map/ij,sjt->sit/dot_general | solution.py:98
  328.7 0.1 stack.126
  328.8 0.1 collective-permute-start.17
  328.9 0.1 collective-permute-start.16
  329.0 1.7 collective-permute-start.15
  331.3 0.7 collective-permute-done.17
  332.0 0.7 collective-permute-done.16
  332.6 0.6 fusion.43
  (37 shorter events, 0.2 us)
Async XLA Ops:
  6.5 85.7 %all-gather.7.cloned.1.call-start = ((), (), s32[]{:S(2)}) async-start(), calls=%async_computation.2 | async-start | bytes 5242880 | tf_op jit(solution)/shard_map/all_gather | solution.py:57
  7.3 117.8 %all-gather.5.cloned.1.call-start = ((), (), s32[]{:S(2)}) async-start(), calls=%async_computation.1 | async-start | bytes 1310720 | tf_op jit(solution)/shard_map/all_gather | solution.py:56
  7.3 52.9 %collective-permute-start.8 = (bf16[128,4096]{1,0:T(8,128)(2,1)}, bf16[128,4096]{1,0:T(8,128)(2,1)S(1)}, u32[]{:S(2)}, u32[]{:S(2)}) collective-permute-start(bf16[128,4096]{1,0:T(8,128)(2,1)} %param.11), channel_id=1, source_target_pairs={{0,3},{1,0},{2,1},{3,2},{4,7},{5,4},{6,5},{7,6},{8,11},{9,8},{10,9... | collective-permute-start | bytes 3145736 | tf_op jit(solution)/shard_map/ppermute | solution.py:29
  9.8 50.4 %collective-permute-start.7 = (bf16[128,4096]{1,0:T(8,128)(2,1)}, bf16[128,4096]{1,0:T(8,128)(2,1)S(1)}, u32[]{:S(2)}, u32[]{:S(2)}) collective-permute-start(bf16[128,4096]{1,0:T(8,128)(2,1)} %param.11), channel_id=1, source_target_pairs={{0,2},{1,3},{2,0},{3,1},{4,6},{5,7},{6,4},{7,5},{8,10},{9,11},{10,... | collective-permute-start | bytes 3145736 | tf_op jit(solution)/shard_map/ppermute | solution.py:29
  10.4 49.8 %collective-permute-start.6 = (bf16[128,4096]{1,0:T(8,128)(2,1)}, bf16[128,4096]{1,0:T(8,128)(2,1)S(1)}, u32[]{:S(2)}, u32[]{:S(2)}) collective-permute-start(bf16[128,4096]{1,0:T(8,128)(2,1)} %param.11), channel_id=1, source_target_pairs={{0,1},{1,2},{2,3},{3,0},{4,5},{5,6},{6,7},{7,4},{8,9},{9,10},{10,1... | collective-permute-start | bytes 3145736 | tf_op jit(solution)/shard_map/ppermute | solution.py:29
  10.6 133.0 %all-gather.9.cloned.1.call-start = ((), (), s32[]{:S(2)}) async-start(), calls=%async_computation.3 | async-start | bytes 2621440 | tf_op jit(solution)/shard_map/all_gather | solution.py:69
  10.6 45.3 %collective-permute-start.11 = (s32[128]{0:T(128)}, s32[128]{0:T(128)S(1)}, u32[]{:S(2)}, u32[]{:S(2)}) collective-permute-start(s32[128]{0:T(128)} %param.12), channel_id=1, source_target_pairs={{0,3},{1,0},{2,1},{3,2},{4,7},{5,4},{6,5},{7,6},{8,11},{9,8},{10,9... | collective-permute-start | bytes 1544 | tf_op jit(solution)/shard_map/ppermute | solution.py:29
  12.3 44.8 %collective-permute-start.10 = (s32[128]{0:T(128)}, s32[128]{0:T(128)S(1)}, u32[]{:S(2)}, u32[]{:S(2)}) collective-permute-start(s32[128]{0:T(128)} %param.12), channel_id=1, source_target_pairs={{0,2},{1,3},{2,0},{3,1},{4,6},{5,7},{6,4},{7,5},{8,10},{9,11},{10,... | collective-permute-start | bytes 1544 | tf_op jit(solution)/shard_map/ppermute | solution.py:29
  56.0 3.5 %collective-permute-start.9 = (s32[128]{0:T(128)}, s32[128]{0:T(128)S(1)}, u32[]{:S(2)}, u32[]{:S(2)}) collective-permute-start(s32[128]{0:T(128)} %param.12), channel_id=1, source_target_pairs={{0,1},{1,2},{2,3},{3,0},{4,5},{5,6},{6,7},{7,4},{8,9},{9,10},{10,1... | collective-permute-start | bytes 1544 | tf_op jit(solution)/shard_map/ppermute | solution.py:29
  98.0 1.2 copy-start.2
  99.1 92.2 %reduce-scatter.2.cloned.1.call-start = ((), (), s32[]{:S(2)}) async-start(), calls=%async_computation.4 | async-start | bytes 2621440 | tf_op jit(solution)/shard_map/reduce_scatter | solution.py:73
  99.2 13.5 %collective-permute-start.5 = (bf16[128,2048]{1,0:T(8,128)(2,1)S(1)}, bf16[128,2048]{1,0:T(8,128)(2,1)S(1)}, u32[]{:S(2)}, u32[]{:S(2)}) collective-permute-start(bf16[128,2048]{1,0:T(8,128)(2,1)S(1)} %copy-done.2), channel_id=1, source_target_pairs={{0,3},{1,0},{2,1},{3,2},{4,7},{5,4},{6,5},{7,6},{8,11},{9,8},{10,9... | collective-permute-start | bytes 1572872 | tf_op jit(solution)/shard_map/ppermute | solution.py:29
  100.4 24.4 %collective-permute-start.4 = (bf16[128,2048]{1,0:T(8,128)(2,1)S(1)}, bf16[128,2048]{1,0:T(8,128)(2,1)S(1)}, u32[]{:S(2)}, u32[]{:S(2)}) collective-permute-start(bf16[128,2048]{1,0:T(8,128)(2,1)S(1)} %copy-done.2), channel_id=1, source_target_pairs={{0,2},{1,3},{2,0},{3,1},{4,6},{5,7},{6,4},{7,5},{8,10},{9,11},{10,... | collective-permute-start | bytes 1572872 | tf_op jit(solution)/shard_map/ppermute | solution.py:29
  100.8 24.0 %collective-permute-start.3 = (bf16[128,2048]{1,0:T(8,128)(2,1)S(1)}, bf16[128,2048]{1,0:T(8,128)(2,1)S(1)}, u32[]{:S(2)}, u32[]{:S(2)}) collective-permute-start(bf16[128,2048]{1,0:T(8,128)(2,1)S(1)} %copy-done.2), channel_id=1, source_target_pairs={{0,1},{1,2},{2,3},{3,0},{4,5},{5,6},{6,7},{7,4},{8,9},{9,10},{10,1... | collective-permute-start | bytes 1572872 | tf_op jit(solution)/shard_map/ppermute | solution.py:29
  147.3 45.6 %copy-start = (bf16[64,2048]{1,0:T(8,128)(2,1)S(1)}, bf16[64,2048]{1,0:T(8,128)(2,1)}, u32[]{:S(2)}) copy-start(bf16[64,2048]{1,0:T(8,128)(2,1)} %param.15) | copy-start | bytes 786436
  147.3 46.4 %copy-start.5 = (bf16[2048,384]{1,0:T(8,128)(2,1)S(1)}, bf16[2048,384]{1,0:T(8,128)(2,1)}, u32[]{:S(2)}) copy-start(bf16[2048,384]{1,0:T(8,128)(2,1)} %param.18) | copy-start | bytes 4718596
  147.3 48.2 %copy-start.1 = (bf16[1024,384]{1,0:T(8,128)(2,1)S(1)}, bf16[1024,384]{1,0:T(8,128)(2,1)}, u32[]{:S(2)}) copy-start(bf16[1024,384]{1,0:T(8,128)(2,1)} %param.17) | copy-start | bytes 2359300
  147.3 151.8 %all-gather.11.cloned.1.call-start = ((), (), s32[]{:S(2)}) async-start(), calls=%async_computation.5 | async-start | bytes 2621440 | tf_op jit(solution)/shard_map/all_gather | solution.py:83
  192.7 101.3 %copy-start.6 = (s32[6]{0:T(128)S(1)}, s32[6]{0:T(128)}, u32[]{:S(2)}) copy-start(s32[6]{0:T(128)} %param.16) | copy-start | bytes 76
  193.7 105.3 %collective-permute-start.2 = (bf16[2048,384]{1,0:T(8,128)(2,1)S(1)}, bf16[2048,384]{1,0:T(8,128)(2,1)}, u32[]{:S(2)}, u32[]{:S(2)}) collective-permute-start(bf16[2048,384]{1,0:T(8,128)(2,1)S(1)} %copy-done.5), channel_id=1, source_target_pairs={{0,3},{1,0},{2,1},{3,2},{4,7},{5,4},{6,5},{7,6},{8,11},{9,8},{10,9... | collective-permute-start | bytes 4718600 | tf_op jit(solution)/shard_map/ppermute | solution.py:29
  194.6 104.5 %collective-permute-start.1 = (bf16[2048,384]{1,0:T(8,128)(2,1)S(1)}, bf16[2048,384]{1,0:T(8,128)(2,1)}, u32[]{:S(2)}, u32[]{:S(2)}) collective-permute-start(bf16[2048,384]{1,0:T(8,128)(2,1)S(1)} %copy-done.5), channel_id=1, source_target_pairs={{0,2},{1,3},{2,0},{3,1},{4,6},{5,7},{6,4},{7,5},{8,10},{9,11},{10,... | collective-permute-start | bytes 4718600 | tf_op jit(solution)/shard_map/ppermute | solution.py:29
  195.4 103.7 %collective-permute-start = (bf16[2048,384]{1,0:T(8,128)(2,1)S(1)}, bf16[2048,384]{1,0:T(8,128)(2,1)}, u32[]{:S(2)}, u32[]{:S(2)}) collective-permute-start(bf16[2048,384]{1,0:T(8,128)(2,1)S(1)} %copy-done.5), channel_id=1, source_target_pairs={{0,1},{1,2},{2,3},{3,0},{4,5},{5,6},{6,7},{7,4},{8,9},{9,10},{10,1... | collective-permute-start | bytes 4718600 | tf_op jit(solution)/shard_map/ppermute | solution.py:29
  195.6 98.1 %collective-permute-start.14 = (bf16[4,64,384]{2,1,0:T(8,128)(2,1)S(1)}, bf16[4,64,384]{2,1,0:T(8,128)(2,1)S(1)}, u32[]{:S(2)}, u32[]{:S(2)}) collective-permute-start(bf16[4,64,384]{2,1,0:T(8,128)(2,1)S(1)} %get-tuple-element.6), channel_id=1, source_target_pairs={{0,3},{1,0},{2,1},{3,2},{4,7},{5,4},{6,5},{7,6},{8,11},{9,8},{10,9... | collective-permute-start | bytes 589832 | tf_op jit(solution)/shard_map/ppermute | solution.py:91
  198.0 96.7 %collective-permute-start.13 = (bf16[4,64,384]{2,1,0:T(8,128)(2,1)S(1)}, bf16[4,64,384]{2,1,0:T(8,128)(2,1)S(1)}, u32[]{:S(2)}, u32[]{:S(2)}) collective-permute-start(bf16[4,64,384]{2,1,0:T(8,128)(2,1)S(1)} %get-tuple-element.7), channel_id=1, source_target_pairs={{0,2},{1,3},{2,0},{3,1},{4,6},{5,7},{6,4},{7,5},{8,10},{9,11},{10,... | collective-permute-start | bytes 589832 | tf_op jit(solution)/shard_map/ppermute | solution.py:91
  293.7 5.3 %collective-permute-start.12 = (bf16[4,64,384]{2,1,0:T(8,128)(2,1)S(1)}, bf16[4,64,384]{2,1,0:T(8,128)(2,1)S(1)}, u32[]{:S(2)}, u32[]{:S(2)}) collective-permute-start(bf16[4,64,384]{2,1,0:T(8,128)(2,1)S(1)} %get-tuple-element.8), channel_id=1, source_target_pairs={{0,1},{1,2},{2,3},{3,0},{4,5},{5,6},{6,7},{7,4},{8,9},{9,10},{10,1... | collective-permute-start | bytes 589832 | tf_op jit(solution)/shard_map/ppermute | solution.py:91
  299.1 5.5 %copy-start.4 = (bf16[256,4096]{1,0:T(8,128)(2,1)S(1)}, bf16[256,4096]{1,0:T(8,128)(2,1)}, u32[]{:S(2)}) copy-start(bf16[256,4096]{1,0:T(8,128)(2,1)} %all-gather.11.cloned.1.call-done) | copy-start | bytes 6291460
  323.9 6.7 %copy-start.3 = (s32[384]{0:T(512)S(1)}, s32[384]{0:T(512)}, u32[]{:S(2)}) copy-start(s32[384]{0:T(512)} %param.19) | copy-start | bytes 4612
  328.8 3.2 collective-permute-start.17
  328.9 3.8 %collective-permute-start.16 = (f32[6,384]{1,0:T(8,128)S(1)}, f32[6,384]{1,0:T(8,128)S(1)}, u32[]{:S(2)}, u32[]{:S(2)}) collective-permute-start(f32[6,384]{1,0:T(8,128)S(1)} %get-tuple-element.11), channel_id=1, source_target_pairs={{0,2},{1,3},{2,0},{3,1},{4,6},{5,7},{6,4},{7,5},{8,10},{9,11},{10,... | collective-permute-start | bytes 27656 | tf_op jit(solution)/shard_map/ppermute | solution.py:103
  329.0 3.7 %collective-permute-start.15 = (f32[6,384]{1,0:T(8,128)S(1)}, f32[6,384]{1,0:T(8,128)S(1)}, u32[]{:S(2)}, u32[]{:S(2)}) collective-permute-start(f32[6,384]{1,0:T(8,128)S(1)} %get-tuple-element.9), channel_id=1, source_target_pairs={{0,3},{1,0},{2,1},{3,2},{4,7},{5,4},{6,5},{7,6},{8,11},{9,8},{10,9... | collective-permute-start | bytes 27656 | tf_op jit(solution)/shard_map/ppermute | solution.py:103
Sparse Core Ops, SparseCore 0:
  8.9 83.2 all-gather.6
  93.8 26.1 all-gather.4
  121.5 22.0 all-gather.8
  147.4 43.8 reduce-scatter.1
  193.8 45.3 all-gather.10

commit v8 on v7

--- a/solution.py
+++ b/solution.py
@@ -50,9 +50,22 @@
     train_positions,
 ):
     nb = lax.axis_size("wb")
+    na = lax.axis_size("wa")
     act_tokens = ring_gather(query_act, "wb")
     grad_tokens = ring_gather(query_grad, "wb")
     positions = ring_gather(query_positions, "wb")
+    eig_total = lax.psum(jnp.sum(eig_values.astype(jnp.float32)), WIDE)
+    eig_total, grad_tokens = lax.optimization_barrier((eig_total, grad_tokens))
+    me = lax.axis_index("wb")
+    half = train_grad_rot.shape[0] // 2
+    first_rows, train_act_rot, _ = lax.optimization_barrier((train_grad_rot[:half], train_act_rot, grad_tokens))
+    grads_first = ring_gather(first_rows, "wb")
+    act_blocks = train_act_rot.reshape(na, nb, -1, train_act_rot.shape[1])
+    acts_near = [act_blocks[:, me]]
+    for shift in range(1, nb):
+        outgoing = lax.dynamic_index_in_dim(act_blocks, (me + shift) % nb, axis=1, keepdims=False)
+        acts_near.append(lax.ppermute(outgoing, "wb", perm=[(i, (i + shift) % nb) for i in range(nb)]))
+    acts_near = jnp.stack(acts_near)
     act_cols = lax.all_gather(act_basis, "wa", axis=1, tiled=True)
     grad_cols = lax.all_gather(grad_basis, "wa", axis=1, tiled=True)
     count = query_act.shape[0]
@@ -66,30 +79,26 @@
     grad_kept = grad_rot * query_weight[:, None]
     act_rot = natural_order(act_rot.reshape(nb, count, -1), "wb").reshape(nb * count, -1)
     grad_kept = natural_order(grad_kept.reshape(nb, count, -1), "wb").reshape(nb * count, -1)
+    grads_first, acts_near, grad_kept = lax.optimization_barrier((grads_first, acts_near, grad_kept))
+    second_rows, _ = lax.optimization_barrier((train_grad_rot[half:], grad_kept))
+    grads_second = ring_gather(second_rows, "wb")
     grad_all = lax.all_gather(grad_kept, "wb", axis=1, tiled=True)
     partial_rows = lax.dot_general(
         act_rot, grad_all, (((0,), (0,)), ((), ())), preferred_element_type=jnp.float32
     )
     gradient_rows = lax.psum_scatter(partial_rows, "wa", scatter_dimension=0, tiled=True)
-    na = lax.axis_size("wa")
     rows = gradient_rows.shape[0]
     gradient_rows = gradient_rows.reshape(rows, nb, na, -1).transpose(0, 2, 1, 3).reshape(rows, -1)
     eig_in = eig_values.shape[0] * lax.axis_size(WIDE)
     eig_out = eig_values.shape[1]
-    eig_total = lax.psum(jnp.sum(eig_values.astype(jnp.float32)), WIDE)
     mean_eig = eig_total / (eig_in * eig_out)
     dampings = mean_eig * jnp.exp2(damping_index.astype(jnp.float32) - 4.0)
     payload = jnp.concatenate([gradient_rows.astype(jnp.bfloat16), eig_values], axis=1)
+    grads_second, payload = lax.optimization_barrier((grads_second, payload))
     rows_held = lax.all_gather(payload, "wa", axis=0, tiled=True)
     gradient_held, eig_held = rows_held[:, :eig_out], rows_held[:, eig_out:]
-    grads_near = ring_gather(train_grad_rot, "wb")
-    me = lax.axis_index("wb")
-    act_blocks = train_act_rot.reshape(na, nb, -1, train_act_rot.shape[1])
-    acts_near = [act_blocks[:, me]]
-    for shift in range(1, nb):
-        outgoing = lax.dynamic_index_in_dim(act_blocks, (me + shift) % nb, axis=1, keepdims=False)
-        acts_near.append(lax.ppermute(outgoing, "wb", perm=[(i, (i + shift) % nb) for i in range(nb)]))
-    acts_near = jnp.stack(acts_near).reshape(nb, na * act_blocks.shape[2], -1).astype(jnp.float32)
+    grads_near = jnp.concatenate([grads_first, grads_second], axis=1)
+    acts_near = acts_near.reshape(nb, na * act_blocks.shape[2], -1).astype(jnp.float32)
     grad_wide = gradient_held.astype(jnp.float32)
     eig_wide = eig_held.astype(jnp.float32)
     results = []

time: 341 us -> 344 us (level)
  blocking collectives: 93.9 us -> 68.5 us
  local copies, waits for them, and re-layouts: 1.4 us -> 17.3 us
  other arithmetic: 8.64 us -> 22.5 us
  matrix products: 40.9 us -> 45 us
    ppermute x12 -> x15, waiting for transfers between devices: 68.7 us -> 108 us  [ring_gather(): lax.ppermute(x, axis, perm=[(i, (i + shift) % n) for i in range(n)])]
    all_gather x1, waiting for transfers between devices: 0.02 us -> 39 us  [shards(): rows_held = lax.all_gather(payload, 'wa', axis=0, tiled=True)]
    reduce_scatter x1, waiting for transfers between devices: 43.9 us -> 6.13 us  [shards(): lax.psum_scatter(partial_rows, 'wa', scatter_dimension=0, tiled=True)]
    all_gather x1, waiting for transfers between devices: 28.7 us -> 0.02 us  [shards(): grad_cols = lax.all_gather(grad_basis, 'wa', axis=1, tiled=True)]
    psum x1, blocking collectives: 93.9 us -> 68.5 us  [shards(): eig_total = lax.psum(jnp.sum(eig_values.astype(jnp.float32)), WIDE)]
    all_gather x1, waiting for transfers between devices: 16.4 us -> 0.02 us  [shards(): grad_all = lax.all_gather(grad_kept, 'wb', axis=1, tiled=True)]
    another operation x2 -> x4, other arithmetic: 3.58 us -> 11.3 us  [ring_gather(): return jnp.stack(parts)]
    unnamed x14 -> x27, local copies, waits for them, and re-layouts: 0.04 us -> 4.48 us
  transfers between devices with their start and end apart: 23 -> 26, of which waited for: 10 -> 15; matrix products, arithmetic and copies ran while one was open for 4% -> 12% of each run, Pallas kernels for 0% -> 0%
where the time goes in v8:
time: 344 us; the launch traced here: 343 us
  waiting for transfers between devices  161 us (47%)
  blocking collectives  68.5 us (20%)
  matrix products  45 us (13%)
  other arithmetic  22.5 us (7%)
  local copies, waits for them, and re-layouts  17.3 us (5%)
  between operations  14.7 us (4%)
  starting transfers between devices  14.2 us (4%)
    ppermute x15, waiting for transfers between devices, ring_gather(): lax.ppermute(x, axis, perm=[(i, (i + shift) % n) for i in range(n)])  108 us
    psum x1, blocking collectives, shards(): eig_total = lax.psum(jnp.sum(eig_values.astype(jnp.float32)), WIDE)  68.5 us
    all_gather x1, waiting for transfers between devices, shards(): rows_held = lax.all_gather(payload, 'wa', axis=0, tiled=True)  39 us
    dot_general x6, matrix products, shards(): jnp.einsum('ij,sjt->sit', precond, grads_near, preferred_element_type=jnp...  32.2 us
    another operation x4, other arithmetic, ring_gather(): return jnp.stack(parts)  11.3 us
    ppermute x15, starting transfers between devices, ring_gather(): lax.ppermute(x, axis, perm=[(i, (i + shift) % n) for i in range(n)])  8.21 us
  transfers between devices with their start and end apart: 26, of which 15 were waited for; matrix products, arithmetic and copies ran while one was open for 12% of the time, Pallas kernels for 0%

profile of v8, /device:TPU:0, one launch (start us, length us, event | category | flops | bytes accessed | tf_op | source)
XLA Modules:
  0.0 343.0 jit_solution(8706634744663358549)
XLA Ops:
  6.5 0.7 all-gather.5.cloned.1.call-update
  7.3 2.5 collective-permute-start.2
  9.8 0.6 collective-permute-start.1
  10.4 0.2 collective-permute-start
  10.6 1.7 convert_reduce_fusion
  12.3 68.5 %psum.7 = f32[]{:T(128)} all-reduce(f32[]{:T(128)} %convert_reduce_fusion), channel_id=1, replica_groups=mesh['groups'=2,'wa'=4,'wb'=4] {'wa','wb'}, use_global_device_ids=true, to_apply=%region_1.0 | all-reduce | flops 1 | bytes 8 | tf_op jit(solution)/shard_map/psum | solution.py:57
  80.7 2.5 fusion.45
  83.2 3.8 %pad_maximum_fusion = bf16[4,128,4096]{2,1,0:T(8,128)(2,1)} fusion(bf16[1,128,4096]{2,1,0:T(8,128)(2,1)S(1)} %bitcast.117, bf16[1,128,4096]{2,1,0:T(8,128)(2,1)} %bitcast.2, bf16[1,128,4096]{2,1,0:T(8,128)(2,1)} %bitcast.1, bf16[1,128,4096]{2,1,0:T(8,128)(2,1)S(1)} %bitcast.116), kind=kLoop, calls=%fused_computation.12 | loop fusion | flops 6291456 | bytes 8388608 | tf_op jit(solution)/shard_map/stack | solution.py:30
  87.0 0.6 collective-permute-start.5
  87.7 0.5 collective-permute-start.4
  88.2 2.1 dynamic-slice_bitcast_fusion.3
  90.2 1.7 collective-permute-start.8
  92.1 32.0 %collective-permute-done.11 = s32[128]{0:T(128)S(1)} collective-permute-done((s32[128]{0:T(128)S(1)}, s32[128]{0:T(128)S(1)}, u32[]{:S(2)}, u32[]{:S(2)}) %collective-permute-start.11) | collective-permute-done | bytes 544 | tf_op jit(solution)/shard_map/ppermute | solution.py:29
  124.1 1.0 collective-permute-start.10
  125.2 2.5 collective-permute-done.10
  127.8 2.8 collective-permute-done.9
  130.6 1.0 collective-permute-start.7
  131.7 0.8 fusion.44
  132.4 6.1 %collective-permute-done.7 = bf16[4,64,384]{2,1,0:T(8,128)(2,1)} collective-permute-done((bf16[4,64,384]{2,1,0:T(8,128)(2,1)}, bf16[4,64,384]{2,1,0:T(8,128)(2,1)}, u32[]{:S(2)}, u32[]{:S(2)}) %collective-permute-start.7) | collective-permute-done | bytes 196640 | tf_op jit(solution)/shard_map/ppermute | solution.py:67
  138.6 0.2 collective-permute-done.6
  138.8 2.1 pad_maximum_fusion.4
  140.9 0.8 copy-done.4
  141.8 0.3 copy-done.5
  142.1 0.2 copy-done.6
  142.4 1.8 pad_maximum_fusion.1
  144.2 6.6 %fusion.12 = bf16[512,512]{1,0:T(8,128)(2,1)} fusion(bf16[512,4096]{1,0:T(8,128)(2,1)} %bitcast.109, bf16[4096,512]{1,0:T(8,128)(2,1)} %all-gather.5.cloned.1.call-done, bf16[512]{0:T(512)(128)(2,1)S(1)} %fusion.44), kind=kOutput, calls=%fused_computation.35 | convolution fusion | flops 2148007936 | bytes 8913920 | tf_op jit(solution)/shard_map/dot_general | solution.py:75
  150.8 1.9 rev.6
  152.7 2.0 fusion.25
  154.9 1.0 collective-permute-start.16
  156.1 13.1 %collective-permute-done.17 = bf16[128,2048]{1,0:T(8,128)(2,1)S(1)} collective-permute-done((bf16[128,2048]{1,0:T(8,128)(2,1)}, bf16[128,2048]{1,0:T(8,128)(2,1)S(1)}, u32[]{:S(2)}, u32[]{:S(2)}) %collective-permute-start.17) | collective-permute-done | bytes 524320 | tf_op jit(solution)/shard_map/ppermute | solution.py:29
  169.2 21.5 %collective-permute-done.16 = bf16[128,2048]{1,0:T(8,128)(2,1)S(1)} collective-permute-done((bf16[128,2048]{1,0:T(8,128)(2,1)}, bf16[128,2048]{1,0:T(8,128)(2,1)S(1)}, u32[]{:S(2)}, u32[]{:S(2)}) %collective-permute-start.16) | collective-permute-done | bytes 524320 | tf_op jit(solution)/shard_map/ppermute | solution.py:29
  190.7 0.6 collective-permute-done.15
  191.3 2.7 pad_maximum_fusion.3
  194.0 2.6 convolution_convert_fusion.1
  196.6 0.7 rev.7
  197.3 1.1 fusion.38
  198.4 3.7 %fusion.47 = f32[256,2048]{1,0:T(8,128)} fusion(bf16[512,256]{1,0:T(8,128)(2,1)S(1)} %bitcast.114, bf16[512,2048]{1,0:T(8,128)(2,1)} %all-gather.9.cloned.1.call-done), kind=kOutput, calls=%fused_computation.86 | convolution fusion | flops 536870912 | bytes 4456448 | tf_op jit(solution)/shard_map/dot_general | solution.py:86
  202.2 1.1 collective-permute-start.13
  203.3 0.2 collective-permute-start.12
  203.5 16.4 %collective-permute-done.14 = bf16[1024,384]{1,0:T(8,128)(2,1)S(1)} collective-permute-done((bf16[1024,384]{1,0:T(8,128)(2,1)}, bf16[1024,384]{1,0:T(8,128)(2,1)S(1)}, u32[]{:S(2)}, u32[]{:S(2)}) %collective-permute-start.14) | collective-permute-done | bytes 786464 | tf_op jit(solution)/shard_map/ppermute | solution.py:29
  219.9 18.3 %collective-permute-done.13 = bf16[1024,384]{1,0:T(8,128)(2,1)S(1)} collective-permute-done((bf16[1024,384]{1,0:T(8,128)(2,1)}, bf16[1024,384]{1,0:T(8,128)(2,1)S(1)}, u32[]{:S(2)}, u32[]{:S(2)}) %collective-permute-start.13) | collective-permute-done | bytes 786464 | tf_op jit(solution)/shard_map/ppermute | solution.py:29
  238.2 0.5 collective-permute-done.12
  238.7 3.0 pad_maximum_fusion.2
  241.7 6.1 %reduce-scatter.2.cloned.1.call-done = f32[64,2048]{1,0:T(8,128)} async-done(((f32[256,2048]{1,0:T(8,128)}), f32[64,2048]{1,0:T(8,128)}) %reduce-scatter.2.cloned.1.call-update) | async-done | bytes 524304 | tf_op jit(solution)/shard_map/reduce_scatter | solution.py:89
  247.8 1.1 convert_element_type.69
  248.9 0.9 convert_element_type.70
  249.7 1.1 copy.11
  250.8 0.9 convert_element_type.72
  251.7 1.9 pad_maximum_fusion.5
  254.3 0.7 fusion.46
  255.0 2.0 constant_dynamic-update-slice_fusion.1
  257.0 1.0 copy-done
  258.0 2.0 constant_dynamic-update-slice_fusion
  260.0 39.0 %all-gather.11.cloned.1.call-done = bf16[256,4096]{1,0:T(8,128)(2,1)} async-done(((bf16[64,4096]{1,0:T(8,128)(2,1)}), bf16[256,4096]{1,0:T(8,128)(2,1)}) %all-gather.11.cloned.1.call-update) | async-done | bytes 2097168 | tf_op jit(solution)/shard_map/all_gather | solution.py:98
  299.0 6.0 %fusion.6 = f32[4,384]{1,0:T(4,128)S(1)} fusion(bf16[4,256,384]{2,1,0:T(8,128)(2,1)S(1)} %bitcast.125, bf16[4,2048,384]{2,1,0:T(8,128)(2,1)} %constant_dynamic-update-slice_fusion, f32[]{:T(128)} %bitcast.36, bf16[256,4096]{1,0:T(8,128)(2,1)} %all-gather.11.cloned.1.call-done), kind=kOutput, calls=%fused_computation.28 | convolution fusion | flops 1614412288 | bytes 9181188 | tf_op jit(solution)/shard_map/ij,sjt->sit/dot_general | solution.py:107
  305.0 5.2 %fusion.7 = f32[4,384]{1,0:T(4,128)S(1)} fusion(bf16[4,256,384]{2,1,0:T(8,128)(2,1)S(1)} %bitcast.126, bf16[4,2048,384]{2,1,0:T(8,128)(2,1)} %constant_dynamic-update-slice_fusion, f32[]{:T(128)} %bitcast.40, bf16[256,4096]{1,0:T(8,128)(2,1)S(1)} %copy-done.11), kind=kOutput, calls=%fused_computation.29 | convolution fusion | flops 1614412288 | bytes 9181188 | tf_op jit(solution)/shard_map/ij,sjt->sit/dot_general | solution.py:107
  310.2 5.3 %fusion.8 = f32[4,384]{1,0:T(4,128)S(1)} fusion(bf16[4,256,384]{2,1,0:T(8,128)(2,1)S(1)} %bitcast.127, bf16[4,2048,384]{2,1,0:T(8,128)(2,1)} %constant_dynamic-update-slice_fusion, f32[]{:T(128)} %bitcast.44, bf16[256,4096]{1,0:T(8,128)(2,1)S(1)} %copy-done.11), kind=kOutput, calls=%fused_computation.30 | convolution fusion | flops 1614412288 | bytes 9181188 | tf_op jit(solution)/shard_map/ij,sjt->sit/dot_general | solution.py:107
  315.5 5.2 %fusion.9 = f32[4,384]{1,0:T(4,128)S(1)} fusion(bf16[4,256,384]{2,1,0:T(8,128)(2,1)S(1)} %bitcast.128, bf16[4,2048,384]{2,1,0:T(8,128)(2,1)} %constant_dynamic-update-slice_fusion, f32[]{:T(128)} %bitcast.47, bf16[256,4096]{1,0:T(8,128)(2,1)S(1)} %copy-done.11), kind=kOutput, calls=%fused_computation.31 | convolution fusion | flops 1614412288 | bytes 9181188 | tf_op jit(solution)/shard_map/ij,sjt->sit/dot_general | solution.py:107
  320.8 5.3 %fusion.10 = f32[4,384]{1,0:T(4,128)S(1)} fusion(bf16[4,256,384]{2,1,0:T(8,128)(2,1)S(1)} %bitcast.129, bf16[4,2048,384]{2,1,0:T(8,128)(2,1)} %constant_dynamic-update-slice_fusion, f32[]{:T(128)} %bitcast.50, bf16[256,4096]{1,0:T(8,128)(2,1)S(1)} %copy-done.11), kind=kOutput, calls=%fused_computation.32 | convolution fusion | flops 1614412288 | bytes 9181188 | tf_op jit(solution)/shard_map/ij,sjt->sit/dot_general | solution.py:107
  326.1 5.2 %fusion.11 = f32[4,384]{1,0:T(4,128)S(1)} fusion(bf16[4,256,384]{2,1,0:T(8,128)(2,1)S(1)} %bitcast.130, bf16[4,2048,384]{2,1,0:T(8,128)(2,1)} %constant_dynamic-update-slice_fusion, f32[]{:T(128)} %bitcast.53, bf16[256,4096]{1,0:T(8,128)(2,1)S(1)} %copy-done.11), kind=kOutput, calls=%fused_computation.33 | convolution fusion | flops 1614412288 | bytes 9181188 | tf_op jit(solution)/shard_map/ij,sjt->sit/dot_general | solution.py:107
  331.5 1.6 collective-permute-start.19
  333.0 1.4 collective-permute-start.18
  335.2 0.6 collective-permute-done.18
  335.8 0.6 fusion.43
  (61 shorter events, 1.2 us)
Async XLA Ops:
  6.5 76.7 %copy-start.3 = (bf16[128,4096]{1,0:T(8,128)(2,1)S(1)}, bf16[128,4096]{1,0:T(8,128)(2,1)}, u32[]{:S(2)}) copy-start(bf16[128,4096]{1,0:T(8,128)(2,1)} %param.11) | copy-start | bytes 3145732
  6.5 137.7 %all-gather.5.cloned.1.call-start = ((), (), s32[]{:S(2)}) async-start(), calls=%async_computation.1 | async-start | bytes 5242880 | tf_op jit(solution)/shard_map/all_gather | solution.py:70
  7.3 186.7 %all-gather.7.cloned.1.call-start = ((), (), s32[]{:S(2)}) async-start(), calls=%async_computation.2 | async-start | bytes 1310720 | tf_op jit(solution)/shard_map/all_gather | solution.py:69
  7.3 75.9 %collective-permute-start.2 = (bf16[128,4096]{1,0:T(8,128)(2,1)}, bf16[128,4096]{1,0:T(8,128)(2,1)S(1)}, u32[]{:S(2)}, u32[]{:S(2)}) collective-permute-start(bf16[128,4096]{1,0:T(8,128)(2,1)} %param.11), channel_id=1, source_target_pairs={{0,3},{1,0},{2,1},{3,2},{4,7},{5,4},{6,5},{7,6},{8,11},{9,8},{10,9... | collective-permute-start | bytes 3145736 | tf_op jit(solution)/shard_map/ppermute | solution.py:29
  9.8 73.4 %collective-permute-start.1 = (bf16[128,4096]{1,0:T(8,128)(2,1)}, bf16[128,4096]{1,0:T(8,128)(2,1)}, u32[]{:S(2)}, u32[]{:S(2)}) collective-permute-start(bf16[128,4096]{1,0:T(8,128)(2,1)} %param.11), channel_id=1, source_target_pairs={{0,2},{1,3},{2,0},{3,1},{4,6},{5,7},{6,4},{7,5},{8,10},{9,11},{10,... | collective-permute-start | bytes 3145736 | tf_op jit(solution)/shard_map/ppermute | solution.py:29
  10.4 72.8 %collective-permute-start = (bf16[128,4096]{1,0:T(8,128)(2,1)}, bf16[128,4096]{1,0:T(8,128)(2,1)}, u32[]{:S(2)}, u32[]{:S(2)}) collective-permute-start(bf16[128,4096]{1,0:T(8,128)(2,1)} %param.11), channel_id=1, source_target_pairs={{0,1},{1,2},{2,3},{3,0},{4,5},{5,6},{6,7},{7,4},{8,9},{9,10},{10,1... | collective-permute-start | bytes 3145736 | tf_op jit(solution)/shard_map/ppermute | solution.py:29
  83.2 5.0 %copy-start.1 = (bf16[1024,384]{1,0:T(8,128)(2,1)}, bf16[1024,384]{1,0:T(8,128)(2,1)S(1)}, u32[]{:S(2)}) copy-start(bf16[1024,384]{1,0:T(8,128)(2,1)S(1)} %get-tuple-element.16) | copy-start | bytes 2359300
  83.2 8.8 %copy-start.9 = (s32[128]{0:T(128)S(1)}, s32[128]{0:T(128)}, u32[]{:S(2)}) copy-start(s32[128]{0:T(128)} %param.12) | copy-start | bytes 1540
  87.0 53.9 %collective-permute-start.5 = (bf16[1024,384]{1,0:T(8,128)(2,1)S(1)}, bf16[1024,384]{1,0:T(8,128)(2,1)S(1)}, u32[]{:S(2)}, u32[]{:S(2)}) collective-permute-start(bf16[1024,384]{1,0:T(8,128)(2,1)S(1)} %get-tuple-element.16), channel_id=1, source_target_pairs={{0,3},{1,0},{2,1},{3,2},{4,7},{5,4},{6,5},{7,6},{8,11},{9,8},{10,9... | collective-permute-start | bytes 2359304 | tf_op jit(solution)/shard_map/ppermute | solution.py:29
  87.7 53.2 %collective-permute-start.4 = (bf16[1024,384]{1,0:T(8,128)(2,1)S(1)}, bf16[1024,384]{1,0:T(8,128)(2,1)S(1)}, u32[]{:S(2)}, u32[]{:S(2)}) collective-permute-start(bf16[1024,384]{1,0:T(8,128)(2,1)S(1)} %get-tuple-element.16), channel_id=1, source_target_pairs={{0,2},{1,3},{2,0},{3,1},{4,6},{5,7},{6,4},{7,5},{8,10},{9,11},{10,... | collective-permute-start | bytes 2359304 | tf_op jit(solution)/shard_map/ppermute | solution.py:29
  88.2 52.8 %collective-permute-start.3 = (bf16[1024,384]{1,0:T(8,128)(2,1)S(1)}, bf16[1024,384]{1,0:T(8,128)(2,1)S(1)}, u32[]{:S(2)}, u32[]{:S(2)}) collective-permute-start(bf16[1024,384]{1,0:T(8,128)(2,1)S(1)} %get-tuple-element.16), channel_id=1, source_target_pairs={{0,1},{1,2},{2,3},{3,0},{4,5},{5,6},{6,7},{7,4},{8,9},{9,10},{10,1... | collective-permute-start | bytes 2359304 | tf_op jit(solution)/shard_map/ppermute | solution.py:29
  90.2 41.4 %collective-permute-start.8 = (bf16[4,64,384]{2,1,0:T(8,128)(2,1)}, bf16[4,64,384]{2,1,0:T(8,128)(2,1)}, u32[]{:S(2)}, u32[]{:S(2)}) collective-permute-start(bf16[4,64,384]{2,1,0:T(8,128)(2,1)} %get-tuple-element.28), channel_id=1, source_target_pairs={{0,3},{1,0},{2,1},{3,2},{4,7},{5,4},{6,5},{7,6},{8,11},{9,8},{10,9... | collective-permute-start | bytes 589832 | tf_op jit(solution)/shard_map/ppermute | solution.py:67
  92.0 106.4 %all-gather.9.cloned.1.call-start = ((), (), s32[]{:S(2)}) async-start(), calls=%async_computation.3 | async-start | bytes 2621440 | tf_op jit(solution)/shard_map/all_gather | solution.py:85
  92.1 32.1 %collective-permute-start.11 = (s32[128]{0:T(128)S(1)}, s32[128]{0:T(128)S(1)}, u32[]{:S(2)}, u32[]{:S(2)}) collective-permute-start(s32[128]{0:T(128)S(1)} %copy-done.9), channel_id=1, source_target_pairs={{0,3},{1,0},{2,1},{3,2},{4,7},{5,4},{6,5},{7,6},{8,11},{9,8},{10,9... | collective-permute-start | bytes 1544 | tf_op jit(solution)/shard_map/ppermute | solution.py:29
  124.1 3.5 %collective-permute-start.10 = (s32[128]{0:T(128)S(1)}, s32[128]{0:T(128)S(1)}, u32[]{:S(2)}, u32[]{:S(2)}) collective-permute-start(s32[128]{0:T(128)S(1)} %copy-done.9), channel_id=1, source_target_pairs={{0,2},{1,3},{2,0},{3,1},{4,6},{5,7},{6,4},{7,5},{8,10},{9,11},{10,... | collective-permute-start | bytes 1544 | tf_op jit(solution)/shard_map/ppermute | solution.py:29
  127.7 3.0 collective-permute-start.9
  130.6 1.0 copy-start.10
  130.6 7.9 %collective-permute-start.7 = (bf16[4,64,384]{2,1,0:T(8,128)(2,1)}, bf16[4,64,384]{2,1,0:T(8,128)(2,1)}, u32[]{:S(2)}, u32[]{:S(2)}) collective-permute-start(bf16[4,64,384]{2,1,0:T(8,128)(2,1)} %get-tuple-element.29), channel_id=1, source_target_pairs={{0,2},{1,3},{2,0},{3,1},{4,6},{5,7},{6,4},{7,5},{8,10},{9,11},{10,... | collective-permute-start | bytes 589832 | tf_op jit(solution)/shard_map/ppermute | solution.py:67
  131.7 7.1 %collective-permute-start.6 = (bf16[4,64,384]{2,1,0:T(8,128)(2,1)S(1)}, bf16[4,64,384]{2,1,0:T(8,128)(2,1)}, u32[]{:S(2)}, u32[]{:S(2)}) collective-permute-start(bf16[4,64,384]{2,1,0:T(8,128)(2,1)S(1)} %get-tuple-element.30), channel_id=1, source_target_pairs={{0,1},{1,2},{2,3},{3,0},{4,5},{5,6},{6,7},{7,4},{8,9},{9,10},{10,1... | collective-permute-start | bytes 589832 | tf_op jit(solution)/shard_map/ppermute | solution.py:67
  131.7 10.7 %copy-start.2 = (bf16[1024,384]{1,0:T(8,128)(2,1)S(1)}, bf16[1024,384]{1,0:T(8,128)(2,1)}, u32[]{:S(2)}) copy-start(bf16[1024,384]{1,0:T(8,128)(2,1)} %copy-done.1) | copy-start | bytes 2359300
  140.9 0.9 copy-start.4
  140.9 1.2 copy-start.5
  140.9 1.4 copy-start.6
  154.8 93.0 %reduce-scatter.2.cloned.1.call-start = ((), (), s32[]{:S(2)}) async-start(), calls=%async_computation.4 | async-start | bytes 2621440 | tf_op jit(solution)/shard_map/reduce_scatter | solution.py:89
  154.8 14.4 %collective-permute-start.17 = (bf16[128,2048]{1,0:T(8,128)(2,1)}, bf16[128,2048]{1,0:T(8,128)(2,1)S(1)}, u32[]{:S(2)}, u32[]{:S(2)}) collective-permute-start(bf16[128,2048]{1,0:T(8,128)(2,1)} %param.10), channel_id=1, source_target_pairs={{0,3},{1,0},{2,1},{3,2},{4,7},{5,4},{6,5},{7,6},{8,11},{9,8},{10,9... | collective-permute-start | bytes 1572872 | tf_op jit(solution)/shard_map/ppermute | solution.py:29
  154.9 35.8 %collective-permute-start.16 = (bf16[128,2048]{1,0:T(8,128)(2,1)}, bf16[128,2048]{1,0:T(8,128)(2,1)S(1)}, u32[]{:S(2)}, u32[]{:S(2)}) collective-permute-start(bf16[128,2048]{1,0:T(8,128)(2,1)} %param.10), channel_id=1, source_target_pairs={{0,2},{1,3},{2,0},{3,1},{4,6},{5,7},{6,4},{7,5},{8,10},{9,11},{10,... | collective-permute-start | bytes 1572872 | tf_op jit(solution)/shard_map/ppermute | solution.py:29
  155.9 35.4 %collective-permute-start.15 = (bf16[128,2048]{1,0:T(8,128)(2,1)}, bf16[128,2048]{1,0:T(8,128)(2,1)S(1)}, u32[]{:S(2)}, u32[]{:S(2)}) collective-permute-start(bf16[128,2048]{1,0:T(8,128)(2,1)} %param.10), channel_id=1, source_target_pairs={{0,1},{1,2},{2,3},{3,0},{4,5},{5,6},{6,7},{7,4},{8,9},{9,10},{10,1... | collective-permute-start | bytes 1572872 | tf_op jit(solution)/shard_map/ppermute | solution.py:29
  202.1 96.9 %all-gather.11.cloned.1.call-start = ((), (), s32[]{:S(2)}) async-start(), calls=%async_computation.5 | async-start | bytes 2621440 | tf_op jit(solution)/shard_map/all_gather | solution.py:98
  202.1 17.8 %collective-permute-start.14 = (bf16[1024,384]{1,0:T(8,128)(2,1)}, bf16[1024,384]{1,0:T(8,128)(2,1)S(1)}, u32[]{:S(2)}, u32[]{:S(2)}) collective-permute-start(bf16[1024,384]{1,0:T(8,128)(2,1)} %get-tuple-element.20), channel_id=1, source_target_pairs={{0,3},{1,0},{2,1},{3,2},{4,7},{5,4},{6,5},{7,6},{8,11},{9,8},{10,9... | collective-permute-start | bytes 2359304 | tf_op jit(solution)/shard_map/ppermute | solution.py:29
  202.2 36.0 %collective-permute-start.13 = (bf16[1024,384]{1,0:T(8,128)(2,1)}, bf16[1024,384]{1,0:T(8,128)(2,1)S(1)}, u32[]{:S(2)}, u32[]{:S(2)}) collective-permute-start(bf16[1024,384]{1,0:T(8,128)(2,1)} %get-tuple-element.20), channel_id=1, source_target_pairs={{0,2},{1,3},{2,0},{3,1},{4,6},{5,7},{6,4},{7,5},{8,10},{9,11},{10,... | collective-permute-start | bytes 2359304 | tf_op jit(solution)/shard_map/ppermute | solution.py:29
  203.3 35.4 %collective-permute-start.12 = (bf16[1024,384]{1,0:T(8,128)(2,1)}, bf16[1024,384]{1,0:T(8,128)(2,1)S(1)}, u32[]{:S(2)}, u32[]{:S(2)}) collective-permute-start(bf16[1024,384]{1,0:T(8,128)(2,1)} %get-tuple-element.20), channel_id=1, source_target_pairs={{0,1},{1,2},{2,3},{3,0},{4,5},{5,6},{6,7},{7,4},{8,9},{9,10},{10,1... | collective-permute-start | bytes 2359304 | tf_op jit(solution)/shard_map/ppermute | solution.py:29
  241.7 12.6 %copy-start.12 = (s32[6]{0:T(128)S(1)}, s32[6]{0:T(128)}, u32[]{:S(2)}) copy-start(s32[6]{0:T(128)} %param.16) | copy-start | bytes 76
  255.0 3.0 copy-start
  258.0 41.0 %copy-start.7 = (bf16[4,4,64,384]{3,2,1,0:T(8,128)(2,1)S(1)}, bf16[4,4,64,384]{3,2,1,0:T(8,128)(2,1)}, u32[]{:S(2)}) copy-start(bf16[4,4,64,384]{3,2,1,0:T(8,128)(2,1)} %pad_maximum_fusion.4) | copy-start | bytes 2359300
  299.0 6.0 %copy-start.11 = (bf16[256,4096]{1,0:T(8,128)(2,1)S(1)}, bf16[256,4096]{1,0:T(8,128)(2,1)}, u32[]{:S(2)}) copy-start(bf16[256,4096]{1,0:T(8,128)(2,1)} %all-gather.11.cloned.1.call-done) | copy-start | bytes 6291460
  326.1 8.3 %copy-start.8 = (s32[384]{0:T(512)S(1)}, s32[384]{0:T(512)}, u32[]{:S(2)}) copy-start(s32[384]{0:T(512)} %param.19) | copy-start | bytes 4612
  331.4 3.7 %collective-permute-start.20 = (f32[6,384]{1,0:T(8,128)S(1)}, f32[6,384]{1,0:T(8,128)S(1)}, u32[]{:S(2)}, u32[]{:S(2)}) collective-permute-start(f32[6,384]{1,0:T(8,128)S(1)} %get-tuple-element.32), channel_id=1, source_target_pairs={{0,1},{1,2},{2,3},{3,0},{4,5},{5,6},{6,7},{7,4},{8,9},{9,10},{10,1... | collective-permute-start | bytes 27656 | tf_op jit(solution)/shard_map/ppermute | solution.py:112
  331.5 3.8 %collective-permute-start.19 = (f32[6,384]{1,0:T(8,128)S(1)}, f32[6,384]{1,0:T(8,128)S(1)}, u32[]{:S(2)}, u32[]{:S(2)}) collective-permute-start(f32[6,384]{1,0:T(8,128)S(1)} %get-tuple-element.33), channel_id=1, source_target_pairs={{0,2},{1,3},{2,0},{3,1},{4,6},{5,7},{6,4},{7,5},{8,10},{9,11},{10,... | collective-permute-start | bytes 27656 | tf_op jit(solution)/shard_map/ppermute | solution.py:112
  333.0 2.8 collective-permute-start.18
Sparse Core Ops, SparseCore 0:
  8.9 83.4 all-gather.4
  94.0 28.4 all-gather.6
  154.9 36.0 all-gather.8
  202.2 45.5 reduce-scatter.1
  253.7 45.2 all-gather.10

commit v9 on v8

--- a/solution.py
+++ b/solution.py
@@ -54,8 +54,6 @@
     act_tokens = ring_gather(query_act, "wb")
     grad_tokens = ring_gather(query_grad, "wb")
     positions = ring_gather(query_positions, "wb")
-    eig_total = lax.psum(jnp.sum(eig_values.astype(jnp.float32)), WIDE)
-    eig_total, grad_tokens = lax.optimization_barrier((eig_total, grad_tokens))
     me = lax.axis_index("wb")
     half = train_grad_rot.shape[0] // 2
     first_rows, train_act_rot, _ = lax.optimization_barrier((train_grad_rot[:half], train_act_rot, grad_tokens))
@@ -86,7 +84,16 @@
     partial_rows = lax.dot_general(
         act_rot, grad_all, (((0,), (0,)), ((), ())), preferred_element_type=jnp.float32
     )
-    gradient_rows = lax.psum_scatter(partial_rows, "wa", scatter_dimension=0, tiled=True)
+    eig_sum = jnp.sum(eig_values.astype(jnp.float32))
+    group_sum = eig_sum
+    for shift in range(1, nb):
+        group_sum = group_sum + lax.ppermute(eig_sum, "wb", perm=[(i, (i + shift) % nb) for i in range(nb)])
+    extra = jnp.broadcast_to(group_sum, (partial_rows.shape[0], 128))
+    reduced = lax.psum_scatter(
+        jnp.concatenate([partial_rows, extra], axis=1), "wa", scatter_dimension=0, tiled=True
+    )
+    gradient_rows = reduced[:, : partial_rows.shape[1]]
+    eig_total = reduced[0, partial_rows.shape[1]]
     rows = gradient_rows.shape[0]
     gradient_rows = gradient_rows.reshape(rows, nb, na, -1).transpose(0, 2, 1, 3).reshape(rows, -1)
     eig_in = eig_values.shape[0] * lax.axis_size(WIDE)

time: 344 us -> 323 us (0.939)
  blocking collectives: 68.5 us -> 0 us
  waiting for transfers between devices: 161 us -> 201 us
  starting transfers between devices: 14.2 us -> 19.2 us
  local copies, waits for them, and re-layouts: 17.3 us -> 21.1 us
    psum x1 -> x0, blocking collectives: 68.5 us -> none  [shards(): eig_total = lax.psum(jnp.sum(eig_values.astype(jnp.float32)), WIDE)]
    ppermute x0 -> x3, waiting for transfers between devices: none -> 32.6 us  [shards(): lax.ppermute(eig_sum, 'wb', perm=[(i, (i + shift) % nb) for i in range(nb)])]
    ppermute x15, waiting for transfers between devices: 108 us -> 114 us  [ring_gather(): lax.ppermute(x, axis, perm=[(i, (i + shift) % n) for i in range(n)])]
  transfers between devices with their start and end apart: 26 -> 29, of which waited for: 15 -> 14; matrix products, arithmetic and copies ran while one was open for 12% -> 12% of each run, Pallas kernels for 0% -> 0%
where the time goes in v9:
time: 323 us; the launch traced here: 322 us
  waiting for transfers between devices  201 us (62%)
  matrix products  43.8 us (14%)
  local copies, waits for them, and re-layouts  21.1 us (7%)
  other arithmetic  19.5 us (6%)
  starting transfers between devices  19.2 us (6%)
  between operations  17.4 us (5%)
    ppermute x15, waiting for transfers between devices, ring_gather(): lax.ppermute(x, axis, perm=[(i, (i + shift) % n) for i in range(n)])  114 us
    all_gather x1, waiting for transfers between devices, shards(): rows_held = lax.all_gather(payload, 'wa', axis=0, tiled=True)  38.9 us
    ppermute x3, waiting for transfers between devices, shards(): lax.ppermute(eig_sum, 'wb', perm=[(i, (i + shift) % nb) for i in range(nb)])  32.6 us
    dot_general x6, matrix products, shards(): jnp.einsum('ij,sjt->sit', precond, grads_near, preferred_element_type=jnp...  32.3 us
    ppermute x15, starting transfers between devices, ring_gather(): lax.ppermute(x, axis, perm=[(i, (i + shift) % n) for i in range(n)])  11 us
    another operation x4, other arithmetic, ring_gather(): return jnp.stack(parts)  10.3 us
    reduce_scatter x1, waiting for transfers between devices, shards(): lax.psum_scatter(jnp.concatenate([partial_rows, extra], axis=1), 'wa', sc...  6.83 us
    dot_general x1, matrix products, shards(): jnp.dot(grad_tokens.reshape(nb * count, -1), grad_cols, preferred_element...  6.58 us
  transfers between devices with their start and end apart: 29, of which 14 were waited for; matrix products, arithmetic and copies ran while one was open for 12% of the time, Pallas kernels for 0%

profile of v9, /device:TPU:0, one launch (start us, length us, event | category | flops | bytes accessed | tf_op | source)
XLA Modules:
  0.0 321.6 jit_solution(4827531323610693451)
XLA Ops:
  6.5 0.7 all-gather.5.cloned.1.call-update
  7.3 2.5 collective-permute-start.2
  9.8 0.6 collective-permute-start.1
  10.6 2.5 fusion.45
  13.0 20.5 %collective-permute-done.2 = bf16[128,4096]{1,0:T(8,128)(2,1)S(1)} collective-permute-done((bf16[128,4096]{1,0:T(8,128)(2,1)}, bf16[128,4096]{1,0:T(8,128)(2,1)S(1)}, u32[]{:S(2)}, u32[]{:S(2)}) %collective-permute-start.2) | collective-permute-done | bytes 1048608 | tf_op jit(solution)/shard_map/ppermute | solution.py:29
  33.5 23.3 %collective-permute-done.1 = bf16[128,4096]{1,0:T(8,128)(2,1)S(1)} collective-permute-done((bf16[128,4096]{1,0:T(8,128)(2,1)}, bf16[128,4096]{1,0:T(8,128)(2,1)S(1)}, u32[]{:S(2)}, u32[]{:S(2)}) %collective-permute-start.1) | collective-permute-done | bytes 1048608 | tf_op jit(solution)/shard_map/ppermute | solution.py:29
  56.8 2.3 pad_maximum_fusion
  59.2 1.6 collective-permute-start.4
  60.8 0.2 collective-permute-start.3
  61.0 2.1 dynamic-slice_bitcast_fusion.3
  63.1 1.5 collective-permute-start.8
  64.8 31.4 %collective-permute-done.11 = s32[128]{0:T(128)S(1)} collective-permute-done((s32[128]{0:T(128)S(1)}, s32[128]{0:T(128)S(1)}, u32[]{:S(2)}, u32[]{:S(2)}) %collective-permute-start.11) | collective-permute-done | bytes 544 | tf_op jit(solution)/shard_map/ppermute | solution.py:29
  96.2 1.6 collective-permute-start.10
  97.8 2.0 collective-permute-done.10
  99.7 0.7 collective-permute-start.9
  100.4 2.3 collective-permute-done.9
  102.7 1.6 collective-permute-start.7
  104.3 0.7 fusion.44
  105.0 5.8 %collective-permute-done.7 = bf16[4,64,384]{2,1,0:T(8,128)(2,1)} collective-permute-done((bf16[4,64,384]{2,1,0:T(8,128)(2,1)}, bf16[4,64,384]{2,1,0:T(8,128)(2,1)}, u32[]{:S(2)}, u32[]{:S(2)}) %collective-permute-start.7) | collective-permute-done | bytes 196640 | tf_op jit(solution)/shard_map/ppermute | solution.py:65
  110.9 0.5 collective-permute-done.6
  111.4 2.1 pad_maximum_fusion.4
  113.5 0.9 copy-done.5
  114.4 0.3 copy-done.6
  115.0 1.9 pad_maximum_fusion.1
  116.9 6.6 %fusion.12 = bf16[512,512]{1,0:T(8,128)(2,1)} fusion(bf16[512,4096]{1,0:T(8,128)(2,1)} %bitcast.111, bf16[4096,512]{1,0:T(8,128)(2,1)} %all-gather.5.cloned.1.call-done, bf16[512]{0:T(512)(128)(2,1)S(1)} %fusion.44), kind=kOutput, calls=%fused_computation.35 | convolution fusion | flops 2148007936 | bytes 8913920 | tf_op jit(solution)/shard_map/dot_general | solution.py:73
  123.4 1.9 rev.6
  125.4 2.0 fusion.25
  127.5 0.7 collective-permute-start.16
  128.4 0.7 convert_reduce_fusion
  129.1 1.4 collective-permute-start.18
  130.5 0.6 collective-permute-start.19
  131.1 32.6 %collective-permute-done.18 = f32[]{:T(128)} collective-permute-done((f32[]{:T(128)}, f32[]{:T(128)}, u32[]{:S(2)}, u32[]{:S(2)}) %collective-permute-start.18) | collective-permute-done | bytes 36 | tf_op jit(solution)/shard_map/ppermute | solution.py:90
  166.4 3.2 pad_maximum_fusion.3
  169.5 2.6 convolution_convert_fusion.1
  172.1 0.8 rev.7
  172.9 1.1 fusion.38
  174.0 2.3 fusion.47
  176.3 1.6 concatenate.17
  177.9 1.5 collective-permute-start.14
  179.5 1.2 collective-permute-start.13
  180.6 17.0 %collective-permute-done.14 = bf16[1024,384]{1,0:T(8,128)(2,1)S(1)} collective-permute-done((bf16[1024,384]{1,0:T(8,128)(2,1)}, bf16[1024,384]{1,0:T(8,128)(2,1)S(1)}, u32[]{:S(2)}, u32[]{:S(2)}) %collective-permute-start.14) | collective-permute-done | bytes 786464 | tf_op jit(solution)/shard_map/ppermute | solution.py:29
  197.6 17.9 %collective-permute-done.13 = bf16[1024,384]{1,0:T(8,128)(2,1)S(1)} collective-permute-done((bf16[1024,384]{1,0:T(8,128)(2,1)}, bf16[1024,384]{1,0:T(8,128)(2,1)S(1)}, u32[]{:S(2)}, u32[]{:S(2)}) %collective-permute-start.13) | collective-permute-done | bytes 786464 | tf_op jit(solution)/shard_map/ppermute | solution.py:29
  215.6 3.0 pad_maximum_fusion.2
  218.5 6.8 %reduce-scatter.2.cloned.1.call-done = f32[64,2176]{1,0:T(8,128)} async-done(((f32[256,2176]{1,0:T(8,128)}), f32[64,2176]{1,0:T(8,128)}) %reduce-scatter.2.cloned.1.call-update) | async-done | bytes 557072 | tf_op jit(solution)/shard_map/reduce_scatter | solution.py:92
  225.4 1.8 slice.136
  227.1 1.1 convert_element_type.67
  228.3 0.8 copy.11
  229.1 1.1 convert_element_type.69
  230.2 1.8 pad_maximum_fusion.5
  232.1 2.0 constant_dynamic-update-slice_fusion.1
  234.1 1.3 slice.68
  236.0 0.7 fusion.46
  236.7 2.0 constant_dynamic-update-slice_fusion
  238.7 38.9 %all-gather.11.cloned.1.call-done = bf16[256,4096]{1,0:T(8,128)(2,1)} async-done(((bf16[64,4096]{1,0:T(8,128)(2,1)}), bf16[256,4096]{1,0:T(8,128)(2,1)}) %all-gather.11.cloned.1.call-update) | async-done | bytes 2097168 | tf_op jit(solution)/shard_map/all_gather | solution.py:105
  277.5 6.0 %fusion.6 = f32[4,384]{1,0:T(4,128)S(1)} fusion(bf16[4,256,384]{2,1,0:T(8,128)(2,1)S(1)} %bitcast.129, bf16[4,2048,384]{2,1,0:T(8,128)(2,1)} %constant_dynamic-update-slice_fusion, f32[]{:T(128)} %bitcast.37, bf16[256,4096]{1,0:T(8,128)(2,1)} %all-gather.11.cloned.1.call-done), kind=kOutput, calls=%fused_computation.28 | convolution fusion | flops 1614412288 | bytes 9181188 | tf_op jit(solution)/shard_map/ij,sjt->sit/dot_general | solution.py:114
  283.5 5.3 %fusion.7 = f32[4,384]{1,0:T(4,128)S(1)} fusion(bf16[4,256,384]{2,1,0:T(8,128)(2,1)S(1)} %bitcast.130, bf16[4,2048,384]{2,1,0:T(8,128)(2,1)} %constant_dynamic-update-slice_fusion, f32[]{:T(128)} %bitcast.41, bf16[256,4096]{1,0:T(8,128)(2,1)S(1)} %copy-done.12), kind=kOutput, calls=%fused_computation.29 | convolution fusion | flops 1614412288 | bytes 9181188 | tf_op jit(solution)/shard_map/ij,sjt->sit/dot_general | solution.py:114
  288.8 5.3 %fusion.8 = f32[4,384]{1,0:T(4,128)S(1)} fusion(bf16[4,256,384]{2,1,0:T(8,128)(2,1)S(1)} %bitcast.131, bf16[4,2048,384]{2,1,0:T(8,128)(2,1)} %constant_dynamic-update-slice_fusion, f32[]{:T(128)} %bitcast.45, bf16[256,4096]{1,0:T(8,128)(2,1)S(1)} %copy-done.12), kind=kOutput, calls=%fused_computation.30 | convolution fusion | flops 1614412288 | bytes 9181188 | tf_op jit(solution)/shard_map/ij,sjt->sit/dot_general | solution.py:114
  294.1 5.3 %fusion.9 = f32[4,384]{1,0:T(4,128)S(1)} fusion(bf16[4,256,384]{2,1,0:T(8,128)(2,1)S(1)} %bitcast.132, bf16[4,2048,384]{2,1,0:T(8,128)(2,1)} %constant_dynamic-update-slice_fusion, f32[]{:T(128)} %bitcast.48, bf16[256,4096]{1,0:T(8,128)(2,1)S(1)} %copy-done.12), kind=kOutput, calls=%fused_computation.31 | convolution fusion | flops 1614412288 | bytes 9181188 | tf_op jit(solution)/shard_map/ij,sjt->sit/dot_general | solution.py:114
  299.4 5.3 %fusion.10 = f32[4,384]{1,0:T(4,128)S(1)} fusion(bf16[4,256,384]{2,1,0:T(8,128)(2,1)S(1)} %bitcast.133, bf16[4,2048,384]{2,1,0:T(8,128)(2,1)} %constant_dynamic-update-slice_fusion, f32[]{:T(128)} %bitcast.51, bf16[256,4096]{1,0:T(8,128)(2,1)S(1)} %copy-done.12), kind=kOutput, calls=%fused_computation.32 | convolution fusion | flops 1614412288 | bytes 9181188 | tf_op jit(solution)/shard_map/ij,sjt->sit/dot_general | solution.py:114
  304.7 5.2 %fusion.11 = f32[4,384]{1,0:T(4,128)S(1)} fusion(bf16[4,256,384]{2,1,0:T(8,128)(2,1)S(1)} %bitcast.134, bf16[4,2048,384]{2,1,0:T(8,128)(2,1)} %constant_dynamic-update-slice_fusion, f32[]{:T(128)} %bitcast.54, bf16[256,4096]{1,0:T(8,128)(2,1)S(1)} %copy-done.12), kind=kOutput, calls=%fused_computation.33 | convolution fusion | flops 1614412288 | bytes 9181188 | tf_op jit(solution)/shard_map/ij,sjt->sit/dot_general | solution.py:114
  310.1 1.5 collective-permute-start.22
  311.7 1.4 collective-permute-start.21
  313.9 0.6 collective-permute-done.21
  314.5 0.6 fusion.43
  (70 shorter events, 1.4 us)
Async XLA Ops:
  6.5 50.3 %copy-start.4 = (bf16[128,4096]{1,0:T(8,128)(2,1)S(1)}, bf16[128,4096]{1,0:T(8,128)(2,1)}, u32[]{:S(2)}) copy-start(bf16[128,4096]{1,0:T(8,128)(2,1)} %param.11) | copy-start | bytes 3145732
  6.5 110.3 %all-gather.5.cloned.1.call-start = ((), (), s32[]{:S(2)}) async-start(), calls=%async_computation.1 | async-start | bytes 5242880 | tf_op jit(solution)/shard_map/all_gather | solution.py:68
  7.3 162.3 %all-gather.7.cloned.1.call-start = ((), (), s32[]{:S(2)}) async-start(), calls=%async_computation.2 | async-start | bytes 1310720 | tf_op jit(solution)/shard_map/all_gather | solution.py:67
  7.3 26.2 %collective-permute-start.2 = (bf16[128,4096]{1,0:T(8,128)(2,1)}, bf16[128,4096]{1,0:T(8,128)(2,1)S(1)}, u32[]{:S(2)}, u32[]{:S(2)}) collective-permute-start(bf16[128,4096]{1,0:T(8,128)(2,1)} %param.11), channel_id=1, source_target_pairs={{0,3},{1,0},{2,1},{3,2},{4,7},{5,4},{6,5},{7,6},{8,11},{9,8},{10,9... | collective-permute-start | bytes 3145736 | tf_op jit(solution)/shard_map/ppermute | solution.py:29
  9.8 47.1 %collective-permute-start.1 = (bf16[128,4096]{1,0:T(8,128)(2,1)}, bf16[128,4096]{1,0:T(8,128)(2,1)S(1)}, u32[]{:S(2)}, u32[]{:S(2)}) collective-permute-start(bf16[128,4096]{1,0:T(8,128)(2,1)} %param.11), channel_id=1, source_target_pairs={{0,2},{1,3},{2,0},{3,1},{4,6},{5,7},{6,4},{7,5},{8,10},{9,11},{10,... | collective-permute-start | bytes 3145736 | tf_op jit(solution)/shard_map/ppermute | solution.py:29
  10.4 46.4 %collective-permute-start = (bf16[128,4096]{1,0:T(8,128)(2,1)}, bf16[128,4096]{1,0:T(8,128)(2,1)S(1)}, u32[]{:S(2)}, u32[]{:S(2)}) collective-permute-start(bf16[128,4096]{1,0:T(8,128)(2,1)} %param.11), channel_id=1, source_target_pairs={{0,1},{1,2},{2,3},{3,0},{4,5},{5,6},{6,7},{7,4},{8,9},{9,10},{10,1... | collective-permute-start | bytes 3145736 | tf_op jit(solution)/shard_map/ppermute | solution.py:29
  13.0 47.8 %copy-start.1 = (bf16[1024,384]{1,0:T(8,128)(2,1)}, bf16[1024,384]{1,0:T(8,128)(2,1)S(1)}, u32[]{:S(2)}) copy-start(bf16[1024,384]{1,0:T(8,128)(2,1)S(1)} %get-tuple-element.13) | copy-start | bytes 2359300
  56.8 7.9 %copy-start.10 = (s32[128]{0:T(128)S(1)}, s32[128]{0:T(128)}, u32[]{:S(2)}) copy-start(s32[128]{0:T(128)} %param.12) | copy-start | bytes 1540
  59.2 54.3 %collective-permute-start.5 = (bf16[1024,384]{1,0:T(8,128)(2,1)S(1)}, bf16[1024,384]{1,0:T(8,128)(2,1)S(1)}, u32[]{:S(2)}, u32[]{:S(2)}) collective-permute-start(bf16[1024,384]{1,0:T(8,128)(2,1)S(1)} %get-tuple-element.13), channel_id=1, source_target_pairs={{0,3},{1,0},{2,1},{3,2},{4,7},{5,4},{6,5},{7,6},{8,11},{9,8},{10,9... | collective-permute-start | bytes 2359304 | tf_op jit(solution)/shard_map/ppermute | solution.py:29
  59.2 54.3 %collective-permute-start.4 = (bf16[1024,384]{1,0:T(8,128)(2,1)S(1)}, bf16[1024,384]{1,0:T(8,128)(2,1)S(1)}, u32[]{:S(2)}, u32[]{:S(2)}) collective-permute-start(bf16[1024,384]{1,0:T(8,128)(2,1)S(1)} %get-tuple-element.13), channel_id=1, source_target_pairs={{0,2},{1,3},{2,0},{3,1},{4,6},{5,7},{6,4},{7,5},{8,10},{9,11},{10,... | collective-permute-start | bytes 2359304 | tf_op jit(solution)/shard_map/ppermute | solution.py:29
  60.8 52.7 %collective-permute-start.3 = (bf16[1024,384]{1,0:T(8,128)(2,1)S(1)}, bf16[1024,384]{1,0:T(8,128)(2,1)S(1)}, u32[]{:S(2)}, u32[]{:S(2)}) collective-permute-start(bf16[1024,384]{1,0:T(8,128)(2,1)S(1)} %get-tuple-element.13), channel_id=1, source_target_pairs={{0,1},{1,2},{2,3},{3,0},{4,5},{5,6},{6,7},{7,4},{8,9},{9,10},{10,1... | collective-permute-start | bytes 2359304 | tf_op jit(solution)/shard_map/ppermute | solution.py:29
  63.1 41.1 %collective-permute-start.8 = (bf16[4,64,384]{2,1,0:T(8,128)(2,1)}, bf16[4,64,384]{2,1,0:T(8,128)(2,1)}, u32[]{:S(2)}, u32[]{:S(2)}) collective-permute-start(bf16[4,64,384]{2,1,0:T(8,128)(2,1)} %get-tuple-element.24), channel_id=1, source_target_pairs={{0,3},{1,0},{2,1},{3,2},{4,7},{5,4},{6,5},{7,6},{8,11},{9,8},{10,9... | collective-permute-start | bytes 589832 | tf_op jit(solution)/shard_map/ppermute | solution.py:65
  64.7 109.3 %all-gather.9.cloned.1.call-start = ((), (), s32[]{:S(2)}) async-start(), calls=%async_computation.3 | async-start | bytes 2621440 | tf_op jit(solution)/shard_map/all_gather | solution.py:83
  64.7 31.5 %collective-permute-start.11 = (s32[128]{0:T(128)S(1)}, s32[128]{0:T(128)S(1)}, u32[]{:S(2)}, u32[]{:S(2)}) collective-permute-start(s32[128]{0:T(128)S(1)} %copy-done.10), channel_id=1, source_target_pairs={{0,3},{1,0},{2,1},{3,2},{4,7},{5,4},{6,5},{7,6},{8,11},{9,8},{10,9... | collective-permute-start | bytes 1544 | tf_op jit(solution)/shard_map/ppermute | solution.py:29
  96.2 3.5 %collective-permute-start.10 = (s32[128]{0:T(128)S(1)}, s32[128]{0:T(128)S(1)}, u32[]{:S(2)}, u32[]{:S(2)}) collective-permute-start(s32[128]{0:T(128)S(1)} %copy-done.10), channel_id=1, source_target_pairs={{0,2},{1,3},{2,0},{3,1},{4,6},{5,7},{6,4},{7,5},{8,10},{9,11},{10,... | collective-permute-start | bytes 1544 | tf_op jit(solution)/shard_map/ppermute | solution.py:29
  99.7 3.0 collective-permute-start.9
  102.7 1.6 copy-start.11
  102.7 8.2 %collective-permute-start.7 = (bf16[4,64,384]{2,1,0:T(8,128)(2,1)}, bf16[4,64,384]{2,1,0:T(8,128)(2,1)}, u32[]{:S(2)}, u32[]{:S(2)}) collective-permute-start(bf16[4,64,384]{2,1,0:T(8,128)(2,1)} %get-tuple-element.25), channel_id=1, source_target_pairs={{0,2},{1,3},{2,0},{3,1},{4,6},{5,7},{6,4},{7,5},{8,10},{9,11},{10,... | collective-permute-start | bytes 589832 | tf_op jit(solution)/shard_map/ppermute | solution.py:65
  104.3 7.1 %collective-permute-start.6 = (bf16[4,64,384]{2,1,0:T(8,128)(2,1)S(1)}, bf16[4,64,384]{2,1,0:T(8,128)(2,1)}, u32[]{:S(2)}, u32[]{:S(2)}) collective-permute-start(bf16[4,64,384]{2,1,0:T(8,128)(2,1)S(1)} %get-tuple-element.26), channel_id=1, source_target_pairs={{0,1},{1,2},{2,3},{3,0},{4,5},{5,6},{6,7},{7,4},{8,9},{9,10},{10,1... | collective-permute-start | bytes 589832 | tf_op jit(solution)/shard_map/ppermute | solution.py:65
  104.3 10.7 %copy-start.2 = (bf16[1024,384]{1,0:T(8,128)(2,1)S(1)}, bf16[1024,384]{1,0:T(8,128)(2,1)}, u32[]{:S(2)}) copy-start(bf16[1024,384]{1,0:T(8,128)(2,1)} %copy-done.1) | copy-start | bytes 2359300
  113.5 0.9 copy-start.5
  113.5 1.2 copy-start.6
  113.5 1.4 copy-start.7
  123.4 5.0 %copy-start.3 = (bf16[64,2048]{1,0:T(8,128)(2,1)S(1)}, bf16[64,2048]{1,0:T(8,128)(2,1)}, u32[]{:S(2)}) copy-start(bf16[64,2048]{1,0:T(8,128)(2,1)} %param.15) | copy-start | bytes 786436
  127.4 97.9 %reduce-scatter.2.cloned.1.call-start = ((), (), s32[]{:S(2)}) async-start(), calls=%async_computation.4 | async-start | bytes 2785280 | tf_op jit(solution)/shard_map/reduce_scatter | solution.py:92
  127.5 38.9 %collective-permute-start.17 = (bf16[128,2048]{1,0:T(8,128)(2,1)}, bf16[128,2048]{1,0:T(8,128)(2,1)}, u32[]{:S(2)}, u32[]{:S(2)}) collective-permute-start(bf16[128,2048]{1,0:T(8,128)(2,1)} %param.10), channel_id=1, source_target_pairs={{0,3},{1,0},{2,1},{3,2},{4,7},{5,4},{6,5},{7,6},{8,11},{9,8},{10,9... | collective-permute-start | bytes 1572872 | tf_op jit(solution)/shard_map/ppermute | solution.py:29
  127.5 38.8 %collective-permute-start.16 = (bf16[128,2048]{1,0:T(8,128)(2,1)}, bf16[128,2048]{1,0:T(8,128)(2,1)}, u32[]{:S(2)}, u32[]{:S(2)}) collective-permute-start(bf16[128,2048]{1,0:T(8,128)(2,1)} %param.10), channel_id=1, source_target_pairs={{0,2},{1,3},{2,0},{3,1},{4,6},{5,7},{6,4},{7,5},{8,10},{9,11},{10,... | collective-permute-start | bytes 1572872 | tf_op jit(solution)/shard_map/ppermute | solution.py:29
  128.2 38.1 %collective-permute-start.15 = (bf16[128,2048]{1,0:T(8,128)(2,1)}, bf16[128,2048]{1,0:T(8,128)(2,1)}, u32[]{:S(2)}, u32[]{:S(2)}) collective-permute-start(bf16[128,2048]{1,0:T(8,128)(2,1)} %param.10), channel_id=1, source_target_pairs={{0,1},{1,2},{2,3},{3,0},{4,5},{5,6},{6,7},{7,4},{8,9},{9,10},{10,1... | collective-permute-start | bytes 1572872 | tf_op jit(solution)/shard_map/ppermute | solution.py:29
  129.1 34.6 %collective-permute-start.18 = (f32[]{:T(128)}, f32[]{:T(128)}, u32[]{:S(2)}, u32[]{:S(2)}) collective-permute-start(f32[]{:T(128)} %convert_reduce_fusion), channel_id=1, source_target_pairs={{0,1},{1,2},{2,3},{3,0},{4,5},{5,6},{6,7},{7,4},{8,9},{9,10},{10,1... | collective-permute-start | bytes 20 | tf_op jit(solution)/shard_map/ppermute | solution.py:90
  130.5 34.5 %collective-permute-start.19 = (f32[]{:T(128)}, f32[]{:T(128)}, u32[]{:S(2)}, u32[]{:S(2)}) collective-permute-start(f32[]{:T(128)} %convert_reduce_fusion), channel_id=1, source_target_pairs={{0,2},{1,3},{2,0},{3,1},{4,6},{5,7},{6,4},{7,5},{8,10},{9,11},{10,... | collective-permute-start | bytes 20 | tf_op jit(solution)/shard_map/ppermute | solution.py:90
  163.7 2.0 collective-permute-start.20
  177.9 99.7 %all-gather.11.cloned.1.call-start = ((), (), s32[]{:S(2)}) async-start(), calls=%async_computation.5 | async-start | bytes 2621440 | tf_op jit(solution)/shard_map/all_gather | solution.py:105
  177.9 19.7 %collective-permute-start.14 = (bf16[1024,384]{1,0:T(8,128)(2,1)}, bf16[1024,384]{1,0:T(8,128)(2,1)S(1)}, u32[]{:S(2)}, u32[]{:S(2)}) collective-permute-start(bf16[1024,384]{1,0:T(8,128)(2,1)} %get-tuple-element.17), channel_id=1, source_target_pairs={{0,3},{1,0},{2,1},{3,2},{4,7},{5,4},{6,5},{7,6},{8,11},{9,8},{10,9... | collective-permute-start | bytes 2359304 | tf_op jit(solution)/shard_map/ppermute | solution.py:29
  179.5 36.1 %collective-permute-start.13 = (bf16[1024,384]{1,0:T(8,128)(2,1)}, bf16[1024,384]{1,0:T(8,128)(2,1)S(1)}, u32[]{:S(2)}, u32[]{:S(2)}) collective-permute-start(bf16[1024,384]{1,0:T(8,128)(2,1)} %get-tuple-element.17), channel_id=1, source_target_pairs={{0,2},{1,3},{2,0},{3,1},{4,6},{5,7},{6,4},{7,5},{8,10},{9,11},{10,... | collective-permute-start | bytes 2359304 | tf_op jit(solution)/shard_map/ppermute | solution.py:29
  180.6 35.0 %collective-permute-start.12 = (bf16[1024,384]{1,0:T(8,128)(2,1)}, bf16[1024,384]{1,0:T(8,128)(2,1)S(1)}, u32[]{:S(2)}, u32[]{:S(2)}) collective-permute-start(bf16[1024,384]{1,0:T(8,128)(2,1)} %get-tuple-element.17), channel_id=1, source_target_pairs={{0,1},{1,2},{2,3},{3,0},{4,5},{5,6},{6,7},{7,4},{8,9},{9,10},{10,1... | collective-permute-start | bytes 2359304 | tf_op jit(solution)/shard_map/ppermute | solution.py:29
  232.1 3.9 %copy-start.13 = (s32[6]{0:T(128)S(1)}, s32[6]{0:T(128)}, u32[]{:S(2)}) copy-start(s32[6]{0:T(128)} %param.16) | copy-start | bytes 76
  232.1 4.6 %copy-start = (bf16[4,1024,384]{2,1,0:T(8,128)(2,1)S(1)}, bf16[4,1024,384]{2,1,0:T(8,128)(2,1)}, u32[]{:S(2)}) copy-start(bf16[4,1024,384]{2,1,0:T(8,128)(2,1)} %pad_maximum_fusion.2) | copy-start | bytes 9437188
  236.7 40.9 %copy-start.8 = (bf16[4,4,64,384]{3,2,1,0:T(8,128)(2,1)S(1)}, bf16[4,4,64,384]{3,2,1,0:T(8,128)(2,1)}, u32[]{:S(2)}) copy-start(bf16[4,4,64,384]{3,2,1,0:T(8,128)(2,1)} %pad_maximum_fusion.4) | copy-start | bytes 2359300
  277.5 6.0 %copy-start.12 = (bf16[256,4096]{1,0:T(8,128)(2,1)S(1)}, bf16[256,4096]{1,0:T(8,128)(2,1)}, u32[]{:S(2)}) copy-start(bf16[256,4096]{1,0:T(8,128)(2,1)} %all-gather.11.cloned.1.call-done) | copy-start | bytes 6291460
  304.7 8.4 %copy-start.9 = (s32[384]{0:T(512)S(1)}, s32[384]{0:T(512)}, u32[]{:S(2)}) copy-start(s32[384]{0:T(512)} %param.19) | copy-start | bytes 4612
  310.1 3.6 %collective-permute-start.23 = (f32[6,384]{1,0:T(8,128)S(1)}, f32[6,384]{1,0:T(8,128)S(1)}, u32[]{:S(2)}, u32[]{:S(2)}) collective-permute-start(f32[6,384]{1,0:T(8,128)S(1)} %get-tuple-element.28), channel_id=1, source_target_pairs={{0,1},{1,2},{2,3},{3,0},{4,5},{5,6},{6,7},{7,4},{8,9},{9,10},{10,1... | collective-permute-start | bytes 27656 | tf_op jit(solution)/shard_map/ppermute | solution.py:119
  310.1 3.8 %collective-permute-start.22 = (f32[6,384]{1,0:T(8,128)S(1)}, f32[6,384]{1,0:T(8,128)S(1)}, u32[]{:S(2)}, u32[]{:S(2)}) collective-permute-start(f32[6,384]{1,0:T(8,128)S(1)} %get-tuple-element.29), channel_id=1, source_target_pairs={{0,2},{1,3},{2,0},{3,1},{4,6},{5,7},{6,4},{7,5},{8,10},{9,11},{10,... | collective-permute-start | bytes 27656 | tf_op jit(solution)/shard_map/ppermute | solution.py:119
  311.7 2.8 collective-permute-start.21
Sparse Core Ops, SparseCore 0:
  8.9 83.2 all-gather.4
  93.8 26.1 all-gather.6
  127.5 34.4 all-gather.8
  178.0 47.3 reduce-scatter.1
  232.2 45.3 all-gather.10

commit v10 on v9

--- a/solution.py
+++ b/solution.py
@@ -54,16 +54,6 @@
     act_tokens = ring_gather(query_act, "wb")
     grad_tokens = ring_gather(query_grad, "wb")
     positions = ring_gather(query_positions, "wb")
-    me = lax.axis_index("wb")
-    half = train_grad_rot.shape[0] // 2
-    first_rows, train_act_rot, _ = lax.optimization_barrier((train_grad_rot[:half], train_act_rot, grad_tokens))
-    grads_first = ring_gather(first_rows, "wb")
-    act_blocks = train_act_rot.reshape(na, nb, -1, train_act_rot.shape[1])
-    acts_near = [act_blocks[:, me]]
-    for shift in range(1, nb):
-        outgoing = lax.dynamic_index_in_dim(act_blocks, (me + shift) % nb, axis=1, keepdims=False)
-        acts_near.append(lax.ppermute(outgoing, "wb", perm=[(i, (i + shift) % nb) for i in range(nb)]))
-    acts_near = jnp.stack(acts_near)
     act_cols = lax.all_gather(act_basis, "wa", axis=1, tiled=True)
     grad_cols = lax.all_gather(grad_basis, "wa", axis=1, tiled=True)
     count = query_act.shape[0]
@@ -77,9 +67,6 @@
     grad_kept = grad_rot * query_weight[:, None]
     act_rot = natural_order(act_rot.reshape(nb, count, -1), "wb").reshape(nb * count, -1)
     grad_kept = natural_order(grad_kept.reshape(nb, count, -1), "wb").reshape(nb * count, -1)
-    grads_first, acts_near, grad_kept = lax.optimization_barrier((grads_first, acts_near, grad_kept))
-    second_rows, _ = lax.optimization_barrier((train_grad_rot[half:], grad_kept))
-    grads_second = ring_gather(second_rows, "wb")
     grad_all = lax.all_gather(grad_kept, "wb", axis=1, tiled=True)
     partial_rows = lax.dot_general(
         act_rot, grad_all, (((0,), (0,)), ((), ())), preferred_element_type=jnp.float32
@@ -93,6 +80,16 @@
         jnp.concatenate([partial_rows, extra], axis=1), "wa", scatter_dimension=0, tiled=True
     )
     gradient_rows = reduced[:, : partial_rows.shape[1]]
+    me = lax.axis_index("wb")
+    half = train_grad_rot.shape[0] // 2
+    first_rows, train_act_rot, _ = lax.optimization_barrier((train_grad_rot[:half], train_act_rot, partial_rows))
+    grads_first = ring_gather(first_rows, "wb")
+    act_blocks = train_act_rot.reshape(na, nb, -1, train_act_rot.shape[1])
+    acts_near = [act_blocks[:, me]]
+    for shift in range(1, nb):
+        outgoing = lax.dynamic_index_in_dim(act_blocks, (me + shift) % nb, axis=1, keepdims=False)
+        acts_near.append(lax.ppermute(outgoing, "wb", perm=[(i, (i + shift) % nb) for i in range(nb)]))
+    acts_near = jnp.stack(acts_near)
     eig_total = reduced[0, partial_rows.shape[1]]
     rows = gradient_rows.shape[0]
     gradient_rows = gradient_rows.reshape(rows, nb, na, -1).transpose(0, 2, 1, 3).reshape(rows, -1)
@@ -101,7 +98,9 @@
     mean_eig = eig_total / (eig_in * eig_out)
     dampings = mean_eig * jnp.exp2(damping_index.astype(jnp.float32) - 4.0)
     payload = jnp.concatenate([gradient_rows.astype(jnp.bfloat16), eig_values], axis=1)
-    grads_second, payload = lax.optimization_barrier((grads_second, payload))
+    grads_first, acts_near, payload = lax.optimization_barrier((grads_first, acts_near, payload))
+    second_rows, _ = lax.optimization_barrier((train_grad_rot[half:], payload))
+    grads_second = ring_gather(second_rows, "wb")
     rows_held = lax.all_gather(payload, "wa", axis=0, tiled=True)
     gradient_held, eig_held = rows_held[:, :eig_out], rows_held[:, eig_out:]
     grads_near = jnp.concatenate([grads_first, grads_second], axis=1)

time: 323 us -> 284 us (0.88)
  waiting for transfers between devices: 201 us -> 184 us
  matrix products: 43.8 us -> 29 us
  local copies, waits for them, and re-layouts: 21.1 us -> 14.5 us
    ppermute x15, waiting for transfers between devices: 114 us -> 77.5 us  [ring_gather(): lax.ppermute(x, axis, perm=[(i, (i + shift) % n) for i in range(n)])]
    all_gather x1, waiting for transfers between devices: 38.9 us -> 6 us  [shards(): rows_held = lax.all_gather(payload, 'wa', axis=0, tiled=True)]
    ppermute x3, waiting for transfers between devices: 6.34 us -> 37.9 us  [shards(): lax.ppermute(outgoing, 'wb', perm=[(i, (i + shift) % nb) for i in range(n...]
    all_gather x1, waiting for transfers between devices: 0.02 us -> 28.6 us  [shards(): grad_cols = lax.all_gather(grad_basis, 'wa', axis=1, tiled=True)]
    dot_general x6, matrix products: 32.3 us -> 18.9 us  [shards(): jnp.einsum('ij,sjt->sit', precond, grads_near, preferred_element_type=jnp...]
    ppermute x3, waiting for transfers between devices: 32.6 us -> 21.1 us  [shards(): lax.ppermute(eig_sum, 'wb', perm=[(i, (i + shift) % nb) for i in range(nb)])]
    all_gather x1, waiting for transfers between devices: 0.02 us -> 11.4 us  [shards(): grad_all = lax.all_gather(grad_kept, 'wb', axis=1, tiled=True)]
    reduce_scatter x1, waiting for transfers between devices: 6.83 us -> 0.02 us  [shards(): lax.psum_scatter(jnp.concatenate([partial_rows, extra], axis=1), 'wa', sc...]
  transfers between devices with their start and end apart: 29 -> 29, of which waited for: 14 -> 14; matrix products, arithmetic and copies ran while one was open for 12% -> 10% of each run, Pallas kernels for 0% -> 0%
where the time goes in v10:
time: 284 us
  waiting for transfers between devices  184 us (65%)
  matrix products  29 us (10%)
  starting transfers between devices  21.2 us (7%)
  other arithmetic  17.6 us (6%)
  between operations  17.3 us (6%)
  local copies, waits for them, and re-layouts  14.5 us (5%)
    ppermute x15, waiting for transfers between devices, ring_gather(): lax.ppermute(x, axis, perm=[(i, (i + shift) % n) for i in range(n)])  77.5 us
    ppermute x3, waiting for transfers between devices, shards(): lax.ppermute(outgoing, 'wb', perm=[(i, (i + shift) % nb) for i in range(n...  37.9 us
    all_gather x1, waiting for transfers between devices, shards(): grad_cols = lax.all_gather(grad_basis, 'wa', axis=1, tiled=True)  28.6 us
    ppermute x3, waiting for transfers between devices, shards(): lax.ppermute(eig_sum, 'wb', perm=[(i, (i + shift) % nb) for i in range(nb)])  21.1 us
    dot_general x6, matrix products, shards(): jnp.einsum('ij,sjt->sit', precond, grads_near, preferred_element_type=jnp...  18.9 us
    ppermute x15, starting transfers between devices, ring_gather(): lax.ppermute(x, axis, perm=[(i, (i + shift) % n) for i in range(n)])  11.8 us
    all_gather x1, waiting for transfers between devices, shards(): grad_all = lax.all_gather(grad_kept, 'wb', axis=1, tiled=True)  11.4 us
    another operation x3, other arithmetic, ring_gather(): return jnp.stack(parts)  7.21 us
  transfers between devices with their start and end apart: 29, of which 14 were waited for; matrix products, arithmetic and copies ran while one was open for 10% of the time, Pallas kernels for 0%

profile of v10, /device:TPU:0, one launch (start us, length us, event | category | flops | bytes accessed | tf_op | source)
XLA Modules:
  0.0 283.7 jit_solution(16537245053389268519)
XLA Ops:
  6.5 0.7 all-gather.7.cloned.1.call-update
  7.3 2.5 collective-permute-start.5
  9.8 0.6 collective-permute-start.4
  10.6 1.6 collective-permute-start.8
  12.3 1.4 collective-permute-start.7
  13.7 42.3 %collective-permute-done.8 = s32[128]{0:T(128)S(1)} collective-permute-done((s32[128]{0:T(128)}, s32[128]{0:T(128)S(1)}, u32[]{:S(2)}, u32[]{:S(2)}) %collective-permute-start.8) | collective-permute-done | bytes 544 | tf_op jit(solution)/shard_map/ppermute | solution.py:29
  56.0 1.1 collective-permute-start.6
  57.0 2.5 collective-permute-done.6
  59.5 0.7 fusion.44
  60.2 3.4 %pad_maximum_fusion = bf16[4,128,4096]{2,1,0:T(8,128)(2,1)} fusion(bf16[1,128,4096]{2,1,0:T(8,128)(2,1)S(1)} %bitcast.119, bf16[1,128,4096]{2,1,0:T(8,128)(2,1)S(1)} %bitcast.120, bf16[1,128,4096]{2,1,0:T(8,128)(2,1)S(1)} %bitcast.121, bf16[1,128,4096]{2,1,0:T(8,128)(2,1)} %bitcast.118), kind=kLoop, calls=%fused_computation.13 | loop fusion | flops 6291456 | bytes 8388608 | tf_op jit(solution)/shard_map/stack | solution.py:30
  63.6 28.6 %all-gather.7.cloned.1.call-done = bf16[4096,512]{1,0:T(8,128)(2,1)} async-done(((bf16[4096,128]{1,0:T(8,128)(2,1)}), bf16[4096,512]{1,0:T(8,128)(2,1)}) %all-gather.7.cloned.1.call-update) | async-done | bytes 4194320 | tf_op jit(solution)/shard_map/all_gather | solution.py:58
  92.2 5.8 %fusion.12 = bf16[512,512]{1,0:T(8,128)(2,1)S(1)} fusion(bf16[512,4096]{1,0:T(8,128)(2,1)} %bitcast.111, bf16[4096,512]{1,0:T(8,128)(2,1)} %all-gather.7.cloned.1.call-done, bf16[512]{0:T(512)(128)(2,1)S(1)} %fusion.44), kind=kOutput, calls=%fused_computation.35 | convolution fusion | flops 2148007936 | bytes 8913920 | tf_op jit(solution)/shard_map/dot_general | solution.py:63
  98.1 1.0 fusion.25
  99.2 1.2 collective-permute-start.2
  100.4 0.5 collective-permute-start.1
  100.9 0.7 convert_reduce_fusion
  101.7 1.6 collective-permute-start.15
  103.2 0.5 collective-permute-start.16
  103.7 21.1 %collective-permute-done.15 = f32[]{:T(128)} collective-permute-done((f32[]{:T(128)}, f32[]{:T(128)}, u32[]{:S(2)}, u32[]{:S(2)}) %collective-permute-start.15) | collective-permute-done | bytes 36 | tf_op jit(solution)/shard_map/ppermute | solution.py:77
  127.4 0.8 copy-done.9
  128.1 0.2 copy-done.10
  128.3 1.7 pad_maximum_fusion.2
  130.1 2.0 convolution_convert_fusion.1
  132.2 11.4 %all-gather.9.cloned.1.call-done = bf16[512,2048]{1,0:T(8,128)(2,1)} async-done(((bf16[512,512]{1,0:T(8,128)(2,1)}), bf16[512,2048]{1,0:T(8,128)(2,1)}) %all-gather.9.cloned.1.call-update) | async-done | bytes 2097168 | tf_op jit(solution)/shard_map/all_gather | solution.py:70
  143.6 2.3 fusion.47
  145.9 1.6 concatenate.17
  147.6 1.3 copy-done.2
  148.9 1.0 fusion.45
  150.1 1.7 collective-permute-start.10
  151.8 1.3 dynamic-slice_bitcast_fusion.3
  153.1 1.8 collective-permute-start.14
  154.9 0.3 collective-permute-start.13
  155.3 33.6 %collective-permute-done.14 = bf16[4,64,384]{2,1,0:T(8,128)(2,1)S(1)} collective-permute-done((bf16[4,64,384]{2,1,0:T(8,128)(2,1)S(1)}, bf16[4,64,384]{2,1,0:T(8,128)(2,1)S(1)}, u32[]{:S(2)}, u32[]{:S(2)}) %collective-permute-start.14) | collective-permute-done | bytes 196640 | tf_op jit(solution)/shard_map/ppermute | solution.py:91
  188.8 2.0 collective-permute-start.12
  190.8 2.9 %collective-permute-done.13 = bf16[4,64,384]{2,1,0:T(8,128)(2,1)S(1)} collective-permute-done((bf16[4,64,384]{2,1,0:T(8,128)(2,1)S(1)}, bf16[4,64,384]{2,1,0:T(8,128)(2,1)S(1)}, u32[]{:S(2)}, u32[]{:S(2)}) %collective-permute-start.13) | collective-permute-done | bytes 196640 | tf_op jit(solution)/shard_map/ppermute | solution.py:91
  193.7 1.5 collective-permute-done.12
  195.2 1.1 pad_maximum_fusion.3
  196.3 0.8 copy-done.4
  197.2 0.3 copy-done.5
  197.4 0.3 copy-done.6
  197.7 2.1 pad_maximum_fusion.1
  199.8 1.8 slice.136
  201.6 1.1 convert_element_type.67
  202.7 0.8 copy.11
  203.5 1.1 convert_element_type.69
  204.6 1.8 pad_maximum_fusion.4
  206.5 0.7 collective-permute-start.19
  207.4 1.2 slice.68
  209.2 0.7 fusion.46
  209.9 14.8 %collective-permute-done.20 = bf16[1024,384]{1,0:T(8,128)(2,1)S(1)} collective-permute-done((bf16[1024,384]{1,0:T(8,128)(2,1)}, bf16[1024,384]{1,0:T(8,128)(2,1)S(1)}, u32[]{:S(2)}, u32[]{:S(2)}) %collective-permute-start.20) | collective-permute-done | bytes 786464 | tf_op jit(solution)/shard_map/ppermute | solution.py:29
  224.6 17.0 %collective-permute-done.19 = bf16[1024,384]{1,0:T(8,128)(2,1)S(1)} collective-permute-done((bf16[1024,384]{1,0:T(8,128)(2,1)}, bf16[1024,384]{1,0:T(8,128)(2,1)S(1)}, u32[]{:S(2)}, u32[]{:S(2)}) %collective-permute-start.19) | collective-permute-done | bytes 786464 | tf_op jit(solution)/shard_map/ppermute | solution.py:29
  241.6 1.0 collective-permute-done.18
  242.6 4.4 %maximum_maximum_fusion = bf16[4,2048,384]{2,1,0:T(8,128)(2,1)} fusion(bf16[1,1024,384]{2,1,0:T(8,128)(2,1)S(1)} %bitcast.125, bf16[1,1024,384]{2,1,0:T(8,128)(2,1)S(1)} %bitcast.126, bf16[1,1024,384]{2,1,0:T(8,128)(2,1)S(1)} %bitcast.127, bf16[1,1024,384]{2,1,0:T(8,128)(2,1)} %bitcast.112, bf16[4,1024,384]{2,1,0:T(8,128)(2,1)S(1)} %pad_maximum_fusion.1), kind=kLoop, calls=%fused_computation | loop fusion | flops 31457280 | bytes 12582912 | tf_op jit(solution)/shard_map/concatenate | solution.py:106
  247.0 6.0 %all-gather.11.cloned.1.call-done = bf16[256,4096]{1,0:T(8,128)(2,1)} async-done(((bf16[64,4096]{1,0:T(8,128)(2,1)}), bf16[256,4096]{1,0:T(8,128)(2,1)}) %all-gather.11.cloned.1.call-update) | async-done | bytes 2097168 | tf_op jit(solution)/shard_map/all_gather | solution.py:104
  253.0 6.5 %fusion.6 = f32[4,384]{1,0:T(4,128)S(1)} fusion(bf16[4,256,384]{2,1,0:T(8,128)(2,1)} %bitcast.129, bf16[4,2048,384]{2,1,0:T(8,128)(2,1)} %maximum_maximum_fusion, f32[]{:T(128)} %bitcast.37, bf16[256,4096]{1,0:T(8,128)(2,1)} %all-gather.11.cloned.1.call-done), kind=kOutput, calls=%fused_computation.28 | convolution fusion | flops 1614412288 | bytes 9181188 | tf_op jit(solution)/shard_map/ij,sjt->sit/dot_general | solution.py:113
  259.5 2.4 fusion.7
  262.0 2.5 fusion.8
  264.5 2.5 fusion.9
  267.0 2.5 fusion.10
  269.5 2.6 fusion.11
  272.2 1.6 collective-permute-start.22
  273.8 1.4 collective-permute-start.21
  276.0 0.6 collective-permute-done.21
  276.6 0.6 fusion.43
  (68 shorter events, 1.5 us)
Async XLA Ops:
  6.5 85.7 %all-gather.7.cloned.1.call-start = ((), (), s32[]{:S(2)}) async-start(), calls=%async_computation.2 | async-start | bytes 5242880 | tf_op jit(solution)/shard_map/all_gather | solution.py:58
  7.3 122.8 %all-gather.5.cloned.1.call-start = ((), (), s32[]{:S(2)}) async-start(), calls=%async_computation.1 | async-start | bytes 1310720 | tf_op jit(solution)/shard_map/all_gather | solution.py:57
  7.3 52.9 %collective-permute-start.5 = (bf16[128,4096]{1,0:T(8,128)(2,1)}, bf16[128,4096]{1,0:T(8,128)(2,1)S(1)}, u32[]{:S(2)}, u32[]{:S(2)}) collective-permute-start(bf16[128,4096]{1,0:T(8,128)(2,1)} %param.11), channel_id=1, source_target_pairs={{0,3},{1,0},{2,1},{3,2},{4,7},{5,4},{6,5},{7,6},{8,11},{9,8},{10,9... | collective-permute-start | bytes 3145736 | tf_op jit(solution)/shard_map/ppermute | solution.py:29
  9.8 50.4 %collective-permute-start.4 = (bf16[128,4096]{1,0:T(8,128)(2,1)}, bf16[128,4096]{1,0:T(8,128)(2,1)S(1)}, u32[]{:S(2)}, u32[]{:S(2)}) collective-permute-start(bf16[128,4096]{1,0:T(8,128)(2,1)} %param.11), channel_id=1, source_target_pairs={{0,2},{1,3},{2,0},{3,1},{4,6},{5,7},{6,4},{7,5},{8,10},{9,11},{10,... | collective-permute-start | bytes 3145736 | tf_op jit(solution)/shard_map/ppermute | solution.py:29
  10.4 49.8 %collective-permute-start.3 = (bf16[128,4096]{1,0:T(8,128)(2,1)}, bf16[128,4096]{1,0:T(8,128)(2,1)S(1)}, u32[]{:S(2)}, u32[]{:S(2)}) collective-permute-start(bf16[128,4096]{1,0:T(8,128)(2,1)} %param.11), channel_id=1, source_target_pairs={{0,1},{1,2},{2,3},{3,0},{4,5},{5,6},{6,7},{7,4},{8,9},{9,10},{10,1... | collective-permute-start | bytes 3145736 | tf_op jit(solution)/shard_map/ppermute | solution.py:29
  10.6 133.0 %all-gather.9.cloned.1.call-start = ((), (), s32[]{:S(2)}) async-start(), calls=%async_computation.3 | async-start | bytes 2621440 | tf_op jit(solution)/shard_map/all_gather | solution.py:70
  10.6 45.3 %collective-permute-start.8 = (s32[128]{0:T(128)}, s32[128]{0:T(128)S(1)}, u32[]{:S(2)}, u32[]{:S(2)}) collective-permute-start(s32[128]{0:T(128)} %param.12), channel_id=1, source_target_pairs={{0,3},{1,0},{2,1},{3,2},{4,7},{5,4},{6,5},{7,6},{8,11},{9,8},{10,9... | collective-permute-start | bytes 1544 | tf_op jit(solution)/shard_map/ppermute | solution.py:29
  12.3 44.8 %collective-permute-start.7 = (s32[128]{0:T(128)}, s32[128]{0:T(128)S(1)}, u32[]{:S(2)}, u32[]{:S(2)}) collective-permute-start(s32[128]{0:T(128)} %param.12), channel_id=1, source_target_pairs={{0,2},{1,3},{2,0},{3,1},{4,6},{5,7},{6,4},{7,5},{8,10},{9,11},{10,... | collective-permute-start | bytes 1544 | tf_op jit(solution)/shard_map/ppermute | solution.py:29
  56.0 3.5 %collective-permute-start.6 = (s32[128]{0:T(128)}, s32[128]{0:T(128)S(1)}, u32[]{:S(2)}, u32[]{:S(2)}) collective-permute-start(s32[128]{0:T(128)} %param.12), channel_id=1, source_target_pairs={{0,1},{1,2},{2,3},{3,0},{4,5},{5,6},{6,7},{7,4},{8,9},{9,10},{10,1... | collective-permute-start | bytes 1544 | tf_op jit(solution)/shard_map/ppermute | solution.py:29
  98.0 1.2 copy-start.8
  98.0 2.9 %copy-start.3 = (bf16[64,2048]{1,0:T(8,128)(2,1)S(1)}, bf16[64,2048]{1,0:T(8,128)(2,1)}, u32[]{:S(2)}) copy-start(bf16[64,2048]{1,0:T(8,128)(2,1)} %param.15) | copy-start | bytes 786436
  99.1 100.7 %reduce-scatter.2.cloned.1.call-start = ((), (), s32[]{:S(2)}) async-start(), calls=%async_computation.4 | async-start | bytes 2785280 | tf_op jit(solution)/shard_map/reduce_scatter | solution.py:79
  99.2 28.1 %collective-permute-start.2 = (bf16[128,2048]{1,0:T(8,128)(2,1)S(1)}, bf16[128,2048]{1,0:T(8,128)(2,1)S(1)}, u32[]{:S(2)}, u32[]{:S(2)}) collective-permute-start(bf16[128,2048]{1,0:T(8,128)(2,1)S(1)} %copy-done.8), channel_id=1, source_target_pairs={{0,3},{1,0},{2,1},{3,2},{4,7},{5,4},{6,5},{7,6},{8,11},{9,8},{10,9... | collective-permute-start | bytes 1572872 | tf_op jit(solution)/shard_map/ppermute | solution.py:29
  100.4 27.0 %collective-permute-start.1 = (bf16[128,2048]{1,0:T(8,128)(2,1)S(1)}, bf16[128,2048]{1,0:T(8,128)(2,1)S(1)}, u32[]{:S(2)}, u32[]{:S(2)}) collective-permute-start(bf16[128,2048]{1,0:T(8,128)(2,1)S(1)} %copy-done.8), channel_id=1, source_target_pairs={{0,2},{1,3},{2,0},{3,1},{4,6},{5,7},{6,4},{7,5},{8,10},{9,11},{10,... | collective-permute-start | bytes 1572872 | tf_op jit(solution)/shard_map/ppermute | solution.py:29
  100.8 26.5 %collective-permute-start = (bf16[128,2048]{1,0:T(8,128)(2,1)S(1)}, bf16[128,2048]{1,0:T(8,128)(2,1)S(1)}, u32[]{:S(2)}, u32[]{:S(2)}) collective-permute-start(bf16[128,2048]{1,0:T(8,128)(2,1)S(1)} %copy-done.8), channel_id=1, source_target_pairs={{0,1},{1,2},{2,3},{3,0},{4,5},{5,6},{6,7},{7,4},{8,9},{9,10},{10,1... | collective-permute-start | bytes 1572872 | tf_op jit(solution)/shard_map/ppermute | solution.py:29
  101.7 23.1 %collective-permute-start.15 = (f32[]{:T(128)}, f32[]{:T(128)}, u32[]{:S(2)}, u32[]{:S(2)}) collective-permute-start(f32[]{:T(128)} %convert_reduce_fusion), channel_id=1, source_target_pairs={{0,1},{1,2},{2,3},{3,0},{4,5},{5,6},{6,7},{7,4},{8,9},{9,10},{10,1... | collective-permute-start | bytes 20 | tf_op jit(solution)/shard_map/ppermute | solution.py:77
  103.2 22.9 %collective-permute-start.16 = (f32[]{:T(128)}, f32[]{:T(128)}, u32[]{:S(2)}, u32[]{:S(2)}) collective-permute-start(f32[]{:T(128)} %convert_reduce_fusion), channel_id=1, source_target_pairs={{0,2},{1,3},{2,0},{3,1},{4,6},{5,7},{6,4},{7,5},{8,10},{9,11},{10,... | collective-permute-start | bytes 20 | tf_op jit(solution)/shard_map/ppermute | solution.py:77
  124.8 2.0 collective-permute-start.17
  127.3 0.8 copy-start.9
  127.3 1.0 copy-start.10
  147.5 1.4 copy-start.2
  147.5 105.4 %all-gather.11.cloned.1.call-start = ((), (), s32[]{:S(2)}) async-start(), calls=%async_computation.5 | async-start | bytes 2621440 | tf_op jit(solution)/shard_map/all_gather | solution.py:104
  150.0 46.3 %copy-start.1 = (bf16[1024,384]{1,0:T(8,128)(2,1)}, bf16[1024,384]{1,0:T(8,128)(2,1)S(1)}, u32[]{:S(2)}) copy-start(bf16[1024,384]{1,0:T(8,128)(2,1)S(1)} %get-tuple-element.11) | copy-start | bytes 2359300
  150.0 46.3 %collective-permute-start.11 = (bf16[1024,384]{1,0:T(8,128)(2,1)S(1)}, bf16[1024,384]{1,0:T(8,128)(2,1)S(1)}, u32[]{:S(2)}, u32[]{:S(2)}) collective-permute-start(bf16[1024,384]{1,0:T(8,128)(2,1)S(1)} %get-tuple-element.11), channel_id=1, source_target_pairs={{0,3},{1,0},{2,1},{3,2},{4,7},{5,4},{6,5},{7,6},{8,11},{9,8},{10,9... | collective-permute-start | bytes 2359304 | tf_op jit(solution)/shard_map/ppermute | solution.py:29
  150.1 46.2 %collective-permute-start.10 = (bf16[1024,384]{1,0:T(8,128)(2,1)S(1)}, bf16[1024,384]{1,0:T(8,128)(2,1)S(1)}, u32[]{:S(2)}, u32[]{:S(2)}) collective-permute-start(bf16[1024,384]{1,0:T(8,128)(2,1)S(1)} %get-tuple-element.11), channel_id=1, source_target_pairs={{0,2},{1,3},{2,0},{3,1},{4,6},{5,7},{6,4},{7,5},{8,10},{9,11},{10,... | collective-permute-start | bytes 2359304 | tf_op jit(solution)/shard_map/ppermute | solution.py:29
  151.8 44.5 %collective-permute-start.9 = (bf16[1024,384]{1,0:T(8,128)(2,1)S(1)}, bf16[1024,384]{1,0:T(8,128)(2,1)S(1)}, u32[]{:S(2)}, u32[]{:S(2)}) collective-permute-start(bf16[1024,384]{1,0:T(8,128)(2,1)S(1)} %get-tuple-element.11), channel_id=1, source_target_pairs={{0,1},{1,2},{2,3},{3,0},{4,5},{5,6},{6,7},{7,4},{8,9},{9,10},{10,1... | collective-permute-start | bytes 2359304 | tf_op jit(solution)/shard_map/ppermute | solution.py:29
  153.1 35.7 %collective-permute-start.14 = (bf16[4,64,384]{2,1,0:T(8,128)(2,1)S(1)}, bf16[4,64,384]{2,1,0:T(8,128)(2,1)S(1)}, u32[]{:S(2)}, u32[]{:S(2)}) collective-permute-start(bf16[4,64,384]{2,1,0:T(8,128)(2,1)S(1)} %get-tuple-element.20), channel_id=1, source_target_pairs={{0,3},{1,0},{2,1},{3,2},{4,7},{5,4},{6,5},{7,6},{8,11},{9,8},{10,9... | collective-permute-start | bytes 589832 | tf_op jit(solution)/shard_map/ppermute | solution.py:91
  154.9 38.8 %collective-permute-start.13 = (bf16[4,64,384]{2,1,0:T(8,128)(2,1)S(1)}, bf16[4,64,384]{2,1,0:T(8,128)(2,1)S(1)}, u32[]{:S(2)}, u32[]{:S(2)}) collective-permute-start(bf16[4,64,384]{2,1,0:T(8,128)(2,1)S(1)} %get-tuple-element.21), channel_id=1, source_target_pairs={{0,2},{1,3},{2,0},{3,1},{4,6},{5,7},{6,4},{7,5},{8,10},{9,11},{10,... | collective-permute-start | bytes 589832 | tf_op jit(solution)/shard_map/ppermute | solution.py:91
  188.8 6.4 %collective-permute-start.12 = (bf16[4,64,384]{2,1,0:T(8,128)(2,1)S(1)}, bf16[4,64,384]{2,1,0:T(8,128)(2,1)S(1)}, u32[]{:S(2)}, u32[]{:S(2)}) collective-permute-start(bf16[4,64,384]{2,1,0:T(8,128)(2,1)S(1)} %get-tuple-element.22), channel_id=1, source_target_pairs={{0,1},{1,2},{2,3},{3,0},{4,5},{5,6},{6,7},{7,4},{8,9},{9,10},{10,1... | collective-permute-start | bytes 589832 | tf_op jit(solution)/shard_map/ppermute | solution.py:91
  196.3 0.9 copy-start.4
  196.3 1.2 copy-start.5
  196.3 1.4 copy-start.6
  199.8 9.4 %copy-start.13 = (s32[6]{0:T(128)S(1)}, s32[6]{0:T(128)}, u32[]{:S(2)}) copy-start(s32[6]{0:T(128)} %param.16) | copy-start | bytes 76
  206.5 18.2 %collective-permute-start.20 = (bf16[1024,384]{1,0:T(8,128)(2,1)}, bf16[1024,384]{1,0:T(8,128)(2,1)S(1)}, u32[]{:S(2)}, u32[]{:S(2)}) collective-permute-start(bf16[1024,384]{1,0:T(8,128)(2,1)} %get-tuple-element.15), channel_id=1, source_target_pairs={{0,3},{1,0},{2,1},{3,2},{4,7},{5,4},{6,5},{7,6},{8,11},{9,8},{10,9... | collective-permute-start | bytes 2359304 | tf_op jit(solution)/shard_map/ppermute | solution.py:29
  206.5 35.1 %collective-permute-start.19 = (bf16[1024,384]{1,0:T(8,128)(2,1)}, bf16[1024,384]{1,0:T(8,128)(2,1)S(1)}, u32[]{:S(2)}, u32[]{:S(2)}) collective-permute-start(bf16[1024,384]{1,0:T(8,128)(2,1)} %get-tuple-element.15), channel_id=1, source_target_pairs={{0,2},{1,3},{2,0},{3,1},{4,6},{5,7},{6,4},{7,5},{8,10},{9,11},{10,... | collective-permute-start | bytes 2359304 | tf_op jit(solution)/shard_map/ppermute | solution.py:29
  207.2 35.4 %collective-permute-start.18 = (bf16[1024,384]{1,0:T(8,128)(2,1)}, bf16[1024,384]{1,0:T(8,128)(2,1)S(1)}, u32[]{:S(2)}, u32[]{:S(2)}) collective-permute-start(bf16[1024,384]{1,0:T(8,128)(2,1)} %get-tuple-element.15), channel_id=1, source_target_pairs={{0,1},{1,2},{2,3},{3,0},{4,5},{5,6},{6,7},{7,4},{8,9},{9,10},{10,1... | collective-permute-start | bytes 2359304 | tf_op jit(solution)/shard_map/ppermute | solution.py:29
  253.0 6.5 %copy-start = (bf16[4,2048,384]{2,1,0:T(8,128)(2,1)S(1)}, bf16[4,2048,384]{2,1,0:T(8,128)(2,1)}, u32[]{:S(2)}) copy-start(bf16[4,2048,384]{2,1,0:T(8,128)(2,1)} %maximum_maximum_fusion) | copy-start | bytes 18874372
  253.0 6.5 %copy-start.7 = (bf16[4,4,64,384]{3,2,1,0:T(8,128)(2,1)S(1)}, bf16[4,4,64,384]{3,2,1,0:T(8,128)(2,1)}, u32[]{:S(2)}) copy-start(bf16[4,4,64,384]{3,2,1,0:T(8,128)(2,1)} %pad_maximum_fusion.3) | copy-start | bytes 2359300
  253.0 6.5 %copy-start.12 = (bf16[256,4096]{1,0:T(8,128)(2,1)S(1)}, bf16[256,4096]{1,0:T(8,128)(2,1)}, u32[]{:S(2)}) copy-start(bf16[256,4096]{1,0:T(8,128)(2,1)} %all-gather.11.cloned.1.call-done) | copy-start | bytes 6291460
  269.5 5.7 %copy-start.11 = (s32[384]{0:T(512)S(1)}, s32[384]{0:T(512)}, u32[]{:S(2)}) copy-start(s32[384]{0:T(512)} %param.19) | copy-start | bytes 4612
  272.1 3.7 %collective-permute-start.23 = (f32[6,384]{1,0:T(8,128)S(1)}, f32[6,384]{1,0:T(8,128)S(1)}, u32[]{:S(2)}, u32[]{:S(2)}) collective-permute-start(f32[6,384]{1,0:T(8,128)S(1)} %get-tuple-element.24), channel_id=1, source_target_pairs={{0,1},{1,2},{2,3},{3,0},{4,5},{5,6},{6,7},{7,4},{8,9},{9,10},{10,1... | collective-permute-start | bytes 27656 | tf_op jit(solution)/shard_map/ppermute | solution.py:118
  272.2 3.8 %collective-permute-start.22 = (f32[6,384]{1,0:T(8,128)S(1)}, f32[6,384]{1,0:T(8,128)S(1)}, u32[]{:S(2)}, u32[]{:S(2)}) collective-permute-start(f32[6,384]{1,0:T(8,128)S(1)} %get-tuple-element.25), channel_id=1, source_target_pairs={{0,2},{1,3},{2,0},{3,1},{4,6},{5,7},{6,4},{7,5},{8,10},{9,11},{10,... | collective-permute-start | bytes 27656 | tf_op jit(solution)/shard_map/ppermute | solution.py:118
  273.8 2.8 collective-permute-start.21
Sparse Core Ops, SparseCore 0:
  8.9 83.2 all-gather.6
  93.8 26.0 all-gather.4
  121.5 22.1 all-gather.8
  147.6 45.9 reduce-scatter.1
  206.6 46.3 all-gather.10

commit v11 on v10

--- a/solution.py
+++ b/solution.py
@@ -54,6 +54,7 @@
     act_tokens = ring_gather(query_act, "wb")
     grad_tokens = ring_gather(query_grad, "wb")
     positions = ring_gather(query_positions, "wb")
+    act_tokens, grad_tokens, positions = lax.optimization_barrier((act_tokens, grad_tokens, positions))
     act_cols = lax.all_gather(act_basis, "wa", axis=1, tiled=True)
     grad_cols = lax.all_gather(grad_basis, "wa", axis=1, tiled=True)
     count = query_act.shape[0]
@@ -67,7 +68,7 @@
     grad_kept = grad_rot * query_weight[:, None]
     act_rot = natural_order(act_rot.reshape(nb, count, -1), "wb").reshape(nb * count, -1)
     grad_kept = natural_order(grad_kept.reshape(nb, count, -1), "wb").reshape(nb * count, -1)
-    grad_all = lax.all_gather(grad_kept, "wb", axis=1, tiled=True)
+    grad_all = jnp.concatenate(list(ring_gather(grad_kept, "wb")), axis=1)
     partial_rows = lax.dot_general(
         act_rot, grad_all, (((0,), (0,)), ((), ())), preferred_element_type=jnp.float32
     )
@@ -79,7 +80,9 @@
     reduced = lax.psum_scatter(
         jnp.concatenate([partial_rows, extra], axis=1), "wa", scatter_dimension=0, tiled=True
     )
-    gradient_rows = reduced[:, : partial_rows.shape[1]]
+    rows = reduced.shape[0]
+    by_shift = reduced[:, : partial_rows.shape[1]].reshape(rows, nb, na, -1).transpose(1, 0, 2, 3)
+    gradient_rows = natural_order(by_shift, "wb").transpose(1, 2, 0, 3).reshape(rows, -1)
     me = lax.axis_index("wb")
     half = train_grad_rot.shape[0] // 2
     first_rows, train_act_rot, _ = lax.optimization_barrier((train_grad_rot[:half], train_act_rot, partial_rows))
@@ -91,8 +94,6 @@
         acts_near.append(lax.ppermute(outgoing, "wb", perm=[(i, (i + shift) % nb) for i in range(nb)]))
     acts_near = jnp.stack(acts_near)
     eig_total = reduced[0, partial_rows.shape[1]]
-    rows = gradient_rows.shape[0]
-    gradient_rows = gradient_rows.reshape(rows, nb, na, -1).transpose(0, 2, 1, 3).reshape(rows, -1)
     eig_in = eig_values.shape[0] * lax.axis_size(WIDE)
     eig_out = eig_values.shape[1]
     mean_eig = eig_total / (eig_in * eig_out)

time: 284 us -> 270 us (0.951)
  waiting for transfers between devices: 184 us -> 171 us
    all_gather x1, waiting for transfers between devices: 28.6 us -> 0.01 us  [shards(): grad_cols = lax.all_gather(grad_basis, 'wa', axis=1, tiled=True)]
    ppermute x15 -> x18, waiting for transfers between devices: 77.5 us -> 105 us  [ring_gather(): lax.ppermute(x, axis, perm=[(i, (i + shift) % n) for i in range(n)])]
    all_gather x1 -> x0, waiting for transfers between devices: 11.4 us -> none  [shards(): grad_all = lax.all_gather(grad_kept, 'wb', axis=1, tiled=True)]
    another operation x3 -> x4, other arithmetic: 7.21 us -> 8.16 us  [ring_gather(): return jnp.stack(parts)]
    ppermute x15 -> x18, starting transfers between devices: 11.8 us -> 11.7 us  [ring_gather(): lax.ppermute(x, axis, perm=[(i, (i + shift) % n) for i in range(n)])]
  transfers between devices with their start and end apart: 29 -> 31, of which waited for: 14 -> 15; matrix products, arithmetic and copies ran while one was open for 10% -> 10% of each run, Pallas kernels for 0% -> 0%
where the time goes in v11:
time: 270 us; the launch traced here: 269 us
  waiting for transfers between devices  171 us (63%)
  matrix products  28.7 us (11%)
  starting transfers between devices  21.2 us (8%)
  other arithmetic  17.5 us (6%)
  between operations  17.3 us (6%)
  local copies, waits for them, and re-layouts  13.4 us (5%)
    ppermute x18, waiting for transfers between devices, ring_gather(): lax.ppermute(x, axis, perm=[(i, (i + shift) % n) for i in range(n)])  105 us
    ppermute x3, waiting for transfers between devices, shards(): lax.ppermute(outgoing, 'wb', perm=[(i, (i + shift) % nb) for i in range(n...  37.4 us
    ppermute x3, waiting for transfers between devices, shards(): lax.ppermute(eig_sum, 'wb', perm=[(i, (i + shift) % nb) for i in range(nb)])  21.2 us
    dot_general x6, matrix products, shards(): jnp.einsum('ij,sjt->sit', precond, grads_near, preferred_element_type=jnp...  18.9 us
    ppermute x18, starting transfers between devices, ring_gather(): lax.ppermute(x, axis, perm=[(i, (i + shift) % n) for i in range(n)])  11.7 us
    another operation x4, other arithmetic, ring_gather(): return jnp.stack(parts)  8.16 us
    all_gather x1, waiting for transfers between devices, shards(): rows_held = lax.all_gather(payload, 'wa', axis=0, tiled=True)  5.9 us
    dot_general x1, matrix products, shards(): jnp.dot(grad_tokens.reshape(nb * count, -1), grad_cols, preferred_element...  5.79 us
  transfers between devices with their start and end apart: 31, of which 15 were waited for; matrix products, arithmetic and copies ran while one was open for 10% of the time, Pallas kernels for 0%

profile of v11, /device:TPU:0, one launch (start us, length us, event | category | flops | bytes accessed | tf_op | source)
XLA Modules:
  0.0 269.1 jit_solution(9443623174416293903)
XLA Ops:
  6.5 0.7 all-gather.6.cloned.1.call-update
  7.3 2.5 collective-permute-start.2
  9.8 0.7 collective-permute-start.5
  10.6 1.6 collective-permute-start.8
  12.2 49.5 %collective-permute-done.8 = s32[128]{0:T(128)S(1)} collective-permute-done((s32[128]{0:T(128)}, s32[128]{0:T(128)S(1)}, u32[]{:S(2)}, u32[]{:S(2)}) %collective-permute-start.8) | collective-permute-done | bytes 544 | tf_op jit(solution)/shard_map/ppermute | solution.py:29
  61.7 0.6 collective-permute-start.7
  62.3 3.1 %collective-permute-done.7 = s32[128]{0:T(128)S(1)} collective-permute-done((s32[128]{0:T(128)}, s32[128]{0:T(128)S(1)}, u32[]{:S(2)}, u32[]{:S(2)}) %collective-permute-start.7) | collective-permute-done | bytes 544 | tf_op jit(solution)/shard_map/ppermute | solution.py:29
  65.4 0.4 collective-permute-start.6
  65.8 2.7 %collective-permute-done.6 = s32[128]{0:T(128)S(1)} collective-permute-done((s32[128]{0:T(128)}, s32[128]{0:T(128)S(1)}, u32[]{:S(2)}, u32[]{:S(2)}) %collective-permute-start.6) | collective-permute-done | bytes 544 | tf_op jit(solution)/shard_map/ppermute | solution.py:29
  68.5 0.6 collective-permute-start.1
  69.2 0.7 pad_add_fusion
  69.9 13.7 %collective-permute-done.1 = bf16[128,2048]{1,0:T(8,128)(2,1)S(1)} collective-permute-done((bf16[128,2048]{1,0:T(8,128)(2,1)}, bf16[128,2048]{1,0:T(8,128)(2,1)S(1)}, u32[]{:S(2)}, u32[]{:S(2)}) %collective-permute-start.1) | collective-permute-done | bytes 524320 | tf_op jit(solution)/shard_map/ppermute | solution.py:29
  83.6 3.1 %collective-permute-done = bf16[128,2048]{1,0:T(8,128)(2,1)S(1)} collective-permute-done((bf16[128,2048]{1,0:T(8,128)(2,1)}, bf16[128,2048]{1,0:T(8,128)(2,1)S(1)}, u32[]{:S(2)}, u32[]{:S(2)}) %collective-permute-start) | collective-permute-done | bytes 524320 | tf_op jit(solution)/shard_map/ppermute | solution.py:29
  86.7 0.8 copy-done.11
  87.5 1.9 pad_maximum_fusion.2
  89.4 3.5 %pad_maximum_fusion = bf16[4,128,4096]{2,1,0:T(8,128)(2,1)} fusion(bf16[1,128,4096]{2,1,0:T(8,128)(2,1)S(1)} %bitcast.118, bf16[1,128,4096]{2,1,0:T(8,128)(2,1)} %bitcast.6, bf16[1,128,4096]{2,1,0:T(8,128)(2,1)} %bitcast.5, bf16[1,128,4096]{2,1,0:T(8,128)(2,1)S(1)} %bitcast.117), kind=kLoop, calls=%fused_computation.13 | loop fusion | flops 6291456 | bytes 8388608 | tf_op jit(solution)/shard_map/stack | solution.py:30
  92.9 5.8 %fusion.20 = bf16[512,512]{1,0:T(8,128)(2,1)S(1)} fusion(bf16[512,4096]{1,0:T(8,128)(2,1)} %bitcast.112, bf16[4096,512]{1,0:T(8,128)(2,1)} %all-gather.6.cloned.1.call-done, bf16[512]{0:T(512)(128)(2,1)S(1)} %fusion.55), kind=kOutput, calls=%fused_computation.43 | convolution fusion | flops 2148007936 | bytes 8913920 | tf_op jit(solution)/shard_map/dot_general | solution.py:64
  99.0 0.5 collective-permute-start.11
  99.5 1.1 collective-permute-start.10
  100.7 0.7 convert_reduce_fusion
  101.5 0.9 collective-permute-start.18
  102.3 1.1 collective-permute-start.19
  103.4 21.2 %collective-permute-done.18 = f32[]{:T(128)} collective-permute-done((f32[]{:T(128)}, f32[]{:T(128)}, u32[]{:S(2)}, u32[]{:S(2)}) %collective-permute-start.18) | collective-permute-done | bytes 36 | tf_op jit(solution)/shard_map/ppermute | solution.py:78
  127.2 2.0 convolution_convert_fusion.1
  129.4 2.1 fusion.6
  131.4 1.6 concatenate.24
  133.1 1.3 copy-done.2
  134.4 1.0 fusion.57
  135.5 1.2 collective-permute-start.14
  136.6 1.0 collective-permute-start.13
  137.6 1.3 dynamic-slice_bitcast_fusion.3
  139.0 1.8 collective-permute-start.17
  140.8 1.0 collective-permute-start.16
  141.8 33.3 %collective-permute-done.17 = bf16[4,64,384]{2,1,0:T(8,128)(2,1)S(1)} collective-permute-done((bf16[4,64,384]{2,1,0:T(8,128)(2,1)S(1)}, bf16[4,64,384]{2,1,0:T(8,128)(2,1)S(1)}, u32[]{:S(2)}, u32[]{:S(2)}) %collective-permute-start.17) | collective-permute-done | bytes 196640 | tf_op jit(solution)/shard_map/ppermute | solution.py:94
  175.1 1.6 collective-permute-start.15
  176.7 2.0 collective-permute-done.16
  178.7 2.1 collective-permute-done.15
  180.8 1.0 pad_maximum_fusion.3
  181.9 0.8 copy-done.5
  183.2 2.1 pad_maximum_fusion.1
  185.4 1.1 slice.64
  186.4 0.9 reshape.52
  187.3 1.0 rev.11
  188.4 0.3 fusion.49
  188.8 0.9 convert_element_type.68
  189.7 1.9 pad_maximum_fusion.4
  191.7 1.1 collective-permute-start.22
  192.9 1.2 slice.67
  194.8 0.6 fusion.58
  195.4 14.0 %collective-permute-done.23 = bf16[1024,384]{1,0:T(8,128)(2,1)S(1)} collective-permute-done((bf16[1024,384]{1,0:T(8,128)(2,1)}, bf16[1024,384]{1,0:T(8,128)(2,1)S(1)}, u32[]{:S(2)}, u32[]{:S(2)}) %collective-permute-start.23) | collective-permute-done | bytes 786464 | tf_op jit(solution)/shard_map/ppermute | solution.py:29
  209.4 18.3 %collective-permute-done.22 = bf16[1024,384]{1,0:T(8,128)(2,1)S(1)} collective-permute-done((bf16[1024,384]{1,0:T(8,128)(2,1)}, bf16[1024,384]{1,0:T(8,128)(2,1)S(1)}, u32[]{:S(2)}, u32[]{:S(2)}) %collective-permute-start.22) | collective-permute-done | bytes 786464 | tf_op jit(solution)/shard_map/ppermute | solution.py:29
  227.7 0.5 collective-permute-done.21
  228.2 4.4 %maximum_maximum_fusion = bf16[4,2048,384]{2,1,0:T(8,128)(2,1)} fusion(bf16[1,1024,384]{2,1,0:T(8,128)(2,1)S(1)} %bitcast.122, bf16[1,1024,384]{2,1,0:T(8,128)(2,1)S(1)} %bitcast.123, bf16[1,1024,384]{2,1,0:T(8,128)(2,1)S(1)} %bitcast.124, bf16[1,1024,384]{2,1,0:T(8,128)(2,1)} %bitcast.113, bf16[4,1024,384]{2,1,0:T(8,128)(2,1)S(1)} %pad_maximum_fusion.1), kind=kLoop, calls=%fused_computation | loop fusion | flops 31457280 | bytes 12582912 | tf_op jit(solution)/shard_map/concatenate | solution.py:107
  232.6 5.9 %all-gather.8.cloned.1.call-done = bf16[256,4096]{1,0:T(8,128)(2,1)} async-done(((bf16[64,4096]{1,0:T(8,128)(2,1)}), bf16[256,4096]{1,0:T(8,128)(2,1)}) %all-gather.8.cloned.1.call-update) | async-done | bytes 2097168 | tf_op jit(solution)/shard_map/all_gather | solution.py:105
  238.5 6.4 %fusion.14 = f32[4,384]{1,0:T(4,128)S(1)} fusion(bf16[4,256,384]{2,1,0:T(8,128)(2,1)} %bitcast.126, bf16[4,2048,384]{2,1,0:T(8,128)(2,1)} %maximum_maximum_fusion, f32[]{:T(128)} %bitcast.38, bf16[256,4096]{1,0:T(8,128)(2,1)} %all-gather.8.cloned.1.call-done), kind=kOutput, calls=%fused_computation.36 | convolution fusion | flops 1614412288 | bytes 9181188 | tf_op jit(solution)/shard_map/ij,sjt->sit/dot_general | solution.py:114
  245.0 2.5 fusion.15
  247.5 2.4 fusion.16
  250.0 2.5 fusion.17
  252.5 2.5 fusion.18
  255.0 2.5 fusion.19
  257.6 1.6 collective-permute-start.25
  259.2 1.4 collective-permute-start.24
  261.4 0.6 collective-permute-done.24
  262.0 0.6 fusion.54
  (76 shorter events, 2.3 us)
Async XLA Ops:
  6.5 86.4 %all-gather.6.cloned.1.call-start = ((), (), s32[]{:S(2)}) async-start(), calls=%async_computation.2 | async-start | bytes 5242880 | tf_op jit(solution)/shard_map/all_gather | solution.py:59
  7.3 119.9 %all-gather.4.cloned.1.call-start = ((), (), s32[]{:S(2)}) async-start(), calls=%async_computation.1 | async-start | bytes 1310720 | tf_op jit(solution)/shard_map/all_gather | solution.py:58
  7.3 61.8 %collective-permute-start.2 = (bf16[128,2048]{1,0:T(8,128)(2,1)}, bf16[128,2048]{1,0:T(8,128)(2,1)S(1)}, u32[]{:S(2)}, u32[]{:S(2)}) collective-permute-start(bf16[128,2048]{1,0:T(8,128)(2,1)} %param.10), channel_id=1, source_target_pairs={{0,3},{1,0},{2,1},{3,2},{4,7},{5,4},{6,5},{7,6},{8,11},{9,8},{10,9... | collective-permute-start | bytes 1572872 | tf_op jit(solution)/shard_map/ppermute | solution.py:29
  9.8 79.6 %collective-permute-start.5 = (bf16[128,4096]{1,0:T(8,128)(2,1)}, bf16[128,4096]{1,0:T(8,128)(2,1)S(1)}, u32[]{:S(2)}, u32[]{:S(2)}) collective-permute-start(bf16[128,4096]{1,0:T(8,128)(2,1)} %param.11), channel_id=1, source_target_pairs={{0,3},{1,0},{2,1},{3,2},{4,7},{5,4},{6,5},{7,6},{8,11},{9,8},{10,9... | collective-permute-start | bytes 3145736 | tf_op jit(solution)/shard_map/ppermute | solution.py:29
  10.4 78.9 %collective-permute-start.4 = (bf16[128,4096]{1,0:T(8,128)(2,1)}, bf16[128,4096]{1,0:T(8,128)(2,1)}, u32[]{:S(2)}, u32[]{:S(2)}) collective-permute-start(bf16[128,4096]{1,0:T(8,128)(2,1)} %param.11), channel_id=1, source_target_pairs={{0,2},{1,3},{2,0},{3,1},{4,6},{5,7},{6,4},{7,5},{8,10},{9,11},{10,... | collective-permute-start | bytes 3145736 | tf_op jit(solution)/shard_map/ppermute | solution.py:29
  10.5 78.9 %collective-permute-start.3 = (bf16[128,4096]{1,0:T(8,128)(2,1)}, bf16[128,4096]{1,0:T(8,128)(2,1)}, u32[]{:S(2)}, u32[]{:S(2)}) collective-permute-start(bf16[128,4096]{1,0:T(8,128)(2,1)} %param.11), channel_id=1, source_target_pairs={{0,1},{1,2},{2,3},{3,0},{4,5},{5,6},{6,7},{7,4},{8,9},{9,10},{10,1... | collective-permute-start | bytes 3145736 | tf_op jit(solution)/shard_map/ppermute | solution.py:29
  10.6 51.1 %collective-permute-start.8 = (s32[128]{0:T(128)}, s32[128]{0:T(128)S(1)}, u32[]{:S(2)}, u32[]{:S(2)}) collective-permute-start(s32[128]{0:T(128)} %param.12), channel_id=1, source_target_pairs={{0,3},{1,0},{2,1},{3,2},{4,7},{5,4},{6,5},{7,6},{8,11},{9,8},{10,9... | collective-permute-start | bytes 1544 | tf_op jit(solution)/shard_map/ppermute | solution.py:29
  61.7 3.7 %collective-permute-start.7 = (s32[128]{0:T(128)}, s32[128]{0:T(128)S(1)}, u32[]{:S(2)}, u32[]{:S(2)}) collective-permute-start(s32[128]{0:T(128)} %param.12), channel_id=1, source_target_pairs={{0,2},{1,3},{2,0},{3,1},{4,6},{5,7},{6,4},{7,5},{8,10},{9,11},{10,... | collective-permute-start | bytes 1544 | tf_op jit(solution)/shard_map/ppermute | solution.py:29
  65.4 3.1 %collective-permute-start.6 = (s32[128]{0:T(128)}, s32[128]{0:T(128)S(1)}, u32[]{:S(2)}, u32[]{:S(2)}) collective-permute-start(s32[128]{0:T(128)} %param.12), channel_id=1, source_target_pairs={{0,1},{1,2},{2,3},{3,0},{4,5},{5,6},{6,7},{7,4},{8,9},{9,10},{10,1... | collective-permute-start | bytes 1544 | tf_op jit(solution)/shard_map/ppermute | solution.py:29
  68.5 15.1 %collective-permute-start.1 = (bf16[128,2048]{1,0:T(8,128)(2,1)}, bf16[128,2048]{1,0:T(8,128)(2,1)S(1)}, u32[]{:S(2)}, u32[]{:S(2)}) collective-permute-start(bf16[128,2048]{1,0:T(8,128)(2,1)} %param.10), channel_id=1, source_target_pairs={{0,2},{1,3},{2,0},{3,1},{4,6},{5,7},{6,4},{7,5},{8,10},{9,11},{10,... | collective-permute-start | bytes 1572872 | tf_op jit(solution)/shard_map/ppermute | solution.py:29
  69.1 17.6 %copy-start.9 = (bf16[128,2048]{1,0:T(8,128)(2,1)}, bf16[128,2048]{1,0:T(8,128)(2,1)S(1)}, u32[]{:S(2)}) copy-start(bf16[128,2048]{1,0:T(8,128)(2,1)S(1)} %collective-permute-done.2) | copy-start | bytes 1572868
  69.1 17.6 %collective-permute-start = (bf16[128,2048]{1,0:T(8,128)(2,1)}, bf16[128,2048]{1,0:T(8,128)(2,1)S(1)}, u32[]{:S(2)}, u32[]{:S(2)}) collective-permute-start(bf16[128,2048]{1,0:T(8,128)(2,1)} %param.10), channel_id=1, source_target_pairs={{0,1},{1,2},{2,3},{3,0},{4,5},{5,6},{6,7},{7,4},{8,9},{9,10},{10,1... | collective-permute-start | bytes 1572872 | tf_op jit(solution)/shard_map/ppermute | solution.py:29
  69.1 116.3 %reduce-scatter.2.cloned.1.call-start = ((), (), s32[]{:S(2)}) async-start(), calls=%async_computation.3 | async-start | bytes 2785280 | tf_op jit(solution)/shard_map/reduce_scatter | solution.py:80
  83.6 3.1 %copy-start.10 = (bf16[128,2048]{1,0:T(8,128)(2,1)}, bf16[128,2048]{1,0:T(8,128)(2,1)S(1)}, u32[]{:S(2)}) copy-start(bf16[128,2048]{1,0:T(8,128)(2,1)S(1)} %collective-permute-done.1) | copy-start | bytes 1572868
  86.7 0.8 copy-start.11
  87.5 1.9 copy-start.4
  98.7 2.0 copy-start.3
  99.0 30.3 %collective-permute-start.11 = (bf16[512,512]{1,0:T(8,128)(2,1)S(1)}, bf16[512,512]{1,0:T(8,128)(2,1)}, u32[]{:S(2)}, u32[]{:S(2)}) collective-permute-start(bf16[512,512]{1,0:T(8,128)(2,1)S(1)} %bitcast.133), channel_id=1, source_target_pairs={{0,3},{1,0},{2,1},{3,2},{4,7},{5,4},{6,5},{7,6},{8,11},{9,8},{10,9... | collective-permute-start | bytes 1572872 | tf_op jit(solution)/shard_map/ppermute | solution.py:29
  99.5 29.9 %collective-permute-start.10 = (bf16[512,512]{1,0:T(8,128)(2,1)S(1)}, bf16[512,512]{1,0:T(8,128)(2,1)}, u32[]{:S(2)}, u32[]{:S(2)}) collective-permute-start(bf16[512,512]{1,0:T(8,128)(2,1)S(1)} %bitcast.134), channel_id=1, source_target_pairs={{0,2},{1,3},{2,0},{3,1},{4,6},{5,7},{6,4},{7,5},{8,10},{9,11},{10,... | collective-permute-start | bytes 1572872 | tf_op jit(solution)/shard_map/ppermute | solution.py:29
  100.6 28.8 %collective-permute-start.9 = (bf16[512,512]{1,0:T(8,128)(2,1)S(1)}, bf16[512,512]{1,0:T(8,128)(2,1)}, u32[]{:S(2)}, u32[]{:S(2)}) collective-permute-start(bf16[512,512]{1,0:T(8,128)(2,1)S(1)} %bitcast.135), channel_id=1, source_target_pairs={{0,1},{1,2},{2,3},{3,0},{4,5},{5,6},{6,7},{7,4},{8,9},{9,10},{10,1... | collective-permute-start | bytes 1572872 | tf_op jit(solution)/shard_map/ppermute | solution.py:29
  101.5 23.2 %collective-permute-start.18 = (f32[]{:T(128)}, f32[]{:T(128)}, u32[]{:S(2)}, u32[]{:S(2)}) collective-permute-start(f32[]{:T(128)} %convert_reduce_fusion), channel_id=1, source_target_pairs={{0,1},{1,2},{2,3},{3,0},{4,5},{5,6},{6,7},{7,4},{8,9},{9,10},{10,1... | collective-permute-start | bytes 20 | tf_op jit(solution)/shard_map/ppermute | solution.py:78
  102.3 23.6 %collective-permute-start.19 = (f32[]{:T(128)}, f32[]{:T(128)}, u32[]{:S(2)}, u32[]{:S(2)}) collective-permute-start(f32[]{:T(128)} %convert_reduce_fusion), channel_id=1, source_target_pairs={{0,2},{1,3},{2,0},{3,1},{4,6},{5,7},{6,4},{7,5},{8,10},{9,11},{10,... | collective-permute-start | bytes 20 | tf_op jit(solution)/shard_map/ppermute | solution.py:78
  124.7 1.9 collective-permute-start.20
  133.0 1.4 copy-start.2
  133.0 105.4 %all-gather.8.cloned.1.call-start = ((), (), s32[]{:S(2)}) async-start(), calls=%async_computation.4 | async-start | bytes 2621440 | tf_op jit(solution)/shard_map/all_gather | solution.py:105
  135.5 46.4 %copy-start.1 = (bf16[1024,384]{1,0:T(8,128)(2,1)}, bf16[1024,384]{1,0:T(8,128)(2,1)S(1)}, u32[]{:S(2)}) copy-start(bf16[1024,384]{1,0:T(8,128)(2,1)S(1)} %get-tuple-element.17) | copy-start | bytes 2359300
  135.5 46.4 %collective-permute-start.14 = (bf16[1024,384]{1,0:T(8,128)(2,1)S(1)}, bf16[1024,384]{1,0:T(8,128)(2,1)S(1)}, u32[]{:S(2)}, u32[]{:S(2)}) collective-permute-start(bf16[1024,384]{1,0:T(8,128)(2,1)S(1)} %get-tuple-element.17), channel_id=1, source_target_pairs={{0,3},{1,0},{2,1},{3,2},{4,7},{5,4},{6,5},{7,6},{8,11},{9,8},{10,9... | collective-permute-start | bytes 2359304 | tf_op jit(solution)/shard_map/ppermute | solution.py:29
  136.6 45.2 %collective-permute-start.13 = (bf16[1024,384]{1,0:T(8,128)(2,1)S(1)}, bf16[1024,384]{1,0:T(8,128)(2,1)S(1)}, u32[]{:S(2)}, u32[]{:S(2)}) collective-permute-start(bf16[1024,384]{1,0:T(8,128)(2,1)S(1)} %get-tuple-element.17), channel_id=1, source_target_pairs={{0,2},{1,3},{2,0},{3,1},{4,6},{5,7},{6,4},{7,5},{8,10},{9,11},{10,... | collective-permute-start | bytes 2359304 | tf_op jit(solution)/shard_map/ppermute | solution.py:29
  137.6 44.2 %collective-permute-start.12 = (bf16[1024,384]{1,0:T(8,128)(2,1)S(1)}, bf16[1024,384]{1,0:T(8,128)(2,1)S(1)}, u32[]{:S(2)}, u32[]{:S(2)}) collective-permute-start(bf16[1024,384]{1,0:T(8,128)(2,1)S(1)} %get-tuple-element.17), channel_id=1, source_target_pairs={{0,1},{1,2},{2,3},{3,0},{4,5},{5,6},{6,7},{7,4},{8,9},{9,10},{10,1... | collective-permute-start | bytes 2359304 | tf_op jit(solution)/shard_map/ppermute | solution.py:29
  139.0 36.1 %collective-permute-start.17 = (bf16[4,64,384]{2,1,0:T(8,128)(2,1)S(1)}, bf16[4,64,384]{2,1,0:T(8,128)(2,1)S(1)}, u32[]{:S(2)}, u32[]{:S(2)}) collective-permute-start(bf16[4,64,384]{2,1,0:T(8,128)(2,1)S(1)} %get-tuple-element.26), channel_id=1, source_target_pairs={{0,3},{1,0},{2,1},{3,2},{4,7},{5,4},{6,5},{7,6},{8,11},{9,8},{10,9... | collective-permute-start | bytes 589832 | tf_op jit(solution)/shard_map/ppermute | solution.py:94
  140.8 37.9 %collective-permute-start.16 = (bf16[4,64,384]{2,1,0:T(8,128)(2,1)S(1)}, bf16[4,64,384]{2,1,0:T(8,128)(2,1)S(1)}, u32[]{:S(2)}, u32[]{:S(2)}) collective-permute-start(bf16[4,64,384]{2,1,0:T(8,128)(2,1)S(1)} %get-tuple-element.27), channel_id=1, source_target_pairs={{0,2},{1,3},{2,0},{3,1},{4,6},{5,7},{6,4},{7,5},{8,10},{9,11},{10,... | collective-permute-start | bytes 589832 | tf_op jit(solution)/shard_map/ppermute | solution.py:94
  175.1 5.7 %collective-permute-start.15 = (bf16[4,64,384]{2,1,0:T(8,128)(2,1)S(1)}, bf16[4,64,384]{2,1,0:T(8,128)(2,1)S(1)}, u32[]{:S(2)}, u32[]{:S(2)}) collective-permute-start(bf16[4,64,384]{2,1,0:T(8,128)(2,1)S(1)} %get-tuple-element.28), channel_id=1, source_target_pairs={{0,1},{1,2},{2,3},{3,0},{4,5},{5,6},{6,7},{7,4},{8,9},{9,10},{10,1... | collective-permute-start | bytes 589832 | tf_op jit(solution)/shard_map/ppermute | solution.py:94
  181.8 0.9 copy-start.5
  181.8 1.2 copy-start.6
  181.9 1.4 copy-start.7
  186.4 8.3 %copy-start.14 = (s32[6]{0:T(128)S(1)}, s32[6]{0:T(128)}, u32[]{:S(2)}) copy-start(s32[6]{0:T(128)} %param.16) | copy-start | bytes 76
  191.6 17.8 %collective-permute-start.23 = (bf16[1024,384]{1,0:T(8,128)(2,1)}, bf16[1024,384]{1,0:T(8,128)(2,1)S(1)}, u32[]{:S(2)}, u32[]{:S(2)}) collective-permute-start(bf16[1024,384]{1,0:T(8,128)(2,1)} %get-tuple-element.21), channel_id=1, source_target_pairs={{0,3},{1,0},{2,1},{3,2},{4,7},{5,4},{6,5},{7,6},{8,11},{9,8},{10,9... | collective-permute-start | bytes 2359304 | tf_op jit(solution)/shard_map/ppermute | solution.py:29
  191.7 36.0 %collective-permute-start.22 = (bf16[1024,384]{1,0:T(8,128)(2,1)}, bf16[1024,384]{1,0:T(8,128)(2,1)S(1)}, u32[]{:S(2)}, u32[]{:S(2)}) collective-permute-start(bf16[1024,384]{1,0:T(8,128)(2,1)} %get-tuple-element.21), channel_id=1, source_target_pairs={{0,2},{1,3},{2,0},{3,1},{4,6},{5,7},{6,4},{7,5},{8,10},{9,11},{10,... | collective-permute-start | bytes 2359304 | tf_op jit(solution)/shard_map/ppermute | solution.py:29
  192.8 35.4 %collective-permute-start.21 = (bf16[1024,384]{1,0:T(8,128)(2,1)}, bf16[1024,384]{1,0:T(8,128)(2,1)S(1)}, u32[]{:S(2)}, u32[]{:S(2)}) collective-permute-start(bf16[1024,384]{1,0:T(8,128)(2,1)} %get-tuple-element.21), channel_id=1, source_target_pairs={{0,1},{1,2},{2,3},{3,0},{4,5},{5,6},{6,7},{7,4},{8,9},{9,10},{10,1... | collective-permute-start | bytes 2359304 | tf_op jit(solution)/shard_map/ppermute | solution.py:29
  238.5 6.5 %copy-start = (bf16[4,2048,384]{2,1,0:T(8,128)(2,1)S(1)}, bf16[4,2048,384]{2,1,0:T(8,128)(2,1)}, u32[]{:S(2)}) copy-start(bf16[4,2048,384]{2,1,0:T(8,128)(2,1)} %maximum_maximum_fusion) | copy-start | bytes 18874372
  238.5 6.5 %copy-start.8 = (bf16[4,4,64,384]{3,2,1,0:T(8,128)(2,1)S(1)}, bf16[4,4,64,384]{3,2,1,0:T(8,128)(2,1)}, u32[]{:S(2)}) copy-start(bf16[4,4,64,384]{3,2,1,0:T(8,128)(2,1)} %pad_maximum_fusion.3) | copy-start | bytes 2359300
  238.5 6.5 %copy-start.13 = (bf16[256,4096]{1,0:T(8,128)(2,1)S(1)}, bf16[256,4096]{1,0:T(8,128)(2,1)}, u32[]{:S(2)}) copy-start(bf16[256,4096]{1,0:T(8,128)(2,1)} %all-gather.8.cloned.1.call-done) | copy-start | bytes 6291460
  255.0 5.6 %copy-start.12 = (s32[384]{0:T(512)S(1)}, s32[384]{0:T(512)}, u32[]{:S(2)}) copy-start(s32[384]{0:T(512)} %param.19) | copy-start | bytes 4612
  257.6 3.7 %collective-permute-start.26 = (f32[6,384]{1,0:T(8,128)S(1)}, f32[6,384]{1,0:T(8,128)S(1)}, u32[]{:S(2)}, u32[]{:S(2)}) collective-permute-start(f32[6,384]{1,0:T(8,128)S(1)} %get-tuple-element.30), channel_id=1, source_target_pairs={{0,1},{1,2},{2,3},{3,0},{4,5},{5,6},{6,7},{7,4},{8,9},{9,10},{10,1... | collective-permute-start | bytes 27656 | tf_op jit(solution)/shard_map/ppermute | solution.py:119
  257.6 3.8 %collective-permute-start.25 = (f32[6,384]{1,0:T(8,128)S(1)}, f32[6,384]{1,0:T(8,128)S(1)}, u32[]{:S(2)}, u32[]{:S(2)}) collective-permute-start(f32[6,384]{1,0:T(8,128)S(1)} %get-tuple-element.31), channel_id=1, source_target_pairs={{0,2},{1,3},{2,0},{3,1},{4,6},{5,7},{6,4},{7,5},{8,10},{9,11},{10,... | collective-permute-start | bytes 27656 | tf_op jit(solution)/shard_map/ppermute | solution.py:119
  259.2 2.8 %collective-permute-start.24 = (f32[6,384]{1,0:T(8,128)S(1)}, f32[6,384]{1,0:T(8,128)S(1)}, u32[]{:S(2)}, u32[]{:S(2)}) collective-permute-start(f32[6,384]{1,0:T(8,128)S(1)} %get-tuple-element.29), channel_id=1, source_target_pairs={{0,3},{1,0},{2,1},{3,2},{4,7},{5,4},{6,5},{7,6},{8,11},{9,8},{10,9... | collective-permute-start | bytes 27656 | tf_op jit(solution)/shard_map/ppermute | solution.py:119
Sparse Core Ops, SparseCore 0:
  8.9 83.2 all-gather.5
  93.8 26.1 all-gather.3
  133.2 46.9 reduce-scatter.1
  191.7 46.6 all-gather.7

commit v12 on v11

--- a/solution.py
+++ b/solution.py
@@ -54,7 +54,13 @@
     act_tokens = ring_gather(query_act, "wb")
     grad_tokens = ring_gather(query_grad, "wb")
     positions = ring_gather(query_positions, "wb")
-    act_tokens, grad_tokens, positions = lax.optimization_barrier((act_tokens, grad_tokens, positions))
+    eig_sum = jnp.sum(eig_values.astype(jnp.float32))
+    group_sum = eig_sum
+    for shift in range(1, nb):
+        group_sum = group_sum + lax.ppermute(eig_sum, "wb", perm=[(i, (i + shift) % nb) for i in range(nb)])
+    act_tokens, grad_tokens, positions, group_sum = lax.optimization_barrier(
+        (act_tokens, grad_tokens, positions, group_sum)
+    )
     act_cols = lax.all_gather(act_basis, "wa", axis=1, tiled=True)
     grad_cols = lax.all_gather(grad_basis, "wa", axis=1, tiled=True)
     count = query_act.shape[0]
@@ -72,10 +78,6 @@
     partial_rows = lax.dot_general(
         act_rot, grad_all, (((0,), (0,)), ((), ())), preferred_element_type=jnp.float32
     )
-    eig_sum = jnp.sum(eig_values.astype(jnp.float32))
-    group_sum = eig_sum
-    for shift in range(1, nb):
-        group_sum = group_sum + lax.ppermute(eig_sum, "wb", perm=[(i, (i + shift) % nb) for i in range(nb)])
     extra = jnp.broadcast_to(group_sum, (partial_rows.shape[0], 128))
     reduced = lax.psum_scatter(
         jnp.concatenate([partial_rows, extra], axis=1), "wa", scatter_dimension=0, tiled=True

time: 270 us -> 271 us (level)
  waiting for transfers between devices: 171 us -> 168 us
    ppermute x18, waiting for transfers between devices: 105 us -> 61.2 us  [ring_gather(): lax.ppermute(x, axis, perm=[(i, (i + shift) % n) for i in range(n)])]
    ppermute x3, waiting for transfers between devices: 21.2 us -> 49.3 us  [shards(): lax.ppermute(eig_sum, 'wb', perm=[(i, (i + shift) % nb) for i in range(nb)])]
    all_gather x1, waiting for transfers between devices: 0.02 us -> 13.1 us  [shards(): act_cols = lax.all_gather(act_basis, 'wa', axis=1, tiled=True)]
  transfers between devices with their start and end apart: 31 -> 31, of which waited for: 15 -> 20; matrix products, arithmetic and copies ran while one was open for 10% -> 10% of each run, Pallas kernels for 0% -> 0%
where the time goes in v12:
time: 271 us; the launch traced here: 270 us
  waiting for transfers between devices  168 us (62%)
  matrix products  28.8 us (11%)
  starting transfers between devices  23.6 us (9%)
  other arithmetic  18.5 us (7%)
  between operations  17.4 us (6%)
  local copies, waits for them, and re-layouts  13.4 us (5%)
    ppermute x18, waiting for transfers between devices, ring_gather(): lax.ppermute(x, axis, perm=[(i, (i + shift) % n) for i in range(n)])  61.2 us
    ppermute x3, waiting for transfers between devices, shards(): lax.ppermute(eig_sum, 'wb', perm=[(i, (i + shift) % nb) for i in range(nb)])  49.3 us
    ppermute x3, waiting for transfers between devices, shards(): lax.ppermute(outgoing, 'wb', perm=[(i, (i + shift) % nb) for i in range(n...  37.3 us
    dot_general x6, matrix products, shards(): jnp.einsum('ij,sjt->sit', precond, grads_near, preferred_element_type=jnp...  18.9 us
    all_gather x1, waiting for transfers between devices, shards(): act_cols = lax.all_gather(act_basis, 'wa', axis=1, tiled=True)  13.1 us
    ppermute x18, starting transfers between devices, ring_gather(): lax.ppermute(x, axis, perm=[(i, (i + shift) % n) for i in range(n)])  13 us
    another operation x4, other arithmetic, ring_gather(): return jnp.stack(parts)  8.17 us
    all_gather x1, waiting for transfers between devices, shards(): rows_held = lax.all_gather(payload, 'wa', axis=0, tiled=True)  5.98 us
  transfers between devices with their start and end apart: 31, of which 20 were waited for; matrix products, arithmetic and copies ran while one was open for 10% of the time, Pallas kernels for 0%

profile of v12, /device:TPU:0, one launch (start us, length us, event | category | flops | bytes accessed | tf_op | source)
XLA Modules:
  0.0 270.0 jit_solution(3555823519522936605)
XLA Ops:
  6.5 0.7 all-gather.6.cloned.1.call-update
  7.3 2.5 collective-permute-start.2
  9.8 0.7 collective-permute-start.5
  10.6 1.7 convert_reduce_fusion
  12.3 1.9 collective-permute-start.9
  14.3 43.8 %collective-permute-done.9 = f32[]{:T(128)} collective-permute-done((f32[]{:T(128)}, f32[]{:T(128)}, u32[]{:S(2)}, u32[]{:S(2)}) %collective-permute-start.9) | collective-permute-done | bytes 36 | tf_op jit(solution)/shard_map/ppermute | solution.py:60
  58.1 0.6 collective-permute-start.10
  58.8 4.1 %collective-permute-done.10 = f32[]{:T(128)} collective-permute-done((f32[]{:T(128)}, f32[]{:T(128)}, u32[]{:S(2)}, u32[]{:S(2)}) %collective-permute-start.10) | collective-permute-done | bytes 36 | tf_op jit(solution)/shard_map/ppermute | solution.py:60
  62.8 1.4 collective-permute-done.11
  64.2 2.1 collective-permute-start.8
  66.3 1.4 collective-permute-done.8
  67.7 1.5 collective-permute-start.7
  69.2 2.2 collective-permute-done.7
  71.4 1.1 collective-permute-start.6
  72.6 2.0 collective-permute-done.6
  74.5 1.5 collective-permute-start.1
  78.6 0.7 pad_add_fusion
  79.3 10.3 %collective-permute-done.1 = bf16[128,2048]{1,0:T(8,128)(2,1)S(1)} collective-permute-done((bf16[128,2048]{1,0:T(8,128)(2,1)}, bf16[128,2048]{1,0:T(8,128)(2,1)S(1)}, u32[]{:S(2)}, u32[]{:S(2)}) %collective-permute-start.1) | collective-permute-done | bytes 524320 | tf_op jit(solution)/shard_map/ppermute | solution.py:29
  89.6 3.9 %collective-permute-done = bf16[128,2048]{1,0:T(8,128)(2,1)S(1)} collective-permute-done((bf16[128,2048]{1,0:T(8,128)(2,1)}, bf16[128,2048]{1,0:T(8,128)(2,1)S(1)}, u32[]{:S(2)}, u32[]{:S(2)}) %collective-permute-start) | collective-permute-done | bytes 524320 | tf_op jit(solution)/shard_map/ppermute | solution.py:29
  93.5 0.8 copy-done.10
  94.3 1.9 pad_maximum_fusion.2
  96.2 3.6 %pad_maximum_fusion = bf16[4,128,4096]{2,1,0:T(8,128)(2,1)} fusion(bf16[1,128,4096]{2,1,0:T(8,128)(2,1)S(1)} %bitcast.118, bf16[1,128,4096]{2,1,0:T(8,128)(2,1)} %bitcast.6, bf16[1,128,4096]{2,1,0:T(8,128)(2,1)} %bitcast.5, bf16[1,128,4096]{2,1,0:T(8,128)(2,1)S(1)} %bitcast.117), kind=kLoop, calls=%fused_computation.13 | loop fusion | flops 6291456 | bytes 8388608 | tf_op jit(solution)/shard_map/stack | solution.py:30
  99.8 5.8 %fusion.20 = bf16[512,512]{1,0:T(8,128)(2,1)S(1)} fusion(bf16[512,4096]{1,0:T(8,128)(2,1)} %bitcast.112, bf16[4096,512]{1,0:T(8,128)(2,1)} %all-gather.6.cloned.1.call-done, bf16[512]{0:T(512)(128)(2,1)S(1)} %fusion.55), kind=kOutput, calls=%fused_computation.43 | convolution fusion | flops 2148007936 | bytes 8913920 | tf_op jit(solution)/shard_map/dot_general | solution.py:70
  105.9 0.8 collective-permute-start.13
  106.9 13.1 %all-gather.4.cloned.1.call-done = bf16[2048,256]{0,1:T(8,128)(2,1)} async-done(((bf16[2048,64]{0,1:T(8,128)(2,1)}), bf16[2048,256]{0,1:T(8,128)(2,1)}) %all-gather.4.cloned.1.call-update) | async-done | bytes 1048592 | tf_op jit(solution)/shard_map/all_gather | solution.py:64
  119.9 2.0 convolution_convert_fusion.1
  122.1 7.8 %collective-permute-done.13 = bf16[512,512]{1,0:T(8,128)(2,1)} collective-permute-done((bf16[512,512]{1,0:T(8,128)(2,1)S(1)}, bf16[512,512]{1,0:T(8,128)(2,1)}, u32[]{:S(2)}, u32[]{:S(2)}) %collective-permute-start.13) | collective-permute-done | bytes 524320 | tf_op jit(solution)/shard_map/ppermute | solution.py:29
  129.9 0.8 collective-permute-done.12
  130.7 2.1 fusion.6
  132.8 1.6 concatenate.24
  134.5 1.3 copy-done.2
  135.8 1.0 fusion.57
  136.8 1.3 collective-permute-start.16
  138.4 1.3 dynamic-slice_bitcast_fusion.3
  139.7 1.6 collective-permute-start.20
  141.3 0.7 collective-permute-start.19
  142.0 33.0 %collective-permute-done.20 = bf16[4,64,384]{2,1,0:T(8,128)(2,1)S(1)} collective-permute-done((bf16[4,64,384]{2,1,0:T(8,128)(2,1)S(1)}, bf16[4,64,384]{2,1,0:T(8,128)(2,1)S(1)}, u32[]{:S(2)}, u32[]{:S(2)}) %collective-permute-start.20) | collective-permute-done | bytes 196640 | tf_op jit(solution)/shard_map/ppermute | solution.py:96
  175.0 2.6 collective-permute-start.18
  177.6 3.2 %collective-permute-done.19 = bf16[4,64,384]{2,1,0:T(8,128)(2,1)S(1)} collective-permute-done((bf16[4,64,384]{2,1,0:T(8,128)(2,1)S(1)}, bf16[4,64,384]{2,1,0:T(8,128)(2,1)S(1)}, u32[]{:S(2)}, u32[]{:S(2)}) %collective-permute-start.19) | collective-permute-done | bytes 196640 | tf_op jit(solution)/shard_map/ppermute | solution.py:96
  180.8 1.0 collective-permute-done.18
  181.8 1.1 pad_maximum_fusion.3
  182.9 0.8 copy-done.4
  184.3 2.1 pad_maximum_fusion.1
  186.4 1.1 slice.64
  187.5 0.9 reshape.52
  188.4 1.0 rev.11
  189.9 0.9 convert_element_type.68
  190.8 1.9 pad_maximum_fusion.4
  192.7 0.8 collective-permute-start.22
  193.7 1.2 slice.67
  195.6 0.7 fusion.58
  196.2 14.5 %collective-permute-done.23 = bf16[1024,384]{1,0:T(8,128)(2,1)S(1)} collective-permute-done((bf16[1024,384]{1,0:T(8,128)(2,1)}, bf16[1024,384]{1,0:T(8,128)(2,1)S(1)}, u32[]{:S(2)}, u32[]{:S(2)}) %collective-permute-start.23) | collective-permute-done | bytes 786464 | tf_op jit(solution)/shard_map/ppermute | solution.py:29
  210.7 17.4 %collective-permute-done.22 = bf16[1024,384]{1,0:T(8,128)(2,1)S(1)} collective-permute-done((bf16[1024,384]{1,0:T(8,128)(2,1)}, bf16[1024,384]{1,0:T(8,128)(2,1)S(1)}, u32[]{:S(2)}, u32[]{:S(2)}) %collective-permute-start.22) | collective-permute-done | bytes 786464 | tf_op jit(solution)/shard_map/ppermute | solution.py:29
  228.1 0.8 collective-permute-done.21
  228.9 4.4 %maximum_maximum_fusion = bf16[4,2048,384]{2,1,0:T(8,128)(2,1)} fusion(bf16[1,1024,384]{2,1,0:T(8,128)(2,1)S(1)} %bitcast.122, bf16[1,1024,384]{2,1,0:T(8,128)(2,1)S(1)} %bitcast.123, bf16[1,1024,384]{2,1,0:T(8,128)(2,1)S(1)} %bitcast.124, bf16[1,1024,384]{2,1,0:T(8,128)(2,1)} %bitcast.113, bf16[4,1024,384]{2,1,0:T(8,128)(2,1)S(1)} %pad_maximum_fusion.1), kind=kLoop, calls=%fused_computation | loop fusion | flops 31457280 | bytes 12582912 | tf_op jit(solution)/shard_map/concatenate | solution.py:109
  233.3 6.0 %all-gather.8.cloned.1.call-done = bf16[256,4096]{1,0:T(8,128)(2,1)} async-done(((bf16[64,4096]{1,0:T(8,128)(2,1)}), bf16[256,4096]{1,0:T(8,128)(2,1)}) %all-gather.8.cloned.1.call-update) | async-done | bytes 2097168 | tf_op jit(solution)/shard_map/all_gather | solution.py:107
  239.3 6.5 %fusion.14 = f32[4,384]{1,0:T(4,128)S(1)} fusion(bf16[4,256,384]{2,1,0:T(8,128)(2,1)} %bitcast.126, bf16[4,2048,384]{2,1,0:T(8,128)(2,1)} %maximum_maximum_fusion, f32[]{:T(128)} %bitcast.38, bf16[256,4096]{1,0:T(8,128)(2,1)} %all-gather.8.cloned.1.call-done), kind=kOutput, calls=%fused_computation.36 | convolution fusion | flops 1614412288 | bytes 9181188 | tf_op jit(solution)/shard_map/ij,sjt->sit/dot_general | solution.py:116
  245.8 2.4 fusion.15
  248.3 2.5 fusion.16
  250.8 2.5 fusion.17
  253.3 2.5 fusion.18
  255.8 2.6 fusion.19
  258.6 1.5 collective-permute-start.25
  260.1 1.4 collective-permute-start.24
  (74 shorter events, 4.0 us)
Async XLA Ops:
  6.5 93.3 %all-gather.6.cloned.1.call-start = ((), (), s32[]{:S(2)}) async-start(), calls=%async_computation.2 | async-start | bytes 5242880 | tf_op jit(solution)/shard_map/all_gather | solution.py:65
  7.3 112.7 %all-gather.4.cloned.1.call-start = ((), (), s32[]{:S(2)}) async-start(), calls=%async_computation.1 | async-start | bytes 1310720 | tf_op jit(solution)/shard_map/all_gather | solution.py:64
  7.3 68.7 %collective-permute-start.2 = (bf16[128,2048]{1,0:T(8,128)(2,1)}, bf16[128,2048]{1,0:T(8,128)(2,1)S(1)}, u32[]{:S(2)}, u32[]{:S(2)}) collective-permute-start(bf16[128,2048]{1,0:T(8,128)(2,1)} %param.10), channel_id=1, source_target_pairs={{0,3},{1,0},{2,1},{3,2},{4,7},{5,4},{6,5},{7,6},{8,11},{9,8},{10,9... | collective-permute-start | bytes 1572872 | tf_op jit(solution)/shard_map/ppermute | solution.py:29
  9.8 86.4 %collective-permute-start.5 = (bf16[128,4096]{1,0:T(8,128)(2,1)}, bf16[128,4096]{1,0:T(8,128)(2,1)S(1)}, u32[]{:S(2)}, u32[]{:S(2)}) collective-permute-start(bf16[128,4096]{1,0:T(8,128)(2,1)} %param.11), channel_id=1, source_target_pairs={{0,3},{1,0},{2,1},{3,2},{4,7},{5,4},{6,5},{7,6},{8,11},{9,8},{10,9... | collective-permute-start | bytes 3145736 | tf_op jit(solution)/shard_map/ppermute | solution.py:29
  10.4 85.8 %collective-permute-start.4 = (bf16[128,4096]{1,0:T(8,128)(2,1)}, bf16[128,4096]{1,0:T(8,128)(2,1)}, u32[]{:S(2)}, u32[]{:S(2)}) collective-permute-start(bf16[128,4096]{1,0:T(8,128)(2,1)} %param.11), channel_id=1, source_target_pairs={{0,2},{1,3},{2,0},{3,1},{4,6},{5,7},{6,4},{7,5},{8,10},{9,11},{10,... | collective-permute-start | bytes 3145736 | tf_op jit(solution)/shard_map/ppermute | solution.py:29
  10.5 85.7 %collective-permute-start.3 = (bf16[128,4096]{1,0:T(8,128)(2,1)}, bf16[128,4096]{1,0:T(8,128)(2,1)}, u32[]{:S(2)}, u32[]{:S(2)}) collective-permute-start(bf16[128,4096]{1,0:T(8,128)(2,1)} %param.11), channel_id=1, source_target_pairs={{0,1},{1,2},{2,3},{3,0},{4,5},{5,6},{6,7},{7,4},{8,9},{9,10},{10,1... | collective-permute-start | bytes 3145736 | tf_op jit(solution)/shard_map/ppermute | solution.py:29
  12.3 45.8 %collective-permute-start.9 = (f32[]{:T(128)}, f32[]{:T(128)}, u32[]{:S(2)}, u32[]{:S(2)}) collective-permute-start(f32[]{:T(128)} %convert_reduce_fusion), channel_id=1, source_target_pairs={{0,1},{1,2},{2,3},{3,0},{4,5},{5,6},{6,7},{7,4},{8,9},{9,10},{10,1... | collective-permute-start | bytes 20 | tf_op jit(solution)/shard_map/ppermute | solution.py:60
  58.1 4.7 %collective-permute-start.10 = (f32[]{:T(128)}, f32[]{:T(128)}, u32[]{:S(2)}, u32[]{:S(2)}) collective-permute-start(f32[]{:T(128)} %convert_reduce_fusion), channel_id=1, source_target_pairs={{0,2},{1,3},{2,0},{3,1},{4,6},{5,7},{6,4},{7,5},{8,10},{9,11},{10,... | collective-permute-start | bytes 20 | tf_op jit(solution)/shard_map/ppermute | solution.py:60
  62.8 1.4 collective-permute-start.11
  64.2 3.5 %collective-permute-start.8 = (s32[128]{0:T(128)}, s32[128]{0:T(128)S(1)}, u32[]{:S(2)}, u32[]{:S(2)}) collective-permute-start(s32[128]{0:T(128)} %param.12), channel_id=1, source_target_pairs={{0,3},{1,0},{2,1},{3,2},{4,7},{5,4},{6,5},{7,6},{8,11},{9,8},{10,9... | collective-permute-start | bytes 1544 | tf_op jit(solution)/shard_map/ppermute | solution.py:29
  67.7 3.7 %collective-permute-start.7 = (s32[128]{0:T(128)}, s32[128]{0:T(128)S(1)}, u32[]{:S(2)}, u32[]{:S(2)}) collective-permute-start(s32[128]{0:T(128)} %param.12), channel_id=1, source_target_pairs={{0,2},{1,3},{2,0},{3,1},{4,6},{5,7},{6,4},{7,5},{8,10},{9,11},{10,... | collective-permute-start | bytes 1544 | tf_op jit(solution)/shard_map/ppermute | solution.py:29
  71.4 3.1 %collective-permute-start.6 = (s32[128]{0:T(128)}, s32[128]{0:T(128)S(1)}, u32[]{:S(2)}, u32[]{:S(2)}) collective-permute-start(s32[128]{0:T(128)} %param.12), channel_id=1, source_target_pairs={{0,1},{1,2},{2,3},{3,0},{4,5},{5,6},{6,7},{7,4},{8,9},{9,10},{10,1... | collective-permute-start | bytes 1544 | tf_op jit(solution)/shard_map/ppermute | solution.py:29
  74.5 15.1 %collective-permute-start.1 = (bf16[128,2048]{1,0:T(8,128)(2,1)}, bf16[128,2048]{1,0:T(8,128)(2,1)S(1)}, u32[]{:S(2)}, u32[]{:S(2)}) collective-permute-start(bf16[128,2048]{1,0:T(8,128)(2,1)} %param.10), channel_id=1, source_target_pairs={{0,2},{1,3},{2,0},{3,1},{4,6},{5,7},{6,4},{7,5},{8,10},{9,11},{10,... | collective-permute-start | bytes 1572872 | tf_op jit(solution)/shard_map/ppermute | solution.py:29
  76.0 17.5 %copy-start.8 = (bf16[128,2048]{1,0:T(8,128)(2,1)}, bf16[128,2048]{1,0:T(8,128)(2,1)S(1)}, u32[]{:S(2)}) copy-start(bf16[128,2048]{1,0:T(8,128)(2,1)S(1)} %collective-permute-done.2) | copy-start | bytes 1572868
  76.0 17.5 %collective-permute-start = (bf16[128,2048]{1,0:T(8,128)(2,1)}, bf16[128,2048]{1,0:T(8,128)(2,1)S(1)}, u32[]{:S(2)}, u32[]{:S(2)}) collective-permute-start(bf16[128,2048]{1,0:T(8,128)(2,1)} %param.10), channel_id=1, source_target_pairs={{0,1},{1,2},{2,3},{3,0},{4,5},{5,6},{6,7},{7,4},{8,9},{9,10},{10,1... | collective-permute-start | bytes 1572872 | tf_op jit(solution)/shard_map/ppermute | solution.py:29
  76.0 110.4 %reduce-scatter.2.cloned.1.call-start = ((), (), s32[]{:S(2)}) async-start(), calls=%async_computation.3 | async-start | bytes 2785280 | tf_op jit(solution)/shard_map/reduce_scatter | solution.py:82
  89.6 3.9 %copy-start.9 = (bf16[128,2048]{1,0:T(8,128)(2,1)}, bf16[128,2048]{1,0:T(8,128)(2,1)S(1)}, u32[]{:S(2)}) copy-start(bf16[128,2048]{1,0:T(8,128)(2,1)S(1)} %collective-permute-done.1) | copy-start | bytes 1572868
  93.5 0.8 copy-start.10
  94.3 1.9 copy-start.3
  105.9 16.2 %collective-permute-start.14 = (bf16[512,512]{1,0:T(8,128)(2,1)S(1)}, bf16[512,512]{1,0:T(8,128)(2,1)}, u32[]{:S(2)}, u32[]{:S(2)}) collective-permute-start(bf16[512,512]{1,0:T(8,128)(2,1)S(1)} %bitcast.133), channel_id=1, source_target_pairs={{0,3},{1,0},{2,1},{3,2},{4,7},{5,4},{6,5},{7,6},{8,11},{9,8},{10,9... | collective-permute-start | bytes 1572872 | tf_op jit(solution)/shard_map/ppermute | solution.py:29
  105.9 24.0 %collective-permute-start.13 = (bf16[512,512]{1,0:T(8,128)(2,1)S(1)}, bf16[512,512]{1,0:T(8,128)(2,1)}, u32[]{:S(2)}, u32[]{:S(2)}) collective-permute-start(bf16[512,512]{1,0:T(8,128)(2,1)S(1)} %bitcast.134), channel_id=1, source_target_pairs={{0,2},{1,3},{2,0},{3,1},{4,6},{5,7},{6,4},{7,5},{8,10},{9,11},{10,... | collective-permute-start | bytes 1572872 | tf_op jit(solution)/shard_map/ppermute | solution.py:29
  106.7 24.0 %collective-permute-start.12 = (bf16[512,512]{1,0:T(8,128)(2,1)S(1)}, bf16[512,512]{1,0:T(8,128)(2,1)}, u32[]{:S(2)}, u32[]{:S(2)}) collective-permute-start(bf16[512,512]{1,0:T(8,128)(2,1)S(1)} %bitcast.135), channel_id=1, source_target_pairs={{0,1},{1,2},{2,3},{3,0},{4,5},{5,6},{6,7},{7,4},{8,9},{9,10},{10,1... | collective-permute-start | bytes 1572872 | tf_op jit(solution)/shard_map/ppermute | solution.py:29
  134.4 1.4 copy-start.2
  134.4 104.9 %all-gather.8.cloned.1.call-start = ((), (), s32[]{:S(2)}) async-start(), calls=%async_computation.4 | async-start | bytes 2621440 | tf_op jit(solution)/shard_map/all_gather | solution.py:107
  136.8 46.1 %copy-start.1 = (bf16[1024,384]{1,0:T(8,128)(2,1)}, bf16[1024,384]{1,0:T(8,128)(2,1)S(1)}, u32[]{:S(2)}) copy-start(bf16[1024,384]{1,0:T(8,128)(2,1)S(1)} %get-tuple-element.18) | copy-start | bytes 2359300
  136.8 46.1 %collective-permute-start.17 = (bf16[1024,384]{1,0:T(8,128)(2,1)S(1)}, bf16[1024,384]{1,0:T(8,128)(2,1)S(1)}, u32[]{:S(2)}, u32[]{:S(2)}) collective-permute-start(bf16[1024,384]{1,0:T(8,128)(2,1)S(1)} %get-tuple-element.18), channel_id=1, source_target_pairs={{0,3},{1,0},{2,1},{3,2},{4,7},{5,4},{6,5},{7,6},{8,11},{9,8},{10,9... | collective-permute-start | bytes 2359304 | tf_op jit(solution)/shard_map/ppermute | solution.py:29
  136.8 46.1 %collective-permute-start.16 = (bf16[1024,384]{1,0:T(8,128)(2,1)S(1)}, bf16[1024,384]{1,0:T(8,128)(2,1)S(1)}, u32[]{:S(2)}, u32[]{:S(2)}) collective-permute-start(bf16[1024,384]{1,0:T(8,128)(2,1)S(1)} %get-tuple-element.18), channel_id=1, source_target_pairs={{0,2},{1,3},{2,0},{3,1},{4,6},{5,7},{6,4},{7,5},{8,10},{9,11},{10,... | collective-permute-start | bytes 2359304 | tf_op jit(solution)/shard_map/ppermute | solution.py:29
  138.2 44.8 %collective-permute-start.15 = (bf16[1024,384]{1,0:T(8,128)(2,1)S(1)}, bf16[1024,384]{1,0:T(8,128)(2,1)S(1)}, u32[]{:S(2)}, u32[]{:S(2)}) collective-permute-start(bf16[1024,384]{1,0:T(8,128)(2,1)S(1)} %get-tuple-element.18), channel_id=1, source_target_pairs={{0,1},{1,2},{2,3},{3,0},{4,5},{5,6},{6,7},{7,4},{8,9},{9,10},{10,1... | collective-permute-start | bytes 2359304 | tf_op jit(solution)/shard_map/ppermute | solution.py:29
  139.7 35.3 %collective-permute-start.20 = (bf16[4,64,384]{2,1,0:T(8,128)(2,1)S(1)}, bf16[4,64,384]{2,1,0:T(8,128)(2,1)S(1)}, u32[]{:S(2)}, u32[]{:S(2)}) collective-permute-start(bf16[4,64,384]{2,1,0:T(8,128)(2,1)S(1)} %get-tuple-element.28), channel_id=1, source_target_pairs={{0,3},{1,0},{2,1},{3,2},{4,7},{5,4},{6,5},{7,6},{8,11},{9,8},{10,9... | collective-permute-start | bytes 589832 | tf_op jit(solution)/shard_map/ppermute | solution.py:96
  141.3 39.5 %collective-permute-start.19 = (bf16[4,64,384]{2,1,0:T(8,128)(2,1)S(1)}, bf16[4,64,384]{2,1,0:T(8,128)(2,1)S(1)}, u32[]{:S(2)}, u32[]{:S(2)}) collective-permute-start(bf16[4,64,384]{2,1,0:T(8,128)(2,1)S(1)} %get-tuple-element.29), channel_id=1, source_target_pairs={{0,2},{1,3},{2,0},{3,1},{4,6},{5,7},{6,4},{7,5},{8,10},{9,11},{10,... | collective-permute-start | bytes 589832 | tf_op jit(solution)/shard_map/ppermute | solution.py:96
  175.0 6.8 %collective-permute-start.18 = (bf16[4,64,384]{2,1,0:T(8,128)(2,1)S(1)}, bf16[4,64,384]{2,1,0:T(8,128)(2,1)S(1)}, u32[]{:S(2)}, u32[]{:S(2)}) collective-permute-start(bf16[4,64,384]{2,1,0:T(8,128)(2,1)S(1)} %get-tuple-element.30), channel_id=1, source_target_pairs={{0,1},{1,2},{2,3},{3,0},{4,5},{5,6},{6,7},{7,4},{8,9},{9,10},{10,1... | collective-permute-start | bytes 589832 | tf_op jit(solution)/shard_map/ppermute | solution.py:96
  182.9 0.9 copy-start.4
  182.9 1.2 copy-start.5
  182.9 1.4 copy-start.6
  187.5 8.0 %copy-start.13 = (s32[6]{0:T(128)S(1)}, s32[6]{0:T(128)}, u32[]{:S(2)}) copy-start(s32[6]{0:T(128)} %param.16) | copy-start | bytes 76
  192.7 18.0 %collective-permute-start.23 = (bf16[1024,384]{1,0:T(8,128)(2,1)}, bf16[1024,384]{1,0:T(8,128)(2,1)S(1)}, u32[]{:S(2)}, u32[]{:S(2)}) collective-permute-start(bf16[1024,384]{1,0:T(8,128)(2,1)} %get-tuple-element.23), channel_id=1, source_target_pairs={{0,3},{1,0},{2,1},{3,2},{4,7},{5,4},{6,5},{7,6},{8,11},{9,8},{10,9... | collective-permute-start | bytes 2359304 | tf_op jit(solution)/shard_map/ppermute | solution.py:29
  192.7 35.4 %collective-permute-start.22 = (bf16[1024,384]{1,0:T(8,128)(2,1)}, bf16[1024,384]{1,0:T(8,128)(2,1)S(1)}, u32[]{:S(2)}, u32[]{:S(2)}) collective-permute-start(bf16[1024,384]{1,0:T(8,128)(2,1)} %get-tuple-element.23), channel_id=1, source_target_pairs={{0,2},{1,3},{2,0},{3,1},{4,6},{5,7},{6,4},{7,5},{8,10},{9,11},{10,... | collective-permute-start | bytes 2359304 | tf_op jit(solution)/shard_map/ppermute | solution.py:29
  193.6 35.4 %collective-permute-start.21 = (bf16[1024,384]{1,0:T(8,128)(2,1)}, bf16[1024,384]{1,0:T(8,128)(2,1)S(1)}, u32[]{:S(2)}, u32[]{:S(2)}) collective-permute-start(bf16[1024,384]{1,0:T(8,128)(2,1)} %get-tuple-element.23), channel_id=1, source_target_pairs={{0,1},{1,2},{2,3},{3,0},{4,5},{5,6},{6,7},{7,4},{8,9},{9,10},{10,1... | collective-permute-start | bytes 2359304 | tf_op jit(solution)/shard_map/ppermute | solution.py:29
  239.3 6.5 %copy-start = (bf16[4,2048,384]{2,1,0:T(8,128)(2,1)S(1)}, bf16[4,2048,384]{2,1,0:T(8,128)(2,1)}, u32[]{:S(2)}) copy-start(bf16[4,2048,384]{2,1,0:T(8,128)(2,1)} %maximum_maximum_fusion) | copy-start | bytes 18874372
  239.3 6.5 %copy-start.7 = (bf16[4,4,64,384]{3,2,1,0:T(8,128)(2,1)S(1)}, bf16[4,4,64,384]{3,2,1,0:T(8,128)(2,1)}, u32[]{:S(2)}) copy-start(bf16[4,4,64,384]{3,2,1,0:T(8,128)(2,1)} %pad_maximum_fusion.3) | copy-start | bytes 2359300
  239.3 6.5 %copy-start.12 = (bf16[256,4096]{1,0:T(8,128)(2,1)S(1)}, bf16[256,4096]{1,0:T(8,128)(2,1)}, u32[]{:S(2)}) copy-start(bf16[256,4096]{1,0:T(8,128)(2,1)} %all-gather.8.cloned.1.call-done) | copy-start | bytes 6291460
  255.8 5.7 %copy-start.11 = (s32[384]{0:T(512)S(1)}, s32[384]{0:T(512)}, u32[]{:S(2)}) copy-start(s32[384]{0:T(512)} %param.19) | copy-start | bytes 4612
  258.5 3.6 %collective-permute-start.26 = (f32[6,384]{1,0:T(8,128)S(1)}, f32[6,384]{1,0:T(8,128)S(1)}, u32[]{:S(2)}, u32[]{:S(2)}) collective-permute-start(f32[6,384]{1,0:T(8,128)S(1)} %get-tuple-element.32), channel_id=1, source_target_pairs={{0,1},{1,2},{2,3},{3,0},{4,5},{5,6},{6,7},{7,4},{8,9},{9,10},{10,1... | collective-permute-start | bytes 27656 | tf_op jit(solution)/shard_map/ppermute | solution.py:121
  258.6 3.8 %collective-permute-start.25 = (f32[6,384]{1,0:T(8,128)S(1)}, f32[6,384]{1,0:T(8,128)S(1)}, u32[]{:S(2)}, u32[]{:S(2)}) collective-permute-start(f32[6,384]{1,0:T(8,128)S(1)} %get-tuple-element.33), channel_id=1, source_target_pairs={{0,2},{1,3},{2,0},{3,1},{4,6},{5,7},{6,4},{7,5},{8,10},{9,11},{10,... | collective-permute-start | bytes 27656 | tf_op jit(solution)/shard_map/ppermute | solution.py:121
  260.1 2.8 %collective-permute-start.24 = (f32[6,384]{1,0:T(8,128)S(1)}, f32[6,384]{1,0:T(8,128)S(1)}, u32[]{:S(2)}, u32[]{:S(2)}) collective-permute-start(f32[6,384]{1,0:T(8,128)S(1)} %get-tuple-element.31), channel_id=1, source_target_pairs={{0,3},{1,0},{2,1},{3,2},{4,7},{5,4},{6,5},{7,6},{8,11},{9,8},{10,9... | collective-permute-start | bytes 27656 | tf_op jit(solution)/shard_map/ppermute | solution.py:121
Sparse Core Ops, SparseCore 0:
  8.9 83.2 all-gather.5
  93.8 26.1 all-gather.3
  134.5 47.0 reduce-scatter.1
  192.8 46.4 all-gather.7

commit v13 on v12

--- a/solution.py
+++ b/solution.py
@@ -37,6 +37,17 @@
     return lax.dynamic_slice_in_dim(doubled, n - 1 - lax.axis_index(axis), n, axis=0)
 
 
+def shared_gather(rows):
+    group_count = lax.axis_size("groups")
+    size = rows.shape[0] // group_count
+    mine = lax.dynamic_slice_in_dim(rows, lax.axis_index("groups") * size, size, axis=0)
+    part = lax.all_gather(mine, "wa", axis=1, tiled=True)
+    if group_count == 1:
+        return part
+    parts = natural_order(ring_gather(part, "groups"), "groups")
+    return parts.reshape(group_count * size, -1)
+
+
 def shards(
     query_act,
     query_grad,
@@ -61,14 +72,17 @@
     act_tokens, grad_tokens, positions, group_sum = lax.optimization_barrier(
         (act_tokens, grad_tokens, positions, group_sum)
     )
-    act_cols = lax.all_gather(act_basis, "wa", axis=1, tiled=True)
-    grad_cols = lax.all_gather(grad_basis, "wa", axis=1, tiled=True)
+    act_cols = shared_gather(act_basis)
+    depth = grad_basis.shape[0] // 2
+    grad_cols = [shared_gather(grad_basis[:depth]), shared_gather(grad_basis[depth:])]
     count = query_act.shape[0]
     act_rot = jnp.dot(
         act_tokens.reshape(nb * count, -1), act_cols, preferred_element_type=jnp.float32
     ).astype(jnp.bfloat16)
-    grad_rot = jnp.dot(
-        grad_tokens.reshape(nb * count, -1), grad_cols, preferred_element_type=jnp.float32
+    grad_flat = grad_tokens.reshape(nb * count, -1)
+    grad_rot = (
+        jnp.dot(grad_flat[:, :depth], grad_cols[0], preferred_element_type=jnp.float32)
+        + jnp.dot(grad_flat[:, depth:], grad_cols[1], preferred_element_type=jnp.float32)
     ).astype(jnp.bfloat16)
     query_weight = jnp.where(positions.reshape(-1) >= PROMPT, 1.0, 0.0).astype(jnp.bfloat16)
     grad_kept = grad_rot * query_weight[:, None]

time: 271 us -> 315 us (1.16)
  blocking collectives: 0 us -> 17.4 us
  local copies, waits for them, and re-layouts: 13.4 us -> 23.6 us
  waiting for transfers between devices: 168 us -> 178 us
  other arithmetic: 18.5 us -> 27 us
  matrix products: 28.8 us -> 25.3 us
    ppermute x18 -> x21, waiting for transfers between devices: 61.2 us -> 117 us  [ring_gather(): lax.ppermute(x, axis, perm=[(i, (i + shift) % n) for i in range(n)])]
    ppermute x3, waiting for transfers between devices: 49.3 us -> 15.3 us  [shards(): lax.ppermute(eig_sum, 'wb', perm=[(i, (i + shift) % nb) for i in range(nb)])]
    all_gather x0 -> x1, blocking collectives: none -> 17.4 us  [shared_gather(): part = lax.all_gather(mine, 'wa', axis=1, tiled=True)]
    all_gather x2, waiting for transfers between devices: 13.1 us -> 0.01 us  [shared_gather(): part = lax.all_gather(mine, 'wa', axis=1, tiled=True)]
    concatenate x2 -> x4, other arithmetic: 0.32 us -> 5.77 us  [natural_order(): doubled = jnp.concatenate([reverse, reverse], axis=0)]
    rev x3 -> x6, local copies, waits for them, and re-layouts: 1.1 us -> 6.17 us  [natural_order(): reverse = stacked[::-1]]
    ppermute x18 -> x21, starting transfers between devices: 13 us -> 17.2 us  [ring_gather(): lax.ppermute(x, axis, perm=[(i, (i + shift) % n) for i in range(n)])]
    another operation x4 -> x7, other arithmetic: 8.17 us -> 12.2 us  [ring_gather(): return jnp.stack(parts)]
  transfers between devices with their start and end apart: 31 -> 34, of which waited for: 20 -> 17; matrix products, arithmetic and copies ran while one was open for 10% -> 8% of each run, Pallas kernels for 0% -> 0%
where the time goes in v13:
time: 315 us; the launch traced here: 314 us
  waiting for transfers between devices  178 us (57%)
  other arithmetic  27 us (9%)
  starting transfers between devices  25.5 us (8%)
  matrix products  25.3 us (8%)
  local copies, waits for them, and re-layouts  23.6 us (7%)
  blocking collectives  17.4 us (6%)
  between operations  17.4 us (6%)
    ppermute x21, waiting for transfers between devices, ring_gather(): lax.ppermute(x, axis, perm=[(i, (i + shift) % n) for i in range(n)])  117 us
    ppermute x3, waiting for transfers between devices, shards(): lax.ppermute(outgoing, 'wb', perm=[(i, (i + shift) % nb) for i in range(n...  39.5 us
    dot_general x6, matrix products, shards(): jnp.einsum('ij,sjt->sit', precond, grads_near, preferred_element_type=jnp...  19 us
    all_gather x1, blocking collectives, shared_gather(): part = lax.all_gather(mine, 'wa', axis=1, tiled=True)  17.4 us
    ppermute x21, starting transfers between devices, ring_gather(): lax.ppermute(x, axis, perm=[(i, (i + shift) % n) for i in range(n)])  17.2 us
    ppermute x3, waiting for transfers between devices, shards(): lax.ppermute(eig_sum, 'wb', perm=[(i, (i + shift) % nb) for i in range(nb)])  15.3 us
    another operation x7, other arithmetic, ring_gather(): return jnp.stack(parts)  12.2 us
  transfers between devices with their start and end apart: 34, of which 17 were waited for; matrix products, arithmetic and copies ran while one was open for 8% of the time, Pallas kernels for 0%

profile of v13, /device:TPU:0, one launch (start us, length us, event | category | flops | bytes accessed | tf_op | source)
XLA Modules:
  0.0 314.5 jit_solution(10850978702687120709)
XLA Ops:
  6.6 1.3 fusion.73
  9.6 2.5 collective-permute-start.2
  12.7 1.7 collective-permute-start.7
  15.2 9.9 %collective-permute-done.9 = f32[]{:T(128)} collective-permute-done((f32[]{:T(128)}, f32[]{:T(128)}, u32[]{:S(2)}, u32[]{:S(2)}) %collective-permute-start.9) | collective-permute-done | bytes 36 | tf_op jit(solution)/shard_map/ppermute | solution.py:71
  25.1 1.9 collective-permute-start.10
  27.0 4.0 %collective-permute-done.10 = f32[]{:T(128)} collective-permute-done((f32[]{:T(128)}, f32[]{:T(128)}, u32[]{:S(2)}, u32[]{:S(2)}) %collective-permute-start.10) | collective-permute-done | bytes 36 | tf_op jit(solution)/shard_map/ppermute | solution.py:71
  31.0 1.4 collective-permute-done.11
  32.4 2.1 collective-permute-start.6
  34.5 1.6 collective-permute-start.4
  37.0 1.3 collective-permute-start
  38.3 17.4 %all_gather.12 = bf16[1024,256]{0,1:T(8,128)(2,1)S(1)} all-gather(bf16[1024,64]{0,1:T(8,128)(2,1)S(1)} %constant_dynamic-slice_fusion.2), channel_id=1, replica_groups=mesh['groups'=2,'wa'=4,'wb'=4] {'wa'}, dimensions={1}, use_global_device_ids=true | all-gather | bytes 655360 | tf_op jit(solution)/shard_map/all_gather | solution.py:44
  55.9 1.4 collective-permute-start.12
  59.8 28.6 %collective-permute-done = bf16[128,2048]{1,0:T(8,128)(2,1)S(1)} collective-permute-done((bf16[128,2048]{1,0:T(8,128)(2,1)S(1)}, bf16[128,2048]{1,0:T(8,128)(2,1)S(1)}, u32[]{:S(2)}, u32[]{:S(2)}) %collective-permute-start) | collective-permute-done | bytes 524320 | tf_op jit(solution)/shard_map/ppermute | solution.py:29
  88.4 0.8 copy-done.17
  89.2 1.5 collective-permute-start.14
  90.7 3.0 pad_maximum_fusion.2
  94.4 3.9 %pad_maximum_fusion = bf16[4,128,4096]{2,1,0:T(8,128)(2,1)} fusion(bf16[1,128,4096]{2,1,0:T(8,128)(2,1)} %bitcast.7, bf16[1,128,4096]{2,1,0:T(8,128)(2,1)} %bitcast.6, bf16[1,128,4096]{2,1,0:T(8,128)(2,1)} %bitcast.5, bf16[1,128,4096]{2,1,0:T(8,128)(2,1)} %bitcast.4), kind=kLoop, calls=%fused_computation.13 | loop fusion | flops 6291456 | bytes 8388608 | tf_op jit(solution)/shard_map/stack | solution.py:30
  98.3 17.2 %collective-permute-done.14 = bf16[1024,512]{1,0:T(8,128)(2,1)S(1)} collective-permute-done((bf16[1024,512]{1,0:T(8,128)(2,1)}, bf16[1024,512]{1,0:T(8,128)(2,1)S(1)}, u32[]{:S(2)}, u32[]{:S(2)}) %collective-permute-start.14) | collective-permute-done | bytes 1048608 | tf_op jit(solution)/shard_map/ppermute | solution.py:29
  115.5 1.0 copy-done.9
  116.5 1.4 pad_maximum_fusion.4
  118.0 1.5 rev.21
  119.5 15.6 %collective-permute-done.13 = bf16[1024,512]{1,0:T(8,128)(2,1)} collective-permute-done((bf16[1024,512]{1,0:T(8,128)(2,1)}, bf16[1024,512]{1,0:T(8,128)(2,1)}, u32[]{:S(2)}, u32[]{:S(2)}) %collective-permute-start.13) | collective-permute-done | bytes 1048608 | tf_op jit(solution)/shard_map/ppermute | solution.py:29
  135.1 1.7 pad_maximum_fusion.3
  136.8 1.5 rev.20
  138.3 3.2 %fusion = (bf16[2,1024,512]{2,1,0:T(8,128)(2,1)S(1)}, bf16[2,1024,512]{2,1,0:T(8,128)(2,1)S(1)}) fusion(s32[]{:T(128)S(6)} %select_n.57, bf16[2,1024,512]{2,1,0:T(8,128)(2,1)} %rev.21, bf16[2,1024,512]{2,1,0:T(8,128)(2,1)} %rev.20), kind=kLoop, calls=%fused_computation.25 | loop fusion | flops 2097152 | bytes 8388612 | tf_op jit(solution)/shard_map/concatenate | solution.py:36
  141.7 1.2 fusion.8
  143.0 2.1 fusion.32
  145.0 2.1 rev.22
  147.1 2.1 fusion.50
  149.1 1.6 collective-permute-start.16
  152.2 8.4 %collective-permute-done.17 = bf16[512,512]{1,0:T(8,128)(2,1)} collective-permute-done((bf16[512,512]{1,0:T(8,128)(2,1)}, bf16[512,512]{1,0:T(8,128)(2,1)}, u32[]{:S(2)}, u32[]{:S(2)}) %collective-permute-start.17) | collective-permute-done | bytes 524320 | tf_op jit(solution)/shard_map/ppermute | solution.py:29
  160.6 14.4 %collective-permute-done.16 = bf16[512,512]{1,0:T(8,128)(2,1)} collective-permute-done((bf16[512,512]{1,0:T(8,128)(2,1)}, bf16[512,512]{1,0:T(8,128)(2,1)}, u32[]{:S(2)}, u32[]{:S(2)}) %collective-permute-start.16) | collective-permute-done | bytes 524320 | tf_op jit(solution)/shard_map/ppermute | solution.py:29
  175.0 2.2 fusion.12
  177.3 1.5 concatenate.36
  178.9 1.3 copy-done.6
  180.2 1.0 fusion.72
  182.0 1.3 dynamic-slice_bitcast_fusion.3
  183.3 1.6 collective-permute-start.23
  184.9 1.6 collective-permute-start.22
  186.4 33.9 %collective-permute-done.23 = bf16[4,64,384]{2,1,0:T(8,128)(2,1)S(1)} collective-permute-done((bf16[4,64,384]{2,1,0:T(8,128)(2,1)S(1)}, bf16[4,64,384]{2,1,0:T(8,128)(2,1)S(1)}, u32[]{:S(2)}, u32[]{:S(2)}) %collective-permute-start.23) | collective-permute-done | bytes 196640 | tf_op jit(solution)/shard_map/ppermute | solution.py:110
  220.3 3.7 %collective-permute-done.22 = bf16[4,64,384]{2,1,0:T(8,128)(2,1)S(1)} collective-permute-done((bf16[4,64,384]{2,1,0:T(8,128)(2,1)S(1)}, bf16[4,64,384]{2,1,0:T(8,128)(2,1)S(1)}, u32[]{:S(2)}, u32[]{:S(2)}) %collective-permute-start.22) | collective-permute-done | bytes 196640 | tf_op jit(solution)/shard_map/ppermute | solution.py:110
  224.0 1.9 collective-permute-done.21
  225.9 1.0 pad_maximum_fusion.6
  227.0 0.8 copy-done.10
  228.4 2.1 pad_maximum_fusion.1
  230.5 1.1 slice.82
  231.6 0.9 reshape.64
  232.5 1.0 rev.23
  234.0 0.9 convert_element_type.68
  234.9 1.9 pad_maximum_fusion.7
  236.8 1.1 collective-permute-start.25
  238.1 1.2 slice.85
  240.6 13.9 %collective-permute-done.26 = bf16[1024,384]{1,0:T(8,128)(2,1)S(1)} collective-permute-done((bf16[1024,384]{1,0:T(8,128)(2,1)}, bf16[1024,384]{1,0:T(8,128)(2,1)S(1)}, u32[]{:S(2)}, u32[]{:S(2)}) %collective-permute-start.26) | collective-permute-done | bytes 786464 | tf_op jit(solution)/shard_map/ppermute | solution.py:29
  254.5 18.3 %collective-permute-done.25 = bf16[1024,384]{1,0:T(8,128)(2,1)S(1)} collective-permute-done((bf16[1024,384]{1,0:T(8,128)(2,1)}, bf16[1024,384]{1,0:T(8,128)(2,1)S(1)}, u32[]{:S(2)}, u32[]{:S(2)}) %collective-permute-start.25) | collective-permute-done | bytes 786464 | tf_op jit(solution)/shard_map/ppermute | solution.py:29
  273.3 4.5 %maximum_maximum_fusion = bf16[4,2048,384]{2,1,0:T(8,128)(2,1)} fusion(bf16[1,1024,384]{2,1,0:T(8,128)(2,1)S(1)} %bitcast.137, bf16[1,1024,384]{2,1,0:T(8,128)(2,1)S(1)} %bitcast.138, bf16[1,1024,384]{2,1,0:T(8,128)(2,1)S(1)} %bitcast.139, bf16[1,1024,384]{2,1,0:T(8,128)(2,1)} %bitcast.123, bf16[4,1024,384]{2,1,0:T(8,128)(2,1)S(1)} %pad_maximum_fusion.1), kind=kLoop, calls=%fused_computation | loop fusion | flops 31457280 | bytes 12582912 | tf_op jit(solution)/shard_map/concatenate | solution.py:123
  277.7 5.9 %all-gather.8.cloned.1.call-done = bf16[256,4096]{1,0:T(8,128)(2,1)} async-done(((bf16[64,4096]{1,0:T(8,128)(2,1)}), bf16[256,4096]{1,0:T(8,128)(2,1)}) %all-gather.8.cloned.1.call-update) | async-done | bytes 2097168 | tf_op jit(solution)/shard_map/all_gather | solution.py:121
  283.6 6.5 %fusion.20 = f32[4,384]{1,0:T(4,128)S(1)} fusion(bf16[4,256,384]{2,1,0:T(8,128)(2,1)} %bitcast.141, bf16[4,2048,384]{2,1,0:T(8,128)(2,1)} %maximum_maximum_fusion, f32[]{:T(128)} %bitcast.47, bf16[256,4096]{1,0:T(8,128)(2,1)} %all-gather.8.cloned.1.call-done), kind=kOutput, calls=%fused_computation.50 | convolution fusion | flops 1614412288 | bytes 9181188 | tf_op jit(solution)/shard_map/ij,sjt->sit/dot_general | solution.py:130
  290.2 2.4 fusion.21
  292.6 2.5 fusion.22
  295.1 2.6 fusion.23
  297.7 2.5 fusion.24
  300.2 2.6 fusion.25
  303.0 1.6 collective-permute-start.28
  304.6 1.4 collective-permute-start.27
  (111 shorter events, 11.3 us)
Async XLA Ops:
  6.5 31.8 %copy-start = (bf16[2048,64]{0,1:T(8,128)(2,1)S(1)}, bf16[2048,64]{0,1:T(8,128)(2,1)}, u32[]{:S(2)}) copy-start(bf16[2048,64]{0,1:T(8,128)(2,1)} %param.13) | copy-start | bytes 786436
  6.5 3.0 copy-start.14
  6.5 6.1 %copy-start.19 = (s32[128]{0:T(128)S(1)}, s32[128]{0:T(128)}, u32[]{:S(2)}) copy-start(s32[128]{0:T(128)} %param.12) | copy-start | bytes 1540
  6.5 7.9 %copy-start.7 = (bf16[64,2048]{1,0:T(8,128)(2,1)S(1)}, bf16[64,2048]{1,0:T(8,128)(2,1)}, u32[]{:S(2)}) copy-start(bf16[64,2048]{1,0:T(8,128)(2,1)} %param.15) | copy-start | bytes 786436
  6.5 82.7 %all-gather.6.cloned.1.call-start = ((), (), s32[]{:S(2)}) async-start(), calls=%async_computation.2 | async-start | bytes 1310720 | tf_op jit(solution)/shard_map/all_gather | solution.py:44
  8.7 85.0 %all-gather.4.cloned.1.call-start = ((), (), s32[]{:S(2)}) async-start(), calls=%async_computation.1 | async-start | bytes 1310720 | tf_op jit(solution)/shard_map/all_gather | solution.py:44
  9.5 221.0 %reduce-scatter.2.cloned.1.call-start = ((), (), s32[]{:S(2)}) async-start(), calls=%async_computation.3 | async-start | bytes 2785280 | tf_op jit(solution)/shard_map/reduce_scatter | solution.py:96
  9.6 26.6 %collective-permute-start.2 = (bf16[128,2048]{1,0:T(8,128)(2,1)S(1)}, bf16[128,2048]{1,0:T(8,128)(2,1)S(1)}, u32[]{:S(2)}, u32[]{:S(2)}) collective-permute-start(bf16[128,2048]{1,0:T(8,128)(2,1)S(1)} %copy-done.14), channel_id=1, source_target_pairs={{0,3},{1,0},{2,1},{3,2},{4,7},{5,4},{6,5},{7,6},{8,11},{9,8},{10,9... | collective-permute-start | bytes 1572872 | tf_op jit(solution)/shard_map/ppermute | solution.py:29
  12.0 43.8 %collective-permute-start.1 = (bf16[128,2048]{1,0:T(8,128)(2,1)S(1)}, bf16[128,2048]{1,0:T(8,128)(2,1)S(1)}, u32[]{:S(2)}, u32[]{:S(2)}) collective-permute-start(bf16[128,2048]{1,0:T(8,128)(2,1)S(1)} %copy-done.14), channel_id=1, source_target_pairs={{0,2},{1,3},{2,0},{3,1},{4,6},{5,7},{6,4},{7,5},{8,10},{9,11},{10,... | collective-permute-start | bytes 1572872 | tf_op jit(solution)/shard_map/ppermute | solution.py:29
  12.7 21.8 %collective-permute-start.8 = (s32[128]{0:T(128)S(1)}, s32[128]{0:T(128)S(1)}, u32[]{:S(2)}, u32[]{:S(2)}) collective-permute-start(s32[128]{0:T(128)S(1)} %copy-done.19), channel_id=1, source_target_pairs={{0,3},{1,0},{2,1},{3,2},{4,7},{5,4},{6,5},{7,6},{8,11},{9,8},{10,9... | collective-permute-start | bytes 1544 | tf_op jit(solution)/shard_map/ppermute | solution.py:29
  12.7 21.8 %collective-permute-start.7 = (s32[128]{0:T(128)S(1)}, s32[128]{0:T(128)S(1)}, u32[]{:S(2)}, u32[]{:S(2)}) collective-permute-start(s32[128]{0:T(128)S(1)} %copy-done.19), channel_id=1, source_target_pairs={{0,2},{1,3},{2,0},{3,1},{4,6},{5,7},{6,4},{7,5},{8,10},{9,11},{10,... | collective-permute-start | bytes 1544 | tf_op jit(solution)/shard_map/ppermute | solution.py:29
  15.2 9.9 %collective-permute-start.9 = (f32[]{:T(128)}, f32[]{:T(128)}, u32[]{:S(2)}, u32[]{:S(2)}) collective-permute-start(f32[]{:T(128)} %convert_reduce_fusion), channel_id=1, source_target_pairs={{0,1},{1,2},{2,3},{3,0},{4,5},{5,6},{6,7},{7,4},{8,9},{9,10},{10,1... | collective-permute-start | bytes 20 | tf_op jit(solution)/shard_map/ppermute | solution.py:71
  25.1 5.9 %collective-permute-start.10 = (f32[]{:T(128)}, f32[]{:T(128)}, u32[]{:S(2)}, u32[]{:S(2)}) collective-permute-start(f32[]{:T(128)} %convert_reduce_fusion), channel_id=1, source_target_pairs={{0,2},{1,3},{2,0},{3,1},{4,6},{5,7},{6,4},{7,5},{8,10},{9,11},{10,... | collective-permute-start | bytes 20 | tf_op jit(solution)/shard_map/ppermute | solution.py:71
  31.0 1.4 collective-permute-start.11
  32.4 3.7 %collective-permute-start.6 = (s32[128]{0:T(128)S(1)}, s32[128]{0:T(128)S(1)}, u32[]{:S(2)}, u32[]{:S(2)}) collective-permute-start(s32[128]{0:T(128)S(1)} %copy-done.19), channel_id=1, source_target_pairs={{0,1},{1,2},{2,3},{3,0},{4,5},{5,6},{6,7},{7,4},{8,9},{9,10},{10,1... | collective-permute-start | bytes 1544 | tf_op jit(solution)/shard_map/ppermute | solution.py:29
  34.5 59.9 %collective-permute-start.5 = (bf16[128,4096]{1,0:T(8,128)(2,1)}, bf16[128,4096]{1,0:T(8,128)(2,1)}, u32[]{:S(2)}, u32[]{:S(2)}) collective-permute-start(bf16[128,4096]{1,0:T(8,128)(2,1)} %param.11), channel_id=1, source_target_pairs={{0,3},{1,0},{2,1},{3,2},{4,7},{5,4},{6,5},{7,6},{8,11},{9,8},{10,9... | collective-permute-start | bytes 3145736 | tf_op jit(solution)/shard_map/ppermute | solution.py:29
  34.5 59.9 %collective-permute-start.4 = (bf16[128,4096]{1,0:T(8,128)(2,1)}, bf16[128,4096]{1,0:T(8,128)(2,1)}, u32[]{:S(2)}, u32[]{:S(2)}) collective-permute-start(bf16[128,4096]{1,0:T(8,128)(2,1)} %param.11), channel_id=1, source_target_pairs={{0,2},{1,3},{2,0},{3,1},{4,6},{5,7},{6,4},{7,5},{8,10},{9,11},{10,... | collective-permute-start | bytes 3145736 | tf_op jit(solution)/shard_map/ppermute | solution.py:29
  36.2 58.3 %collective-permute-start.3 = (bf16[128,4096]{1,0:T(8,128)(2,1)}, bf16[128,4096]{1,0:T(8,128)(2,1)}, u32[]{:S(2)}, u32[]{:S(2)}) collective-permute-start(bf16[128,4096]{1,0:T(8,128)(2,1)} %param.11), channel_id=1, source_target_pairs={{0,1},{1,2},{2,3},{3,0},{4,5},{5,6},{6,7},{7,4},{8,9},{9,10},{10,1... | collective-permute-start | bytes 3145736 | tf_op jit(solution)/shard_map/ppermute | solution.py:29
  36.2 0.8 copy-start.15
  37.0 51.4 %collective-permute-start = (bf16[128,2048]{1,0:T(8,128)(2,1)S(1)}, bf16[128,2048]{1,0:T(8,128)(2,1)S(1)}, u32[]{:S(2)}, u32[]{:S(2)}) collective-permute-start(bf16[128,2048]{1,0:T(8,128)(2,1)S(1)} %copy-done.14), channel_id=1, source_target_pairs={{0,1},{1,2},{2,3},{3,0},{4,5},{5,6},{6,7},{7,4},{8,9},{9,10},{10,1... | collective-permute-start | bytes 1572872 | tf_op jit(solution)/shard_map/ppermute | solution.py:29
  55.9 32.5 %copy-start.16 = (bf16[128,2048]{1,0:T(8,128)(2,1)}, bf16[128,2048]{1,0:T(8,128)(2,1)S(1)}, u32[]{:S(2)}) copy-start(bf16[128,2048]{1,0:T(8,128)(2,1)S(1)} %collective-permute-done.1) | copy-start | bytes 1572868
  55.9 37.8 %collective-permute-start.12 = (bf16[1024,256]{1,0:T(8,128)(2,1)S(1)}, bf16[1024,256]{1,0:T(8,128)(2,1)S(1)}, u32[]{:S(2)}, u32[]{:S(2)}) collective-permute-start(bf16[1024,256]{1,0:T(8,128)(2,1)S(1)} %copy.14), channel_id=1, source_target_pairs={{0,16},{16,0},{1,17},{17,1},{2,18},{18,2},{3,19},{19,3},{4,20},{20... | collective-permute-start | bytes 1572872 | tf_op jit(solution)/shard_map/ppermute | solution.py:29
  88.4 0.8 copy-start.17
  89.2 26.3 %collective-permute-start.14 = (bf16[1024,512]{1,0:T(8,128)(2,1)}, bf16[1024,512]{1,0:T(8,128)(2,1)S(1)}, u32[]{:S(2)}, u32[]{:S(2)}) collective-permute-start(bf16[1024,512]{1,0:T(8,128)(2,1)} %all-gather.6.cloned.1.call-done), channel_id=1, source_target_pairs={{0,16},{16,0},{1,17},{17,1},{2,18},{18,2},{3,19},{19,3},{4,20},{20... | collective-permute-start | bytes 3145736 | tf_op jit(solution)/shard_map/ppermute | solution.py:29
  93.7 41.4 %collective-permute-start.13 = (bf16[1024,512]{1,0:T(8,128)(2,1)}, bf16[1024,512]{1,0:T(8,128)(2,1)}, u32[]{:S(2)}, u32[]{:S(2)}) collective-permute-start(bf16[1024,512]{1,0:T(8,128)(2,1)} %all-gather.4.cloned.1.call-done), channel_id=1, source_target_pairs={{0,16},{16,0},{1,17},{17,1},{2,18},{18,2},{3,19},{19,3},{4,20},{20... | collective-permute-start | bytes 3145736 | tf_op jit(solution)/shard_map/ppermute | solution.py:29
  94.4 22.1 %copy-start.8 = (bf16[1024,512]{1,0:T(8,128)(2,1)S(1)}, bf16[1024,512]{1,0:T(8,128)(2,1)}, u32[]{:S(2)}) copy-start(bf16[1024,512]{1,0:T(8,128)(2,1)} %all-gather.6.cloned.1.call-done) | copy-start | bytes 3145732
  115.5 1.0 copy-start.9
  138.3 3.4 %copy-start.3 = (bf16[4,128,4096]{2,1,0:T(8,128)(2,1)S(1)}, bf16[4,128,4096]{2,1,0:T(8,128)(2,1)}, u32[]{:S(2)}) copy-start(bf16[4,128,4096]{2,1,0:T(8,128)(2,1)} %pad_maximum_fusion) | copy-start | bytes 12582916
  145.0 6.3 %copy-start.5 = (bf16[4,128,2048]{2,1,0:T(8,128)(2,1)S(1)}, bf16[4,128,2048]{2,1,0:T(8,128)(2,1)}, u32[]{:S(2)}) copy-start(bf16[4,128,2048]{2,1,0:T(8,128)(2,1)} %pad_maximum_fusion.2) | copy-start | bytes 6291460
  149.1 11.5 %collective-permute-start.17 = (bf16[512,512]{1,0:T(8,128)(2,1)}, bf16[512,512]{1,0:T(8,128)(2,1)}, u32[]{:S(2)}, u32[]{:S(2)}) collective-permute-start(bf16[512,512]{1,0:T(8,128)(2,1)} %bitcast.27), channel_id=1, source_target_pairs={{0,3},{1,0},{2,1},{3,2},{4,7},{5,4},{6,5},{7,6},{8,11},{9,8},{10,9... | collective-permute-start | bytes 1572872 | tf_op jit(solution)/shard_map/ppermute | solution.py:29
  149.1 25.9 %collective-permute-start.16 = (bf16[512,512]{1,0:T(8,128)(2,1)}, bf16[512,512]{1,0:T(8,128)(2,1)}, u32[]{:S(2)}, u32[]{:S(2)}) collective-permute-start(bf16[512,512]{1,0:T(8,128)(2,1)} %bitcast.27), channel_id=1, source_target_pairs={{0,2},{1,3},{2,0},{3,1},{4,6},{5,7},{6,4},{7,5},{8,10},{9,11},{10,... | collective-permute-start | bytes 1572872 | tf_op jit(solution)/shard_map/ppermute | solution.py:29
  150.7 24.3 %collective-permute-start.15 = (bf16[512,512]{1,0:T(8,128)(2,1)}, bf16[512,512]{1,0:T(8,128)(2,1)}, u32[]{:S(2)}, u32[]{:S(2)}) collective-permute-start(bf16[512,512]{1,0:T(8,128)(2,1)} %bitcast.27), channel_id=1, source_target_pairs={{0,1},{1,2},{2,3},{3,0},{4,5},{5,6},{6,7},{7,4},{8,9},{9,10},{10,1... | collective-permute-start | bytes 1572872 | tf_op jit(solution)/shard_map/ppermute | solution.py:29
  178.8 1.4 copy-start.6
  178.9 104.8 %all-gather.8.cloned.1.call-start = ((), (), s32[]{:S(2)}) async-start(), calls=%async_computation.4 | async-start | bytes 2621440 | tf_op jit(solution)/shard_map/all_gather | solution.py:121
  181.3 45.7 %copy-start.4 = (bf16[1024,384]{1,0:T(8,128)(2,1)}, bf16[1024,384]{1,0:T(8,128)(2,1)S(1)}, u32[]{:S(2)}) copy-start(bf16[1024,384]{1,0:T(8,128)(2,1)S(1)} %get-tuple-element.18) | copy-start | bytes 2359300
  181.3 45.7 %collective-permute-start.20 = (bf16[1024,384]{1,0:T(8,128)(2,1)S(1)}, bf16[1024,384]{1,0:T(8,128)(2,1)S(1)}, u32[]{:S(2)}, u32[]{:S(2)}) collective-permute-start(bf16[1024,384]{1,0:T(8,128)(2,1)S(1)} %get-tuple-element.18), channel_id=1, source_target_pairs={{0,3},{1,0},{2,1},{3,2},{4,7},{5,4},{6,5},{7,6},{8,11},{9,8},{10,9... | collective-permute-start | bytes 2359304 | tf_op jit(solution)/shard_map/ppermute | solution.py:29
  181.3 45.7 %collective-permute-start.19 = (bf16[1024,384]{1,0:T(8,128)(2,1)S(1)}, bf16[1024,384]{1,0:T(8,128)(2,1)S(1)}, u32[]{:S(2)}, u32[]{:S(2)}) collective-permute-start(bf16[1024,384]{1,0:T(8,128)(2,1)S(1)} %get-tuple-element.18), channel_id=1, source_target_pairs={{0,2},{1,3},{2,0},{3,1},{4,6},{5,7},{6,4},{7,5},{8,10},{9,11},{10,... | collective-permute-start | bytes 2359304 | tf_op jit(solution)/shard_map/ppermute | solution.py:29
  181.7 45.2 %collective-permute-start.18 = (bf16[1024,384]{1,0:T(8,128)(2,1)S(1)}, bf16[1024,384]{1,0:T(8,128)(2,1)S(1)}, u32[]{:S(2)}, u32[]{:S(2)}) collective-permute-start(bf16[1024,384]{1,0:T(8,128)(2,1)S(1)} %get-tuple-element.18), channel_id=1, source_target_pairs={{0,1},{1,2},{2,3},{3,0},{4,5},{5,6},{6,7},{7,4},{8,9},{9,10},{10,1... | collective-permute-start | bytes 2359304 | tf_op jit(solution)/shard_map/ppermute | solution.py:29
  183.3 37.0 %collective-permute-start.23 = (bf16[4,64,384]{2,1,0:T(8,128)(2,1)S(1)}, bf16[4,64,384]{2,1,0:T(8,128)(2,1)S(1)}, u32[]{:S(2)}, u32[]{:S(2)}) collective-permute-start(bf16[4,64,384]{2,1,0:T(8,128)(2,1)S(1)} %get-tuple-element.30), channel_id=1, source_target_pairs={{0,3},{1,0},{2,1},{3,2},{4,7},{5,4},{6,5},{7,6},{8,11},{9,8},{10,9... | collective-permute-start | bytes 589832 | tf_op jit(solution)/shard_map/ppermute | solution.py:110
  184.9 39.2 %collective-permute-start.22 = (bf16[4,64,384]{2,1,0:T(8,128)(2,1)S(1)}, bf16[4,64,384]{2,1,0:T(8,128)(2,1)S(1)}, u32[]{:S(2)}, u32[]{:S(2)}) collective-permute-start(bf16[4,64,384]{2,1,0:T(8,128)(2,1)S(1)} %get-tuple-element.31), channel_id=1, source_target_pairs={{0,2},{1,3},{2,0},{3,1},{4,6},{5,7},{6,4},{7,5},{8,10},{9,11},{10,... | collective-permute-start | bytes 589832 | tf_op jit(solution)/shard_map/ppermute | solution.py:110
  220.3 5.7 %collective-permute-start.21 = (bf16[4,64,384]{2,1,0:T(8,128)(2,1)S(1)}, bf16[4,64,384]{2,1,0:T(8,128)(2,1)S(1)}, u32[]{:S(2)}, u32[]{:S(2)}) collective-permute-start(bf16[4,64,384]{2,1,0:T(8,128)(2,1)S(1)} %get-tuple-element.32), channel_id=1, source_target_pairs={{0,1},{1,2},{2,3},{3,0},{4,5},{5,6},{6,7},{7,4},{8,9},{9,10},{10,1... | collective-permute-start | bytes 589832 | tf_op jit(solution)/shard_map/ppermute | solution.py:110
  227.0 0.9 copy-start.10
  227.0 1.1 copy-start.11
  227.0 1.4 copy-start.12
  231.6 8.3 %copy-start.21 = (s32[6]{0:T(128)S(1)}, s32[6]{0:T(128)}, u32[]{:S(2)}) copy-start(s32[6]{0:T(128)} %param.16) | copy-start | bytes 76
  236.7 17.8 %collective-permute-start.26 = (bf16[1024,384]{1,0:T(8,128)(2,1)}, bf16[1024,384]{1,0:T(8,128)(2,1)S(1)}, u32[]{:S(2)}, u32[]{:S(2)}) collective-permute-start(bf16[1024,384]{1,0:T(8,128)(2,1)} %get-tuple-element.23), channel_id=1, source_target_pairs={{0,3},{1,0},{2,1},{3,2},{4,7},{5,4},{6,5},{7,6},{8,11},{9,8},{10,9... | collective-permute-start | bytes 2359304 | tf_op jit(solution)/shard_map/ppermute | solution.py:29
  236.8 36.0 %collective-permute-start.25 = (bf16[1024,384]{1,0:T(8,128)(2,1)}, bf16[1024,384]{1,0:T(8,128)(2,1)S(1)}, u32[]{:S(2)}, u32[]{:S(2)}) collective-permute-start(bf16[1024,384]{1,0:T(8,128)(2,1)} %get-tuple-element.23), channel_id=1, source_target_pairs={{0,2},{1,3},{2,0},{3,1},{4,6},{5,7},{6,4},{7,5},{8,10},{9,11},{10,... | collective-permute-start | bytes 2359304 | tf_op jit(solution)/shard_map/ppermute | solution.py:29
  237.9 35.4 %collective-permute-start.24 = (bf16[1024,384]{1,0:T(8,128)(2,1)}, bf16[1024,384]{1,0:T(8,128)(2,1)S(1)}, u32[]{:S(2)}, u32[]{:S(2)}) collective-permute-start(bf16[1024,384]{1,0:T(8,128)(2,1)} %get-tuple-element.23), channel_id=1, source_target_pairs={{0,1},{1,2},{2,3},{3,0},{4,5},{5,6},{6,7},{7,4},{8,9},{9,10},{10,1... | collective-permute-start | bytes 2359304 | tf_op jit(solution)/shard_map/ppermute | solution.py:29
  283.6 6.5 %copy-start.2 = (bf16[4,2048,384]{2,1,0:T(8,128)(2,1)S(1)}, bf16[4,2048,384]{2,1,0:T(8,128)(2,1)}, u32[]{:S(2)}) copy-start(bf16[4,2048,384]{2,1,0:T(8,128)(2,1)} %maximum_maximum_fusion) | copy-start | bytes 18874372
  283.6 6.5 %copy-start.13 = (bf16[4,4,64,384]{3,2,1,0:T(8,128)(2,1)S(1)}, bf16[4,4,64,384]{3,2,1,0:T(8,128)(2,1)}, u32[]{:S(2)}) copy-start(bf16[4,4,64,384]{3,2,1,0:T(8,128)(2,1)} %pad_maximum_fusion.6) | copy-start | bytes 2359300
  283.6 6.5 %copy-start.20 = (bf16[256,4096]{1,0:T(8,128)(2,1)S(1)}, bf16[256,4096]{1,0:T(8,128)(2,1)}, u32[]{:S(2)}) copy-start(bf16[256,4096]{1,0:T(8,128)(2,1)} %all-gather.8.cloned.1.call-done) | copy-start | bytes 6291460
  300.2 5.8 %copy-start.18 = (s32[384]{0:T(512)S(1)}, s32[384]{0:T(512)}, u32[]{:S(2)}) copy-start(s32[384]{0:T(512)} %param.19) | copy-start | bytes 4612
  300.2 7.8 %copy-start.1 = (bf16[2048,64]{0,1:T(8,128)(2,1)S(1)}, bf16[2048,64]{0,1:T(8,128)(2,1)}, u32[]{:S(2)}) copy-start(bf16[2048,64]{0,1:T(8,128)(2,1)} %param.13) | copy-start | bytes 786436
  302.9 3.7 %collective-permute-start.29 = (f32[6,384]{1,0:T(8,128)S(1)}, f32[6,384]{1,0:T(8,128)S(1)}, u32[]{:S(2)}, u32[]{:S(2)}) collective-permute-start(f32[6,384]{1,0:T(8,128)S(1)} %get-tuple-element.34), channel_id=1, source_target_pairs={{0,1},{1,2},{2,3},{3,0},{4,5},{5,6},{6,7},{7,4},{8,9},{9,10},{10,1... | collective-permute-start | bytes 27656 | tf_op jit(solution)/shard_map/ppermute | solution.py:135
  303.0 3.8 %collective-permute-start.28 = (f32[6,384]{1,0:T(8,128)S(1)}, f32[6,384]{1,0:T(8,128)S(1)}, u32[]{:S(2)}, u32[]{:S(2)}) collective-permute-start(f32[6,384]{1,0:T(8,128)S(1)} %get-tuple-element.35), channel_id=1, source_target_pairs={{0,2},{1,3},{2,0},{3,1},{4,6},{5,7},{6,4},{7,5},{8,10},{9,11},{10,... | collective-permute-start | bytes 27656 | tf_op jit(solution)/shard_map/ppermute | solution.py:135
  304.6 2.8 collective-permute-start.27
Sparse Core Ops, SparseCore 0:
  8.9 32.8 all-gather.5
  43.4 30.8 all-gather.3
  179.0 46.3 reduce-scatter.1
  236.9 46.7 all-gather.7

commit v14 on v12

--- a/solution.py
+++ b/solution.py
@@ -58,8 +58,11 @@
     group_sum = eig_sum
     for shift in range(1, nb):
         group_sum = group_sum + lax.ppermute(eig_sum, "wb", perm=[(i, (i + shift) % nb) for i in range(nb)])
-    act_tokens, grad_tokens, positions, group_sum = lax.optimization_barrier(
-        (act_tokens, grad_tokens, positions, group_sum)
+    eig_total = group_sum
+    for shift in range(1, na):
+        eig_total = eig_total + lax.ppermute(group_sum, "wa", perm=[(i, (i + shift) % na) for i in range(na)])
+    act_tokens, grad_tokens, positions, eig_total = lax.optimization_barrier(
+        (act_tokens, grad_tokens, positions, eig_total)
     )
     act_cols = lax.all_gather(act_basis, "wa", axis=1, tiled=True)
     grad_cols = lax.all_gather(grad_basis, "wa", axis=1, tiled=True)
@@ -78,15 +81,12 @@
     partial_rows = lax.dot_general(
         act_rot, grad_all, (((0,), (0,)), ((), ())), preferred_element_type=jnp.float32
     )
-    extra = jnp.broadcast_to(group_sum, (partial_rows.shape[0], 128))
-    reduced = lax.psum_scatter(
-        jnp.concatenate([partial_rows, extra], axis=1), "wa", scatter_dimension=0, tiled=True
-    )
+    reduced = lax.psum_scatter(partial_rows.astype(jnp.bfloat16), "wa", scatter_dimension=0, tiled=True)
     rows = reduced.shape[0]
-    by_shift = reduced[:, : partial_rows.shape[1]].reshape(rows, nb, na, -1).transpose(1, 0, 2, 3)
+    by_shift = reduced.reshape(rows, nb, na, -1).transpose(1, 0, 2, 3)
     gradient_rows = natural_order(by_shift, "wb").transpose(1, 2, 0, 3).reshape(rows, -1)
     me = lax.axis_index("wb")
-    half = train_grad_rot.shape[0] // 2
+    half = train_grad_rot.shape[0] * 3 // 8
     first_rows, train_act_rot, _ = lax.optimization_barrier((train_grad_rot[:half], train_act_rot, partial_rows))
     grads_first = ring_gather(first_rows, "wb")
     act_blocks = train_act_rot.reshape(na, nb, -1, train_act_rot.shape[1])
@@ -95,7 +95,6 @@
         outgoing = lax.dynamic_index_in_dim(act_blocks, (me + shift) % nb, axis=1, keepdims=False)
         acts_near.append(lax.ppermute(outgoing, "wb", perm=[(i, (i + shift) % nb) for i in range(nb)]))
     acts_near = jnp.stack(acts_near)
-    eig_total = reduced[0, partial_rows.shape[1]]
     eig_in = eig_values.shape[0] * lax.axis_size(WIDE)
     eig_out = eig_values.shape[1]
     mean_eig = eig_total / (eig_in * eig_out)

time: 271 us -> 277 us (1.022)
  local copies, waits for them, and re-layouts: 13.4 us -> 5.79 us
  starting transfers between devices: 23.6 us -> 31.2 us
  waiting for transfers between devices: 168 us -> 174 us
    ppermute x18, waiting for transfers between devices: 61.2 us -> 85.8 us  [ring_gather(): lax.ppermute(x, axis, perm=[(i, (i + shift) % n) for i in range(n)])]
    all_gather x1, waiting for transfers between devices: 13.1 us -> 0.01 us  [shards(): act_cols = lax.all_gather(act_basis, 'wa', axis=1, tiled=True)]
    ppermute x0 -> x3, starting transfers between devices: none -> 9.17 us  [shards(): lax.ppermute(group_sum, 'wa', perm=[(i, (i + shift) % na) for i in range(...]
    ppermute x0 -> x3, waiting for transfers between devices: none -> 8.3 us  [shards(): lax.ppermute(group_sum, 'wa', perm=[(i, (i + shift) % na) for i in range(...]
    ppermute x3, waiting for transfers between devices: 37.3 us -> 30.8 us  [shards(): lax.ppermute(outgoing, 'wb', perm=[(i, (i + shift) % nb) for i in range(n...]
    all_gather x1, waiting for transfers between devices: 5.98 us -> 0.01 us  [shards(): rows_held = lax.all_gather(payload, 'wa', axis=0, tiled=True)]
  transfers between devices with their start and end apart: 31 -> 34, of which waited for: 20 -> 22; matrix products, arithmetic and copies ran while one was open for 10% -> 9% of each run, Pallas kernels for 0% -> 0%
where the time goes in v14:
time: 277 us; the launch traced here: 276 us
  waiting for transfers between devices  174 us (63%)
  starting transfers between devices  31.2 us (11%)
  matrix products  29.8 us (11%)
  between operations  18.1 us (7%)
  other arithmetic  16.2 us (6%)
  local copies, waits for them, and re-layouts  5.79 us (2%)
    ppermute x18, waiting for transfers between devices, ring_gather(): lax.ppermute(x, axis, perm=[(i, (i + shift) % n) for i in range(n)])  85.8 us
    ppermute x3, waiting for transfers between devices, shards(): lax.ppermute(eig_sum, 'wb', perm=[(i, (i + shift) % nb) for i in range(nb)])  47.3 us
    ppermute x3, waiting for transfers between devices, shards(): lax.ppermute(outgoing, 'wb', perm=[(i, (i + shift) % nb) for i in range(n...  30.8 us
    dot_general x6, matrix products, shards(): jnp.einsum('ij,sjt->sit', precond, grads_near, preferred_element_type=jnp...  19 us
    ppermute x18, starting transfers between devices, ring_gather(): lax.ppermute(x, axis, perm=[(i, (i + shift) % n) for i in range(n)])  12.7 us
    ppermute x3, starting transfers between devices, shards(): lax.ppermute(group_sum, 'wa', perm=[(i, (i + shift) % na) for i in range(...  9.17 us
    ppermute x3, waiting for transfers between devices, shards(): lax.ppermute(group_sum, 'wa', perm=[(i, (i + shift) % na) for i in range(...  8.3 us
    another operation x4, other arithmetic, ring_gather(): return jnp.stack(parts)  6.44 us
  transfers between devices with their start and end apart: 34, of which 22 were waited for; matrix products, arithmetic and copies ran while one was open for 9% of the time, Pallas kernels for 0%

profile of v14, /device:TPU:0, one launch (start us, length us, event | category | flops | bytes accessed | tf_op | source)
XLA Modules:
  0.0 275.5 jit_solution(6437768676371864473)
XLA Ops:
  6.5 0.7 all-gather.6.cloned.1.call-update
  7.3 2.5 collective-permute-start.2
  9.8 0.7 collective-permute-start.5
  10.6 1.7 convert_reduce_fusion
  12.3 1.9 collective-permute-start.9
  14.3 43.8 %collective-permute-done.9 = f32[]{:T(128)} collective-permute-done((f32[]{:T(128)}, f32[]{:T(128)}, u32[]{:S(2)}, u32[]{:S(2)}) %collective-permute-start.9) | collective-permute-done | bytes 36 | tf_op jit(solution)/shard_map/ppermute | solution.py:60
  58.1 0.6 collective-permute-start.10
  60.1 2.6 collective-permute-done.10
  63.4 0.8 collective-permute-done.11
  64.9 2.9 %collective-permute-start.12 = (f32[]{:T(128)}, f32[]{:T(128)}, u32[]{:S(2)}, u32[]{:S(2)}) collective-permute-start(f32[]{:T(128)} %add.106), channel_id=1, source_target_pairs={{0,4},{4,8},{8,12},{12,0},{1,5},{5,9},{9,13},{13,1},{2,6},{6,10},{... | collective-permute-start | bytes 20 | tf_op jit(solution)/shard_map/ppermute | solution.py:63
  67.8 2.4 collective-permute-done.12
  70.2 2.1 collective-permute-start.13
  72.3 5.9 %collective-permute-done.13 = f32[]{:T(128)} collective-permute-done((f32[]{:T(128)}, f32[]{:T(128)}, u32[]{:S(2)}, u32[]{:S(2)}) %collective-permute-start.13) | collective-permute-done | bytes 36 | tf_op jit(solution)/shard_map/ppermute | solution.py:63
  78.2 4.1 %collective-permute-start.14 = (f32[]{:T(128)}, f32[]{:T(128)}, u32[]{:S(2)}, u32[]{:S(2)}) collective-permute-start(f32[]{:T(128)} %add.106), channel_id=1, source_target_pairs={{0,12},{4,0},{8,4},{12,8},{1,13},{5,1},{9,5},{13,9},{2,14},{6,2},{... | collective-permute-start | bytes 20 | tf_op jit(solution)/shard_map/ppermute | solution.py:63
  82.3 2.5 collective-permute-start.8
  84.8 1.4 collective-permute-done.8
  86.3 1.1 collective-permute-start.7
  87.4 2.6 collective-permute-done.7
  89.9 0.8 collective-permute-start.6
  90.7 2.3 collective-permute-done.6
  93.0 1.1 collective-permute-start.1
  96.1 0.7 pad_add_fusion
  96.8 11.3 %collective-permute-done.1 = bf16[128,2048]{1,0:T(8,128)(2,1)S(1)} collective-permute-done((bf16[128,2048]{1,0:T(8,128)(2,1)}, bf16[128,2048]{1,0:T(8,128)(2,1)S(1)}, u32[]{:S(2)}, u32[]{:S(2)}) %collective-permute-start.1) | collective-permute-done | bytes 524320 | tf_op jit(solution)/shard_map/ppermute | solution.py:29
  108.1 3.6 %collective-permute-done = bf16[128,2048]{1,0:T(8,128)(2,1)S(1)} collective-permute-done((bf16[128,2048]{1,0:T(8,128)(2,1)}, bf16[128,2048]{1,0:T(8,128)(2,1)S(1)}, u32[]{:S(2)}, u32[]{:S(2)}) %collective-permute-start) | collective-permute-done | bytes 524320 | tf_op jit(solution)/shard_map/ppermute | solution.py:29
  111.7 0.8 copy-done.7
  112.5 1.9 pad_maximum_fusion.2
  114.4 3.5 %pad_maximum_fusion = bf16[4,128,4096]{2,1,0:T(8,128)(2,1)} fusion(bf16[1,128,4096]{2,1,0:T(8,128)(2,1)S(1)} %bitcast.116, bf16[1,128,4096]{2,1,0:T(8,128)(2,1)} %bitcast.6, bf16[1,128,4096]{2,1,0:T(8,128)(2,1)} %bitcast.5, bf16[1,128,4096]{2,1,0:T(8,128)(2,1)S(1)} %bitcast.115), kind=kLoop, calls=%fused_computation.13 | loop fusion | flops 6291456 | bytes 8388608 | tf_op jit(solution)/shard_map/stack | solution.py:30
  117.9 5.8 %fusion.20 = bf16[512,512]{1,0:T(8,128)(2,1)S(1)} fusion(bf16[512,4096]{1,0:T(8,128)(2,1)} %bitcast.110, bf16[4096,512]{1,0:T(8,128)(2,1)} %all-gather.6.cloned.1.call-done, bf16[512]{0:T(512)(128)(2,1)S(1)} %fusion.54), kind=kOutput, calls=%fused_computation.43 | convolution fusion | flops 2148007936 | bytes 8913920 | tf_op jit(solution)/shard_map/dot_general | solution.py:73
  124.1 1.0 collective-permute-start.16
  125.3 2.0 convolution_convert_fusion.1
  127.4 8.6 %collective-permute-done.17 = bf16[512,512]{1,0:T(8,128)(2,1)} collective-permute-done((bf16[512,512]{1,0:T(8,128)(2,1)S(1)}, bf16[512,512]{1,0:T(8,128)(2,1)}, u32[]{:S(2)}, u32[]{:S(2)}) %collective-permute-start.17) | collective-permute-done | bytes 524320 | tf_op jit(solution)/shard_map/ppermute | solution.py:29
  136.0 12.6 %collective-permute-done.16 = bf16[512,512]{1,0:T(8,128)(2,1)} collective-permute-done((bf16[512,512]{1,0:T(8,128)(2,1)S(1)}, bf16[512,512]{1,0:T(8,128)(2,1)}, u32[]{:S(2)}, u32[]{:S(2)}) %collective-permute-start.16) | collective-permute-done | bytes 524320 | tf_op jit(solution)/shard_map/ppermute | solution.py:29
  148.6 0.6 collective-permute-done.15
  149.1 3.1 %fusion.6 = bf16[256,2048]{1,0:T(8,128)(2,1)} fusion(bf16[512,256]{1,0:T(8,128)(2,1)S(1)} %bitcast.136, bf16[512,512]{1,0:T(8,128)(2,1)} %collective-permute-done.17, bf16[512,512]{1,0:T(8,128)(2,1)} %collective-permute-done.16, bf16[512,512]{1,0:T(8,128)(2,1)} %collective-permute-done.15, bf16[512,512]{1,0:T(8,128)(2,1)S(1)} %bitcast.131), kind=kOutput, calls=%fused_computation.28 | convolution fusion | flops 545259520 | bytes 3407872 | tf_op jit(solution)/shard_map/dot_general | solution.py:81
  152.3 1.2 slice.42
  153.6 1.1 collective-permute-start.19
  155.0 1.6 collective-permute-start.23
  156.6 1.0 collective-permute-start.22
  157.6 26.0 %collective-permute-done.23 = bf16[4,64,384]{2,1,0:T(8,128)(2,1)S(1)} collective-permute-done((bf16[4,64,384]{2,1,0:T(8,128)(2,1)S(1)}, bf16[4,64,384]{2,1,0:T(8,128)(2,1)S(1)}, u32[]{:S(2)}, u32[]{:S(2)}) %collective-permute-start.23) | collective-permute-done | bytes 196640 | tf_op jit(solution)/shard_map/ppermute | solution.py:96
  183.6 1.5 collective-permute-start.21
  185.1 3.7 %collective-permute-done.22 = bf16[4,64,384]{2,1,0:T(8,128)(2,1)S(1)} collective-permute-done((bf16[4,64,384]{2,1,0:T(8,128)(2,1)S(1)}, bf16[4,64,384]{2,1,0:T(8,128)(2,1)S(1)}, u32[]{:S(2)}, u32[]{:S(2)}) %collective-permute-start.22) | collective-permute-done | bytes 196640 | tf_op jit(solution)/shard_map/ppermute | solution.py:96
  188.8 1.1 collective-permute-done.21
  189.9 1.0 pad_maximum_fusion.3
  190.9 0.4 pad_maximum_fusion.1
  191.3 1.2 reshape.49
  193.3 0.8 pad_maximum_fusion.4
  194.1 1.3 slice.43
  195.5 1.0 collective-permute-start.25
  196.7 0.7 fusion.56
  197.4 19.8 %collective-permute-done.26 = bf16[1280,384]{1,0:T(8,128)(2,1)} collective-permute-done((bf16[1280,384]{1,0:T(8,128)(2,1)S(1)}, bf16[1280,384]{1,0:T(8,128)(2,1)}, u32[]{:S(2)}, u32[]{:S(2)}) %collective-permute-start.26) | collective-permute-done | bytes 983072 | tf_op jit(solution)/shard_map/ppermute | solution.py:29
  217.2 22.4 %collective-permute-done.25 = bf16[1280,384]{1,0:T(8,128)(2,1)} collective-permute-done((bf16[1280,384]{1,0:T(8,128)(2,1)S(1)}, bf16[1280,384]{1,0:T(8,128)(2,1)}, u32[]{:S(2)}, u32[]{:S(2)}) %collective-permute-start.25) | collective-permute-done | bytes 983072 | tf_op jit(solution)/shard_map/ppermute | solution.py:29
  239.7 0.6 collective-permute-done.24
  240.2 4.9 %maximum_maximum_fusion = bf16[4,2048,384]{2,1,0:T(8,128)(2,1)} fusion(bf16[1,1280,384]{2,1,0:T(8,128)(2,1)} %bitcast.36, bf16[1,1280,384]{2,1,0:T(8,128)(2,1)} %bitcast.35, bf16[1,1280,384]{2,1,0:T(8,128)(2,1)} %bitcast.34, bf16[1,1280,384]{2,1,0:T(8,128)(2,1)S(1)} %bitcast.111, bf16[4,768,384]{2,1,0:T(8,128)(2,1)S(1)} %pad_maximum_fusion.1), kind=kLoop, calls=%fused_computation | loop fusion | flops 31457280 | bytes 12582912 | tf_op jit(solution)/shard_map/concatenate | solution.py:108
  245.2 6.5 %fusion.14 = f32[4,384]{1,0:T(4,128)S(1)} fusion(bf16[4,256,384]{2,1,0:T(8,128)(2,1)} %bitcast.118, bf16[4,2048,384]{2,1,0:T(8,128)(2,1)} %maximum_maximum_fusion, f32[]{:T(128)} %bitcast.37, bf16[256,4096]{1,0:T(8,128)(2,1)} %all-gather.8.cloned.1.call-done), kind=kOutput, calls=%fused_computation.36 | convolution fusion | flops 1614412288 | bytes 9181188 | tf_op jit(solution)/shard_map/ij,sjt->sit/dot_general | solution.py:115
  251.7 2.4 fusion.15
  254.2 2.6 fusion.16
  256.7 2.5 fusion.17
  259.3 2.5 fusion.18
  261.8 2.5 fusion.19
  264.5 1.1 collective-permute-start.28
  265.6 1.4 collective-permute-start.27
  267.0 0.6 collective-permute-done.29
  267.6 0.7 collective-permute-done.28
  268.4 0.6 fusion.53
  (72 shorter events, 2.7 us)
Async XLA Ops:
  6.5 111.4 %all-gather.6.cloned.1.call-start = ((), (), s32[]{:S(2)}) async-start(), calls=%async_computation.2 | async-start | bytes 5242880 | tf_op jit(solution)/shard_map/all_gather | solution.py:68
  7.3 118.0 %all-gather.4.cloned.1.call-start = ((), (), s32[]{:S(2)}) async-start(), calls=%async_computation.1 | async-start | bytes 1310720 | tf_op jit(solution)/shard_map/all_gather | solution.py:67
  7.3 86.8 %collective-permute-start.2 = (bf16[128,2048]{1,0:T(8,128)(2,1)}, bf16[128,2048]{1,0:T(8,128)(2,1)S(1)}, u32[]{:S(2)}, u32[]{:S(2)}) collective-permute-start(bf16[128,2048]{1,0:T(8,128)(2,1)} %param.10), channel_id=1, source_target_pairs={{0,3},{1,0},{2,1},{3,2},{4,7},{5,4},{6,5},{7,6},{8,11},{9,8},{10,9... | collective-permute-start | bytes 1572872 | tf_op jit(solution)/shard_map/ppermute | solution.py:29
  9.8 104.6 %collective-permute-start.5 = (bf16[128,4096]{1,0:T(8,128)(2,1)}, bf16[128,4096]{1,0:T(8,128)(2,1)S(1)}, u32[]{:S(2)}, u32[]{:S(2)}) collective-permute-start(bf16[128,4096]{1,0:T(8,128)(2,1)} %param.11), channel_id=1, source_target_pairs={{0,3},{1,0},{2,1},{3,2},{4,7},{5,4},{6,5},{7,6},{8,11},{9,8},{10,9... | collective-permute-start | bytes 3145736 | tf_op jit(solution)/shard_map/ppermute | solution.py:29
  10.4 103.9 %collective-permute-start.4 = (bf16[128,4096]{1,0:T(8,128)(2,1)}, bf16[128,4096]{1,0:T(8,128)(2,1)}, u32[]{:S(2)}, u32[]{:S(2)}) collective-permute-start(bf16[128,4096]{1,0:T(8,128)(2,1)} %param.11), channel_id=1, source_target_pairs={{0,2},{1,3},{2,0},{3,1},{4,6},{5,7},{6,4},{7,5},{8,10},{9,11},{10,... | collective-permute-start | bytes 3145736 | tf_op jit(solution)/shard_map/ppermute | solution.py:29
  10.5 103.9 %collective-permute-start.3 = (bf16[128,4096]{1,0:T(8,128)(2,1)}, bf16[128,4096]{1,0:T(8,128)(2,1)}, u32[]{:S(2)}, u32[]{:S(2)}) collective-permute-start(bf16[128,4096]{1,0:T(8,128)(2,1)} %param.11), channel_id=1, source_target_pairs={{0,1},{1,2},{2,3},{3,0},{4,5},{5,6},{6,7},{7,4},{8,9},{9,10},{10,1... | collective-permute-start | bytes 3145736 | tf_op jit(solution)/shard_map/ppermute | solution.py:29
  12.3 45.8 %collective-permute-start.9 = (f32[]{:T(128)}, f32[]{:T(128)}, u32[]{:S(2)}, u32[]{:S(2)}) collective-permute-start(f32[]{:T(128)} %convert_reduce_fusion), channel_id=1, source_target_pairs={{0,1},{1,2},{2,3},{3,0},{4,5},{5,6},{6,7},{7,4},{8,9},{9,10},{10,1... | collective-permute-start | bytes 20 | tf_op jit(solution)/shard_map/ppermute | solution.py:60
  58.1 4.6 %collective-permute-start.10 = (f32[]{:T(128)}, f32[]{:T(128)}, u32[]{:S(2)}, u32[]{:S(2)}) collective-permute-start(f32[]{:T(128)} %convert_reduce_fusion), channel_id=1, source_target_pairs={{0,2},{1,3},{2,0},{3,1},{4,6},{5,7},{6,4},{7,5},{8,10},{9,11},{10,... | collective-permute-start | bytes 20 | tf_op jit(solution)/shard_map/ppermute | solution.py:60
  62.8 1.4 collective-permute-start.11
  64.9 5.3 %collective-permute-start.12 = (f32[]{:T(128)}, f32[]{:T(128)}, u32[]{:S(2)}, u32[]{:S(2)}) collective-permute-start(f32[]{:T(128)} %add.106), channel_id=1, source_target_pairs={{0,4},{4,8},{8,12},{12,0},{1,5},{5,9},{9,13},{13,1},{2,6},{6,10},{... | collective-permute-start | bytes 20 | tf_op jit(solution)/shard_map/ppermute | solution.py:63
  70.2 8.0 %collective-permute-start.13 = (f32[]{:T(128)}, f32[]{:T(128)}, u32[]{:S(2)}, u32[]{:S(2)}) collective-permute-start(f32[]{:T(128)} %add.106), channel_id=1, source_target_pairs={{0,8},{4,12},{8,0},{12,4},{1,9},{5,13},{9,1},{13,5},{2,10},{6,14},... | collective-permute-start | bytes 20 | tf_op jit(solution)/shard_map/ppermute | solution.py:63
  78.2 4.1 %collective-permute-start.14 = (f32[]{:T(128)}, f32[]{:T(128)}, u32[]{:S(2)}, u32[]{:S(2)}) collective-permute-start(f32[]{:T(128)} %add.106), channel_id=1, source_target_pairs={{0,12},{4,0},{8,4},{12,8},{1,13},{5,1},{9,5},{13,9},{2,14},{6,2},{... | collective-permute-start | bytes 20 | tf_op jit(solution)/shard_map/ppermute | solution.py:63
  82.3 3.9 %collective-permute-start.8 = (s32[128]{0:T(128)}, s32[128]{0:T(128)S(1)}, u32[]{:S(2)}, u32[]{:S(2)}) collective-permute-start(s32[128]{0:T(128)} %param.12), channel_id=1, source_target_pairs={{0,3},{1,0},{2,1},{3,2},{4,7},{5,4},{6,5},{7,6},{8,11},{9,8},{10,9... | collective-permute-start | bytes 1544 | tf_op jit(solution)/shard_map/ppermute | solution.py:29
  86.3 3.7 %collective-permute-start.7 = (s32[128]{0:T(128)}, s32[128]{0:T(128)S(1)}, u32[]{:S(2)}, u32[]{:S(2)}) collective-permute-start(s32[128]{0:T(128)} %param.12), channel_id=1, source_target_pairs={{0,2},{1,3},{2,0},{3,1},{4,6},{5,7},{6,4},{7,5},{8,10},{9,11},{10,... | collective-permute-start | bytes 1544 | tf_op jit(solution)/shard_map/ppermute | solution.py:29
  89.9 3.1 %collective-permute-start.6 = (s32[128]{0:T(128)}, s32[128]{0:T(128)S(1)}, u32[]{:S(2)}, u32[]{:S(2)}) collective-permute-start(s32[128]{0:T(128)} %param.12), channel_id=1, source_target_pairs={{0,1},{1,2},{2,3},{3,0},{4,5},{5,6},{6,7},{7,4},{8,9},{9,10},{10,1... | collective-permute-start | bytes 1544 | tf_op jit(solution)/shard_map/ppermute | solution.py:29
  93.0 15.1 %collective-permute-start.1 = (bf16[128,2048]{1,0:T(8,128)(2,1)}, bf16[128,2048]{1,0:T(8,128)(2,1)S(1)}, u32[]{:S(2)}, u32[]{:S(2)}) collective-permute-start(bf16[128,2048]{1,0:T(8,128)(2,1)} %param.10), channel_id=1, source_target_pairs={{0,2},{1,3},{2,0},{3,1},{4,6},{5,7},{6,4},{7,5},{8,10},{9,11},{10,... | collective-permute-start | bytes 1572872 | tf_op jit(solution)/shard_map/ppermute | solution.py:29
  94.1 17.5 %copy-start.5 = (bf16[128,2048]{1,0:T(8,128)(2,1)}, bf16[128,2048]{1,0:T(8,128)(2,1)S(1)}, u32[]{:S(2)}) copy-start(bf16[128,2048]{1,0:T(8,128)(2,1)S(1)} %collective-permute-done.2) | copy-start | bytes 1572868
  94.1 17.5 %collective-permute-start = (bf16[128,2048]{1,0:T(8,128)(2,1)}, bf16[128,2048]{1,0:T(8,128)(2,1)S(1)}, u32[]{:S(2)}, u32[]{:S(2)}) collective-permute-start(bf16[128,2048]{1,0:T(8,128)(2,1)} %param.10), channel_id=1, source_target_pairs={{0,1},{1,2},{2,3},{3,0},{4,5},{5,6},{6,7},{7,4},{8,9},{9,10},{10,1... | collective-permute-start | bytes 1572872 | tf_op jit(solution)/shard_map/ppermute | solution.py:29
  94.2 97.2 %reduce-scatter.2.cloned.1.call-start = ((), (), s32[]{:S(2)}) async-start(), calls=%async_computation.3 | async-start | bytes 1310720 | tf_op jit(solution)/shard_map/reduce_scatter | solution.py:84
  108.1 3.6 %copy-start.6 = (bf16[128,2048]{1,0:T(8,128)(2,1)}, bf16[128,2048]{1,0:T(8,128)(2,1)S(1)}, u32[]{:S(2)}) copy-start(bf16[128,2048]{1,0:T(8,128)(2,1)S(1)} %collective-permute-done.1) | copy-start | bytes 1572868
  111.7 0.8 copy-start.7
  112.5 1.9 copy-start.2
  124.0 11.9 %collective-permute-start.17 = (bf16[512,512]{1,0:T(8,128)(2,1)S(1)}, bf16[512,512]{1,0:T(8,128)(2,1)}, u32[]{:S(2)}, u32[]{:S(2)}) collective-permute-start(bf16[512,512]{1,0:T(8,128)(2,1)S(1)} %bitcast.128), channel_id=1, source_target_pairs={{0,3},{1,0},{2,1},{3,2},{4,7},{5,4},{6,5},{7,6},{8,11},{9,8},{10,9... | collective-permute-start | bytes 1572872 | tf_op jit(solution)/shard_map/ppermute | solution.py:29
  124.1 24.5 %collective-permute-start.16 = (bf16[512,512]{1,0:T(8,128)(2,1)S(1)}, bf16[512,512]{1,0:T(8,128)(2,1)}, u32[]{:S(2)}, u32[]{:S(2)}) collective-permute-start(bf16[512,512]{1,0:T(8,128)(2,1)S(1)} %bitcast.129), channel_id=1, source_target_pairs={{0,2},{1,3},{2,0},{3,1},{4,6},{5,7},{6,4},{7,5},{8,10},{9,11},{10,... | collective-permute-start | bytes 1572872 | tf_op jit(solution)/shard_map/ppermute | solution.py:29
  125.1 24.0 %collective-permute-start.15 = (bf16[512,512]{1,0:T(8,128)(2,1)S(1)}, bf16[512,512]{1,0:T(8,128)(2,1)}, u32[]{:S(2)}, u32[]{:S(2)}) collective-permute-start(bf16[512,512]{1,0:T(8,128)(2,1)S(1)} %bitcast.130), channel_id=1, source_target_pairs={{0,1},{1,2},{2,3},{3,0},{4,5},{5,6},{6,7},{7,4},{8,9},{9,10},{10,1... | collective-permute-start | bytes 1572872 | tf_op jit(solution)/shard_map/ppermute | solution.py:29
  152.2 2.7 copy-start.3
  152.2 93.0 %all-gather.8.cloned.1.call-start = ((), (), s32[]{:S(2)}) async-start(), calls=%async_computation.4 | async-start | bytes 2621440 | tf_op jit(solution)/shard_map/all_gather | solution.py:106
  153.5 37.4 %collective-permute-start.20 = (bf16[768,384]{1,0:T(8,128)(2,1)S(1)}, bf16[768,384]{1,0:T(8,128)(2,1)S(1)}, u32[]{:S(2)}, u32[]{:S(2)}) collective-permute-start(bf16[768,384]{1,0:T(8,128)(2,1)S(1)} %slice.42), channel_id=1, source_target_pairs={{0,3},{1,0},{2,1},{3,2},{4,7},{5,4},{6,5},{7,6},{8,11},{9,8},{10,9... | collective-permute-start | bytes 1769480 | tf_op jit(solution)/shard_map/ppermute | solution.py:29
  153.6 37.3 %collective-permute-start.19 = (bf16[768,384]{1,0:T(8,128)(2,1)S(1)}, bf16[768,384]{1,0:T(8,128)(2,1)S(1)}, u32[]{:S(2)}, u32[]{:S(2)}) collective-permute-start(bf16[768,384]{1,0:T(8,128)(2,1)S(1)} %slice.42), channel_id=1, source_target_pairs={{0,2},{1,3},{2,0},{3,1},{4,6},{5,7},{6,4},{7,5},{8,10},{9,11},{10,... | collective-permute-start | bytes 1769480 | tf_op jit(solution)/shard_map/ppermute | solution.py:29
  154.7 36.2 %collective-permute-start.18 = (bf16[768,384]{1,0:T(8,128)(2,1)S(1)}, bf16[768,384]{1,0:T(8,128)(2,1)S(1)}, u32[]{:S(2)}, u32[]{:S(2)}) collective-permute-start(bf16[768,384]{1,0:T(8,128)(2,1)S(1)} %slice.42), channel_id=1, source_target_pairs={{0,1},{1,2},{2,3},{3,0},{4,5},{5,6},{6,7},{7,4},{8,9},{9,10},{10,1... | collective-permute-start | bytes 1769480 | tf_op jit(solution)/shard_map/ppermute | solution.py:29
  155.0 28.6 %collective-permute-start.23 = (bf16[4,64,384]{2,1,0:T(8,128)(2,1)S(1)}, bf16[4,64,384]{2,1,0:T(8,128)(2,1)S(1)}, u32[]{:S(2)}, u32[]{:S(2)}) collective-permute-start(bf16[4,64,384]{2,1,0:T(8,128)(2,1)S(1)} %get-tuple-element.26), channel_id=1, source_target_pairs={{0,3},{1,0},{2,1},{3,2},{4,7},{5,4},{6,5},{7,6},{8,11},{9,8},{10,9... | collective-permute-start | bytes 589832 | tf_op jit(solution)/shard_map/ppermute | solution.py:96
  156.6 32.1 %collective-permute-start.22 = (bf16[4,64,384]{2,1,0:T(8,128)(2,1)S(1)}, bf16[4,64,384]{2,1,0:T(8,128)(2,1)S(1)}, u32[]{:S(2)}, u32[]{:S(2)}) collective-permute-start(bf16[4,64,384]{2,1,0:T(8,128)(2,1)S(1)} %get-tuple-element.27), channel_id=1, source_target_pairs={{0,2},{1,3},{2,0},{3,1},{4,6},{5,7},{6,4},{7,5},{8,10},{9,11},{10,... | collective-permute-start | bytes 589832 | tf_op jit(solution)/shard_map/ppermute | solution.py:96
  183.6 6.3 %collective-permute-start.21 = (bf16[4,64,384]{2,1,0:T(8,128)(2,1)S(1)}, bf16[4,64,384]{2,1,0:T(8,128)(2,1)S(1)}, u32[]{:S(2)}, u32[]{:S(2)}) collective-permute-start(bf16[4,64,384]{2,1,0:T(8,128)(2,1)S(1)} %get-tuple-element.28), channel_id=1, source_target_pairs={{0,1},{1,2},{2,3},{3,0},{4,5},{5,6},{6,7},{7,4},{8,9},{9,10},{10,1... | collective-permute-start | bytes 589832 | tf_op jit(solution)/shard_map/ppermute | solution.py:96
  191.3 2.0 copy-start.1
  193.1 3.6 %copy-start.10 = (s32[6]{0:T(128)S(1)}, s32[6]{0:T(128)}, u32[]{:S(2)}) copy-start(s32[6]{0:T(128)} %param.16) | copy-start | bytes 76
  195.4 21.8 %collective-permute-start.26 = (bf16[1280,384]{1,0:T(8,128)(2,1)S(1)}, bf16[1280,384]{1,0:T(8,128)(2,1)}, u32[]{:S(2)}, u32[]{:S(2)}) collective-permute-start(bf16[1280,384]{1,0:T(8,128)(2,1)S(1)} %slice.43), channel_id=1, source_target_pairs={{0,3},{1,0},{2,1},{3,2},{4,7},{5,4},{6,5},{7,6},{8,11},{9,8},{10,9... | collective-permute-start | bytes 2949128 | tf_op jit(solution)/shard_map/ppermute | solution.py:29
  195.5 44.2 %collective-permute-start.25 = (bf16[1280,384]{1,0:T(8,128)(2,1)S(1)}, bf16[1280,384]{1,0:T(8,128)(2,1)}, u32[]{:S(2)}, u32[]{:S(2)}) collective-permute-start(bf16[1280,384]{1,0:T(8,128)(2,1)S(1)} %slice.43), channel_id=1, source_target_pairs={{0,2},{1,3},{2,0},{3,1},{4,6},{5,7},{6,4},{7,5},{8,10},{9,11},{10,... | collective-permute-start | bytes 2949128 | tf_op jit(solution)/shard_map/ppermute | solution.py:29
  196.5 43.7 %collective-permute-start.24 = (bf16[1280,384]{1,0:T(8,128)(2,1)S(1)}, bf16[1280,384]{1,0:T(8,128)(2,1)}, u32[]{:S(2)}, u32[]{:S(2)}) collective-permute-start(bf16[1280,384]{1,0:T(8,128)(2,1)S(1)} %slice.43), channel_id=1, source_target_pairs={{0,1},{1,2},{2,3},{3,0},{4,5},{5,6},{6,7},{7,4},{8,9},{9,10},{10,1... | collective-permute-start | bytes 2949128 | tf_op jit(solution)/shard_map/ppermute | solution.py:29
  245.2 6.5 %copy-start = (bf16[4,2048,384]{2,1,0:T(8,128)(2,1)S(1)}, bf16[4,2048,384]{2,1,0:T(8,128)(2,1)}, u32[]{:S(2)}) copy-start(bf16[4,2048,384]{2,1,0:T(8,128)(2,1)} %maximum_maximum_fusion) | copy-start | bytes 18874372
  245.2 6.5 %copy-start.4 = (bf16[4,4,64,384]{3,2,1,0:T(8,128)(2,1)S(1)}, bf16[4,4,64,384]{3,2,1,0:T(8,128)(2,1)}, u32[]{:S(2)}) copy-start(bf16[4,4,64,384]{3,2,1,0:T(8,128)(2,1)} %pad_maximum_fusion.3) | copy-start | bytes 2359300
  245.2 6.5 %copy-start.9 = (bf16[256,4096]{1,0:T(8,128)(2,1)S(1)}, bf16[256,4096]{1,0:T(8,128)(2,1)}, u32[]{:S(2)}) copy-start(bf16[256,4096]{1,0:T(8,128)(2,1)} %all-gather.8.cloned.1.call-done) | copy-start | bytes 6291460
  261.8 5.2 %copy-start.8 = (s32[384]{0:T(512)S(1)}, s32[384]{0:T(512)}, u32[]{:S(2)}) copy-start(s32[384]{0:T(512)} %param.19) | copy-start | bytes 4612
  264.4 3.2 %collective-permute-start.29 = (f32[6,384]{1,0:T(8,128)S(1)}, f32[6,384]{1,0:T(8,128)S(1)}, u32[]{:S(2)}, u32[]{:S(2)}) collective-permute-start(f32[6,384]{1,0:T(8,128)S(1)} %get-tuple-element.30), channel_id=1, source_target_pairs={{0,1},{1,2},{2,3},{3,0},{4,5},{5,6},{6,7},{7,4},{8,9},{9,10},{10,1... | collective-permute-start | bytes 27656 | tf_op jit(solution)/shard_map/ppermute | solution.py:120
  264.5 3.8 %collective-permute-start.28 = (f32[6,384]{1,0:T(8,128)S(1)}, f32[6,384]{1,0:T(8,128)S(1)}, u32[]{:S(2)}, u32[]{:S(2)}) collective-permute-start(f32[6,384]{1,0:T(8,128)S(1)} %get-tuple-element.31), channel_id=1, source_target_pairs={{0,2},{1,3},{2,0},{3,1},{4,6},{5,7},{6,4},{7,5},{8,10},{9,11},{10,... | collective-permute-start | bytes 27656 | tf_op jit(solution)/shard_map/ppermute | solution.py:120
  265.6 2.8 %collective-permute-start.27 = (f32[6,384]{1,0:T(8,128)S(1)}, f32[6,384]{1,0:T(8,128)S(1)}, u32[]{:S(2)}, u32[]{:S(2)}) collective-permute-start(f32[6,384]{1,0:T(8,128)S(1)} %get-tuple-element.29), channel_id=1, source_target_pairs={{0,3},{1,0},{2,1},{3,2},{4,7},{5,4},{6,5},{7,6},{8,11},{9,8},{10,9... | collective-permute-start | bytes 27656 | tf_op jit(solution)/shard_map/ppermute | solution.py:120
Sparse Core Ops, SparseCore 0:
  8.9 83.2 all-gather.5
  94.3 28.1 all-gather.3
  152.3 26.5 reduce-scatter.1
  194.3 44.8 all-gather.7

commit v15 on v12

--- a/solution.py
+++ b/solution.py
@@ -64,6 +64,8 @@
     act_cols = lax.all_gather(act_basis, "wa", axis=1, tiled=True)
     grad_cols = lax.all_gather(grad_basis, "wa", axis=1, tiled=True)
     count = query_act.shape[0]
+    eig_ready, _ = lax.optimization_barrier((eig_values, act_cols))
+    eig_held = lax.all_gather(eig_ready, "wa", axis=0, tiled=True)
     act_rot = jnp.dot(
         act_tokens.reshape(nb * count, -1), act_cols, preferred_element_type=jnp.float32
     ).astype(jnp.bfloat16)
@@ -79,6 +81,7 @@
         act_rot, grad_all, (((0,), (0,)), ((), ())), preferred_element_type=jnp.float32
     )
     extra = jnp.broadcast_to(group_sum, (partial_rows.shape[0], 128))
+    partial_rows, eig_held = lax.optimization_barrier((partial_rows, eig_held))
     reduced = lax.psum_scatter(
         jnp.concatenate([partial_rows, extra], axis=1), "wa", scatter_dimension=0, tiled=True
     )
@@ -86,7 +89,7 @@
     by_shift = reduced[:, : partial_rows.shape[1]].reshape(rows, nb, na, -1).transpose(1, 0, 2, 3)
     gradient_rows = natural_order(by_shift, "wb").transpose(1, 2, 0, 3).reshape(rows, -1)
     me = lax.axis_index("wb")
-    half = train_grad_rot.shape[0] // 2
+    half = train_grad_rot.shape[0] * 5 // 8
     first_rows, train_act_rot, _ = lax.optimization_barrier((train_grad_rot[:half], train_act_rot, partial_rows))
     grads_first = ring_gather(first_rows, "wb")
     act_blocks = train_act_rot.reshape(na, nb, -1, train_act_rot.shape[1])
@@ -100,12 +103,11 @@
     eig_out = eig_values.shape[1]
     mean_eig = eig_total / (eig_in * eig_out)
     dampings = mean_eig * jnp.exp2(damping_index.astype(jnp.float32) - 4.0)
-    payload = jnp.concatenate([gradient_rows.astype(jnp.bfloat16), eig_values], axis=1)
+    payload = gradient_rows.astype(jnp.bfloat16)
     grads_first, acts_near, payload = lax.optimization_barrier((grads_first, acts_near, payload))
     second_rows, _ = lax.optimization_barrier((train_grad_rot[half:], payload))
     grads_second = ring_gather(second_rows, "wb")
-    rows_held = lax.all_gather(payload, "wa", axis=0, tiled=True)
-    gradient_held, eig_held = rows_held[:, :eig_out], rows_held[:, eig_out:]
+    gradient_held = lax.all_gather(payload, "wa", axis=0, tiled=True)
     grads_near = jnp.concatenate([grads_first, grads_second], axis=1)
     acts_near = acts_near.reshape(nb, na * act_blocks.shape[2], -1).astype(jnp.float32)
     grad_wide = gradient_held.astype(jnp.float32)

time: 271 us -> 284 us (1.048)
  waiting for transfers between devices: 168 us -> 183 us
  local copies, waits for them, and re-layouts: 13.4 us -> 9.72 us
    all_gather x1, waiting for transfers between devices: 0.01 us -> 20.7 us  [shards(): grad_cols = lax.all_gather(grad_basis, 'wa', axis=1, tiled=True)]
    all_gather x1, waiting for transfers between devices: 13.1 us -> 0.01 us  [shards(): act_cols = lax.all_gather(act_basis, 'wa', axis=1, tiled=True)]
    ppermute x3, waiting for transfers between devices: 37.3 us -> 45.4 us  [shards(): lax.ppermute(outgoing, 'wb', perm=[(i, (i + shift) % nb) for i in range(n...]
    all_gather x1 -> x2, waiting for transfers between devices: 5.98 us -> 0.02 us  [the longest x1 0.02 us: shards(): eig_held = lax.all_gather(eig_ready, 'wa', axis=0, tiled=True)]
    ppermute x18, waiting for transfers between devices: 61.2 us -> 65.8 us  [ring_gather(): lax.ppermute(x, axis, perm=[(i, (i + shift) % n) for i in range(n)])]
  transfers between devices with their start and end apart: 31 -> 32, of which waited for: 20 -> 19; matrix products, arithmetic and copies ran while one was open for 10% -> 11% of each run, Pallas kernels for 0% -> 0%
where the time goes in v15:
time: 284 us; the launch traced here: 283 us
  waiting for transfers between devices  183 us (64%)
  matrix products  28.7 us (10%)
  starting transfers between devices  24.5 us (9%)
  other arithmetic  19.2 us (7%)
  between operations  17.4 us (6%)
  local copies, waits for them, and re-layouts  9.72 us (3%)
    ppermute x18, waiting for transfers between devices, ring_gather(): lax.ppermute(x, axis, perm=[(i, (i + shift) % n) for i in range(n)])  65.8 us
    ppermute x3, waiting for transfers between devices, shards(): lax.ppermute(eig_sum, 'wb', perm=[(i, (i + shift) % nb) for i in range(nb)])  49.3 us
    ppermute x3, waiting for transfers between devices, shards(): lax.ppermute(outgoing, 'wb', perm=[(i, (i + shift) % nb) for i in range(n...  45.4 us
    all_gather x1, waiting for transfers between devices, shards(): grad_cols = lax.all_gather(grad_basis, 'wa', axis=1, tiled=True)  20.7 us
    dot_general x6, matrix products, shards(): jnp.einsum('ij,sjt->sit', precond, grads_near, preferred_element_type=jnp...  18.7 us
    ppermute x18, starting transfers between devices, ring_gather(): lax.ppermute(x, axis, perm=[(i, (i + shift) % n) for i in range(n)])  13.8 us
    another operation x4, other arithmetic, ring_gather(): return jnp.stack(parts)  9.47 us
    dot_general x1, matrix products, shards(): jnp.dot(grad_tokens.reshape(nb * count, -1), grad_cols, preferred_element...  5.79 us
  transfers between devices with their start and end apart: 32, of which 19 were waited for; matrix products, arithmetic and copies ran while one was open for 11% of the time, Pallas kernels for 0%

profile of v15, /device:TPU:0, one launch (start us, length us, event | category | flops | bytes accessed | tf_op | source)
XLA Modules:
  0.0 282.9 jit_solution(17447484695278143266)
XLA Ops:
  6.5 0.7 all-gather.5.cloned.1.call-update
  7.3 0.7 all-gather.7.cloned.1.call-update
  8.1 2.5 collective-permute-start.2
  10.5 0.7 collective-permute-start.5
  11.4 1.7 convert_reduce_fusion
  13.1 1.9 collective-permute-start.9
  15.0 43.8 %collective-permute-done.9 = f32[]{:T(128)} collective-permute-done((f32[]{:T(128)}, f32[]{:T(128)}, u32[]{:S(2)}, u32[]{:S(2)}) %collective-permute-start.9) | collective-permute-done | bytes 36 | tf_op jit(solution)/shard_map/ppermute | solution.py:60
  58.9 0.6 collective-permute-start.10
  59.5 4.1 %collective-permute-done.10 = f32[]{:T(128)} collective-permute-done((f32[]{:T(128)}, f32[]{:T(128)}, u32[]{:S(2)}, u32[]{:S(2)}) %collective-permute-start.10) | collective-permute-done | bytes 36 | tf_op jit(solution)/shard_map/ppermute | solution.py:60
  63.6 1.4 collective-permute-done.11
  65.0 2.1 collective-permute-start.8
  67.1 1.4 collective-permute-done.8
  68.5 1.5 collective-permute-start.7
  70.0 2.2 collective-permute-done.7
  72.2 1.1 collective-permute-start.6
  73.3 2.0 collective-permute-done.6
  75.3 1.5 collective-permute-start.1
  79.3 0.7 pad_add_fusion
  80.0 10.4 %collective-permute-done.1 = bf16[128,2048]{1,0:T(8,128)(2,1)S(1)} collective-permute-done((bf16[128,2048]{1,0:T(8,128)(2,1)}, bf16[128,2048]{1,0:T(8,128)(2,1)S(1)}, u32[]{:S(2)}, u32[]{:S(2)}) %collective-permute-start.1) | collective-permute-done | bytes 524320 | tf_op jit(solution)/shard_map/ppermute | solution.py:29
  90.3 3.9 %collective-permute-done = bf16[128,2048]{1,0:T(8,128)(2,1)S(1)} collective-permute-done((bf16[128,2048]{1,0:T(8,128)(2,1)}, bf16[128,2048]{1,0:T(8,128)(2,1)S(1)}, u32[]{:S(2)}, u32[]{:S(2)}) %collective-permute-start) | collective-permute-done | bytes 524320 | tf_op jit(solution)/shard_map/ppermute | solution.py:29
  94.3 0.8 copy-done.7
  95.1 1.9 pad_maximum_fusion.2
  97.0 3.5 %pad_maximum_fusion = bf16[4,128,4096]{2,1,0:T(8,128)(2,1)} fusion(bf16[1,128,4096]{2,1,0:T(8,128)(2,1)S(1)} %bitcast.118, bf16[1,128,4096]{2,1,0:T(8,128)(2,1)} %bitcast.6, bf16[1,128,4096]{2,1,0:T(8,128)(2,1)} %bitcast.5, bf16[1,128,4096]{2,1,0:T(8,128)(2,1)S(1)} %bitcast.117), kind=kLoop, calls=%fused_computation.13 | loop fusion | flops 6291456 | bytes 8388608 | tf_op jit(solution)/shard_map/stack | solution.py:30
  100.6 20.7 %all-gather.7.cloned.1.call-done = bf16[4096,512]{1,0:T(8,128)(2,1)} async-done(((bf16[4096,128]{1,0:T(8,128)(2,1)}), bf16[4096,512]{1,0:T(8,128)(2,1)}) %all-gather.7.cloned.1.call-update) | async-done | bytes 4194320 | tf_op jit(solution)/shard_map/all_gather | solution.py:65
  121.2 5.8 %fusion.20 = bf16[512,512]{1,0:T(8,128)(2,1)S(1)} fusion(bf16[512,4096]{1,0:T(8,128)(2,1)} %bitcast.112, bf16[4096,512]{1,0:T(8,128)(2,1)} %all-gather.7.cloned.1.call-done, bf16[512]{0:T(512)(128)(2,1)S(1)} %fusion.43), kind=kOutput, calls=%fused_computation.43 | convolution fusion | flops 2148007936 | bytes 8913920 | tf_op jit(solution)/shard_map/dot_general | solution.py:72
  127.1 0.2 fusion.35
  127.3 1.2 collective-permute-start.14
  128.5 0.5 collective-permute-start.13
  129.1 2.0 convolution_convert_fusion.1
  131.2 9.6 %collective-permute-done.14 = bf16[512,512]{1,0:T(8,128)(2,1)} collective-permute-done((bf16[512,512]{1,0:T(8,128)(2,1)S(1)}, bf16[512,512]{1,0:T(8,128)(2,1)}, u32[]{:S(2)}, u32[]{:S(2)}) %collective-permute-start.14) | collective-permute-done | bytes 524320 | tf_op jit(solution)/shard_map/ppermute | solution.py:29
  140.8 12.2 %collective-permute-done.13 = bf16[512,512]{1,0:T(8,128)(2,1)} collective-permute-done((bf16[512,512]{1,0:T(8,128)(2,1)S(1)}, bf16[512,512]{1,0:T(8,128)(2,1)}, u32[]{:S(2)}, u32[]{:S(2)}) %collective-permute-start.13) | collective-permute-done | bytes 524320 | tf_op jit(solution)/shard_map/ppermute | solution.py:29
  153.0 2.2 fusion.6
  155.3 1.6 concatenate.21
  156.9 1.3 copy-done.1
  158.4 1.5 collective-permute-start.16
  160.2 1.5 dynamic-slice_bitcast_fusion.3
  161.7 1.6 collective-permute-start.20
  163.3 0.6 collective-permute-start.19
  163.9 41.0 %collective-permute-done.20 = bf16[4,64,384]{2,1,0:T(8,128)(2,1)S(1)} collective-permute-done((bf16[4,64,384]{2,1,0:T(8,128)(2,1)S(1)}, bf16[4,64,384]{2,1,0:T(8,128)(2,1)S(1)}, u32[]{:S(2)}, u32[]{:S(2)}) %collective-permute-start.20) | collective-permute-done | bytes 196640 | tf_op jit(solution)/shard_map/ppermute | solution.py:99
  204.8 2.7 collective-permute-start.18
  207.5 4.2 %collective-permute-done.19 = bf16[4,64,384]{2,1,0:T(8,128)(2,1)S(1)} collective-permute-done((bf16[4,64,384]{2,1,0:T(8,128)(2,1)S(1)}, bf16[4,64,384]{2,1,0:T(8,128)(2,1)S(1)}, u32[]{:S(2)}, u32[]{:S(2)}) %collective-permute-start.19) | collective-permute-done | bytes 196640 | tf_op jit(solution)/shard_map/ppermute | solution.py:99
  211.8 0.3 collective-permute-done.18
  212.0 1.1 pad_maximum_fusion.3
  213.1 3.4 %pad_maximum_fusion.1 = bf16[4,1280,384]{2,1,0:T(8,128)(2,1)} fusion(bf16[1,1280,384]{2,1,0:T(8,128)(2,1)S(1)} %bitcast.119, bf16[1,1280,384]{2,1,0:T(8,128)(2,1)} %bitcast.21, bf16[1,1280,384]{2,1,0:T(8,128)(2,1)} %bitcast.20, bf16[1,1280,384]{2,1,0:T(8,128)(2,1)S(1)} %bitcast.113), kind=kLoop, calls=%fused_computation.14 | loop fusion | flops 5898240 | bytes 7864320 | tf_op jit(solution)/shard_map/stack | solution.py:30
  216.5 1.1 slice.56
  217.9 0.3 fusion.37
  218.3 0.9 convert_element_type.68
  219.4 0.6 collective-permute-start.22
  220.2 1.2 slice.57
  222.0 0.7 fusion.45
  222.7 10.3 %collective-permute-done.23 = bf16[768,384]{1,0:T(8,128)(2,1)S(1)} collective-permute-done((bf16[768,384]{1,0:T(8,128)(2,1)S(1)}, bf16[768,384]{1,0:T(8,128)(2,1)S(1)}, u32[]{:S(2)}, u32[]{:S(2)}) %collective-permute-start.23) | collective-permute-done | bytes 589856 | tf_op jit(solution)/shard_map/ppermute | solution.py:29
  233.0 12.7 %collective-permute-done.22 = bf16[768,384]{1,0:T(8,128)(2,1)S(1)} collective-permute-done((bf16[768,384]{1,0:T(8,128)(2,1)S(1)}, bf16[768,384]{1,0:T(8,128)(2,1)S(1)}, u32[]{:S(2)}, u32[]{:S(2)}) %collective-permute-start.22) | collective-permute-done | bytes 589856 | tf_op jit(solution)/shard_map/ppermute | solution.py:29
  245.7 1.0 collective-permute-done.21
  246.7 5.7 %maximum_maximum_fusion = bf16[4,2048,384]{2,1,0:T(8,128)(2,1)} fusion(bf16[1,768,384]{2,1,0:T(8,128)(2,1)S(1)} %bitcast.127, bf16[1,768,384]{2,1,0:T(8,128)(2,1)S(1)} %bitcast.128, bf16[1,768,384]{2,1,0:T(8,128)(2,1)S(1)} %bitcast.129, bf16[1,768,384]{2,1,0:T(8,128)(2,1)S(1)} %bitcast.114, bf16[4,1280,384]{2,1,0:T(8,128)(2,1)} %pad_maximum_fusion.1), kind=kLoop, calls=%fused_computation | loop fusion | flops 31457280 | bytes 12582912 | tf_op jit(solution)/shard_map/concatenate | solution.py:111
  252.4 6.2 %fusion.14 = f32[4,384]{1,0:T(4,128)S(1)} fusion(bf16[4,256,384]{2,1,0:T(8,128)(2,1)S(1)} %bitcast.121, bf16[4,2048,384]{2,1,0:T(8,128)(2,1)} %maximum_maximum_fusion, bf16[256,2048]{1,0:T(8,128)(2,1)} %all-gather.11.cloned.1.call-done, bf16[256,2048]{1,0:T(8,128)(2,1)S(1)} %copy-done.9, f32[]{:T(128)} %bitcast.38), kind=kOutput, calls=%fused_computation.36 | convolution fusion | flops 1614412288 | bytes 9181188 | tf_op jit(solution)/shard_map/ij,sjt->sit/dot_general | solution.py:118
  258.7 2.4 fusion.15
  261.1 2.5 fusion.16
  263.6 2.5 fusion.17
  266.1 2.6 fusion.18
  268.7 2.5 fusion.19
  271.4 1.6 collective-permute-start.25
  273.0 1.4 collective-permute-start.24
  275.2 0.6 collective-permute-done.24
  275.8 0.6 fusion.42
  (73 shorter events, 2.1 us)
Async XLA Ops:
  6.5 94.0 %all-gather.5.cloned.1.call-start = ((), (), s32[]{:S(2)}) async-start(), calls=%async_computation.1 | async-start | bytes 1310720 | tf_op jit(solution)/shard_map/all_gather | solution.py:64
  7.3 114.0 %all-gather.7.cloned.1.call-start = ((), (), s32[]{:S(2)}) async-start(), calls=%async_computation.2 | async-start | bytes 5242880 | tf_op jit(solution)/shard_map/all_gather | solution.py:65
  8.0 147.3 %all-gather.9.cloned.1.call-start = ((), (), s32[]{:S(2)}) async-start(), calls=%async_computation.3 | async-start | bytes 1310720 | tf_op jit(solution)/shard_map/all_gather | solution.py:68
  8.1 68.7 %collective-permute-start.2 = (bf16[128,2048]{1,0:T(8,128)(2,1)}, bf16[128,2048]{1,0:T(8,128)(2,1)S(1)}, u32[]{:S(2)}, u32[]{:S(2)}) collective-permute-start(bf16[128,2048]{1,0:T(8,128)(2,1)} %param.10), channel_id=1, source_target_pairs={{0,3},{1,0},{2,1},{3,2},{4,7},{5,4},{6,5},{7,6},{8,11},{9,8},{10,9... | collective-permute-start | bytes 1572872 | tf_op jit(solution)/shard_map/ppermute | solution.py:29
  10.5 86.4 %collective-permute-start.5 = (bf16[128,4096]{1,0:T(8,128)(2,1)}, bf16[128,4096]{1,0:T(8,128)(2,1)S(1)}, u32[]{:S(2)}, u32[]{:S(2)}) collective-permute-start(bf16[128,4096]{1,0:T(8,128)(2,1)} %param.11), channel_id=1, source_target_pairs={{0,3},{1,0},{2,1},{3,2},{4,7},{5,4},{6,5},{7,6},{8,11},{9,8},{10,9... | collective-permute-start | bytes 3145736 | tf_op jit(solution)/shard_map/ppermute | solution.py:29
  11.2 85.8 %collective-permute-start.4 = (bf16[128,4096]{1,0:T(8,128)(2,1)}, bf16[128,4096]{1,0:T(8,128)(2,1)}, u32[]{:S(2)}, u32[]{:S(2)}) collective-permute-start(bf16[128,4096]{1,0:T(8,128)(2,1)} %param.11), channel_id=1, source_target_pairs={{0,2},{1,3},{2,0},{3,1},{4,6},{5,7},{6,4},{7,5},{8,10},{9,11},{10,... | collective-permute-start | bytes 3145736 | tf_op jit(solution)/shard_map/ppermute | solution.py:29
  11.2 85.7 %collective-permute-start.3 = (bf16[128,4096]{1,0:T(8,128)(2,1)}, bf16[128,4096]{1,0:T(8,128)(2,1)}, u32[]{:S(2)}, u32[]{:S(2)}) collective-permute-start(bf16[128,4096]{1,0:T(8,128)(2,1)} %param.11), channel_id=1, source_target_pairs={{0,1},{1,2},{2,3},{3,0},{4,5},{5,6},{6,7},{7,4},{8,9},{9,10},{10,1... | collective-permute-start | bytes 3145736 | tf_op jit(solution)/shard_map/ppermute | solution.py:29
  13.1 45.8 %collective-permute-start.9 = (f32[]{:T(128)}, f32[]{:T(128)}, u32[]{:S(2)}, u32[]{:S(2)}) collective-permute-start(f32[]{:T(128)} %convert_reduce_fusion), channel_id=1, source_target_pairs={{0,1},{1,2},{2,3},{3,0},{4,5},{5,6},{6,7},{7,4},{8,9},{9,10},{10,1... | collective-permute-start | bytes 20 | tf_op jit(solution)/shard_map/ppermute | solution.py:60
  58.9 4.7 %collective-permute-start.10 = (f32[]{:T(128)}, f32[]{:T(128)}, u32[]{:S(2)}, u32[]{:S(2)}) collective-permute-start(f32[]{:T(128)} %convert_reduce_fusion), channel_id=1, source_target_pairs={{0,2},{1,3},{2,0},{3,1},{4,6},{5,7},{6,4},{7,5},{8,10},{9,11},{10,... | collective-permute-start | bytes 20 | tf_op jit(solution)/shard_map/ppermute | solution.py:60
  63.6 1.4 collective-permute-start.11
  65.0 3.5 %collective-permute-start.8 = (s32[128]{0:T(128)}, s32[128]{0:T(128)S(1)}, u32[]{:S(2)}, u32[]{:S(2)}) collective-permute-start(s32[128]{0:T(128)} %param.12), channel_id=1, source_target_pairs={{0,3},{1,0},{2,1},{3,2},{4,7},{5,4},{6,5},{7,6},{8,11},{9,8},{10,9... | collective-permute-start | bytes 1544 | tf_op jit(solution)/shard_map/ppermute | solution.py:29
  68.5 3.7 %collective-permute-start.7 = (s32[128]{0:T(128)}, s32[128]{0:T(128)S(1)}, u32[]{:S(2)}, u32[]{:S(2)}) collective-permute-start(s32[128]{0:T(128)} %param.12), channel_id=1, source_target_pairs={{0,2},{1,3},{2,0},{3,1},{4,6},{5,7},{6,4},{7,5},{8,10},{9,11},{10,... | collective-permute-start | bytes 1544 | tf_op jit(solution)/shard_map/ppermute | solution.py:29
  72.2 3.1 %collective-permute-start.6 = (s32[128]{0:T(128)}, s32[128]{0:T(128)S(1)}, u32[]{:S(2)}, u32[]{:S(2)}) collective-permute-start(s32[128]{0:T(128)} %param.12), channel_id=1, source_target_pairs={{0,1},{1,2},{2,3},{3,0},{4,5},{5,6},{6,7},{7,4},{8,9},{9,10},{10,1... | collective-permute-start | bytes 1544 | tf_op jit(solution)/shard_map/ppermute | solution.py:29
  75.3 15.1 %collective-permute-start.1 = (bf16[128,2048]{1,0:T(8,128)(2,1)}, bf16[128,2048]{1,0:T(8,128)(2,1)S(1)}, u32[]{:S(2)}, u32[]{:S(2)}) collective-permute-start(bf16[128,2048]{1,0:T(8,128)(2,1)} %param.10), channel_id=1, source_target_pairs={{0,2},{1,3},{2,0},{3,1},{4,6},{5,7},{6,4},{7,5},{8,10},{9,11},{10,... | collective-permute-start | bytes 1572872 | tf_op jit(solution)/shard_map/ppermute | solution.py:29
  76.7 17.5 %copy-start.5 = (bf16[128,2048]{1,0:T(8,128)(2,1)}, bf16[128,2048]{1,0:T(8,128)(2,1)S(1)}, u32[]{:S(2)}) copy-start(bf16[128,2048]{1,0:T(8,128)(2,1)S(1)} %collective-permute-done.2) | copy-start | bytes 1572868
  76.7 17.5 %collective-permute-start = (bf16[128,2048]{1,0:T(8,128)(2,1)}, bf16[128,2048]{1,0:T(8,128)(2,1)S(1)}, u32[]{:S(2)}, u32[]{:S(2)}) collective-permute-start(bf16[128,2048]{1,0:T(8,128)(2,1)} %param.10), channel_id=1, source_target_pairs={{0,1},{1,2},{2,3},{3,0},{4,5},{5,6},{6,7},{7,4},{8,9},{9,10},{10,1... | collective-permute-start | bytes 1572872 | tf_op jit(solution)/shard_map/ppermute | solution.py:29
  90.3 3.9 %copy-start.6 = (bf16[128,2048]{1,0:T(8,128)(2,1)}, bf16[128,2048]{1,0:T(8,128)(2,1)S(1)}, u32[]{:S(2)}) copy-start(bf16[128,2048]{1,0:T(8,128)(2,1)S(1)} %collective-permute-done.1) | copy-start | bytes 1572868
  94.3 0.8 copy-start.7
  95.1 1.9 copy-start.2
  100.5 116.0 %reduce-scatter.2.cloned.1.call-start = ((), (), s32[]{:S(2)}) async-start(), calls=%async_computation.4 | async-start | bytes 2785280 | tf_op jit(solution)/shard_map/reduce_scatter | solution.py:85
  127.3 3.8 %copy-start.4 = (bf16[4,128,512]{2,1,0:T(8,128)(2,1)}, bf16[4,128,512]{2,1,0:T(8,128)(2,1)S(1)}, u32[]{:S(2)}) copy-start(bf16[4,128,512]{2,1,0:T(8,128)(2,1)S(1)} %fusion.35) | copy-start | bytes 1572868
  127.3 13.5 %collective-permute-start.14 = (bf16[512,512]{1,0:T(8,128)(2,1)S(1)}, bf16[512,512]{1,0:T(8,128)(2,1)}, u32[]{:S(2)}, u32[]{:S(2)}) collective-permute-start(bf16[512,512]{1,0:T(8,128)(2,1)S(1)} %bitcast.131), channel_id=1, source_target_pairs={{0,3},{1,0},{2,1},{3,2},{4,7},{5,4},{6,5},{7,6},{8,11},{9,8},{10,9... | collective-permute-start | bytes 1572872 | tf_op jit(solution)/shard_map/ppermute | solution.py:29
  128.5 24.5 %collective-permute-start.13 = (bf16[512,512]{1,0:T(8,128)(2,1)S(1)}, bf16[512,512]{1,0:T(8,128)(2,1)}, u32[]{:S(2)}, u32[]{:S(2)}) collective-permute-start(bf16[512,512]{1,0:T(8,128)(2,1)S(1)} %bitcast.132), channel_id=1, source_target_pairs={{0,2},{1,3},{2,0},{3,1},{4,6},{5,7},{6,4},{7,5},{8,10},{9,11},{10,... | collective-permute-start | bytes 1572872 | tf_op jit(solution)/shard_map/ppermute | solution.py:29
  129.0 24.1 %collective-permute-start.12 = (bf16[512,512]{1,0:T(8,128)(2,1)S(1)}, bf16[512,512]{1,0:T(8,128)(2,1)}, u32[]{:S(2)}, u32[]{:S(2)}) collective-permute-start(bf16[512,512]{1,0:T(8,128)(2,1)S(1)} %bitcast.133), channel_id=1, source_target_pairs={{0,1},{1,2},{2,3},{3,0},{4,5},{5,6},{6,7},{7,4},{8,9},{9,10},{10,1... | collective-permute-start | bytes 1572872 | tf_op jit(solution)/shard_map/ppermute | solution.py:29
  156.9 1.4 copy-start.1
  156.9 95.5 %all-gather.11.cloned.1.call-start = ((), (), s32[]{:S(2)}) async-start(), calls=%async_computation.5 | async-start | bytes 1310720 | tf_op jit(solution)/shard_map/all_gather | solution.py:110
  158.4 54.7 %collective-permute-start.17 = (bf16[1280,384]{1,0:T(8,128)(2,1)S(1)}, bf16[1280,384]{1,0:T(8,128)(2,1)S(1)}, u32[]{:S(2)}, u32[]{:S(2)}) collective-permute-start(bf16[1280,384]{1,0:T(8,128)(2,1)S(1)} %slice.42), channel_id=1, source_target_pairs={{0,3},{1,0},{2,1},{3,2},{4,7},{5,4},{6,5},{7,6},{8,11},{9,8},{10,9... | collective-permute-start | bytes 2949128 | tf_op jit(solution)/shard_map/ppermute | solution.py:29
  158.4 54.6 %collective-permute-start.16 = (bf16[1280,384]{1,0:T(8,128)(2,1)S(1)}, bf16[1280,384]{1,0:T(8,128)(2,1)}, u32[]{:S(2)}, u32[]{:S(2)}) collective-permute-start(bf16[1280,384]{1,0:T(8,128)(2,1)S(1)} %slice.42), channel_id=1, source_target_pairs={{0,2},{1,3},{2,0},{3,1},{4,6},{5,7},{6,4},{7,5},{8,10},{9,11},{10,... | collective-permute-start | bytes 2949128 | tf_op jit(solution)/shard_map/ppermute | solution.py:29
  160.0 53.1 %collective-permute-start.15 = (bf16[1280,384]{1,0:T(8,128)(2,1)S(1)}, bf16[1280,384]{1,0:T(8,128)(2,1)}, u32[]{:S(2)}, u32[]{:S(2)}) collective-permute-start(bf16[1280,384]{1,0:T(8,128)(2,1)S(1)} %slice.42), channel_id=1, source_target_pairs={{0,1},{1,2},{2,3},{3,0},{4,5},{5,6},{6,7},{7,4},{8,9},{9,10},{10,1... | collective-permute-start | bytes 2949128 | tf_op jit(solution)/shard_map/ppermute | solution.py:29
  161.7 43.2 %collective-permute-start.20 = (bf16[4,64,384]{2,1,0:T(8,128)(2,1)S(1)}, bf16[4,64,384]{2,1,0:T(8,128)(2,1)S(1)}, u32[]{:S(2)}, u32[]{:S(2)}) collective-permute-start(bf16[4,64,384]{2,1,0:T(8,128)(2,1)S(1)} %get-tuple-element.32), channel_id=1, source_target_pairs={{0,3},{1,0},{2,1},{3,2},{4,7},{5,4},{6,5},{7,6},{8,11},{9,8},{10,9... | collective-permute-start | bytes 589832 | tf_op jit(solution)/shard_map/ppermute | solution.py:99
  163.3 48.5 %collective-permute-start.19 = (bf16[4,64,384]{2,1,0:T(8,128)(2,1)S(1)}, bf16[4,64,384]{2,1,0:T(8,128)(2,1)S(1)}, u32[]{:S(2)}, u32[]{:S(2)}) collective-permute-start(bf16[4,64,384]{2,1,0:T(8,128)(2,1)S(1)} %get-tuple-element.33), channel_id=1, source_target_pairs={{0,2},{1,3},{2,0},{3,1},{4,6},{5,7},{6,4},{7,5},{8,10},{9,11},{10,... | collective-permute-start | bytes 589832 | tf_op jit(solution)/shard_map/ppermute | solution.py:99
  204.8 7.2 %collective-permute-start.18 = (bf16[4,64,384]{2,1,0:T(8,128)(2,1)S(1)}, bf16[4,64,384]{2,1,0:T(8,128)(2,1)S(1)}, u32[]{:S(2)}, u32[]{:S(2)}) collective-permute-start(bf16[4,64,384]{2,1,0:T(8,128)(2,1)S(1)} %get-tuple-element.34), channel_id=1, source_target_pairs={{0,1},{1,2},{2,3},{3,0},{4,5},{5,6},{6,7},{7,4},{8,9},{9,10},{10,1... | collective-permute-start | bytes 589832 | tf_op jit(solution)/shard_map/ppermute | solution.py:99
  217.6 4.4 %copy-start.11 = (s32[6]{0:T(128)S(1)}, s32[6]{0:T(128)}, u32[]{:S(2)}) copy-start(s32[6]{0:T(128)} %param.16) | copy-start | bytes 76
  219.3 13.7 %collective-permute-start.23 = (bf16[768,384]{1,0:T(8,128)(2,1)S(1)}, bf16[768,384]{1,0:T(8,128)(2,1)S(1)}, u32[]{:S(2)}, u32[]{:S(2)}) collective-permute-start(bf16[768,384]{1,0:T(8,128)(2,1)S(1)} %slice.44), channel_id=1, source_target_pairs={{0,3},{1,0},{2,1},{3,2},{4,7},{5,4},{6,5},{7,6},{8,11},{9,8},{10,9... | collective-permute-start | bytes 1769480 | tf_op jit(solution)/shard_map/ppermute | solution.py:29
  219.4 26.3 %collective-permute-start.22 = (bf16[768,384]{1,0:T(8,128)(2,1)S(1)}, bf16[768,384]{1,0:T(8,128)(2,1)S(1)}, u32[]{:S(2)}, u32[]{:S(2)}) collective-permute-start(bf16[768,384]{1,0:T(8,128)(2,1)S(1)} %slice.44), channel_id=1, source_target_pairs={{0,2},{1,3},{2,0},{3,1},{4,6},{5,7},{6,4},{7,5},{8,10},{9,11},{10,... | collective-permute-start | bytes 1769480 | tf_op jit(solution)/shard_map/ppermute | solution.py:29
  220.0 26.7 %collective-permute-start.21 = (bf16[768,384]{1,0:T(8,128)(2,1)S(1)}, bf16[768,384]{1,0:T(8,128)(2,1)S(1)}, u32[]{:S(2)}, u32[]{:S(2)}) collective-permute-start(bf16[768,384]{1,0:T(8,128)(2,1)S(1)} %slice.44), channel_id=1, source_target_pairs={{0,1},{1,2},{2,3},{3,0},{4,5},{5,6},{6,7},{7,4},{8,9},{9,10},{10,1... | collective-permute-start | bytes 1769480 | tf_op jit(solution)/shard_map/ppermute | solution.py:29
  246.7 5.7 %copy-start.3 = (bf16[4,4,64,384]{3,2,1,0:T(8,128)(2,1)S(1)}, bf16[4,4,64,384]{3,2,1,0:T(8,128)(2,1)}, u32[]{:S(2)}) copy-start(bf16[4,4,64,384]{3,2,1,0:T(8,128)(2,1)} %pad_maximum_fusion.3) | copy-start | bytes 2359300
  246.7 5.7 %copy-start.9 = (bf16[256,2048]{1,0:T(8,128)(2,1)S(1)}, bf16[256,2048]{1,0:T(8,128)(2,1)}, u32[]{:S(2)}) copy-start(bf16[256,2048]{1,0:T(8,128)(2,1)} %all-gather.9.cloned.1.call-done) | copy-start | bytes 3145732
  252.4 6.2 %copy-start = (bf16[4,2048,384]{2,1,0:T(8,128)(2,1)S(1)}, bf16[4,2048,384]{2,1,0:T(8,128)(2,1)}, u32[]{:S(2)}) copy-start(bf16[4,2048,384]{2,1,0:T(8,128)(2,1)} %maximum_maximum_fusion) | copy-start | bytes 18874372
  252.4 6.2 %copy-start.10 = (bf16[256,2048]{1,0:T(8,128)(2,1)S(1)}, bf16[256,2048]{1,0:T(8,128)(2,1)}, u32[]{:S(2)}) copy-start(bf16[256,2048]{1,0:T(8,128)(2,1)} %all-gather.11.cloned.1.call-done) | copy-start | bytes 3145732
  268.7 5.6 %copy-start.8 = (s32[384]{0:T(512)S(1)}, s32[384]{0:T(512)}, u32[]{:S(2)}) copy-start(s32[384]{0:T(512)} %param.19) | copy-start | bytes 4612
  271.3 3.7 %collective-permute-start.26 = (f32[6,384]{1,0:T(8,128)S(1)}, f32[6,384]{1,0:T(8,128)S(1)}, u32[]{:S(2)}, u32[]{:S(2)}) collective-permute-start(f32[6,384]{1,0:T(8,128)S(1)} %get-tuple-element.36), channel_id=1, source_target_pairs={{0,1},{1,2},{2,3},{3,0},{4,5},{5,6},{6,7},{7,4},{8,9},{9,10},{10,1... | collective-permute-start | bytes 27656 | tf_op jit(solution)/shard_map/ppermute | solution.py:123
  271.4 3.8 %collective-permute-start.25 = (f32[6,384]{1,0:T(8,128)S(1)}, f32[6,384]{1,0:T(8,128)S(1)}, u32[]{:S(2)}, u32[]{:S(2)}) collective-permute-start(f32[6,384]{1,0:T(8,128)S(1)} %get-tuple-element.37), channel_id=1, source_target_pairs={{0,2},{1,3},{2,0},{3,1},{4,6},{5,7},{6,4},{7,5},{8,10},{9,11},{10,... | collective-permute-start | bytes 27656 | tf_op jit(solution)/shard_map/ppermute | solution.py:123
  273.0 2.8 collective-permute-start.24
Sparse Core Ops, SparseCore 0:
  8.9 30.6 all-gather.4
  41.1 80.0 all-gather.6
  122.8 26.1 all-gather.8
  157.0 44.1 reduce-scatter.1
  219.4 25.2 all-gather.10

commit v16 on v11

--- a/solution.py
+++ b/solution.py
@@ -35,6 +35,12 @@
     reverse = stacked[::-1]
     doubled = jnp.concatenate([reverse, reverse], axis=0)
     return lax.dynamic_slice_in_dim(doubled, n - 1 - lax.axis_index(axis), n, axis=0)
+
+
+def rotate(x, start, axis):
+    n = x.shape[axis]
+    doubled = jnp.concatenate([x, x], axis=axis)
+    return lax.dynamic_slice_in_dim(doubled, start, n, axis=axis)
 
 
 def shards(
@@ -102,18 +108,26 @@
     grads_first, acts_near, payload = lax.optimization_barrier((grads_first, acts_near, payload))
     second_rows, _ = lax.optimization_barrier((train_grad_rot[half:], payload))
     grads_second = ring_gather(second_rows, "wb")
-    rows_held = lax.all_gather(payload, "wa", axis=0, tiled=True)
-    gradient_held, eig_held = rows_held[:, :eig_out], rows_held[:, eig_out:]
     grads_near = jnp.concatenate([grads_first, grads_second], axis=1)
-    acts_near = acts_near.reshape(nb, na * act_blocks.shape[2], -1).astype(jnp.float32)
-    grad_wide = gradient_held.astype(jnp.float32)
-    eig_wide = eig_held.astype(jnp.float32)
-    results = []
-    for damping in range(dampings.shape[0]):
-        precond = (grad_wide / (eig_wide + dampings[damping])).astype(jnp.bfloat16)
-        projected = jnp.einsum("ij,sjt->sit", precond, grads_near, preferred_element_type=jnp.float32)
-        results.append(jnp.sum(projected * acts_near, axis=1))
-    partial = jnp.stack(results, axis=1)
+    acts_near = acts_near.astype(jnp.float32)
+
+    def score_part(held, acts):
+        grad_wide = held[:, :eig_out].astype(jnp.float32)
+        eig_wide = held[:, eig_out:].astype(jnp.float32)
+        results = []
+        for damping in range(dampings.shape[0]):
+            precond = (grad_wide / (eig_wide + dampings[damping])).astype(jnp.bfloat16)
+            projected = jnp.einsum("ij,sjt->sit", precond, grads_near, preferred_element_type=jnp.float32)
+            results.append(jnp.sum(projected * acts, axis=1))
+        return jnp.stack(results, axis=1)
+
+    mine = lax.axis_index("wa")
+    own = score_part(payload, lax.dynamic_index_in_dim(acts_near, mine, axis=1, keepdims=False))
+    rows_held = rotate(lax.all_gather(payload, "wa", axis=0), mine, 0)[1:]
+    acts_rest = rotate(acts_near, mine, 1)[:, 1:]
+    partial = own + score_part(
+        rows_held.reshape(-1, rows_held.shape[-1]), acts_rest.reshape(nb, -1, acts_rest.shape[-1])
+    )
     totals = partial[0]
     for shift in range(1, nb):
         totals = totals + lax.ppermute(partial[shift], "wb", perm=[(i, (i - shift) % nb) for i in range(nb)])

time: 270 us -> 266 us (0.985)
  waiting for transfers between devices: 171 us -> 161 us
  matrix products: 28.7 us -> 36 us
  local copies, waits for them, and re-layouts: 13.4 us -> 9.27 us
  starting transfers between devices: 21.2 us -> 24.5 us
    dot_general x6 -> x12, matrix products: 18.9 us -> 26.2 us  [score_part(): jnp.einsum('ij,sjt->sit', precond, grads_near, preferred_element_type=jnp...]
    ppermute x18, waiting for transfers between devices: 105 us -> 97.6 us  [ring_gather(): lax.ppermute(x, axis, perm=[(i, (i + shift) % n) for i in range(n)])]
    ppermute x18, starting transfers between devices: 11.7 us -> 17.7 us  [ring_gather(): lax.ppermute(x, axis, perm=[(i, (i + shift) % n) for i in range(n)])]
    all_gather x1, waiting for transfers between devices: 5.9 us -> 0.02 us  [shards(): rows_held = rotate(lax.all_gather(payload, 'wa', axis=0), mine, 0)[1:]]
    ppermute x3, starting transfers between devices: 4.39 us -> 0.78 us  [shards(): lax.ppermute(outgoing, 'wb', perm=[(i, (i + shift) % nb) for i in range(n...]
  transfers between devices with their start and end apart: 31 -> 31, of which waited for: 15 -> 14; matrix products, arithmetic and copies ran while one was open for 10% -> 14% of each run, Pallas kernels for 0% -> 0%
where the time goes in v16:
time: 266 us
  waiting for transfers between devices  161 us (61%)
  matrix products  36 us (14%)
  starting transfers between devices  24.5 us (9%)
  between operations  17.7 us (7%)
  other arithmetic  17.6 us (7%)
  local copies, waits for them, and re-layouts  9.27 us (3%)
    ppermute x18, waiting for transfers between devices, ring_gather(): lax.ppermute(x, axis, perm=[(i, (i + shift) % n) for i in range(n)])  97.6 us
    ppermute x3, waiting for transfers between devices, shards(): lax.ppermute(outgoing, 'wb', perm=[(i, (i + shift) % nb) for i in range(n...  39.1 us
    dot_general x12, matrix products, score_part(): jnp.einsum('ij,sjt->sit', precond, grads_near, preferred_element_type=jnp...  26.2 us
    ppermute x3, waiting for transfers between devices, shards(): lax.ppermute(eig_sum, 'wb', perm=[(i, (i + shift) % nb) for i in range(nb)])  20.8 us
    ppermute x18, starting transfers between devices, ring_gather(): lax.ppermute(x, axis, perm=[(i, (i + shift) % n) for i in range(n)])  17.7 us
    another operation x4, other arithmetic, ring_gather(): return jnp.stack(parts)  9.03 us
    dot_general x1, matrix products, shards(): jnp.dot(grad_tokens.reshape(nb * count, -1), grad_cols, preferred_element...  5.79 us
  transfers between devices with their start and end apart: 31, of which 14 were waited for; matrix products, arithmetic and copies ran while one was open for 14% of the time, Pallas kernels for 0%

profile of v16, /device:TPU:0, one launch (start us, length us, event | category | flops | bytes accessed | tf_op | source)
XLA Modules:
  0.0 265.8 jit_solution(16935507830828154864)
XLA Ops:
  6.5 0.7 all-gather.7.cloned.1.call-update
  7.3 0.5 collective-permute-start
  7.8 2.6 collective-permute-start.3
  10.5 1.4 collective-permute-start.5
  11.9 0.6 collective-permute-start.7
  12.5 46.7 %collective-permute-done.7 = s32[128]{0:T(128)S(1)} collective-permute-done((s32[128]{0:T(128)}, s32[128]{0:T(128)S(1)}, u32[]{:S(2)}, u32[]{:S(2)}) %collective-permute-start.7) | collective-permute-done | bytes 544 | tf_op jit(solution)/shard_map/ppermute | solution.py:29
  59.2 4.7 %collective-permute-start.8 = (s32[128]{0:T(128)}, s32[128]{0:T(128)S(1)}, u32[]{:S(2)}, u32[]{:S(2)}) collective-permute-start(s32[128]{0:T(128)} %param.12), channel_id=1, source_target_pairs={{0,3},{1,0},{2,1},{3,2},{4,7},{5,4},{6,5},{7,6},{8,11},{9,8},{10,9... | collective-permute-start | bytes 1544 | tf_op jit(solution)/shard_map/ppermute | solution.py:29
  63.9 1.4 collective-permute-done.8
  65.5 3.3 %collective-permute-done.6 = s32[128]{0:T(128)S(1)} collective-permute-done((s32[128]{0:T(128)}, s32[128]{0:T(128)S(1)}, u32[]{:S(2)}, u32[]{:S(2)}) %collective-permute-start.6) | collective-permute-done | bytes 544 | tf_op jit(solution)/shard_map/ppermute | solution.py:29
  68.9 0.7 pad_add_fusion
  69.6 11.7 %collective-permute-done.1 = bf16[128,2048]{1,0:T(8,128)(2,1)S(1)} collective-permute-done((bf16[128,2048]{1,0:T(8,128)(2,1)}, bf16[128,2048]{1,0:T(8,128)(2,1)S(1)}, u32[]{:S(2)}, u32[]{:S(2)}) %collective-permute-start.1) | collective-permute-done | bytes 524320 | tf_op jit(solution)/shard_map/ppermute | solution.py:29
  81.4 5.0 %collective-permute-done.2 = bf16[128,2048]{1,0:T(8,128)(2,1)S(1)} collective-permute-done((bf16[128,2048]{1,0:T(8,128)(2,1)}, bf16[128,2048]{1,0:T(8,128)(2,1)S(1)}, u32[]{:S(2)}, u32[]{:S(2)}) %collective-permute-start.2) | collective-permute-done | bytes 524320 | tf_op jit(solution)/shard_map/ppermute | solution.py:29
  86.4 0.8 copy-done.8
  87.1 1.9 pad_maximum_fusion.2
  89.1 3.4 %pad_maximum_fusion = bf16[4,128,4096]{2,1,0:T(8,128)(2,1)} fusion(bf16[1,128,4096]{2,1,0:T(8,128)(2,1)} %bitcast.7, bf16[1,128,4096]{2,1,0:T(8,128)(2,1)} %bitcast.6, bf16[1,128,4096]{2,1,0:T(8,128)(2,1)S(1)} %bitcast.225, bf16[1,128,4096]{2,1,0:T(8,128)(2,1)S(1)} %bitcast.224), kind=kLoop, calls=%fused_computation.1 | loop fusion | flops 6291456 | bytes 8388608 | tf_op jit(solution)/shard_map/stack | solution.py:30
  92.5 5.8 %fusion.27 = bf16[512,512]{1,0:T(8,128)(2,1)S(1)} fusion(bf16[512,4096]{1,0:T(8,128)(2,1)} %bitcast.206, bf16[4096,512]{1,0:T(8,128)(2,1)} %all-gather.7.cloned.1.call-done, bf16[512]{0:T(512)(128)(2,1)S(1)} %fusion.105), kind=kOutput, calls=%fused_computation.54 | convolution fusion | flops 2148007936 | bytes 8913920 | tf_op jit(solution)/shard_map/dot_general | solution.py:70
  98.6 1.2 collective-permute-start.10
  99.8 1.1 collective-permute-start.11
  101.0 0.7 convert_reduce_fusion
  101.7 1.7 collective-permute-start.18
  103.5 0.3 collective-permute-start.19
  103.8 20.8 %collective-permute-done.18 = f32[]{:T(128)} collective-permute-done((f32[]{:T(128)}, f32[]{:T(128)}, u32[]{:S(2)}, u32[]{:S(2)}) %collective-permute-start.18) | collective-permute-done | bytes 36 | tf_op jit(solution)/shard_map/ppermute | solution.py:84
  127.3 2.0 convolution_convert_fusion.1
  129.5 2.1 fusion
  131.6 1.6 concatenate.30
  133.2 1.3 copy-done.3
  134.7 0.9 collective-permute-start.12
  135.7 1.0 collective-permute-start.13
  136.6 1.0 collective-permute-start.14
  137.6 1.3 dynamic-slice_bitcast_fusion.3
  139.0 0.7 collective-permute-start.16
  139.7 34.4 %collective-permute-done.15 = bf16[4,64,384]{2,1,0:T(8,128)(2,1)S(1)} collective-permute-done((bf16[4,64,384]{2,1,0:T(8,128)(2,1)S(1)}, bf16[4,64,384]{2,1,0:T(8,128)(2,1)S(1)}, u32[]{:S(2)}, u32[]{:S(2)}) %collective-permute-start.15) | collective-permute-done | bytes 196640 | tf_op jit(solution)/shard_map/ppermute | solution.py:100
  174.2 3.0 %collective-permute-done.16 = bf16[4,64,384]{2,1,0:T(8,128)(2,1)S(1)} collective-permute-done((bf16[4,64,384]{2,1,0:T(8,128)(2,1)S(1)}, bf16[4,64,384]{2,1,0:T(8,128)(2,1)S(1)}, u32[]{:S(2)}, u32[]{:S(2)}) %collective-permute-start.16) | collective-permute-done | bytes 196640 | tf_op jit(solution)/shard_map/ppermute | solution.py:100
  177.2 1.6 collective-permute-done.17
  179.0 3.0 %pad_maximum_fusion.1 = bf16[4,1024,384]{2,1,0:T(8,128)(2,1)} fusion(bf16[1,1024,384]{2,1,0:T(8,128)(2,1)} %bitcast.22, bf16[1,1024,384]{2,1,0:T(8,128)(2,1)} %bitcast.21, bf16[1,1024,384]{2,1,0:T(8,128)(2,1)S(1)} %bitcast.226, bf16[1,1024,384]{2,1,0:T(8,128)(2,1)S(1)} %bitcast.208), kind=kLoop, calls=%fused_computation.16 | loop fusion | flops 4718592 | bytes 6291456 | tf_op jit(solution)/shard_map/stack | solution.py:30
  182.0 1.1 slice.86
  183.3 0.3 fusion.87
  184.0 0.8 pad_maximum_fusion.4
  184.8 0.9 collective-permute-start.21
  185.8 1.4 collective-permute-start.22
  187.7 1.4 slice.87
  189.8 0.7 fusion.108
  190.4 13.1 %collective-permute-done.21 = bf16[1024,384]{1,0:T(8,128)(2,1)S(1)} collective-permute-done((bf16[1024,384]{1,0:T(8,128)(2,1)S(1)}, bf16[1024,384]{1,0:T(8,128)(2,1)S(1)}, u32[]{:S(2)}, u32[]{:S(2)}) %collective-permute-start.21) | collective-permute-done | bytes 786464 | tf_op jit(solution)/shard_map/ppermute | solution.py:29
  203.5 2.9 %collective-permute-done.22 = bf16[1024,384]{1,0:T(8,128)(2,1)} collective-permute-done((bf16[1024,384]{1,0:T(8,128)(2,1)S(1)}, bf16[1024,384]{1,0:T(8,128)(2,1)}, u32[]{:S(2)}, u32[]{:S(2)}) %collective-permute-start.22) | collective-permute-done | bytes 786464 | tf_op jit(solution)/shard_map/ppermute | solution.py:29
  206.3 13.5 %collective-permute-done.23 = bf16[1024,384]{1,0:T(8,128)(2,1)} collective-permute-done((bf16[1024,384]{1,0:T(8,128)(2,1)S(1)}, bf16[1024,384]{1,0:T(8,128)(2,1)}, u32[]{:S(2)}, u32[]{:S(2)}) %collective-permute-start.23) | collective-permute-done | bytes 786464 | tf_op jit(solution)/shard_map/ppermute | solution.py:29
  219.9 3.1 %maximum_maximum_fusion = bf16[4,2048,384]{2,1,0:T(8,128)(2,1)S(1)} fusion(bf16[1,1024,384]{2,1,0:T(8,128)(2,1)} %bitcast.36, bf16[1,1024,384]{2,1,0:T(8,128)(2,1)} %bitcast.35, bf16[1,1024,384]{2,1,0:T(8,128)(2,1)S(1)} %bitcast.227, bf16[1,1024,384]{2,1,0:T(8,128)(2,1)S(1)} %bitcast.207, bf16[4,1024,384]{2,1,0:T(8,128)(2,1)S(1)} %copy-done.2), kind=kLoop, calls=%fused_computation | loop fusion | flops 31457280 | bytes 12582912 | tf_op jit(solution)/shard_map/concatenate | solution.py:111
  223.0 1.9 fusion.35
  224.9 1.8 fusion.36
  226.7 1.8 fusion.37
  228.5 1.8 fusion.38
  230.3 1.8 fusion.39
  232.2 1.8 fusion.40
  234.2 2.1 fusion.14
  236.3 5.1 %fusion.26 = f32[4,384]{1,0:T(4,128)S(1)} fusion(f32[4,192,384]{2,1,0:T(8,128)S(1)} %bitcast.217, bf16[4,2048,384]{2,1,0:T(8,128)(2,1)} %copy-done, f32[]{:T(128)} %bitcast.54, bf16[192,4096]{1,0:T(8,128)(2,1)S(1)} %bitcast.211), kind=kOutput, calls=%fused_computation.53 | convolution fusion | flops 1210513920 | bytes 9050116 | tf_op jit(solution)/shard_map/ij,sjt->sit/dot_general | solution.py:120
  241.4 2.0 fusion.25
  243.4 2.0 fusion.24
  245.5 2.0 fusion.23
  247.4 2.1 fusion.22
  249.5 2.1 fusion.21
  251.8 2.4 collective-permute-start.24
  254.1 1.4 collective-permute-start.25
  256.2 1.6 collective-permute-done.25
  257.8 0.8 collective-permute-done.26
  258.6 0.6 fusion.104
  (91 shorter events, 2.6 us)
Async XLA Ops:
  6.5 86.0 %all-gather.7.cloned.1.call-start = ((), (), s32[]{:S(2)}) async-start(), calls=%async_computation.2 | async-start | bytes 5242880 | tf_op jit(solution)/shard_map/all_gather | solution.py:65
  7.3 120.1 %all-gather.5.cloned.1.call-start = ((), (), s32[]{:S(2)}) async-start(), calls=%async_computation.1 | async-start | bytes 1310720 | tf_op jit(solution)/shard_map/all_gather | solution.py:64
  7.3 61.5 %collective-permute-start = (bf16[128,2048]{1,0:T(8,128)(2,1)}, bf16[128,2048]{1,0:T(8,128)(2,1)S(1)}, u32[]{:S(2)}, u32[]{:S(2)}) collective-permute-start(bf16[128,2048]{1,0:T(8,128)(2,1)} %param.10), channel_id=1, source_target_pairs={{0,1},{1,2},{2,3},{3,0},{4,5},{5,6},{6,7},{7,4},{8,9},{9,10},{10,1... | collective-permute-start | bytes 1572872 | tf_op jit(solution)/shard_map/ppermute | solution.py:29
  7.8 81.2 %collective-permute-start.3 = (bf16[128,4096]{1,0:T(8,128)(2,1)}, bf16[128,4096]{1,0:T(8,128)(2,1)S(1)}, u32[]{:S(2)}, u32[]{:S(2)}) collective-permute-start(bf16[128,4096]{1,0:T(8,128)(2,1)} %param.11), channel_id=1, source_target_pairs={{0,1},{1,2},{2,3},{3,0},{4,5},{5,6},{6,7},{7,4},{8,9},{9,10},{10,1... | collective-permute-start | bytes 3145736 | tf_op jit(solution)/shard_map/ppermute | solution.py:29
  10.4 78.6 %collective-permute-start.4 = (bf16[128,4096]{1,0:T(8,128)(2,1)}, bf16[128,4096]{1,0:T(8,128)(2,1)}, u32[]{:S(2)}, u32[]{:S(2)}) collective-permute-start(bf16[128,4096]{1,0:T(8,128)(2,1)} %param.11), channel_id=1, source_target_pairs={{0,2},{1,3},{2,0},{3,1},{4,6},{5,7},{6,4},{7,5},{8,10},{9,11},{10,... | collective-permute-start | bytes 3145736 | tf_op jit(solution)/shard_map/ppermute | solution.py:29
  10.5 78.6 %collective-permute-start.5 = (bf16[128,4096]{1,0:T(8,128)(2,1)}, bf16[128,4096]{1,0:T(8,128)(2,1)}, u32[]{:S(2)}, u32[]{:S(2)}) collective-permute-start(bf16[128,4096]{1,0:T(8,128)(2,1)} %param.11), channel_id=1, source_target_pairs={{0,3},{1,0},{2,1},{3,2},{4,7},{5,4},{6,5},{7,6},{8,11},{9,8},{10,9... | collective-permute-start | bytes 3145736 | tf_op jit(solution)/shard_map/ppermute | solution.py:29
  11.9 47.3 %collective-permute-start.7 = (s32[128]{0:T(128)}, s32[128]{0:T(128)S(1)}, u32[]{:S(2)}, u32[]{:S(2)}) collective-permute-start(s32[128]{0:T(128)} %param.12), channel_id=1, source_target_pairs={{0,2},{1,3},{2,0},{3,1},{4,6},{5,7},{6,4},{7,5},{8,10},{9,11},{10,... | collective-permute-start | bytes 1544 | tf_op jit(solution)/shard_map/ppermute | solution.py:29
  59.2 6.1 %collective-permute-start.8 = (s32[128]{0:T(128)}, s32[128]{0:T(128)S(1)}, u32[]{:S(2)}, u32[]{:S(2)}) collective-permute-start(s32[128]{0:T(128)} %param.12), channel_id=1, source_target_pairs={{0,3},{1,0},{2,1},{3,2},{4,7},{5,4},{6,5},{7,6},{8,11},{9,8},{10,9... | collective-permute-start | bytes 1544 | tf_op jit(solution)/shard_map/ppermute | solution.py:29
  65.3 3.4 %collective-permute-start.6 = (s32[128]{0:T(128)}, s32[128]{0:T(128)S(1)}, u32[]{:S(2)}, u32[]{:S(2)}) collective-permute-start(s32[128]{0:T(128)} %param.12), channel_id=1, source_target_pairs={{0,1},{1,2},{2,3},{3,0},{4,5},{5,6},{6,7},{7,4},{8,9},{9,10},{10,1... | collective-permute-start | bytes 1544 | tf_op jit(solution)/shard_map/ppermute | solution.py:29
  68.8 12.6 %collective-permute-start.1 = (bf16[128,2048]{1,0:T(8,128)(2,1)}, bf16[128,2048]{1,0:T(8,128)(2,1)S(1)}, u32[]{:S(2)}, u32[]{:S(2)}) collective-permute-start(bf16[128,2048]{1,0:T(8,128)(2,1)} %param.10), channel_id=1, source_target_pairs={{0,2},{1,3},{2,0},{3,1},{4,6},{5,7},{6,4},{7,5},{8,10},{9,11},{10,... | collective-permute-start | bytes 1572872 | tf_op jit(solution)/shard_map/ppermute | solution.py:29
  68.8 17.6 %copy-start.6 = (bf16[128,2048]{1,0:T(8,128)(2,1)}, bf16[128,2048]{1,0:T(8,128)(2,1)S(1)}, u32[]{:S(2)}) copy-start(bf16[128,2048]{1,0:T(8,128)(2,1)S(1)} %collective-permute-done) | copy-start | bytes 1572868
  68.8 17.6 %collective-permute-start.2 = (bf16[128,2048]{1,0:T(8,128)(2,1)}, bf16[128,2048]{1,0:T(8,128)(2,1)S(1)}, u32[]{:S(2)}, u32[]{:S(2)}) collective-permute-start(bf16[128,2048]{1,0:T(8,128)(2,1)} %param.10), channel_id=1, source_target_pairs={{0,3},{1,0},{2,1},{3,2},{4,7},{5,4},{6,5},{7,6},{8,11},{9,8},{10,9... | collective-permute-start | bytes 1572872 | tf_op jit(solution)/shard_map/ppermute | solution.py:29
  68.9 113.1 %reduce-scatter.2.cloned.1.call-start = ((), (), s32[]{:S(2)}) async-start(), calls=%async_computation.3 | async-start | bytes 2785280 | tf_op jit(solution)/shard_map/reduce_scatter | solution.py:86
  81.4 5.0 %copy-start.7 = (bf16[128,2048]{1,0:T(8,128)(2,1)}, bf16[128,2048]{1,0:T(8,128)(2,1)S(1)}, u32[]{:S(2)}) copy-start(bf16[128,2048]{1,0:T(8,128)(2,1)S(1)} %collective-permute-done.1) | copy-start | bytes 1572868
  86.3 0.8 copy-start.8
  87.1 1.9 copy-start.5
  98.3 2.7 %copy-start.4 = (bf16[64,2048]{1,0:T(8,128)(2,1)S(1)}, bf16[64,2048]{1,0:T(8,128)(2,1)}, u32[]{:S(2)}) copy-start(bf16[64,2048]{1,0:T(8,128)(2,1)} %param.15) | copy-start | bytes 786436
  98.6 30.8 %collective-permute-start.10 = (bf16[512,512]{1,0:T(8,128)(2,1)S(1)}, bf16[512,512]{1,0:T(8,128)(2,1)}, u32[]{:S(2)}, u32[]{:S(2)}) collective-permute-start(bf16[512,512]{1,0:T(8,128)(2,1)S(1)} %bitcast.230), channel_id=1, source_target_pairs={{0,2},{1,3},{2,0},{3,1},{4,6},{5,7},{6,4},{7,5},{8,10},{9,11},{10,... | collective-permute-start | bytes 1572872 | tf_op jit(solution)/shard_map/ppermute | solution.py:29
  99.8 29.6 %collective-permute-start.11 = (bf16[512,512]{1,0:T(8,128)(2,1)S(1)}, bf16[512,512]{1,0:T(8,128)(2,1)}, u32[]{:S(2)}, u32[]{:S(2)}) collective-permute-start(bf16[512,512]{1,0:T(8,128)(2,1)S(1)} %bitcast.231), channel_id=1, source_target_pairs={{0,3},{1,0},{2,1},{3,2},{4,7},{5,4},{6,5},{7,6},{8,11},{9,8},{10,9... | collective-permute-start | bytes 1572872 | tf_op jit(solution)/shard_map/ppermute | solution.py:29
  100.9 28.5 %collective-permute-start.9 = (bf16[512,512]{1,0:T(8,128)(2,1)S(1)}, bf16[512,512]{1,0:T(8,128)(2,1)}, u32[]{:S(2)}, u32[]{:S(2)}) collective-permute-start(bf16[512,512]{1,0:T(8,128)(2,1)S(1)} %bitcast.232), channel_id=1, source_target_pairs={{0,1},{1,2},{2,3},{3,0},{4,5},{5,6},{6,7},{7,4},{8,9},{9,10},{10,1... | collective-permute-start | bytes 1572872 | tf_op jit(solution)/shard_map/ppermute | solution.py:29
  101.7 22.9 %collective-permute-start.18 = (f32[]{:T(128)}, f32[]{:T(128)}, u32[]{:S(2)}, u32[]{:S(2)}) collective-permute-start(f32[]{:T(128)} %convert_reduce_fusion), channel_id=1, source_target_pairs={{0,1},{1,2},{2,3},{3,0},{4,5},{5,6},{6,7},{7,4},{8,9},{9,10},{10,1... | collective-permute-start | bytes 20 | tf_op jit(solution)/shard_map/ppermute | solution.py:84
  103.5 22.5 %collective-permute-start.19 = (f32[]{:T(128)}, f32[]{:T(128)}, u32[]{:S(2)}, u32[]{:S(2)}) collective-permute-start(f32[]{:T(128)} %convert_reduce_fusion), channel_id=1, source_target_pairs={{0,2},{1,3},{2,0},{3,1},{4,6},{5,7},{6,4},{7,5},{8,10},{9,11},{10,... | collective-permute-start | bytes 20 | tf_op jit(solution)/shard_map/ppermute | solution.py:84
  124.6 2.1 collective-permute-start.20
  133.2 1.4 copy-start.3
  133.2 100.9 %all-gather.9.cloned.1.call-start = ((), (), s32[]{:S(2)}) async-start(), calls=%async_computation.4 | async-start | bytes 2621440 | tf_op jit(solution)/shard_map/all_gather | solution.py:126
  134.7 44.2 %collective-permute-start.12 = (bf16[1024,384]{1,0:T(8,128)(2,1)S(1)}, bf16[1024,384]{1,0:T(8,128)(2,1)S(1)}, u32[]{:S(2)}, u32[]{:S(2)}) collective-permute-start(bf16[1024,384]{1,0:T(8,128)(2,1)S(1)} %get-tuple-element.17), channel_id=1, source_target_pairs={{0,1},{1,2},{2,3},{3,0},{4,5},{5,6},{6,7},{7,4},{8,9},{9,10},{10,1... | collective-permute-start | bytes 2359304 | tf_op jit(solution)/shard_map/ppermute | solution.py:29
  135.7 43.3 %collective-permute-start.13 = (bf16[1024,384]{1,0:T(8,128)(2,1)S(1)}, bf16[1024,384]{1,0:T(8,128)(2,1)}, u32[]{:S(2)}, u32[]{:S(2)}) collective-permute-start(bf16[1024,384]{1,0:T(8,128)(2,1)S(1)} %get-tuple-element.17), channel_id=1, source_target_pairs={{0,2},{1,3},{2,0},{3,1},{4,6},{5,7},{6,4},{7,5},{8,10},{9,11},{10,... | collective-permute-start | bytes 2359304 | tf_op jit(solution)/shard_map/ppermute | solution.py:29
  136.6 42.3 %collective-permute-start.14 = (bf16[1024,384]{1,0:T(8,128)(2,1)S(1)}, bf16[1024,384]{1,0:T(8,128)(2,1)}, u32[]{:S(2)}, u32[]{:S(2)}) collective-permute-start(bf16[1024,384]{1,0:T(8,128)(2,1)S(1)} %get-tuple-element.17), channel_id=1, source_target_pairs={{0,3},{1,0},{2,1},{3,2},{4,7},{5,4},{6,5},{7,6},{8,11},{9,8},{10,9... | collective-permute-start | bytes 2359304 | tf_op jit(solution)/shard_map/ppermute | solution.py:29
  139.0 35.2 %collective-permute-start.15 = (bf16[4,64,384]{2,1,0:T(8,128)(2,1)S(1)}, bf16[4,64,384]{2,1,0:T(8,128)(2,1)S(1)}, u32[]{:S(2)}, u32[]{:S(2)}) collective-permute-start(bf16[4,64,384]{2,1,0:T(8,128)(2,1)S(1)} %get-tuple-element.28), channel_id=1, source_target_pairs={{0,1},{1,2},{2,3},{3,0},{4,5},{5,6},{6,7},{7,4},{8,9},{9,10},{10,1... | collective-permute-start | bytes 589832 | tf_op jit(solution)/shard_map/ppermute | solution.py:100
  139.0 38.2 %collective-permute-start.16 = (bf16[4,64,384]{2,1,0:T(8,128)(2,1)S(1)}, bf16[4,64,384]{2,1,0:T(8,128)(2,1)S(1)}, u32[]{:S(2)}, u32[]{:S(2)}) collective-permute-start(bf16[4,64,384]{2,1,0:T(8,128)(2,1)S(1)} %get-tuple-element.27), channel_id=1, source_target_pairs={{0,2},{1,3},{2,0},{3,1},{4,6},{5,7},{6,4},{7,5},{8,10},{9,11},{10,... | collective-permute-start | bytes 589832 | tf_op jit(solution)/shard_map/ppermute | solution.py:100
  174.2 4.6 %collective-permute-start.17 = (bf16[4,64,384]{2,1,0:T(8,128)(2,1)S(1)}, bf16[4,64,384]{2,1,0:T(8,128)(2,1)S(1)}, u32[]{:S(2)}, u32[]{:S(2)}) collective-permute-start(bf16[4,64,384]{2,1,0:T(8,128)(2,1)S(1)} %get-tuple-element.26), channel_id=1, source_target_pairs={{0,3},{1,0},{2,1},{3,2},{4,7},{5,4},{6,5},{7,6},{8,11},{9,8},{10,9... | collective-permute-start | bytes 589832 | tf_op jit(solution)/shard_map/ppermute | solution.py:100
  184.8 18.6 %collective-permute-start.21 = (bf16[1024,384]{1,0:T(8,128)(2,1)S(1)}, bf16[1024,384]{1,0:T(8,128)(2,1)S(1)}, u32[]{:S(2)}, u32[]{:S(2)}) collective-permute-start(bf16[1024,384]{1,0:T(8,128)(2,1)S(1)} %get-tuple-element.21), channel_id=1, source_target_pairs={{0,1},{1,2},{2,3},{3,0},{4,5},{5,6},{6,7},{7,4},{8,9},{9,10},{10,1... | collective-permute-start | bytes 2359304 | tf_op jit(solution)/shard_map/ppermute | solution.py:29
  185.8 20.6 %collective-permute-start.22 = (bf16[1024,384]{1,0:T(8,128)(2,1)S(1)}, bf16[1024,384]{1,0:T(8,128)(2,1)}, u32[]{:S(2)}, u32[]{:S(2)}) collective-permute-start(bf16[1024,384]{1,0:T(8,128)(2,1)S(1)} %get-tuple-element.21), channel_id=1, source_target_pairs={{0,2},{1,3},{2,0},{3,1},{4,6},{5,7},{6,4},{7,5},{8,10},{9,11},{10,... | collective-permute-start | bytes 2359304 | tf_op jit(solution)/shard_map/ppermute | solution.py:29
  187.2 32.7 %collective-permute-start.23 = (bf16[1024,384]{1,0:T(8,128)(2,1)S(1)}, bf16[1024,384]{1,0:T(8,128)(2,1)}, u32[]{:S(2)}, u32[]{:S(2)}) collective-permute-start(bf16[1024,384]{1,0:T(8,128)(2,1)S(1)} %get-tuple-element.21), channel_id=1, source_target_pairs={{0,3},{1,0},{2,1},{3,2},{4,7},{5,4},{6,5},{7,6},{8,11},{9,8},{10,9... | collective-permute-start | bytes 2359304 | tf_op jit(solution)/shard_map/ppermute | solution.py:29
  187.4 2.4 copy-start.10
  187.4 32.5 %copy-start.2 = (bf16[4,1024,384]{2,1,0:T(8,128)(2,1)S(1)}, bf16[4,1024,384]{2,1,0:T(8,128)(2,1)}, u32[]{:S(2)}) copy-start(bf16[4,1024,384]{2,1,0:T(8,128)(2,1)} %pad_maximum_fusion.1) | copy-start | bytes 9437188
  219.9 3.1 %copy-start.1 = (bf16[64,4096]{1,0:T(8,128)(2,1)S(1)}, bf16[64,4096]{1,0:T(8,128)(2,1)}, u32[]{:S(2)}) copy-start(bf16[64,4096]{1,0:T(8,128)(2,1)} %pad_maximum_fusion.4) | copy-start | bytes 1572868
  222.9 9.2 %copy-start = (bf16[4,2048,384]{2,1,0:T(8,128)(2,1)}, bf16[4,2048,384]{2,1,0:T(8,128)(2,1)S(1)}, u32[]{:S(2)}) copy-start(bf16[4,2048,384]{2,1,0:T(8,128)(2,1)S(1)} %maximum_maximum_fusion) | copy-start | bytes 18874372
  234.1 7.2 %slice-start = ((s8[6291456]{0:T(1024)(128)(4,1)}), s8[4194304]{0:T(1024)(128)(4,1)S(1)}, s32[]{:S(2)}) async-start(s8[6291456]{0:T(1024)(128)(4,1)} %bitcast.204), calls=%async_computation.5 | async-start | bytes 8388608
  236.3 5.1 %slice-start.1 = ((s8[6291456]{0:T(1024)(128)(4,1)}), s8[2097152]{0:T(1024)(128)(4,1)S(1)}, s32[]{:S(2)}) async-start(s8[6291456]{0:T(1024)(128)(4,1)} %bitcast.204), calls=%async_computation.6 | async-start | bytes 4194304
  249.5 6.0 %copy-start.9 = (s32[384]{0:T(512)S(1)}, s32[384]{0:T(512)}, u32[]{:S(2)}) copy-start(s32[384]{0:T(512)} %param.19) | copy-start | bytes 4612
  251.8 4.4 %collective-permute-start.24 = (f32[6,384]{1,0:T(8,128)S(1)}, f32[6,384]{1,0:T(8,128)S(1)}, u32[]{:S(2)}, u32[]{:S(2)}) collective-permute-start(f32[6,384]{1,0:T(8,128)S(1)} %get-tuple-element.29), channel_id=1, source_target_pairs={{0,3},{1,0},{2,1},{3,2},{4,7},{5,4},{6,5},{7,6},{8,11},{9,8},{10,9... | collective-permute-start | bytes 27656 | tf_op jit(solution)/shard_map/ppermute | solution.py:133
  254.1 3.7 %collective-permute-start.25 = (f32[6,384]{1,0:T(8,128)S(1)}, f32[6,384]{1,0:T(8,128)S(1)}, u32[]{:S(2)}, u32[]{:S(2)}) collective-permute-start(f32[6,384]{1,0:T(8,128)S(1)} %get-tuple-element.31), channel_id=1, source_target_pairs={{0,2},{1,3},{2,0},{3,1},{4,6},{5,7},{6,4},{7,5},{8,10},{9,11},{10,... | collective-permute-start | bytes 27656 | tf_op jit(solution)/shard_map/ppermute | solution.py:133
  255.5 3.1 %collective-permute-start.26 = (f32[6,384]{1,0:T(8,128)S(1)}, f32[6,384]{1,0:T(8,128)S(1)}, u32[]{:S(2)}, u32[]{:S(2)}) collective-permute-start(f32[6,384]{1,0:T(8,128)S(1)} %get-tuple-element.30), channel_id=1, source_target_pairs={{0,1},{1,2},{2,3},{3,0},{4,5},{5,6},{6,7},{7,4},{8,9},{9,10},{10,1... | collective-permute-start | bytes 27656 | tf_op jit(solution)/shard_map/ppermute | solution.py:133
Sparse Core Ops, SparseCore 0:
  8.9 83.2 all-gather.6
  93.8 26.0 all-gather.4
  133.3 47.1 reduce-scatter.1
  187.3 46.6 all-gather.8

commit v17 on v16

--- a/solution.py
+++ b/solution.py
@@ -79,10 +79,7 @@
         act_rot, grad_all, (((0,), (0,)), ((), ())), preferred_element_type=jnp.float32
     )
     eig_sum = jnp.sum(eig_values.astype(jnp.float32))
-    group_sum = eig_sum
-    for shift in range(1, nb):
-        group_sum = group_sum + lax.ppermute(eig_sum, "wb", perm=[(i, (i + shift) % nb) for i in range(nb)])
-    extra = jnp.broadcast_to(group_sum, (partial_rows.shape[0], 128))
+    extra = jnp.broadcast_to(eig_sum, (partial_rows.shape[0], 128))
     reduced = lax.psum_scatter(
         jnp.concatenate([partial_rows, extra], axis=1), "wa", scatter_dimension=0, tiled=True
     )
@@ -99,14 +96,17 @@
         outgoing = lax.dynamic_index_in_dim(act_blocks, (me + shift) % nb, axis=1, keepdims=False)
         acts_near.append(lax.ppermute(outgoing, "wb", perm=[(i, (i + shift) % nb) for i in range(nb)]))
     acts_near = jnp.stack(acts_near)
-    eig_total = reduced[0, partial_rows.shape[1]]
+    column_sum = reduced[0, partial_rows.shape[1]]
+    eig_total = column_sum
+    for shift in range(1, nb):
+        eig_total = eig_total + lax.ppermute(column_sum, "wb", perm=[(i, (i + shift) % nb) for i in range(nb)])
     eig_in = eig_values.shape[0] * lax.axis_size(WIDE)
     eig_out = eig_values.shape[1]
     mean_eig = eig_total / (eig_in * eig_out)
     dampings = mean_eig * jnp.exp2(damping_index.astype(jnp.float32) - 4.0)
     payload = jnp.concatenate([gradient_rows.astype(jnp.bfloat16), eig_values], axis=1)
     grads_first, acts_near, payload = lax.optimization_barrier((grads_first, acts_near, payload))
-    second_rows, _ = lax.optimization_barrier((train_grad_rot[half:], payload))
+    second_rows, _, eig_total = lax.optimization_barrier((train_grad_rot[half:], payload, eig_total))
     grads_second = ring_gather(second_rows, "wb")
     grads_near = jnp.concatenate([grads_first, grads_second], axis=1)
     acts_near = acts_near.astype(jnp.float32)

time: 266 us -> 269 us (1.011)
  waiting for transfers between devices: 161 us -> 164 us
    ppermute x3, waiting for transfers between devices: 20.8 us -> 0.01 us  [shards(): lax.ppermute(column_sum, 'wb', perm=[(i, (i + shift) % nb) for i in range...]
    all_gather x1, waiting for transfers between devices: 0.02 us -> 18.2 us  [shards(): act_cols = lax.all_gather(act_basis, 'wa', axis=1, tiled=True)]
    ppermute x18, waiting for transfers between devices: 97.6 us -> 102 us  [ring_gather(): lax.ppermute(x, axis, perm=[(i, (i + shift) % n) for i in range(n)])]
  transfers between devices with their start and end apart: 31 -> 31, of which waited for: 14 -> 17; matrix products, arithmetic and copies ran while one was open for 14% -> 14% of each run, Pallas kernels for 0% -> 0%
where the time goes in v17:
time: 269 us
  waiting for transfers between devices  164 us (61%)
  matrix products  36 us (13%)
  starting transfers between devices  24.6 us (9%)
  other arithmetic  18.6 us (7%)
  between operations  16.3 us (6%)
  local copies, waits for them, and re-layouts  8.9 us (3%)
    ppermute x18, waiting for transfers between devices, ring_gather(): lax.ppermute(x, axis, perm=[(i, (i + shift) % n) for i in range(n)])  102 us
    ppermute x3, waiting for transfers between devices, shards(): lax.ppermute(outgoing, 'wb', perm=[(i, (i + shift) % nb) for i in range(n...  40.3 us
    dot_general x12, matrix products, score_part(): jnp.einsum('ij,sjt->sit', precond, grads_near, preferred_element_type=jnp...  26.2 us
    all_gather x1, waiting for transfers between devices, shards(): act_cols = lax.all_gather(act_basis, 'wa', axis=1, tiled=True)  18.2 us
    ppermute x18, starting transfers between devices, ring_gather(): lax.ppermute(x, axis, perm=[(i, (i + shift) % n) for i in range(n)])  18.1 us
    another operation x4, other arithmetic, ring_gather(): return jnp.stack(parts)  9.04 us
    dot_general x1, matrix products, shards(): jnp.dot(grad_tokens.reshape(nb * count, -1), grad_cols, preferred_element...  5.8 us
  transfers between devices with their start and end apart: 31, of which 17 were waited for; matrix products, arithmetic and copies ran while one was open for 14% of the time, Pallas kernels for 0%

profile of v17, /device:TPU:0, one launch (start us, length us, event | category | flops | bytes accessed | tf_op | source)
XLA Modules:
  0.0 268.7 jit_solution(7430807071861610864)
XLA Ops:
  6.5 0.7 all-gather.7.cloned.1.call-update
  7.3 0.5 collective-permute-start
  7.8 2.6 collective-permute-start.3
  10.5 1.4 collective-permute-start.5
  11.9 0.6 collective-permute-start.7
  12.5 46.7 %collective-permute-done.7 = s32[128]{0:T(128)S(1)} collective-permute-done((s32[128]{0:T(128)}, s32[128]{0:T(128)S(1)}, u32[]{:S(2)}, u32[]{:S(2)}) %collective-permute-start.7) | collective-permute-done | bytes 544 | tf_op jit(solution)/shard_map/ppermute | solution.py:29
  59.2 4.7 %collective-permute-start.8 = (s32[128]{0:T(128)}, s32[128]{0:T(128)S(1)}, u32[]{:S(2)}, u32[]{:S(2)}) collective-permute-start(s32[128]{0:T(128)} %param.12), channel_id=1, source_target_pairs={{0,3},{1,0},{2,1},{3,2},{4,7},{5,4},{6,5},{7,6},{8,11},{9,8},{10,9... | collective-permute-start | bytes 1544 | tf_op jit(solution)/shard_map/ppermute | solution.py:29
  63.9 1.4 collective-permute-done.8
  65.5 3.3 %collective-permute-done.6 = s32[128]{0:T(128)S(1)} collective-permute-done((s32[128]{0:T(128)}, s32[128]{0:T(128)S(1)}, u32[]{:S(2)}, u32[]{:S(2)}) %collective-permute-start.6) | collective-permute-done | bytes 544 | tf_op jit(solution)/shard_map/ppermute | solution.py:29
  68.9 0.7 pad_add_fusion
  69.6 11.7 %collective-permute-done.1 = bf16[128,2048]{1,0:T(8,128)(2,1)S(1)} collective-permute-done((bf16[128,2048]{1,0:T(8,128)(2,1)}, bf16[128,2048]{1,0:T(8,128)(2,1)S(1)}, u32[]{:S(2)}, u32[]{:S(2)}) %collective-permute-start.1) | collective-permute-done | bytes 524320 | tf_op jit(solution)/shard_map/ppermute | solution.py:29
  81.4 5.0 %collective-permute-done.2 = bf16[128,2048]{1,0:T(8,128)(2,1)S(1)} collective-permute-done((bf16[128,2048]{1,0:T(8,128)(2,1)}, bf16[128,2048]{1,0:T(8,128)(2,1)S(1)}, u32[]{:S(2)}, u32[]{:S(2)}) %collective-permute-start.2) | collective-permute-done | bytes 524320 | tf_op jit(solution)/shard_map/ppermute | solution.py:29
  86.4 0.8 copy-done.7
  87.1 1.9 pad_maximum_fusion.2
  89.1 3.4 %pad_maximum_fusion = bf16[4,128,4096]{2,1,0:T(8,128)(2,1)} fusion(bf16[1,128,4096]{2,1,0:T(8,128)(2,1)} %bitcast.7, bf16[1,128,4096]{2,1,0:T(8,128)(2,1)} %bitcast.6, bf16[1,128,4096]{2,1,0:T(8,128)(2,1)S(1)} %bitcast.224, bf16[1,128,4096]{2,1,0:T(8,128)(2,1)S(1)} %bitcast.223), kind=kLoop, calls=%fused_computation.1 | loop fusion | flops 6291456 | bytes 8388608 | tf_op jit(solution)/shard_map/stack | solution.py:30
  92.5 5.8 %fusion.27 = bf16[512,512]{1,0:T(8,128)(2,1)S(1)} fusion(bf16[512,4096]{1,0:T(8,128)(2,1)} %bitcast.205, bf16[4096,512]{1,0:T(8,128)(2,1)} %all-gather.7.cloned.1.call-done, bf16[512]{0:T(512)(128)(2,1)S(1)} %fusion.105), kind=kOutput, calls=%fused_computation.54 | convolution fusion | flops 2148007936 | bytes 8913920 | tf_op jit(solution)/shard_map/dot_general | solution.py:70
  98.6 1.2 collective-permute-start.10
  99.8 1.1 collective-permute-start.11
  101.0 0.7 convert_reduce_fusion
  101.7 18.2 %all-gather.5.cloned.1.call-done = bf16[2048,256]{0,1:T(8,128)(2,1)} async-done(((bf16[2048,64]{0,1:T(8,128)(2,1)}), bf16[2048,256]{0,1:T(8,128)(2,1)}) %all-gather.5.cloned.1.call-update) | async-done | bytes 1048592 | tf_op jit(solution)/shard_map/all_gather | solution.py:64
  119.9 2.0 convolution_convert_fusion.1
  122.1 0.9 collective-permute-done.11
  123.0 1.6 collective-permute-done.9
  124.5 2.1 fusion
  126.6 2.2 concatenate.30
  128.9 1.6 fusion.107
  130.7 1.4 collective-permute-start.13
  132.1 1.4 collective-permute-start.14
  133.6 0.7 collective-permute-start.16
  134.3 36.5 %collective-permute-done.15 = bf16[4,64,384]{2,1,0:T(8,128)(2,1)S(1)} collective-permute-done((bf16[4,64,384]{2,1,0:T(8,128)(2,1)S(1)}, bf16[4,64,384]{2,1,0:T(8,128)(2,1)S(1)}, u32[]{:S(2)}, u32[]{:S(2)}) %collective-permute-start.15) | collective-permute-done | bytes 196640 | tf_op jit(solution)/shard_map/ppermute | solution.py:97
  170.9 1.3 collective-permute-done.16
  172.1 2.5 collective-permute-done.17
  174.8 3.1 %pad_maximum_fusion.1 = bf16[4,1024,384]{2,1,0:T(8,128)(2,1)} fusion(bf16[1,1024,384]{2,1,0:T(8,128)(2,1)} %bitcast.22, bf16[1,1024,384]{2,1,0:T(8,128)(2,1)} %bitcast.21, bf16[1,1024,384]{2,1,0:T(8,128)(2,1)S(1)} %bitcast.225, bf16[1,1024,384]{2,1,0:T(8,128)(2,1)S(1)} %bitcast.207), kind=kLoop, calls=%fused_computation.16 | loop fusion | flops 4718592 | bytes 6291456 | tf_op jit(solution)/shard_map/stack | solution.py:30
  177.9 1.2 slice.87
  179.0 1.1 collective-permute-start.18
  180.1 1.2 collective-permute-start.19
  181.5 1.1 slice.86
  183.5 0.9 pad_maximum_fusion.4
  187.0 0.4 collective-permute-start.21
  187.4 0.9 collective-permute-start.22
  188.3 1.4 collective-permute-start.23
  190.5 0.7 fusion.108
  191.2 14.9 %collective-permute-done.21 = bf16[1024,384]{1,0:T(8,128)(2,1)} collective-permute-done((bf16[1024,384]{1,0:T(8,128)(2,1)S(1)}, bf16[1024,384]{1,0:T(8,128)(2,1)}, u32[]{:S(2)}, u32[]{:S(2)}) %collective-permute-start.21) | collective-permute-done | bytes 786464 | tf_op jit(solution)/shard_map/ppermute | solution.py:29
  206.1 1.8 collective-permute-done.22
  207.9 14.6 %collective-permute-done.23 = bf16[1024,384]{1,0:T(8,128)(2,1)} collective-permute-done((bf16[1024,384]{1,0:T(8,128)(2,1)S(1)}, bf16[1024,384]{1,0:T(8,128)(2,1)}, u32[]{:S(2)}, u32[]{:S(2)}) %collective-permute-start.23) | collective-permute-done | bytes 786464 | tf_op jit(solution)/shard_map/ppermute | solution.py:29
  222.4 4.0 %maximum_maximum_fusion = bf16[4,2048,384]{2,1,0:T(8,128)(2,1)S(1)} fusion(bf16[1,1024,384]{2,1,0:T(8,128)(2,1)} %bitcast.37, bf16[1,1024,384]{2,1,0:T(8,128)(2,1)} %bitcast.36, bf16[1,1024,384]{2,1,0:T(8,128)(2,1)} %bitcast.35, bf16[1,1024,384]{2,1,0:T(8,128)(2,1)S(1)} %bitcast.206, bf16[4,1024,384]{2,1,0:T(8,128)(2,1)} %pad_maximum_fusion.1), kind=kLoop, calls=%fused_computation | loop fusion | flops 31457280 | bytes 12582912 | tf_op jit(solution)/shard_map/concatenate | solution.py:111
  226.4 1.9 fusion.35
  228.3 1.8 fusion.36
  230.2 1.8 fusion.37
  232.0 1.9 fusion.38
  233.9 1.8 fusion.39
  235.7 1.8 fusion.40
  237.7 2.1 fusion.14
  239.8 5.0 %fusion.26 = f32[4,384]{1,0:T(4,128)S(1)} fusion(f32[4,192,384]{2,1,0:T(8,128)S(1)} %bitcast.216, bf16[4,2048,384]{2,1,0:T(8,128)(2,1)} %copy-done, f32[]{:T(128)} %bitcast.54, bf16[192,4096]{1,0:T(8,128)(2,1)S(1)} %bitcast.210), kind=kOutput, calls=%fused_computation.53 | convolution fusion | flops 1210513920 | bytes 9050116 | tf_op jit(solution)/shard_map/ij,sjt->sit/dot_general | solution.py:120
  244.9 2.0 fusion.25
  246.9 2.0 fusion.24
  248.9 2.1 fusion.23
  251.0 2.0 fusion.22
  253.1 2.0 fusion.21
  255.3 2.3 collective-permute-start.24
  257.6 0.8 collective-permute-start.25
  258.5 0.5 collective-permute-done.24
  259.0 2.3 collective-permute-done.25
  261.6 0.6 fusion.104
  (89 shorter events, 3.8 us)
Async XLA Ops:
  6.5 86.0 %all-gather.7.cloned.1.call-start = ((), (), s32[]{:S(2)}) async-start(), calls=%async_computation.2 | async-start | bytes 5242880 | tf_op jit(solution)/shard_map/all_gather | solution.py:65
  7.3 112.7 %all-gather.5.cloned.1.call-start = ((), (), s32[]{:S(2)}) async-start(), calls=%async_computation.1 | async-start | bytes 1310720 | tf_op jit(solution)/shard_map/all_gather | solution.py:64
  7.3 61.5 %collective-permute-start = (bf16[128,2048]{1,0:T(8,128)(2,1)}, bf16[128,2048]{1,0:T(8,128)(2,1)S(1)}, u32[]{:S(2)}, u32[]{:S(2)}) collective-permute-start(bf16[128,2048]{1,0:T(8,128)(2,1)} %param.10), channel_id=1, source_target_pairs={{0,1},{1,2},{2,3},{3,0},{4,5},{5,6},{6,7},{7,4},{8,9},{9,10},{10,1... | collective-permute-start | bytes 1572872 | tf_op jit(solution)/shard_map/ppermute | solution.py:29
  7.8 81.2 %collective-permute-start.3 = (bf16[128,4096]{1,0:T(8,128)(2,1)}, bf16[128,4096]{1,0:T(8,128)(2,1)S(1)}, u32[]{:S(2)}, u32[]{:S(2)}) collective-permute-start(bf16[128,4096]{1,0:T(8,128)(2,1)} %param.11), channel_id=1, source_target_pairs={{0,1},{1,2},{2,3},{3,0},{4,5},{5,6},{6,7},{7,4},{8,9},{9,10},{10,1... | collective-permute-start | bytes 3145736 | tf_op jit(solution)/shard_map/ppermute | solution.py:29
  10.4 78.6 %collective-permute-start.4 = (bf16[128,4096]{1,0:T(8,128)(2,1)}, bf16[128,4096]{1,0:T(8,128)(2,1)}, u32[]{:S(2)}, u32[]{:S(2)}) collective-permute-start(bf16[128,4096]{1,0:T(8,128)(2,1)} %param.11), channel_id=1, source_target_pairs={{0,2},{1,3},{2,0},{3,1},{4,6},{5,7},{6,4},{7,5},{8,10},{9,11},{10,... | collective-permute-start | bytes 3145736 | tf_op jit(solution)/shard_map/ppermute | solution.py:29
  10.5 78.6 %collective-permute-start.5 = (bf16[128,4096]{1,0:T(8,128)(2,1)}, bf16[128,4096]{1,0:T(8,128)(2,1)}, u32[]{:S(2)}, u32[]{:S(2)}) collective-permute-start(bf16[128,4096]{1,0:T(8,128)(2,1)} %param.11), channel_id=1, source_target_pairs={{0,3},{1,0},{2,1},{3,2},{4,7},{5,4},{6,5},{7,6},{8,11},{9,8},{10,9... | collective-permute-start | bytes 3145736 | tf_op jit(solution)/shard_map/ppermute | solution.py:29
  11.9 47.3 %collective-permute-start.7 = (s32[128]{0:T(128)}, s32[128]{0:T(128)S(1)}, u32[]{:S(2)}, u32[]{:S(2)}) collective-permute-start(s32[128]{0:T(128)} %param.12), channel_id=1, source_target_pairs={{0,2},{1,3},{2,0},{3,1},{4,6},{5,7},{6,4},{7,5},{8,10},{9,11},{10,... | collective-permute-start | bytes 1544 | tf_op jit(solution)/shard_map/ppermute | solution.py:29
  59.2 6.1 %collective-permute-start.8 = (s32[128]{0:T(128)}, s32[128]{0:T(128)S(1)}, u32[]{:S(2)}, u32[]{:S(2)}) collective-permute-start(s32[128]{0:T(128)} %param.12), channel_id=1, source_target_pairs={{0,3},{1,0},{2,1},{3,2},{4,7},{5,4},{6,5},{7,6},{8,11},{9,8},{10,9... | collective-permute-start | bytes 1544 | tf_op jit(solution)/shard_map/ppermute | solution.py:29
  65.3 3.4 %collective-permute-start.6 = (s32[128]{0:T(128)}, s32[128]{0:T(128)S(1)}, u32[]{:S(2)}, u32[]{:S(2)}) collective-permute-start(s32[128]{0:T(128)} %param.12), channel_id=1, source_target_pairs={{0,1},{1,2},{2,3},{3,0},{4,5},{5,6},{6,7},{7,4},{8,9},{9,10},{10,1... | collective-permute-start | bytes 1544 | tf_op jit(solution)/shard_map/ppermute | solution.py:29
  68.8 12.6 %collective-permute-start.1 = (bf16[128,2048]{1,0:T(8,128)(2,1)}, bf16[128,2048]{1,0:T(8,128)(2,1)S(1)}, u32[]{:S(2)}, u32[]{:S(2)}) collective-permute-start(bf16[128,2048]{1,0:T(8,128)(2,1)} %param.10), channel_id=1, source_target_pairs={{0,2},{1,3},{2,0},{3,1},{4,6},{5,7},{6,4},{7,5},{8,10},{9,11},{10,... | collective-permute-start | bytes 1572872 | tf_op jit(solution)/shard_map/ppermute | solution.py:29
  68.8 17.6 %copy-start.5 = (bf16[128,2048]{1,0:T(8,128)(2,1)}, bf16[128,2048]{1,0:T(8,128)(2,1)S(1)}, u32[]{:S(2)}) copy-start(bf16[128,2048]{1,0:T(8,128)(2,1)S(1)} %collective-permute-done) | copy-start | bytes 1572868
  68.8 17.6 %collective-permute-start.2 = (bf16[128,2048]{1,0:T(8,128)(2,1)}, bf16[128,2048]{1,0:T(8,128)(2,1)S(1)}, u32[]{:S(2)}, u32[]{:S(2)}) collective-permute-start(bf16[128,2048]{1,0:T(8,128)(2,1)} %param.10), channel_id=1, source_target_pairs={{0,3},{1,0},{2,1},{3,2},{4,7},{5,4},{6,5},{7,6},{8,11},{9,8},{10,9... | collective-permute-start | bytes 1572872 | tf_op jit(solution)/shard_map/ppermute | solution.py:29
  68.9 109.0 %reduce-scatter.2.cloned.1.call-start = ((), (), s32[]{:S(2)}) async-start(), calls=%async_computation.3 | async-start | bytes 2785280 | tf_op jit(solution)/shard_map/reduce_scatter | solution.py:83
  81.4 5.0 %copy-start.6 = (bf16[128,2048]{1,0:T(8,128)(2,1)}, bf16[128,2048]{1,0:T(8,128)(2,1)S(1)}, u32[]{:S(2)}) copy-start(bf16[128,2048]{1,0:T(8,128)(2,1)S(1)} %collective-permute-done.1) | copy-start | bytes 1572868
  86.3 0.8 copy-start.7
  87.1 1.9 copy-start.3
  98.3 2.7 copy-start.2
  98.6 23.5 %collective-permute-start.10 = (bf16[512,512]{1,0:T(8,128)(2,1)S(1)}, bf16[512,512]{1,0:T(8,128)(2,1)}, u32[]{:S(2)}, u32[]{:S(2)}) collective-permute-start(bf16[512,512]{1,0:T(8,128)(2,1)S(1)} %bitcast.228), channel_id=1, source_target_pairs={{0,2},{1,3},{2,0},{3,1},{4,6},{5,7},{6,4},{7,5},{8,10},{9,11},{10,... | collective-permute-start | bytes 1572872 | tf_op jit(solution)/shard_map/ppermute | solution.py:29
  99.8 23.2 %collective-permute-start.11 = (bf16[512,512]{1,0:T(8,128)(2,1)S(1)}, bf16[512,512]{1,0:T(8,128)(2,1)}, u32[]{:S(2)}, u32[]{:S(2)}) collective-permute-start(bf16[512,512]{1,0:T(8,128)(2,1)S(1)} %bitcast.229), channel_id=1, source_target_pairs={{0,3},{1,0},{2,1},{3,2},{4,7},{5,4},{6,5},{7,6},{8,11},{9,8},{10,9... | collective-permute-start | bytes 1572872 | tf_op jit(solution)/shard_map/ppermute | solution.py:29
  100.9 23.6 %collective-permute-start.9 = (bf16[512,512]{1,0:T(8,128)(2,1)S(1)}, bf16[512,512]{1,0:T(8,128)(2,1)}, u32[]{:S(2)}, u32[]{:S(2)}) collective-permute-start(bf16[512,512]{1,0:T(8,128)(2,1)S(1)} %bitcast.230), channel_id=1, source_target_pairs={{0,1},{1,2},{2,3},{3,0},{4,5},{5,6},{6,7},{7,4},{8,9},{9,10},{10,1... | collective-permute-start | bytes 1572872 | tf_op jit(solution)/shard_map/ppermute | solution.py:29
  128.9 4.6 %copy-start.4 = (bf16[1024,384]{1,0:T(8,128)(2,1)S(1)}, bf16[1024,384]{1,0:T(8,128)(2,1)}, u32[]{:S(2)}) copy-start(bf16[1024,384]{1,0:T(8,128)(2,1)} %param.17) | copy-start | bytes 2359300
  128.9 108.7 %all-gather.9.cloned.1.call-start = ((), (), s32[]{:S(2)}) async-start(), calls=%async_computation.4 | async-start | bytes 2621440 | tf_op jit(solution)/shard_map/all_gather | solution.py:126
  130.5 44.2 %collective-permute-start.12 = (bf16[1024,384]{1,0:T(8,128)(2,1)S(1)}, bf16[1024,384]{1,0:T(8,128)(2,1)S(1)}, u32[]{:S(2)}, u32[]{:S(2)}) collective-permute-start(bf16[1024,384]{1,0:T(8,128)(2,1)S(1)} %get-tuple-element.17), channel_id=1, source_target_pairs={{0,1},{1,2},{2,3},{3,0},{4,5},{5,6},{6,7},{7,4},{8,9},{9,10},{10,1... | collective-permute-start | bytes 2359304 | tf_op jit(solution)/shard_map/ppermute | solution.py:29
  130.7 44.1 %collective-permute-start.13 = (bf16[1024,384]{1,0:T(8,128)(2,1)S(1)}, bf16[1024,384]{1,0:T(8,128)(2,1)}, u32[]{:S(2)}, u32[]{:S(2)}) collective-permute-start(bf16[1024,384]{1,0:T(8,128)(2,1)S(1)} %get-tuple-element.17), channel_id=1, source_target_pairs={{0,2},{1,3},{2,0},{3,1},{4,6},{5,7},{6,4},{7,5},{8,10},{9,11},{10,... | collective-permute-start | bytes 2359304 | tf_op jit(solution)/shard_map/ppermute | solution.py:29
  132.1 42.7 %collective-permute-start.14 = (bf16[1024,384]{1,0:T(8,128)(2,1)S(1)}, bf16[1024,384]{1,0:T(8,128)(2,1)}, u32[]{:S(2)}, u32[]{:S(2)}) collective-permute-start(bf16[1024,384]{1,0:T(8,128)(2,1)S(1)} %get-tuple-element.17), channel_id=1, source_target_pairs={{0,3},{1,0},{2,1},{3,2},{4,7},{5,4},{6,5},{7,6},{8,11},{9,8},{10,9... | collective-permute-start | bytes 2359304 | tf_op jit(solution)/shard_map/ppermute | solution.py:29
  133.6 37.3 %collective-permute-start.15 = (bf16[4,64,384]{2,1,0:T(8,128)(2,1)S(1)}, bf16[4,64,384]{2,1,0:T(8,128)(2,1)S(1)}, u32[]{:S(2)}, u32[]{:S(2)}) collective-permute-start(bf16[4,64,384]{2,1,0:T(8,128)(2,1)S(1)} %get-tuple-element.28), channel_id=1, source_target_pairs={{0,1},{1,2},{2,3},{3,0},{4,5},{5,6},{6,7},{7,4},{8,9},{9,10},{10,1... | collective-permute-start | bytes 589832 | tf_op jit(solution)/shard_map/ppermute | solution.py:97
  133.6 38.5 %collective-permute-start.16 = (bf16[4,64,384]{2,1,0:T(8,128)(2,1)S(1)}, bf16[4,64,384]{2,1,0:T(8,128)(2,1)S(1)}, u32[]{:S(2)}, u32[]{:S(2)}) collective-permute-start(bf16[4,64,384]{2,1,0:T(8,128)(2,1)S(1)} %get-tuple-element.27), channel_id=1, source_target_pairs={{0,2},{1,3},{2,0},{3,1},{4,6},{5,7},{6,4},{7,5},{8,10},{9,11},{10,... | collective-permute-start | bytes 589832 | tf_op jit(solution)/shard_map/ppermute | solution.py:97
  170.8 3.8 %collective-permute-start.17 = (bf16[4,64,384]{2,1,0:T(8,128)(2,1)S(1)}, bf16[4,64,384]{2,1,0:T(8,128)(2,1)S(1)}, u32[]{:S(2)}, u32[]{:S(2)}) collective-permute-start(bf16[4,64,384]{2,1,0:T(8,128)(2,1)S(1)} %get-tuple-element.26), channel_id=1, source_target_pairs={{0,3},{1,0},{2,1},{3,2},{4,7},{5,4},{6,5},{7,6},{8,11},{9,8},{10,9... | collective-permute-start | bytes 589832 | tf_op jit(solution)/shard_map/ppermute | solution.py:97
  179.0 5.3 %collective-permute-start.18 = (f32[]{:T(128)}, f32[]{:T(128)}, u32[]{:S(2)}, u32[]{:S(2)}) collective-permute-start(f32[]{:T(128)} %bitcast.33), channel_id=1, source_target_pairs={{0,1},{1,2},{2,3},{3,0},{4,5},{5,6},{6,7},{7,4},{8,9},{9,10},{10,1... | collective-permute-start | bytes 20 | tf_op jit(solution)/shard_map/ppermute | solution.py:102
  180.1 5.5 %collective-permute-start.19 = (f32[]{:T(128)}, f32[]{:T(128)}, u32[]{:S(2)}, u32[]{:S(2)}) collective-permute-start(f32[]{:T(128)} %bitcast.33), channel_id=1, source_target_pairs={{0,2},{1,3},{2,0},{3,1},{4,6},{5,7},{6,4},{7,5},{8,10},{9,11},{10,... | collective-permute-start | bytes 20 | tf_op jit(solution)/shard_map/ppermute | solution.py:102
  181.3 5.0 %collective-permute-start.20 = (f32[]{:T(128)}, f32[]{:T(128)}, u32[]{:S(2)}, u32[]{:S(2)}) collective-permute-start(f32[]{:T(128)} %bitcast.33), channel_id=1, source_target_pairs={{0,3},{1,0},{2,1},{3,2},{4,7},{5,4},{6,5},{7,6},{8,11},{9,8},{10,9... | collective-permute-start | bytes 20 | tf_op jit(solution)/shard_map/ppermute | solution.py:102
  187.0 19.1 %collective-permute-start.21 = (bf16[1024,384]{1,0:T(8,128)(2,1)S(1)}, bf16[1024,384]{1,0:T(8,128)(2,1)}, u32[]{:S(2)}, u32[]{:S(2)}) collective-permute-start(bf16[1024,384]{1,0:T(8,128)(2,1)S(1)} %get-tuple-element.21), channel_id=1, source_target_pairs={{0,1},{1,2},{2,3},{3,0},{4,5},{5,6},{6,7},{7,4},{8,9},{9,10},{10,1... | collective-permute-start | bytes 2359304 | tf_op jit(solution)/shard_map/ppermute | solution.py:29
  187.4 20.5 %collective-permute-start.22 = (bf16[1024,384]{1,0:T(8,128)(2,1)S(1)}, bf16[1024,384]{1,0:T(8,128)(2,1)}, u32[]{:S(2)}, u32[]{:S(2)}) collective-permute-start(bf16[1024,384]{1,0:T(8,128)(2,1)S(1)} %get-tuple-element.21), channel_id=1, source_target_pairs={{0,2},{1,3},{2,0},{3,1},{4,6},{5,7},{6,4},{7,5},{8,10},{9,11},{10,... | collective-permute-start | bytes 2359304 | tf_op jit(solution)/shard_map/ppermute | solution.py:29
  188.3 34.1 %collective-permute-start.23 = (bf16[1024,384]{1,0:T(8,128)(2,1)S(1)}, bf16[1024,384]{1,0:T(8,128)(2,1)}, u32[]{:S(2)}, u32[]{:S(2)}) collective-permute-start(bf16[1024,384]{1,0:T(8,128)(2,1)S(1)} %get-tuple-element.21), channel_id=1, source_target_pairs={{0,3},{1,0},{2,1},{3,2},{4,7},{5,4},{6,5},{7,6},{8,11},{9,8},{10,9... | collective-permute-start | bytes 2359304 | tf_op jit(solution)/shard_map/ppermute | solution.py:29
  189.9 0.7 copy-start.9
  222.4 4.0 %copy-start.1 = (bf16[64,4096]{1,0:T(8,128)(2,1)S(1)}, bf16[64,4096]{1,0:T(8,128)(2,1)}, u32[]{:S(2)}) copy-start(bf16[64,4096]{1,0:T(8,128)(2,1)} %pad_maximum_fusion.4) | copy-start | bytes 1572868
  226.4 9.3 %copy-start = (bf16[4,2048,384]{2,1,0:T(8,128)(2,1)}, bf16[4,2048,384]{2,1,0:T(8,128)(2,1)S(1)}, u32[]{:S(2)}) copy-start(bf16[4,2048,384]{2,1,0:T(8,128)(2,1)S(1)} %maximum_maximum_fusion) | copy-start | bytes 18874372
  237.6 7.2 %slice-start = ((s8[6291456]{0:T(1024)(128)(4,1)}), s8[4194304]{0:T(1024)(128)(4,1)S(1)}, s32[]{:S(2)}) async-start(s8[6291456]{0:T(1024)(128)(4,1)} %bitcast.203), calls=%async_computation.5 | async-start | bytes 8388608
  239.8 5.1 %slice-start.1 = ((s8[6291456]{0:T(1024)(128)(4,1)}), s8[2097152]{0:T(1024)(128)(4,1)S(1)}, s32[]{:S(2)}) async-start(s8[6291456]{0:T(1024)(128)(4,1)} %bitcast.203), calls=%async_computation.6 | async-start | bytes 4194304
  253.0 5.4 %copy-start.8 = (s32[384]{0:T(512)S(1)}, s32[384]{0:T(512)}, u32[]{:S(2)}) copy-start(s32[384]{0:T(512)} %param.19) | copy-start | bytes 4612
  255.3 3.7 %collective-permute-start.24 = (f32[6,384]{1,0:T(8,128)S(1)}, f32[6,384]{1,0:T(8,128)S(1)}, u32[]{:S(2)}, u32[]{:S(2)}) collective-permute-start(f32[6,384]{1,0:T(8,128)S(1)} %get-tuple-element.29), channel_id=1, source_target_pairs={{0,3},{1,0},{2,1},{3,2},{4,7},{5,4},{6,5},{7,6},{8,11},{9,8},{10,9... | collective-permute-start | bytes 27656 | tf_op jit(solution)/shard_map/ppermute | solution.py:133
  257.6 3.7 %collective-permute-start.25 = (f32[6,384]{1,0:T(8,128)S(1)}, f32[6,384]{1,0:T(8,128)S(1)}, u32[]{:S(2)}, u32[]{:S(2)}) collective-permute-start(f32[6,384]{1,0:T(8,128)S(1)} %get-tuple-element.31), channel_id=1, source_target_pairs={{0,2},{1,3},{2,0},{3,1},{4,6},{5,7},{6,4},{7,5},{8,10},{9,11},{10,... | collective-permute-start | bytes 27656 | tf_op jit(solution)/shard_map/ppermute | solution.py:133
  258.4 3.1 %collective-permute-start.26 = (f32[6,384]{1,0:T(8,128)S(1)}, f32[6,384]{1,0:T(8,128)S(1)}, u32[]{:S(2)}, u32[]{:S(2)}) collective-permute-start(f32[6,384]{1,0:T(8,128)S(1)} %get-tuple-element.30), channel_id=1, source_target_pairs={{0,1},{1,2},{2,3},{3,0},{4,5},{5,6},{6,7},{7,4},{8,9},{9,10},{10,1... | collective-permute-start | bytes 27656 | tf_op jit(solution)/shard_map/ppermute | solution.py:133
Sparse Core Ops, SparseCore 0:
  8.9 83.2 all-gather.6
  93.8 26.0 all-gather.4
  129.0 46.5 reduce-scatter.1
  189.8 46.5 all-gather.8

commit v18 on v16

--- a/solution.py
+++ b/solution.py
@@ -109,16 +109,18 @@
     second_rows, _ = lax.optimization_barrier((train_grad_rot[half:], payload))
     grads_second = ring_gather(second_rows, "wb")
     grads_near = jnp.concatenate([grads_first, grads_second], axis=1)
+    grads_side = grads_near.transpose(1, 0, 2).reshape(grads_near.shape[1], -1)
     acts_near = acts_near.astype(jnp.float32)
 
     def score_part(held, acts):
         grad_wide = held[:, :eig_out].astype(jnp.float32)
         eig_wide = held[:, eig_out:].astype(jnp.float32)
+        acts_side = acts.transpose(1, 0, 2).reshape(acts.shape[1], -1)
         results = []
         for damping in range(dampings.shape[0]):
             precond = (grad_wide / (eig_wide + dampings[damping])).astype(jnp.bfloat16)
-            projected = jnp.einsum("ij,sjt->sit", precond, grads_near, preferred_element_type=jnp.float32)
-            results.append(jnp.sum(projected * acts, axis=1))
+            projected = jnp.dot(precond, grads_side, preferred_element_type=jnp.float32)
+            results.append(jnp.sum(projected * acts_side, axis=0).reshape(nb, -1))
         return jnp.stack(results, axis=1)
 
     mine = lax.axis_index("wa")

time: 266 us -> 297 us (1.12)
  matrix products: 36 us -> 60.7 us
  local copies, waits for them, and re-layouts: 9.27 us -> 14.4 us
    dot_general x12, matrix products: 26.2 us -> 49.9 us  [score_part(): projected = jnp.dot(precond, grads_side, preferred_element_type=jnp.float32)]
  transfers between devices with their start and end apart: 31 -> 31, of which waited for: 14 -> 14; matrix products, arithmetic and copies ran while one was open for 14% -> 21% of each run, Pallas kernels for 0% -> 0%
where the time goes in v18:
time: 297 us; the launch traced here: 296 us
  waiting for transfers between devices  160 us (54%)
  matrix products  60.7 us (20%)
  starting transfers between devices  24.5 us (8%)
  other arithmetic  19.2 us (6%)
  between operations  17.6 us (6%)
  local copies, waits for them, and re-layouts  14.4 us (5%)
    ppermute x18, waiting for transfers between devices, ring_gather(): lax.ppermute(x, axis, perm=[(i, (i + shift) % n) for i in range(n)])  96.8 us
    dot_general x12, matrix products, score_part(): projected = jnp.dot(precond, grads_side, preferred_element_type=jnp.float32)  49.9 us
    ppermute x3, waiting for transfers between devices, shards(): lax.ppermute(outgoing, 'wb', perm=[(i, (i + shift) % nb) for i in range(n...  38.7 us
    ppermute x3, waiting for transfers between devices, shards(): lax.ppermute(eig_sum, 'wb', perm=[(i, (i + shift) % nb) for i in range(nb)])  21.1 us
    ppermute x18, starting transfers between devices, ring_gather(): lax.ppermute(x, axis, perm=[(i, (i + shift) % n) for i in range(n)])  17.8 us
    another operation x4, other arithmetic, ring_gather(): return jnp.stack(parts)  9.1 us
    dot_general x1, matrix products, shards(): jnp.dot(grad_tokens.reshape(nb * count, -1), grad_cols, preferred_element...  6.6 us
  transfers between devices with their start and end apart: 31, of which 14 were waited for; matrix products, arithmetic and copies ran while one was open for 21% of the time, Pallas kernels for 0%

profile of v18, /device:TPU:0, one launch (start us, length us, event | category | flops | bytes accessed | tf_op | source)
XLA Modules:
  0.0 296.3 jit_solution(3491514850002710774)
XLA Ops:
  6.5 0.7 all-gather.7.cloned.1.call-update
  7.8 2.6 collective-permute-start.3
  10.5 1.4 collective-permute-start.5
  12.5 46.7 %collective-permute-done.7 = s32[128]{0:T(128)S(1)} collective-permute-done((s32[128]{0:T(128)}, s32[128]{0:T(128)S(1)}, u32[]{:S(2)}, u32[]{:S(2)}) %collective-permute-start.7) | collective-permute-done | bytes 544 | tf_op jit(solution)/shard_map/ppermute | solution.py:29
  59.2 4.7 %collective-permute-start.8 = (s32[128]{0:T(128)}, s32[128]{0:T(128)S(1)}, u32[]{:S(2)}, u32[]{:S(2)}) collective-permute-start(s32[128]{0:T(128)} %param.12), channel_id=1, source_target_pairs={{0,3},{1,0},{2,1},{3,2},{4,7},{5,4},{6,5},{7,6},{8,11},{9,8},{10,9... | collective-permute-start | bytes 1544 | tf_op jit(solution)/shard_map/ppermute | solution.py:29
  63.9 1.4 collective-permute-done.8
  65.5 3.3 %collective-permute-done.6 = s32[128]{0:T(128)S(1)} collective-permute-done((s32[128]{0:T(128)}, s32[128]{0:T(128)S(1)}, u32[]{:S(2)}, u32[]{:S(2)}) %collective-permute-start.6) | collective-permute-done | bytes 544 | tf_op jit(solution)/shard_map/ppermute | solution.py:29
  68.9 0.7 pad_add_fusion
  69.6 11.7 %collective-permute-done.1 = bf16[128,2048]{1,0:T(8,128)(2,1)S(1)} collective-permute-done((bf16[128,2048]{1,0:T(8,128)(2,1)}, bf16[128,2048]{1,0:T(8,128)(2,1)S(1)}, u32[]{:S(2)}, u32[]{:S(2)}) %collective-permute-start.1) | collective-permute-done | bytes 524320 | tf_op jit(solution)/shard_map/ppermute | solution.py:29
  81.4 5.0 %collective-permute-done.2 = bf16[128,2048]{1,0:T(8,128)(2,1)S(1)} collective-permute-done((bf16[128,2048]{1,0:T(8,128)(2,1)}, bf16[128,2048]{1,0:T(8,128)(2,1)S(1)}, u32[]{:S(2)}, u32[]{:S(2)}) %collective-permute-start.2) | collective-permute-done | bytes 524320 | tf_op jit(solution)/shard_map/ppermute | solution.py:29
  86.4 0.8 copy-done.7
  87.1 1.9 pad_maximum_fusion.2
  89.1 3.4 %pad_maximum_fusion = bf16[4,128,4096]{2,1,0:T(8,128)(2,1)} fusion(bf16[1,128,4096]{2,1,0:T(8,128)(2,1)} %bitcast.7, bf16[1,128,4096]{2,1,0:T(8,128)(2,1)} %bitcast.6, bf16[1,128,4096]{2,1,0:T(8,128)(2,1)S(1)} %bitcast.142, bf16[1,128,4096]{2,1,0:T(8,128)(2,1)S(1)} %bitcast.141), kind=kLoop, calls=%fused_computation.1 | loop fusion | flops 6291456 | bytes 8388608 | tf_op jit(solution)/shard_map/stack | solution.py:30
  92.5 6.6 %fusion.21 = bf16[512,512]{1,0:T(8,128)(2,1)} fusion(bf16[512,4096]{1,0:T(8,128)(2,1)} %bitcast.123, bf16[4096,512]{1,0:T(8,128)(2,1)} %all-gather.7.cloned.1.call-done, bf16[512]{0:T(512)(128)(2,1)S(1)} %fusion.93), kind=kOutput, calls=%fused_computation.54 | convolution fusion | flops 2148007936 | bytes 8913920 | tf_op jit(solution)/shard_map/dot_general | solution.py:70
  99.1 1.1 rev.10
  100.2 1.0 fusion.43
  101.2 1.2 collective-permute-start.10
  102.4 1.1 collective-permute-start.11
  103.6 0.7 convert_reduce_fusion
  104.3 1.7 collective-permute-start.18
  106.4 21.1 %collective-permute-done.18 = f32[]{:T(128)} collective-permute-done((f32[]{:T(128)}, f32[]{:T(128)}, u32[]{:S(2)}, u32[]{:S(2)}) %collective-permute-start.18) | collective-permute-done | bytes 36 | tf_op jit(solution)/shard_map/ppermute | solution.py:84
  130.1 2.0 convolution_convert_fusion.1
  132.2 2.2 fusion
  134.5 1.6 concatenate.30
  136.1 1.5 fusion.95
  138.0 1.1 collective-permute-start.12
  139.1 0.8 collective-permute-start.13
  139.9 1.0 collective-permute-start.14
  140.9 1.3 dynamic-slice_bitcast_fusion.4
  142.3 0.7 collective-permute-start.16
  143.0 34.3 %collective-permute-done.15 = bf16[4,64,384]{2,1,0:T(8,128)(2,1)S(1)} collective-permute-done((bf16[4,64,384]{2,1,0:T(8,128)(2,1)S(1)}, bf16[4,64,384]{2,1,0:T(8,128)(2,1)S(1)}, u32[]{:S(2)}, u32[]{:S(2)}) %collective-permute-start.15) | collective-permute-done | bytes 196640 | tf_op jit(solution)/shard_map/ppermute | solution.py:100
  177.5 3.2 %collective-permute-done.16 = bf16[4,64,384]{2,1,0:T(8,128)(2,1)} collective-permute-done((bf16[4,64,384]{2,1,0:T(8,128)(2,1)S(1)}, bf16[4,64,384]{2,1,0:T(8,128)(2,1)}, u32[]{:S(2)}, u32[]{:S(2)}) %collective-permute-start.16) | collective-permute-done | bytes 196640 | tf_op jit(solution)/shard_map/ppermute | solution.py:100
  180.7 1.3 collective-permute-done.17
  182.0 1.1 pad_maximum_fusion.3
  183.2 3.1 %pad_maximum_fusion.1 = bf16[4,1024,384]{1,2,0:T(8,128)(2,1)} fusion(bf16[1,1024,384]{1,2,0:T(8,128)(2,1)} %bitcast.22, bf16[1,1024,384]{1,2,0:T(8,128)(2,1)} %bitcast.21, bf16[1,1024,384]{1,2,0:T(8,128)(2,1)} %bitcast.20, bf16[1,1024,384]{1,2,0:T(8,128)(2,1)S(1)} %bitcast.124), kind=kLoop, calls=%fused_computation.16 | loop fusion | flops 4718592 | bytes 6291456 | tf_op jit(solution)/shard_map/stack | solution.py:30
  186.3 1.1 slice.86
  188.3 0.8 pad_maximum_fusion.4
  189.2 1.0 collective-permute-start.21
  190.2 1.4 collective-permute-start.22
  192.0 0.8 copy.20
  193.0 1.3 slice.87
  195.0 0.7 fusion.96
  195.7 12.3 %collective-permute-done.21 = bf16[1024,384]{0,1:T(8,128)(2,1)} collective-permute-done((bf16[1024,384]{0,1:T(8,128)(2,1)S(1)}, bf16[1024,384]{0,1:T(8,128)(2,1)}, u32[]{:S(2)}, u32[]{:S(2)}) %collective-permute-start.21) | collective-permute-done | bytes 786464 | tf_op jit(solution)/shard_map/ppermute | solution.py:29
  208.0 2.8 collective-permute-done.22
  210.8 13.5 %collective-permute-done.23 = bf16[1024,384]{0,1:T(8,128)(2,1)} collective-permute-done((bf16[1024,384]{0,1:T(8,128)(2,1)S(1)}, bf16[1024,384]{0,1:T(8,128)(2,1)}, u32[]{:S(2)}, u32[]{:S(2)}) %collective-permute-start.23) | collective-permute-done | bytes 786464 | tf_op jit(solution)/shard_map/ppermute | solution.py:29
  224.3 2.8 maximum_maximum_fusion
  227.1 2.6 copy-done
  229.8 2.7 fusion.28
  232.5 5.4 %fusion.27 = f32[1536]{0:T(1024)S(1)} fusion(f32[64,1536]{1,0:T(8,128)S(1)} %bitcast.116, bf16[2048,1536]{0,1:T(8,128)(2,1)} %bitcast.102, f32[]{:T(128)} %bitcast.47, bf16[64,4096]{1,0:T(8,128)(2,1)S(1)} %copy-done.1), kind=kOutput, calls=%fused_computation.73 | convolution fusion | flops 403503616 | bytes 7215108 | tf_op jit(solution)/shard_map/dot_general | solution.py:122
  237.9 5.4 %fusion.26 = f32[1536]{0:T(1024)S(1)} fusion(f32[64,1536]{1,0:T(8,128)S(1)} %bitcast.117, bf16[2048,1536]{0,1:T(8,128)(2,1)} %bitcast.103, f32[]{:T(128)} %bitcast.46, bf16[64,4096]{1,0:T(8,128)(2,1)S(1)} %copy-done.1), kind=kOutput, calls=%fused_computation.72 | convolution fusion | flops 403503616 | bytes 7215108 | tf_op jit(solution)/shard_map/dot_general | solution.py:122
  243.3 5.4 %fusion.25 = f32[1536]{0:T(1024)S(1)} fusion(f32[64,1536]{1,0:T(8,128)S(1)} %bitcast.118, bf16[2048,1536]{0,1:T(8,128)(2,1)} %bitcast.104, f32[]{:T(128)} %bitcast.45, bf16[64,4096]{1,0:T(8,128)(2,1)S(1)} %copy-done.1), kind=kOutput, calls=%fused_computation.71 | convolution fusion | flops 403503616 | bytes 7215108 | tf_op jit(solution)/shard_map/dot_general | solution.py:122
  248.8 5.4 %fusion.24 = f32[1536]{0:T(1024)S(1)} fusion(f32[64,1536]{1,0:T(8,128)S(1)} %bitcast.119, bf16[2048,1536]{0,1:T(8,128)(2,1)} %bitcast.105, f32[]{:T(128)} %bitcast.43, bf16[64,4096]{1,0:T(8,128)(2,1)S(1)} %copy-done.1), kind=kOutput, calls=%fused_computation.70 | convolution fusion | flops 403503616 | bytes 7215108 | tf_op jit(solution)/shard_map/dot_general | solution.py:122
  254.2 5.5 %fusion.23 = f32[1536]{0:T(1024)S(1)} fusion(f32[64,1536]{1,0:T(8,128)S(1)} %bitcast.120, bf16[2048,1536]{0,1:T(8,128)(2,1)} %bitcast.106, f32[]{:T(128)} %bitcast.34, bf16[64,4096]{1,0:T(8,128)(2,1)S(1)} %copy-done.1), kind=kOutput, calls=%fused_computation.69 | convolution fusion | flops 403503616 | bytes 7215108 | tf_op jit(solution)/shard_map/dot_general | solution.py:122
  259.8 2.1 fusion.14
  261.9 5.8 %fusion.20 = f32[1536]{0:T(1024)S(1)} fusion(f32[192,1536]{1,0:T(8,128)S(1)} %bitcast.134, bf16[2048,1536]{0,1:T(8,128)(2,1)} %bitcast.107, f32[]{:T(128)} %bitcast.48, bf16[192,4096]{1,0:T(8,128)(2,1)S(1)} %bitcast.128), kind=kOutput, calls=%fused_computation.53 | convolution fusion | flops 1210513920 | bytes 9050116 | tf_op jit(solution)/shard_map/dot_general | solution.py:122
  267.7 3.1 %fusion.19 = f32[1536]{0:T(1024)S(1)} fusion(f32[192,1536]{1,0:T(8,128)S(1)} %bitcast.135, bf16[2048,1536]{0,1:T(8,128)(2,1)S(1)} %bitcast.110, f32[]{:T(128)} %bitcast.47, bf16[192,4096]{1,0:T(8,128)(2,1)S(1)} %bitcast.129), kind=kOutput, calls=%fused_computation.52 | convolution fusion | flops 1210513920 | bytes 9050116 | tf_op jit(solution)/shard_map/dot_general | solution.py:122
  270.8 2.8 fusion.18
  273.6 2.8 fusion.17
  276.5 2.8 fusion.16
  279.3 2.9 fusion.15
  282.3 2.4 collective-permute-start.24
  284.7 1.4 collective-permute-start.25
  286.7 1.7 collective-permute-done.25
  288.4 0.8 collective-permute-done.26
  (94 shorter events, 5.2 us)
Async XLA Ops:
  6.5 86.0 %all-gather.7.cloned.1.call-start = ((), (), s32[]{:S(2)}) async-start(), calls=%async_computation.2 | async-start | bytes 5242880 | tf_op jit(solution)/shard_map/all_gather | solution.py:65
  7.3 122.8 %all-gather.5.cloned.1.call-start = ((), (), s32[]{:S(2)}) async-start(), calls=%async_computation.1 | async-start | bytes 1310720 | tf_op jit(solution)/shard_map/all_gather | solution.py:64
  7.3 61.5 %collective-permute-start = (bf16[128,2048]{1,0:T(8,128)(2,1)}, bf16[128,2048]{1,0:T(8,128)(2,1)S(1)}, u32[]{:S(2)}, u32[]{:S(2)}) collective-permute-start(bf16[128,2048]{1,0:T(8,128)(2,1)} %param.10), channel_id=1, source_target_pairs={{0,1},{1,2},{2,3},{3,0},{4,5},{5,6},{6,7},{7,4},{8,9},{9,10},{10,1... | collective-permute-start | bytes 1572872 | tf_op jit(solution)/shard_map/ppermute | solution.py:29
  7.8 81.2 %collective-permute-start.3 = (bf16[128,4096]{1,0:T(8,128)(2,1)}, bf16[128,4096]{1,0:T(8,128)(2,1)S(1)}, u32[]{:S(2)}, u32[]{:S(2)}) collective-permute-start(bf16[128,4096]{1,0:T(8,128)(2,1)} %param.11), channel_id=1, source_target_pairs={{0,1},{1,2},{2,3},{3,0},{4,5},{5,6},{6,7},{7,4},{8,9},{9,10},{10,1... | collective-permute-start | bytes 3145736 | tf_op jit(solution)/shard_map/ppermute | solution.py:29
  10.4 78.6 %collective-permute-start.4 = (bf16[128,4096]{1,0:T(8,128)(2,1)}, bf16[128,4096]{1,0:T(8,128)(2,1)}, u32[]{:S(2)}, u32[]{:S(2)}) collective-permute-start(bf16[128,4096]{1,0:T(8,128)(2,1)} %param.11), channel_id=1, source_target_pairs={{0,2},{1,3},{2,0},{3,1},{4,6},{5,7},{6,4},{7,5},{8,10},{9,11},{10,... | collective-permute-start | bytes 3145736 | tf_op jit(solution)/shard_map/ppermute | solution.py:29
  10.5 78.6 %collective-permute-start.5 = (bf16[128,4096]{1,0:T(8,128)(2,1)}, bf16[128,4096]{1,0:T(8,128)(2,1)}, u32[]{:S(2)}, u32[]{:S(2)}) collective-permute-start(bf16[128,4096]{1,0:T(8,128)(2,1)} %param.11), channel_id=1, source_target_pairs={{0,3},{1,0},{2,1},{3,2},{4,7},{5,4},{6,5},{7,6},{8,11},{9,8},{10,9... | collective-permute-start | bytes 3145736 | tf_op jit(solution)/shard_map/ppermute | solution.py:29
  11.9 47.3 %collective-permute-start.7 = (s32[128]{0:T(128)}, s32[128]{0:T(128)S(1)}, u32[]{:S(2)}, u32[]{:S(2)}) collective-permute-start(s32[128]{0:T(128)} %param.12), channel_id=1, source_target_pairs={{0,2},{1,3},{2,0},{3,1},{4,6},{5,7},{6,4},{7,5},{8,10},{9,11},{10,... | collective-permute-start | bytes 1544 | tf_op jit(solution)/shard_map/ppermute | solution.py:29
  59.2 6.1 %collective-permute-start.8 = (s32[128]{0:T(128)}, s32[128]{0:T(128)S(1)}, u32[]{:S(2)}, u32[]{:S(2)}) collective-permute-start(s32[128]{0:T(128)} %param.12), channel_id=1, source_target_pairs={{0,3},{1,0},{2,1},{3,2},{4,7},{5,4},{6,5},{7,6},{8,11},{9,8},{10,9... | collective-permute-start | bytes 1544 | tf_op jit(solution)/shard_map/ppermute | solution.py:29
  65.3 3.4 %collective-permute-start.6 = (s32[128]{0:T(128)}, s32[128]{0:T(128)S(1)}, u32[]{:S(2)}, u32[]{:S(2)}) collective-permute-start(s32[128]{0:T(128)} %param.12), channel_id=1, source_target_pairs={{0,1},{1,2},{2,3},{3,0},{4,5},{5,6},{6,7},{7,4},{8,9},{9,10},{10,1... | collective-permute-start | bytes 1544 | tf_op jit(solution)/shard_map/ppermute | solution.py:29
  68.8 12.6 %collective-permute-start.1 = (bf16[128,2048]{1,0:T(8,128)(2,1)}, bf16[128,2048]{1,0:T(8,128)(2,1)S(1)}, u32[]{:S(2)}, u32[]{:S(2)}) collective-permute-start(bf16[128,2048]{1,0:T(8,128)(2,1)} %param.10), channel_id=1, source_target_pairs={{0,2},{1,3},{2,0},{3,1},{4,6},{5,7},{6,4},{7,5},{8,10},{9,11},{10,... | collective-permute-start | bytes 1572872 | tf_op jit(solution)/shard_map/ppermute | solution.py:29
  68.8 17.6 %copy-start.5 = (bf16[128,2048]{1,0:T(8,128)(2,1)}, bf16[128,2048]{1,0:T(8,128)(2,1)S(1)}, u32[]{:S(2)}) copy-start(bf16[128,2048]{1,0:T(8,128)(2,1)S(1)} %collective-permute-done) | copy-start | bytes 1572868
  68.8 17.6 %collective-permute-start.2 = (bf16[128,2048]{1,0:T(8,128)(2,1)}, bf16[128,2048]{1,0:T(8,128)(2,1)S(1)}, u32[]{:S(2)}, u32[]{:S(2)}) collective-permute-start(bf16[128,2048]{1,0:T(8,128)(2,1)} %param.10), channel_id=1, source_target_pairs={{0,3},{1,0},{2,1},{3,2},{4,7},{5,4},{6,5},{7,6},{8,11},{9,8},{10,9... | collective-permute-start | bytes 1572872 | tf_op jit(solution)/shard_map/ppermute | solution.py:29
  68.9 117.5 %reduce-scatter.2.cloned.1.call-start = ((), (), s32[]{:S(2)}) async-start(), calls=%async_computation.3 | async-start | bytes 2785280 | tf_op jit(solution)/shard_map/reduce_scatter | solution.py:86
  81.4 5.0 %copy-start.6 = (bf16[128,2048]{1,0:T(8,128)(2,1)}, bf16[128,2048]{1,0:T(8,128)(2,1)S(1)}, u32[]{:S(2)}) copy-start(bf16[128,2048]{1,0:T(8,128)(2,1)S(1)} %collective-permute-done.1) | copy-start | bytes 1572868
  86.3 0.8 copy-start.7
  87.1 1.9 copy-start.4
  99.1 4.5 %copy-start.3 = (bf16[64,2048]{1,0:T(8,128)(2,1)S(1)}, bf16[64,2048]{1,0:T(8,128)(2,1)}, u32[]{:S(2)}) copy-start(bf16[64,2048]{1,0:T(8,128)(2,1)} %param.15) | copy-start | bytes 786436
  101.2 31.0 %collective-permute-start.10 = (bf16[512,512]{1,0:T(8,128)(2,1)}, bf16[512,512]{1,0:T(8,128)(2,1)}, u32[]{:S(2)}, u32[]{:S(2)}) collective-permute-start(bf16[512,512]{1,0:T(8,128)(2,1)} %bitcast.18), channel_id=1, source_target_pairs={{0,2},{1,3},{2,0},{3,1},{4,6},{5,7},{6,4},{7,5},{8,10},{9,11},{10,... | collective-permute-start | bytes 1572872 | tf_op jit(solution)/shard_map/ppermute | solution.py:29
  102.4 29.8 %collective-permute-start.11 = (bf16[512,512]{1,0:T(8,128)(2,1)}, bf16[512,512]{1,0:T(8,128)(2,1)}, u32[]{:S(2)}, u32[]{:S(2)}) collective-permute-start(bf16[512,512]{1,0:T(8,128)(2,1)} %bitcast.18), channel_id=1, source_target_pairs={{0,3},{1,0},{2,1},{3,2},{4,7},{5,4},{6,5},{7,6},{8,11},{9,8},{10,9... | collective-permute-start | bytes 1572872 | tf_op jit(solution)/shard_map/ppermute | solution.py:29
  103.5 28.7 %collective-permute-start.9 = (bf16[512,512]{1,0:T(8,128)(2,1)}, bf16[512,512]{1,0:T(8,128)(2,1)}, u32[]{:S(2)}, u32[]{:S(2)}) collective-permute-start(bf16[512,512]{1,0:T(8,128)(2,1)} %bitcast.18), channel_id=1, source_target_pairs={{0,1},{1,2},{2,3},{3,0},{4,5},{5,6},{6,7},{7,4},{8,9},{9,10},{10,1... | collective-permute-start | bytes 1572872 | tf_op jit(solution)/shard_map/ppermute | solution.py:29
  104.3 23.2 %collective-permute-start.18 = (f32[]{:T(128)}, f32[]{:T(128)}, u32[]{:S(2)}, u32[]{:S(2)}) collective-permute-start(f32[]{:T(128)} %convert_reduce_fusion), channel_id=1, source_target_pairs={{0,1},{1,2},{2,3},{3,0},{4,5},{5,6},{6,7},{7,4},{8,9},{9,10},{10,1... | collective-permute-start | bytes 20 | tf_op jit(solution)/shard_map/ppermute | solution.py:84
  106.1 22.7 %collective-permute-start.19 = (f32[]{:T(128)}, f32[]{:T(128)}, u32[]{:S(2)}, u32[]{:S(2)}) collective-permute-start(f32[]{:T(128)} %convert_reduce_fusion), channel_id=1, source_target_pairs={{0,2},{1,3},{2,0},{3,1},{4,6},{5,7},{6,4},{7,5},{8,10},{9,11},{10,... | collective-permute-start | bytes 20 | tf_op jit(solution)/shard_map/ppermute | solution.py:84
  127.5 1.9 collective-permute-start.20
  136.1 123.7 %all-gather.9.cloned.1.call-start = ((), (), s32[]{:S(2)}) async-start(), calls=%async_computation.4 | async-start | bytes 2621440 | tf_op jit(solution)/shard_map/all_gather | solution.py:128
  138.0 45.2 %collective-permute-start.12 = (bf16[1024,384]{0,1:T(8,128)(2,1)S(1)}, bf16[1024,384]{0,1:T(8,128)(2,1)}, u32[]{:S(2)}, u32[]{:S(2)}) collective-permute-start(bf16[1024,384]{0,1:T(8,128)(2,1)S(1)} %copy.21), channel_id=1, source_target_pairs={{0,1},{1,2},{2,3},{3,0},{4,5},{5,6},{6,7},{7,4},{8,9},{9,10},{10,1... | collective-permute-start | bytes 2359304 | tf_op jit(solution)/shard_map/ppermute | solution.py:29
  139.1 44.1 %collective-permute-start.13 = (bf16[1024,384]{0,1:T(8,128)(2,1)S(1)}, bf16[1024,384]{0,1:T(8,128)(2,1)}, u32[]{:S(2)}, u32[]{:S(2)}) collective-permute-start(bf16[1024,384]{0,1:T(8,128)(2,1)S(1)} %copy.21), channel_id=1, source_target_pairs={{0,2},{1,3},{2,0},{3,1},{4,6},{5,7},{6,4},{7,5},{8,10},{9,11},{10,... | collective-permute-start | bytes 2359304 | tf_op jit(solution)/shard_map/ppermute | solution.py:29
  139.9 43.3 %collective-permute-start.14 = (bf16[1024,384]{0,1:T(8,128)(2,1)S(1)}, bf16[1024,384]{0,1:T(8,128)(2,1)}, u32[]{:S(2)}, u32[]{:S(2)}) collective-permute-start(bf16[1024,384]{0,1:T(8,128)(2,1)S(1)} %copy.21), channel_id=1, source_target_pairs={{0,3},{1,0},{2,1},{3,2},{4,7},{5,4},{6,5},{7,6},{8,11},{9,8},{10,9... | collective-permute-start | bytes 2359304 | tf_op jit(solution)/shard_map/ppermute | solution.py:29
  142.2 35.1 %collective-permute-start.15 = (bf16[4,64,384]{2,1,0:T(8,128)(2,1)S(1)}, bf16[4,64,384]{2,1,0:T(8,128)(2,1)S(1)}, u32[]{:S(2)}, u32[]{:S(2)}) collective-permute-start(bf16[4,64,384]{2,1,0:T(8,128)(2,1)S(1)} %get-tuple-element.28), channel_id=1, source_target_pairs={{0,1},{1,2},{2,3},{3,0},{4,5},{5,6},{6,7},{7,4},{8,9},{9,10},{10,1... | collective-permute-start | bytes 589832 | tf_op jit(solution)/shard_map/ppermute | solution.py:100
  142.3 38.5 %collective-permute-start.16 = (bf16[4,64,384]{2,1,0:T(8,128)(2,1)S(1)}, bf16[4,64,384]{2,1,0:T(8,128)(2,1)}, u32[]{:S(2)}, u32[]{:S(2)}) collective-permute-start(bf16[4,64,384]{2,1,0:T(8,128)(2,1)S(1)} %get-tuple-element.27), channel_id=1, source_target_pairs={{0,2},{1,3},{2,0},{3,1},{4,6},{5,7},{6,4},{7,5},{8,10},{9,11},{10,... | collective-permute-start | bytes 589832 | tf_op jit(solution)/shard_map/ppermute | solution.py:100
  177.2 4.8 %collective-permute-start.17 = (bf16[4,64,384]{2,1,0:T(8,128)(2,1)S(1)}, bf16[4,64,384]{2,1,0:T(8,128)(2,1)}, u32[]{:S(2)}, u32[]{:S(2)}) collective-permute-start(bf16[4,64,384]{2,1,0:T(8,128)(2,1)S(1)} %get-tuple-element.26), channel_id=1, source_target_pairs={{0,3},{1,0},{2,1},{3,2},{4,7},{5,4},{6,5},{7,6},{8,11},{9,8},{10,9... | collective-permute-start | bytes 589832 | tf_op jit(solution)/shard_map/ppermute | solution.py:100
  189.2 18.8 %collective-permute-start.21 = (bf16[1024,384]{0,1:T(8,128)(2,1)S(1)}, bf16[1024,384]{0,1:T(8,128)(2,1)}, u32[]{:S(2)}, u32[]{:S(2)}) collective-permute-start(bf16[1024,384]{0,1:T(8,128)(2,1)S(1)} %copy.22), channel_id=1, source_target_pairs={{0,1},{1,2},{2,3},{3,0},{4,5},{5,6},{6,7},{7,4},{8,9},{9,10},{10,1... | collective-permute-start | bytes 2359304 | tf_op jit(solution)/shard_map/ppermute | solution.py:29
  190.2 20.6 %collective-permute-start.22 = (bf16[1024,384]{0,1:T(8,128)(2,1)S(1)}, bf16[1024,384]{0,1:T(8,128)(2,1)}, u32[]{:S(2)}, u32[]{:S(2)}) collective-permute-start(bf16[1024,384]{0,1:T(8,128)(2,1)S(1)} %copy.22), channel_id=1, source_target_pairs={{0,2},{1,3},{2,0},{3,1},{4,6},{5,7},{6,4},{7,5},{8,10},{9,11},{10,... | collective-permute-start | bytes 2359304 | tf_op jit(solution)/shard_map/ppermute | solution.py:29
  191.6 32.7 %collective-permute-start.23 = (bf16[1024,384]{0,1:T(8,128)(2,1)S(1)}, bf16[1024,384]{0,1:T(8,128)(2,1)}, u32[]{:S(2)}, u32[]{:S(2)}) collective-permute-start(bf16[1024,384]{0,1:T(8,128)(2,1)S(1)} %copy.22), channel_id=1, source_target_pairs={{0,3},{1,0},{2,1},{3,2},{4,7},{5,4},{6,5},{7,6},{8,11},{9,8},{10,9... | collective-permute-start | bytes 2359304 | tf_op jit(solution)/shard_map/ppermute | solution.py:29
  192.8 2.2 copy-start.9
  192.8 31.5 %copy-start.2 = (bf16[4,1024,384]{1,2,0:T(8,128)(2,1)S(1)}, bf16[4,1024,384]{1,2,0:T(8,128)(2,1)}, u32[]{:S(2)}) copy-start(bf16[4,1024,384]{1,2,0:T(8,128)(2,1)} %pad_maximum_fusion.1) | copy-start | bytes 9437188
  224.3 5.5 %copy-start.1 = (bf16[64,4096]{1,0:T(8,128)(2,1)S(1)}, bf16[64,4096]{1,0:T(8,128)(2,1)}, u32[]{:S(2)}) copy-start(bf16[64,4096]{1,0:T(8,128)(2,1)} %pad_maximum_fusion.4) | copy-start | bytes 1572868
  227.1 2.7 copy-start
  259.8 8.0 %slice-start = ((s8[6291456]{0:T(1024)(128)(4,1)}), s8[4194304]{0:T(1024)(128)(4,1)S(1)}, s32[]{:S(2)}) async-start(s8[6291456]{0:T(1024)(128)(4,1)} %bitcast.108), calls=%async_computation.5 | async-start | bytes 8388608
  261.9 5.8 %slice-start.1 = ((s8[6291456]{0:T(1024)(128)(4,1)}), s8[2097152]{0:T(1024)(128)(4,1)S(1)}, s32[]{:S(2)}) async-start(s8[6291456]{0:T(1024)(128)(4,1)} %bitcast.108), calls=%async_computation.6 | async-start | bytes 4194304
  279.3 6.8 %copy-start.8 = (s32[384]{0:T(512)S(1)}, s32[384]{0:T(512)}, u32[]{:S(2)}) copy-start(s32[384]{0:T(512)} %param.19) | copy-start | bytes 4612
  282.3 4.4 %collective-permute-start.24 = (f32[6,384]{1,0:T(8,128)S(1)}, f32[6,384]{1,0:T(8,128)S(1)}, u32[]{:S(2)}, u32[]{:S(2)}) collective-permute-start(f32[6,384]{1,0:T(8,128)S(1)} %get-tuple-element.29), channel_id=1, source_target_pairs={{0,3},{1,0},{2,1},{3,2},{4,7},{5,4},{6,5},{7,6},{8,11},{9,8},{10,9... | collective-permute-start | bytes 27656 | tf_op jit(solution)/shard_map/ppermute | solution.py:135
  284.7 3.7 %collective-permute-start.25 = (f32[6,384]{1,0:T(8,128)S(1)}, f32[6,384]{1,0:T(8,128)S(1)}, u32[]{:S(2)}, u32[]{:S(2)}) collective-permute-start(f32[6,384]{1,0:T(8,128)S(1)} %get-tuple-element.31), channel_id=1, source_target_pairs={{0,2},{1,3},{2,0},{3,1},{4,6},{5,7},{6,4},{7,5},{8,10},{9,11},{10,... | collective-permute-start | bytes 27656 | tf_op jit(solution)/shard_map/ppermute | solution.py:135
  286.1 3.1 %collective-permute-start.26 = (f32[6,384]{1,0:T(8,128)S(1)}, f32[6,384]{1,0:T(8,128)S(1)}, u32[]{:S(2)}, u32[]{:S(2)}) collective-permute-start(f32[6,384]{1,0:T(8,128)S(1)} %get-tuple-element.30), channel_id=1, source_target_pairs={{0,1},{1,2},{2,3},{3,0},{4,5},{5,6},{6,7},{7,4},{8,9},{9,10},{10,1... | collective-permute-start | bytes 27656 | tf_op jit(solution)/shard_map/ppermute | solution.py:135
Sparse Core Ops, SparseCore 0:
  8.9 83.2 all-gather.6
  93.8 26.0 all-gather.4
  136.2 47.2 reduce-scatter.1
  191.7 46.6 all-gather.8

commit v19 on v16

--- a/solution.py
+++ b/solution.py
@@ -62,22 +62,29 @@
     positions = ring_gather(query_positions, "wb")
     act_tokens, grad_tokens, positions = lax.optimization_barrier((act_tokens, grad_tokens, positions))
     act_cols = lax.all_gather(act_basis, "wa", axis=1, tiled=True)
-    grad_cols = lax.all_gather(grad_basis, "wa", axis=1, tiled=True)
+    width = grad_basis.shape[1] // 2
+    grad_cols = [
+        lax.all_gather(grad_basis[:, :width], "wa", axis=1, tiled=True),
+        lax.all_gather(grad_basis[:, width:], "wa", axis=1, tiled=True),
+    ]
     count = query_act.shape[0]
     act_rot = jnp.dot(
         act_tokens.reshape(nb * count, -1), act_cols, preferred_element_type=jnp.float32
     ).astype(jnp.bfloat16)
-    grad_rot = jnp.dot(
-        grad_tokens.reshape(nb * count, -1), grad_cols, preferred_element_type=jnp.float32
-    ).astype(jnp.bfloat16)
     query_weight = jnp.where(positions.reshape(-1) >= PROMPT, 1.0, 0.0).astype(jnp.bfloat16)
-    grad_kept = grad_rot * query_weight[:, None]
     act_rot = natural_order(act_rot.reshape(nb, count, -1), "wb").reshape(nb * count, -1)
-    grad_kept = natural_order(grad_kept.reshape(nb, count, -1), "wb").reshape(nb * count, -1)
-    grad_all = jnp.concatenate(list(ring_gather(grad_kept, "wb")), axis=1)
-    partial_rows = lax.dot_general(
-        act_rot, grad_all, (((0,), (0,)), ((), ())), preferred_element_type=jnp.float32
-    )
+    partials = []
+    for cols in grad_cols:
+        grad_rot = jnp.dot(
+            grad_tokens.reshape(nb * count, -1), cols, preferred_element_type=jnp.float32
+        ).astype(jnp.bfloat16)
+        grad_kept = grad_rot * query_weight[:, None]
+        grad_kept = natural_order(grad_kept.reshape(nb, count, -1), "wb").reshape(nb * count, -1)
+        grad_all = jnp.concatenate(list(ring_gather(grad_kept, "wb")), axis=1)
+        partials.append(lax.dot_general(
+            act_rot, grad_all, (((0,), (0,)), ((), ())), preferred_element_type=jnp.float32
+        ))
+    partial_rows = jnp.concatenate(partials, axis=1)
     eig_sum = jnp.sum(eig_values.astype(jnp.float32))
     group_sum = eig_sum
     for shift in range(1, nb):
@@ -87,8 +94,8 @@
         jnp.concatenate([partial_rows, extra], axis=1), "wa", scatter_dimension=0, tiled=True
     )
     rows = reduced.shape[0]
-    by_shift = reduced[:, : partial_rows.shape[1]].reshape(rows, nb, na, -1).transpose(1, 0, 2, 3)
-    gradient_rows = natural_order(by_shift, "wb").transpose(1, 2, 0, 3).reshape(rows, -1)
+    by_shift = reduced[:, : partial_rows.shape[1]].reshape(rows, 2, nb, na, -1).transpose(2, 0, 1, 3, 4)
+    gradient_rows = natural_order(by_shift, "wb").transpose(1, 3, 0, 2, 4).reshape(rows, -1)
     me = lax.axis_index("wb")
     half = train_grad_rot.shape[0] // 2
     first_rows, train_act_rot, _ = lax.optimization_barrier((train_grad_rot[:half], train_act_rot, partial_rows))

time: 266 us -> 290 us (1.090)
  waiting for transfers between devices: 161 us -> 170 us
  starting transfers between devices: 24.5 us -> 31.8 us
  local copies, waits for them, and re-layouts: 9.27 us -> 13 us
    ppermute x18 -> x21, waiting for transfers between devices: 97.6 us -> 56.1 us  [ring_gather(): lax.ppermute(x, axis, perm=[(i, (i + shift) % n) for i in range(n)])]
    ppermute x3, waiting for transfers between devices: 20.8 us -> 52.1 us  [shards(): lax.ppermute(eig_sum, 'wb', perm=[(i, (i + shift) % nb) for i in range(nb)])]
    all_gather x1 -> x2, waiting for transfers between devices: 0.01 us -> 18.3 us  [the longest x1 18.2 us: shards(): lax.all_gather(grad_basis[:, width:], 'wa', axis=1, tiled=True)]
    ppermute x18 -> x21, starting transfers between devices: 17.7 us -> 24.5 us  [ring_gather(): lax.ppermute(x, axis, perm=[(i, (i + shift) % n) for i in range(n)])]
    dot_general x1 -> x2, matrix products: 5.79 us -> 8.34 us  [shards(): jnp.dot(grad_tokens.reshape(nb * count, -1), cols, preferred_element_type...]
  transfers between devices with their start and end apart: 31 -> 35, of which waited for: 14 -> 19; matrix products, arithmetic and copies ran while one was open for 14% -> 15% of each run, Pallas kernels for 0% -> 0%
where the time goes in v19:
time: 290 us; the launch traced here: 289 us
  waiting for transfers between devices  170 us (59%)
  matrix products  37.7 us (13%)
  starting transfers between devices  31.8 us (11%)
  other arithmetic  18.8 us (6%)
  between operations  17.6 us (6%)
  local copies, waits for them, and re-layouts  13 us (4%)
    ppermute x21, waiting for transfers between devices, ring_gather(): lax.ppermute(x, axis, perm=[(i, (i + shift) % n) for i in range(n)])  56.1 us
    ppermute x3, waiting for transfers between devices, shards(): lax.ppermute(eig_sum, 'wb', perm=[(i, (i + shift) % nb) for i in range(nb)])  52.1 us
    ppermute x3, waiting for transfers between devices, shards(): lax.ppermute(outgoing, 'wb', perm=[(i, (i + shift) % nb) for i in range(n...  40.2 us
    dot_general x12, matrix products, score_part(): jnp.einsum('ij,sjt->sit', precond, grads_near, preferred_element_type=jnp...  26.5 us
    ppermute x21, starting transfers between devices, ring_gather(): lax.ppermute(x, axis, perm=[(i, (i + shift) % n) for i in range(n)])  24.5 us
    all_gather x1, waiting for transfers between devices, shards(): lax.all_gather(grad_basis[:, width:], 'wa', axis=1, tiled=True)  18.2 us
    another operation x4, other arithmetic, ring_gather(): return jnp.stack(parts)  8.37 us
    dot_general x2, matrix products, shards(): jnp.dot(grad_tokens.reshape(nb * count, -1), cols, preferred_element_type...  8.34 us
  transfers between devices with their start and end apart: 35, of which 19 were waited for; matrix products, arithmetic and copies ran while one was open for 15% of the time, Pallas kernels for 0%

profile of v19, /device:TPU:0, one launch (start us, length us, event | category | flops | bytes accessed | tf_op | source)
XLA Modules:
  0.0 289.2 jit_solution(2832417106954106568)
XLA Ops:
  7.3 1.9 fusion.119
  9.3 1.1 copy.17
  10.5 1.2 copy.18
  12.3 2.6 collective-permute-start.9
  14.9 1.4 collective-permute-start.11
  17.1 48.9 %collective-permute-done.21 = f32[]{:T(128)} collective-permute-done((f32[]{:T(128)}, f32[]{:T(128)}, u32[]{:S(2)}, u32[]{:S(2)}) %collective-permute-start.21) | collective-permute-done | bytes 36 | tf_op jit(solution)/shard_map/ppermute | solution.py:91
  66.0 2.3 collective-permute-start.22
  68.3 1.8 collective-permute-done.22
  70.0 1.4 collective-permute-done.23
  71.5 2.5 collective-permute-start.12
  73.9 0.8 collective-permute-done.12
  74.7 2.0 collective-permute-start.13
  76.8 1.5 collective-permute-done.13
  78.3 1.3 collective-permute-done.14
  79.6 2.0 collective-permute-start.7
  81.6 1.8 collective-permute-start.8
  86.0 7.7 %collective-permute-done.7 = bf16[128,2048]{1,0:T(8,128)(2,1)S(1)} collective-permute-done((bf16[128,2048]{1,0:T(8,128)(2,1)S(1)}, bf16[128,2048]{1,0:T(8,128)(2,1)S(1)}, u32[]{:S(2)}, u32[]{:S(2)}) %collective-permute-start.7) | collective-permute-done | bytes 524320 | tf_op jit(solution)/shard_map/ppermute | solution.py:29
  93.7 5.6 %collective-permute-done.8 = bf16[128,2048]{1,0:T(8,128)(2,1)S(1)} collective-permute-done((bf16[128,2048]{1,0:T(8,128)(2,1)S(1)}, bf16[128,2048]{1,0:T(8,128)(2,1)S(1)}, u32[]{:S(2)}, u32[]{:S(2)}) %collective-permute-start.8) | collective-permute-done | bytes 524320 | tf_op jit(solution)/shard_map/ppermute | solution.py:29
  100.1 1.8 pad_maximum_fusion.2
  101.9 3.6 %pad_maximum_fusion = bf16[4,128,4096]{2,1,0:T(8,128)(2,1)} fusion(bf16[1,128,4096]{2,1,0:T(8,128)(2,1)} %bitcast.19, bf16[1,128,4096]{2,1,0:T(8,128)(2,1)} %bitcast.18, bf16[1,128,4096]{2,1,0:T(8,128)(2,1)} %bitcast.17, bf16[1,128,4096]{2,1,0:T(8,128)(2,1)S(1)} %bitcast.230), kind=kLoop, calls=%fused_computation.1 | loop fusion | flops 6291456 | bytes 8388608 | tf_op jit(solution)/shard_map/stack | solution.py:30
  105.5 2.0 convolution_convert_fusion.2
  107.6 4.2 %fusion.26 = bf16[512,256]{1,0:T(8,128)(2,1)S(1)} fusion(bf16[512,4096]{1,0:T(8,128)(2,1)} %bitcast.211, bf16[4096,256]{0,1:T(8,128)(2,1)} %all-gather.8.cloned.1.call-done, bf16[512]{0:T(512)(128)(2,1)S(1)} %fusion.115), kind=kOutput, calls=%fused_computation.76 | convolution fusion | flops 1074003968 | bytes 6554624 | tf_op jit(solution)/shard_map/dot_general | solution.py:78
  111.9 0.9 collective-permute-start.15
  112.8 1.8 collective-permute-start.16
  114.7 18.2 %all-gather.10.cloned.1.call-done = bf16[4096,256]{0,1:T(8,128)(2,1)} async-done(((bf16[4096,64]{0,1:T(8,128)(2,1)}), bf16[4096,256]{0,1:T(8,128)(2,1)}) %all-gather.10.cloned.1.call-update) | async-done | bytes 2097168 | tf_op jit(solution)/shard_map/all_gather | solution.py:68
  132.9 4.1 %fusion.27 = bf16[512,256]{1,0:T(8,128)(2,1)S(1)} fusion(bf16[512,4096]{1,0:T(8,128)(2,1)} %bitcast.212, bf16[4096,256]{0,1:T(8,128)(2,1)} %all-gather.10.cloned.1.call-done, bf16[512]{0:T(512)(128)(2,1)S(1)} %fusion.115), kind=kOutput, calls=%fused_computation.77 | convolution fusion | flops 1074003968 | bytes 6554624 | tf_op jit(solution)/shard_map/dot_general | solution.py:78
  137.3 1.5 collective-permute-start.19
  138.8 1.4 collective-permute-start.20
  140.8 4.5 %collective-permute-done.18 = bf16[512,256]{1,0:T(8,128)(2,1)S(1)} collective-permute-done((bf16[512,256]{1,0:T(8,128)(2,1)S(1)}, bf16[512,256]{1,0:T(8,128)(2,1)S(1)}, u32[]{:S(2)}, u32[]{:S(2)}) %collective-permute-start.18) | collective-permute-done | bytes 262176 | tf_op jit(solution)/shard_map/ppermute | solution.py:29
  145.2 1.2 collective-permute-done.19
  146.5 4.0 %collective-permute-done.20 = bf16[512,256]{1,0:T(8,128)(2,1)S(1)} collective-permute-done((bf16[512,256]{1,0:T(8,128)(2,1)S(1)}, bf16[512,256]{1,0:T(8,128)(2,1)S(1)}, u32[]{:S(2)}, u32[]{:S(2)}) %collective-permute-start.20) | collective-permute-done | bytes 262176 | tf_op jit(solution)/shard_map/ppermute | solution.py:29
  150.9 1.6 maximum_maximum_fusion.1
  152.6 1.3 copy-done.3
  154.1 0.9 collective-permute-start
  154.9 1.5 collective-permute-start.1
  156.4 1.3 dynamic-slice_bitcast_fusion.3
  158.6 34.6 %collective-permute-done.5 = bf16[4,64,384]{2,1,0:T(8,128)(2,1)S(1)} collective-permute-done((bf16[4,64,384]{2,1,0:T(8,128)(2,1)S(1)}, bf16[4,64,384]{2,1,0:T(8,128)(2,1)S(1)}, u32[]{:S(2)}, u32[]{:S(2)}) %collective-permute-start.5) | collective-permute-done | bytes 196640 | tf_op jit(solution)/shard_map/ppermute | solution.py:107
  193.3 1.5 collective-permute-start.4
  194.7 5.5 %collective-permute-done.4 = bf16[4,64,384]{2,1,0:T(8,128)(2,1)S(1)} collective-permute-done((bf16[4,64,384]{2,1,0:T(8,128)(2,1)S(1)}, bf16[4,64,384]{2,1,0:T(8,128)(2,1)S(1)}, u32[]{:S(2)}, u32[]{:S(2)}) %collective-permute-start.4) | collective-permute-done | bytes 196640 | tf_op jit(solution)/shard_map/ppermute | solution.py:107
  200.4 3.0 %pad_maximum_fusion.1 = bf16[4,1024,384]{2,1,0:T(8,128)(2,1)} fusion(bf16[1,1024,384]{2,1,0:T(8,128)(2,1)} %bitcast.3, bf16[1,1024,384]{2,1,0:T(8,128)(2,1)} %bitcast.2, bf16[1,1024,384]{2,1,0:T(8,128)(2,1)S(1)} %bitcast.231, bf16[1,1024,384]{2,1,0:T(8,128)(2,1)S(1)} %bitcast.214), kind=kLoop, calls=%fused_computation.16 | loop fusion | flops 4718592 | bytes 6291456 | tf_op jit(solution)/shard_map/stack | solution.py:30
  203.4 1.1 slice.94
  206.9 0.8 pad_maximum_fusion.4
  208.3 1.6 collective-permute-start.25
  209.9 1.4 collective-permute-start.26
  211.8 1.4 slice.95
  214.5 12.0 %collective-permute-done.24 = bf16[1024,384]{1,0:T(8,128)(2,1)S(1)} collective-permute-done((bf16[1024,384]{1,0:T(8,128)(2,1)S(1)}, bf16[1024,384]{1,0:T(8,128)(2,1)S(1)}, u32[]{:S(2)}, u32[]{:S(2)}) %collective-permute-start.24) | collective-permute-done | bytes 786464 | tf_op jit(solution)/shard_map/ppermute | solution.py:29
  226.5 2.3 collective-permute-done.25
  228.8 15.2 %collective-permute-done.26 = bf16[1024,384]{1,0:T(8,128)(2,1)} collective-permute-done((bf16[1024,384]{1,0:T(8,128)(2,1)S(1)}, bf16[1024,384]{1,0:T(8,128)(2,1)}, u32[]{:S(2)}, u32[]{:S(2)}) %collective-permute-start.26) | collective-permute-done | bytes 786464 | tf_op jit(solution)/shard_map/ppermute | solution.py:29
  244.0 2.9 maximum_maximum_fusion
  246.9 1.8 fusion.28
  248.7 1.9 fusion.29
  250.6 1.9 fusion.30
  252.5 1.8 fusion.31
  254.4 1.9 fusion.32
  256.3 1.9 fusion.33
  258.3 2.1 fusion.6
  260.4 4.9 %fusion.18 = f32[4,384]{1,0:T(4,128)S(1)} fusion(f32[4,192,384]{2,1,0:T(8,128)S(1)} %bitcast.224, bf16[4,2048,384]{2,1,0:T(8,128)(2,1)} %copy-done, f32[]{:T(128)} %bitcast.56, bf16[192,4096]{1,0:T(8,128)(2,1)S(1)} %bitcast.218), kind=kOutput, calls=%fused_computation.47 | convolution fusion | flops 1210513920 | bytes 9050116 | tf_op jit(solution)/shard_map/ij,sjt->sit/dot_general | solution.py:127
  265.4 2.0 fusion.17
  267.4 2.1 fusion.16
  269.6 2.1 fusion.15
  271.6 2.1 fusion.14
  273.7 2.1 fusion.13
  276.0 2.4 collective-permute-start.27
  279.8 2.3 collective-permute-done.28
  (113 shorter events, 11.4 us)
Async XLA Ops:
  6.5 99.0 %all-gather.6.cloned.1.call-start = ((), (), s32[]{:S(2)}) async-start(), calls=%async_computation.1 | async-start | bytes 1310720 | tf_op jit(solution)/shard_map/all_gather | solution.py:64
  7.3 100.3 %all-gather.8.cloned.1.call-start = ((), (), s32[]{:S(2)}) async-start(), calls=%async_computation.2 | async-start | bytes 2621440 | tf_op jit(solution)/shard_map/all_gather | solution.py:67
  9.2 3.0 %copy-start.5 = (bf16[128,4096]{1,0:T(8,128)(2,1)S(1)}, bf16[128,4096]{1,0:T(8,128)(2,1)}, u32[]{:S(2)}) copy-start(bf16[128,4096]{1,0:T(8,128)(2,1)} %param.11) | copy-start | bytes 3145732
  9.3 7.1 %copy-start.4 = (bf16[64,2048]{1,0:T(8,128)(2,1)S(1)}, bf16[64,2048]{1,0:T(8,128)(2,1)}, u32[]{:S(2)}) copy-start(bf16[64,2048]{1,0:T(8,128)(2,1)} %param.15) | copy-start | bytes 786436
  9.3 62.2 %copy-start.11 = (s32[128]{0:T(128)S(1)}, s32[128]{0:T(128)}, u32[]{:S(2)}) copy-start(s32[128]{0:T(128)} %param.12) | copy-start | bytes 1540
  10.4 1.3 copy-start.6
  10.4 122.4 %all-gather.10.cloned.1.call-start = ((), (), s32[]{:S(2)}) async-start(), calls=%async_computation.3 | async-start | bytes 2621440 | tf_op jit(solution)/shard_map/all_gather | solution.py:68
  11.7 191.7 %reduce-scatter.2.cloned.1.call-start = ((), (), s32[]{:S(2)}) async-start(), calls=%async_computation.4 | async-start | bytes 2785280 | tf_op jit(solution)/shard_map/reduce_scatter | solution.py:93
  11.8 69.8 %collective-permute-start.6 = (bf16[128,2048]{1,0:T(8,128)(2,1)S(1)}, bf16[128,2048]{1,0:T(8,128)(2,1)S(1)}, u32[]{:S(2)}, u32[]{:S(2)}) collective-permute-start(bf16[128,2048]{1,0:T(8,128)(2,1)S(1)} %copy-done.6), channel_id=1, source_target_pairs={{0,1},{1,2},{2,3},{3,0},{4,5},{5,6},{6,7},{7,4},{8,9},{9,10},{10,1... | collective-permute-start | bytes 1572872 | tf_op jit(solution)/shard_map/ppermute | solution.py:29
  12.3 89.6 %collective-permute-start.9 = (bf16[128,4096]{1,0:T(8,128)(2,1)S(1)}, bf16[128,4096]{1,0:T(8,128)(2,1)}, u32[]{:S(2)}, u32[]{:S(2)}) collective-permute-start(bf16[128,4096]{1,0:T(8,128)(2,1)S(1)} %copy-done.5), channel_id=1, source_target_pairs={{0,1},{1,2},{2,3},{3,0},{4,5},{5,6},{6,7},{7,4},{8,9},{9,10},{10,1... | collective-permute-start | bytes 3145736 | tf_op jit(solution)/shard_map/ppermute | solution.py:29
  14.9 87.0 %collective-permute-start.10 = (bf16[128,4096]{1,0:T(8,128)(2,1)S(1)}, bf16[128,4096]{1,0:T(8,128)(2,1)}, u32[]{:S(2)}, u32[]{:S(2)}) collective-permute-start(bf16[128,4096]{1,0:T(8,128)(2,1)S(1)} %copy-done.5), channel_id=1, source_target_pairs={{0,2},{1,3},{2,0},{3,1},{4,6},{5,7},{6,4},{7,5},{8,10},{9,11},{10,... | collective-permute-start | bytes 3145736 | tf_op jit(solution)/shard_map/ppermute | solution.py:29
  14.9 87.0 %collective-permute-start.11 = (bf16[128,4096]{1,0:T(8,128)(2,1)S(1)}, bf16[128,4096]{1,0:T(8,128)(2,1)}, u32[]{:S(2)}, u32[]{:S(2)}) collective-permute-start(bf16[128,4096]{1,0:T(8,128)(2,1)S(1)} %copy-done.5), channel_id=1, source_target_pairs={{0,3},{1,0},{2,1},{3,2},{4,7},{5,4},{6,5},{7,6},{8,11},{9,8},{10,9... | collective-permute-start | bytes 3145736 | tf_op jit(solution)/shard_map/ppermute | solution.py:29
  17.1 48.9 %collective-permute-start.21 = (f32[]{:T(128)}, f32[]{:T(128)}, u32[]{:S(2)}, u32[]{:S(2)}) collective-permute-start(f32[]{:T(128)} %convert_reduce_fusion), channel_id=1, source_target_pairs={{0,1},{1,2},{2,3},{3,0},{4,5},{5,6},{6,7},{7,4},{8,9},{9,10},{10,1... | collective-permute-start | bytes 20 | tf_op jit(solution)/shard_map/ppermute | solution.py:91
  66.0 4.1 %collective-permute-start.22 = (f32[]{:T(128)}, f32[]{:T(128)}, u32[]{:S(2)}, u32[]{:S(2)}) collective-permute-start(f32[]{:T(128)} %convert_reduce_fusion), channel_id=1, source_target_pairs={{0,2},{1,3},{2,0},{3,1},{4,6},{5,7},{6,4},{7,5},{8,10},{9,11},{10,... | collective-permute-start | bytes 20 | tf_op jit(solution)/shard_map/ppermute | solution.py:91
  70.0 1.4 collective-permute-start.23
  71.5 3.3 %collective-permute-start.12 = (s32[128]{0:T(128)S(1)}, s32[128]{0:T(128)S(1)}, u32[]{:S(2)}, u32[]{:S(2)}) collective-permute-start(s32[128]{0:T(128)S(1)} %copy-done.11), channel_id=1, source_target_pairs={{0,1},{1,2},{2,3},{3,0},{4,5},{5,6},{6,7},{7,4},{8,9},{9,10},{10,1... | collective-permute-start | bytes 1544 | tf_op jit(solution)/shard_map/ppermute | solution.py:29
  74.7 3.5 %collective-permute-start.13 = (s32[128]{0:T(128)S(1)}, s32[128]{0:T(128)S(1)}, u32[]{:S(2)}, u32[]{:S(2)}) collective-permute-start(s32[128]{0:T(128)S(1)} %copy-done.11), channel_id=1, source_target_pairs={{0,2},{1,3},{2,0},{3,1},{4,6},{5,7},{6,4},{7,5},{8,10},{9,11},{10,... | collective-permute-start | bytes 1544 | tf_op jit(solution)/shard_map/ppermute | solution.py:29
  78.3 1.3 collective-permute-start.14
  79.6 14.1 %collective-permute-start.7 = (bf16[128,2048]{1,0:T(8,128)(2,1)S(1)}, bf16[128,2048]{1,0:T(8,128)(2,1)S(1)}, u32[]{:S(2)}, u32[]{:S(2)}) collective-permute-start(bf16[128,2048]{1,0:T(8,128)(2,1)S(1)} %copy-done.6), channel_id=1, source_target_pairs={{0,2},{1,3},{2,0},{3,1},{4,6},{5,7},{6,4},{7,5},{8,10},{9,11},{10,... | collective-permute-start | bytes 1572872 | tf_op jit(solution)/shard_map/ppermute | solution.py:29
  81.6 17.7 %copy-start.7 = (bf16[128,2048]{1,0:T(8,128)(2,1)}, bf16[128,2048]{1,0:T(8,128)(2,1)S(1)}, u32[]{:S(2)}) copy-start(bf16[128,2048]{1,0:T(8,128)(2,1)S(1)} %collective-permute-done.6) | copy-start | bytes 1572868
  81.6 17.7 %collective-permute-start.8 = (bf16[128,2048]{1,0:T(8,128)(2,1)S(1)}, bf16[128,2048]{1,0:T(8,128)(2,1)S(1)}, u32[]{:S(2)}, u32[]{:S(2)}) collective-permute-start(bf16[128,2048]{1,0:T(8,128)(2,1)S(1)} %copy-done.6), channel_id=1, source_target_pairs={{0,3},{1,0},{2,1},{3,2},{4,7},{5,4},{6,5},{7,6},{8,11},{9,8},{10,9... | collective-permute-start | bytes 1572872 | tf_op jit(solution)/shard_map/ppermute | solution.py:29
  93.7 5.6 %copy-start.8 = (bf16[128,2048]{1,0:T(8,128)(2,1)}, bf16[128,2048]{1,0:T(8,128)(2,1)S(1)}, u32[]{:S(2)}) copy-start(bf16[128,2048]{1,0:T(8,128)(2,1)S(1)} %collective-permute-done.7) | copy-start | bytes 1572868
  99.3 0.8 copy-start.9
  111.9 26.9 %collective-permute-start.15 = (bf16[512,256]{1,0:T(8,128)(2,1)S(1)}, bf16[512,256]{1,0:T(8,128)(2,1)S(1)}, u32[]{:S(2)}, u32[]{:S(2)}) collective-permute-start(bf16[512,256]{1,0:T(8,128)(2,1)S(1)} %bitcast.238), channel_id=1, source_target_pairs={{0,1},{1,2},{2,3},{3,0},{4,5},{5,6},{6,7},{7,4},{8,9},{9,10},{10,1... | collective-permute-start | bytes 786440 | tf_op jit(solution)/shard_map/ppermute | solution.py:29
  112.8 27.5 %collective-permute-start.16 = (bf16[512,256]{1,0:T(8,128)(2,1)S(1)}, bf16[512,256]{1,0:T(8,128)(2,1)S(1)}, u32[]{:S(2)}, u32[]{:S(2)}) collective-permute-start(bf16[512,256]{1,0:T(8,128)(2,1)S(1)} %bitcast.239), channel_id=1, source_target_pairs={{0,2},{1,3},{2,0},{3,1},{4,6},{5,7},{6,4},{7,5},{8,10},{9,11},{10,... | collective-permute-start | bytes 786440 | tf_op jit(solution)/shard_map/ppermute | solution.py:29
  114.6 25.7 %collective-permute-start.17 = (bf16[512,256]{1,0:T(8,128)(2,1)S(1)}, bf16[512,256]{1,0:T(8,128)(2,1)S(1)}, u32[]{:S(2)}, u32[]{:S(2)}) collective-permute-start(bf16[512,256]{1,0:T(8,128)(2,1)S(1)} %bitcast.240), channel_id=1, source_target_pairs={{0,3},{1,0},{2,1},{3,2},{4,7},{5,4},{6,5},{7,6},{8,11},{9,8},{10,9... | collective-permute-start | bytes 786440 | tf_op jit(solution)/shard_map/ppermute | solution.py:29
  137.2 8.0 %collective-permute-start.18 = (bf16[512,256]{1,0:T(8,128)(2,1)S(1)}, bf16[512,256]{1,0:T(8,128)(2,1)S(1)}, u32[]{:S(2)}, u32[]{:S(2)}) collective-permute-start(bf16[512,256]{1,0:T(8,128)(2,1)S(1)} %bitcast.242), channel_id=1, source_target_pairs={{0,1},{1,2},{2,3},{3,0},{4,5},{5,6},{6,7},{7,4},{8,9},{9,10},{10,1... | collective-permute-start | bytes 786440 | tf_op jit(solution)/shard_map/ppermute | solution.py:29
  137.3 9.2 %collective-permute-start.19 = (bf16[512,256]{1,0:T(8,128)(2,1)S(1)}, bf16[512,256]{1,0:T(8,128)(2,1)S(1)}, u32[]{:S(2)}, u32[]{:S(2)}) collective-permute-start(bf16[512,256]{1,0:T(8,128)(2,1)S(1)} %bitcast.243), channel_id=1, source_target_pairs={{0,2},{1,3},{2,0},{3,1},{4,6},{5,7},{6,4},{7,5},{8,10},{9,11},{10,... | collective-permute-start | bytes 786440 | tf_op jit(solution)/shard_map/ppermute | solution.py:29
  138.8 11.7 %collective-permute-start.20 = (bf16[512,256]{1,0:T(8,128)(2,1)S(1)}, bf16[512,256]{1,0:T(8,128)(2,1)S(1)}, u32[]{:S(2)}, u32[]{:S(2)}) collective-permute-start(bf16[512,256]{1,0:T(8,128)(2,1)S(1)} %bitcast.244), channel_id=1, source_target_pairs={{0,3},{1,0},{2,1},{3,2},{4,7},{5,4},{6,5},{7,6},{8,11},{9,8},{10,9... | collective-permute-start | bytes 786440 | tf_op jit(solution)/shard_map/ppermute | solution.py:29
  152.5 1.4 copy-start.3
  152.5 105.7 %all-gather.12.cloned.1.call-start = ((), (), s32[]{:S(2)}) async-start(), calls=%async_computation.5 | async-start | bytes 2621440 | tf_op jit(solution)/shard_map/all_gather | solution.py:133
  154.1 46.3 %collective-permute-start = (bf16[1024,384]{1,0:T(8,128)(2,1)S(1)}, bf16[1024,384]{1,0:T(8,128)(2,1)S(1)}, u32[]{:S(2)}, u32[]{:S(2)}) collective-permute-start(bf16[1024,384]{1,0:T(8,128)(2,1)S(1)} %get-tuple-element.14), channel_id=1, source_target_pairs={{0,1},{1,2},{2,3},{3,0},{4,5},{5,6},{6,7},{7,4},{8,9},{9,10},{10,1... | collective-permute-start | bytes 2359304 | tf_op jit(solution)/shard_map/ppermute | solution.py:29
  154.9 45.5 %collective-permute-start.1 = (bf16[1024,384]{1,0:T(8,128)(2,1)S(1)}, bf16[1024,384]{1,0:T(8,128)(2,1)}, u32[]{:S(2)}, u32[]{:S(2)}) collective-permute-start(bf16[1024,384]{1,0:T(8,128)(2,1)S(1)} %get-tuple-element.14), channel_id=1, source_target_pairs={{0,2},{1,3},{2,0},{3,1},{4,6},{5,7},{6,4},{7,5},{8,10},{9,11},{10,... | collective-permute-start | bytes 2359304 | tf_op jit(solution)/shard_map/ppermute | solution.py:29
  156.4 44.0 %collective-permute-start.2 = (bf16[1024,384]{1,0:T(8,128)(2,1)S(1)}, bf16[1024,384]{1,0:T(8,128)(2,1)}, u32[]{:S(2)}, u32[]{:S(2)}) collective-permute-start(bf16[1024,384]{1,0:T(8,128)(2,1)S(1)} %get-tuple-element.14), channel_id=1, source_target_pairs={{0,3},{1,0},{2,1},{3,2},{4,7},{5,4},{6,5},{7,6},{8,11},{9,8},{10,9... | collective-permute-start | bytes 2359304 | tf_op jit(solution)/shard_map/ppermute | solution.py:29
  157.8 35.5 %collective-permute-start.5 = (bf16[4,64,384]{2,1,0:T(8,128)(2,1)S(1)}, bf16[4,64,384]{2,1,0:T(8,128)(2,1)S(1)}, u32[]{:S(2)}, u32[]{:S(2)}) collective-permute-start(bf16[4,64,384]{2,1,0:T(8,128)(2,1)S(1)} %get-tuple-element.28), channel_id=1, source_target_pairs={{0,3},{1,0},{2,1},{3,2},{4,7},{5,4},{6,5},{7,6},{8,11},{9,8},{10,9... | collective-permute-start | bytes 589832 | tf_op jit(solution)/shard_map/ppermute | solution.py:107
  158.5 36.3 %collective-permute-start.3 = (bf16[4,64,384]{2,1,0:T(8,128)(2,1)S(1)}, bf16[4,64,384]{2,1,0:T(8,128)(2,1)S(1)}, u32[]{:S(2)}, u32[]{:S(2)}) collective-permute-start(bf16[4,64,384]{2,1,0:T(8,128)(2,1)S(1)} %get-tuple-element.30), channel_id=1, source_target_pairs={{0,1},{1,2},{2,3},{3,0},{4,5},{5,6},{6,7},{7,4},{8,9},{9,10},{10,1... | collective-permute-start | bytes 589832 | tf_op jit(solution)/shard_map/ppermute | solution.py:107
  193.3 7.0 %collective-permute-start.4 = (bf16[4,64,384]{2,1,0:T(8,128)(2,1)S(1)}, bf16[4,64,384]{2,1,0:T(8,128)(2,1)S(1)}, u32[]{:S(2)}, u32[]{:S(2)}) collective-permute-start(bf16[4,64,384]{2,1,0:T(8,128)(2,1)S(1)} %get-tuple-element.29), channel_id=1, source_target_pairs={{0,2},{1,3},{2,0},{3,1},{4,6},{5,7},{6,4},{7,5},{8,10},{9,11},{10,... | collective-permute-start | bytes 589832 | tf_op jit(solution)/shard_map/ppermute | solution.py:107
  207.7 18.8 %collective-permute-start.24 = (bf16[1024,384]{1,0:T(8,128)(2,1)S(1)}, bf16[1024,384]{1,0:T(8,128)(2,1)S(1)}, u32[]{:S(2)}, u32[]{:S(2)}) collective-permute-start(bf16[1024,384]{1,0:T(8,128)(2,1)S(1)} %get-tuple-element.21), channel_id=1, source_target_pairs={{0,1},{1,2},{2,3},{3,0},{4,5},{5,6},{6,7},{7,4},{8,9},{9,10},{10,1... | collective-permute-start | bytes 2359304 | tf_op jit(solution)/shard_map/ppermute | solution.py:29
  208.3 20.5 %collective-permute-start.25 = (bf16[1024,384]{1,0:T(8,128)(2,1)S(1)}, bf16[1024,384]{1,0:T(8,128)(2,1)}, u32[]{:S(2)}, u32[]{:S(2)}) collective-permute-start(bf16[1024,384]{1,0:T(8,128)(2,1)S(1)} %get-tuple-element.21), channel_id=1, source_target_pairs={{0,2},{1,3},{2,0},{3,1},{4,6},{5,7},{6,4},{7,5},{8,10},{9,11},{10,... | collective-permute-start | bytes 2359304 | tf_op jit(solution)/shard_map/ppermute | solution.py:29
  209.9 34.1 %collective-permute-start.26 = (bf16[1024,384]{1,0:T(8,128)(2,1)S(1)}, bf16[1024,384]{1,0:T(8,128)(2,1)}, u32[]{:S(2)}, u32[]{:S(2)}) collective-permute-start(bf16[1024,384]{1,0:T(8,128)(2,1)S(1)} %get-tuple-element.21), channel_id=1, source_target_pairs={{0,3},{1,0},{2,1},{3,2},{4,7},{5,4},{6,5},{7,6},{8,11},{9,8},{10,9... | collective-permute-start | bytes 2359304 | tf_op jit(solution)/shard_map/ppermute | solution.py:29
  211.5 2.4 copy-start.12
  211.5 32.5 %copy-start.2 = (bf16[4,1024,384]{2,1,0:T(8,128)(2,1)S(1)}, bf16[4,1024,384]{2,1,0:T(8,128)(2,1)}, u32[]{:S(2)}) copy-start(bf16[4,1024,384]{2,1,0:T(8,128)(2,1)} %pad_maximum_fusion.1) | copy-start | bytes 9437188
  244.0 2.9 %copy-start.1 = (bf16[64,4096]{1,0:T(8,128)(2,1)S(1)}, bf16[64,4096]{1,0:T(8,128)(2,1)}, u32[]{:S(2)}) copy-start(bf16[64,4096]{1,0:T(8,128)(2,1)} %pad_maximum_fusion.4) | copy-start | bytes 1572868
  246.9 9.3 %copy-start = (bf16[4,2048,384]{2,1,0:T(8,128)(2,1)}, bf16[4,2048,384]{2,1,0:T(8,128)(2,1)S(1)}, u32[]{:S(2)}) copy-start(bf16[4,2048,384]{2,1,0:T(8,128)(2,1)S(1)} %maximum_maximum_fusion) | copy-start | bytes 18874372
  258.3 7.1 %slice-start = ((s8[6291456]{0:T(1024)(128)(4,1)}), s8[4194304]{0:T(1024)(128)(4,1)S(1)}, s32[]{:S(2)}) async-start(s8[6291456]{0:T(1024)(128)(4,1)} %bitcast.209), calls=%async_computation.6 | async-start | bytes 8388608
  260.4 5.0 %slice-start.1 = ((s8[6291456]{0:T(1024)(128)(4,1)}), s8[2097152]{0:T(1024)(128)(4,1)S(1)}, s32[]{:S(2)}) async-start(s8[6291456]{0:T(1024)(128)(4,1)} %bitcast.209), calls=%async_computation.7 | async-start | bytes 4194304
  273.7 4.9 %copy-start.10 = (s32[384]{0:T(512)S(1)}, s32[384]{0:T(512)}, u32[]{:S(2)}) copy-start(s32[384]{0:T(512)} %param.19) | copy-start | bytes 4612
  276.0 3.8 %collective-permute-start.27 = (f32[6,384]{1,0:T(8,128)S(1)}, f32[6,384]{1,0:T(8,128)S(1)}, u32[]{:S(2)}, u32[]{:S(2)}) collective-permute-start(f32[6,384]{1,0:T(8,128)S(1)} %get-tuple-element.31), channel_id=1, source_target_pairs={{0,3},{1,0},{2,1},{3,2},{4,7},{5,4},{6,5},{7,6},{8,11},{9,8},{10,9... | collective-permute-start | bytes 27656 | tf_op jit(solution)/shard_map/ppermute | solution.py:140
  278.4 3.7 %collective-permute-start.28 = (f32[6,384]{1,0:T(8,128)S(1)}, f32[6,384]{1,0:T(8,128)S(1)}, u32[]{:S(2)}, u32[]{:S(2)}) collective-permute-start(f32[6,384]{1,0:T(8,128)S(1)} %get-tuple-element.33), channel_id=1, source_target_pairs={{0,2},{1,3},{2,0},{3,1},{4,6},{5,7},{6,4},{7,5},{8,10},{9,11},{10,... | collective-permute-start | bytes 27656 | tf_op jit(solution)/shard_map/ppermute | solution.py:140
  278.4 3.7 %collective-permute-start.29 = (f32[6,384]{1,0:T(8,128)S(1)}, f32[6,384]{1,0:T(8,128)S(1)}, u32[]{:S(2)}, u32[]{:S(2)}) collective-permute-start(f32[6,384]{1,0:T(8,128)S(1)} %get-tuple-element.32), channel_id=1, source_target_pairs={{0,1},{1,2},{2,3},{3,0},{4,5},{5,6},{6,7},{7,4},{8,9},{9,10},{10,1... | collective-permute-start | bytes 27656 | tf_op jit(solution)/shard_map/ppermute | solution.py:140
Sparse Core Ops, SparseCore 0:
  8.9 30.6 all-gather.5
  41.2 45.3 all-gather.7
  88.2 44.6 all-gather.9
  152.6 45.1 reduce-scatter.1
  211.4 43.6 all-gather.11

commit v20 on v16

--- a/solution.py
+++ b/solution.py
@@ -87,7 +87,7 @@
         jnp.concatenate([partial_rows, extra], axis=1), "wa", scatter_dimension=0, tiled=True
     )
     rows = reduced.shape[0]
-    by_shift = reduced[:, : partial_rows.shape[1]].reshape(rows, nb, na, -1).transpose(1, 0, 2, 3)
+    by_shift = reduced[:, : partial_rows.shape[1]].astype(jnp.bfloat16).reshape(rows, nb, na, -1).transpose(1, 0, 2, 3)
     gradient_rows = natural_order(by_shift, "wb").transpose(1, 2, 0, 3).reshape(rows, -1)
     me = lax.axis_index("wb")
     half = train_grad_rot.shape[0] // 2
@@ -104,7 +104,7 @@
     eig_out = eig_values.shape[1]
     mean_eig = eig_total / (eig_in * eig_out)
     dampings = mean_eig * jnp.exp2(damping_index.astype(jnp.float32) - 4.0)
-    payload = jnp.concatenate([gradient_rows.astype(jnp.bfloat16), eig_values], axis=1)
+    payload = jnp.concatenate([gradient_rows, eig_values], axis=1)
     grads_first, acts_near, payload = lax.optimization_barrier((grads_first, acts_near, payload))
     second_rows, _ = lax.optimization_barrier((train_grad_rot[half:], payload))
     grads_second = ring_gather(second_rows, "wb")

time: 266 us -> 266 us (level)
  no operation moved by 1% of the time
where the time goes in v20:
time: 266 us
  waiting for transfers between devices  161 us (61%)
  matrix products  36 us (14%)
  starting transfers between devices  24.5 us (9%)
  between operations  17.7 us (7%)
  other arithmetic  17.6 us (7%)
  local copies, waits for them, and re-layouts  9.27 us (3%)
    ppermute x18, waiting for transfers between devices, ring_gather(): lax.ppermute(x, axis, perm=[(i, (i + shift) % n) for i in range(n)])  97.6 us
    ppermute x3, waiting for transfers between devices, shards(): lax.ppermute(outgoing, 'wb', perm=[(i, (i + shift) % nb) for i in range(n...  39.1 us
    dot_general x12, matrix products, score_part(): jnp.einsum('ij,sjt->sit', precond, grads_near, preferred_element_type=jnp...  26.2 us
    ppermute x3, waiting for transfers between devices, shards(): lax.ppermute(eig_sum, 'wb', perm=[(i, (i + shift) % nb) for i in range(nb)])  20.8 us
    ppermute x18, starting transfers between devices, ring_gather(): lax.ppermute(x, axis, perm=[(i, (i + shift) % n) for i in range(n)])  17.7 us
    another operation x4, other arithmetic, ring_gather(): return jnp.stack(parts)  9.03 us
    dot_general x1, matrix products, shards(): jnp.dot(grad_tokens.reshape(nb * count, -1), grad_cols, preferred_element...  5.79 us
  transfers between devices with their start and end apart: 31, of which 14 were waited for; matrix products, arithmetic and copies ran while one was open for 14% of the time, Pallas kernels for 0%

profile of v20, /device:TPU:0, one launch (start us, length us, event | category | flops | bytes accessed | tf_op | source)
XLA Modules:
  0.0 265.8 jit_solution(16935507830828154864)
XLA Ops:
  6.5 0.7 all-gather.7.cloned.1.call-update
  7.3 0.5 collective-permute-start
  7.8 2.6 collective-permute-start.3
  10.5 1.4 collective-permute-start.5
  11.9 0.6 collective-permute-start.7
  12.5 46.7 %collective-permute-done.7 = s32[128]{0:T(128)S(1)} collective-permute-done((s32[128]{0:T(128)}, s32[128]{0:T(128)S(1)}, u32[]{:S(2)}, u32[]{:S(2)}) %collective-permute-start.7) | collective-permute-done | bytes 544 | tf_op jit(solution)/shard_map/ppermute | solution.py:29
  59.2 4.7 %collective-permute-start.8 = (s32[128]{0:T(128)}, s32[128]{0:T(128)S(1)}, u32[]{:S(2)}, u32[]{:S(2)}) collective-permute-start(s32[128]{0:T(128)} %param.12), channel_id=1, source_target_pairs={{0,3},{1,0},{2,1},{3,2},{4,7},{5,4},{6,5},{7,6},{8,11},{9,8},{10,9... | collective-permute-start | bytes 1544 | tf_op jit(solution)/shard_map/ppermute | solution.py:29
  63.9 1.4 collective-permute-done.8
  65.5 3.3 %collective-permute-done.6 = s32[128]{0:T(128)S(1)} collective-permute-done((s32[128]{0:T(128)}, s32[128]{0:T(128)S(1)}, u32[]{:S(2)}, u32[]{:S(2)}) %collective-permute-start.6) | collective-permute-done | bytes 544 | tf_op jit(solution)/shard_map/ppermute | solution.py:29
  68.9 0.7 pad_add_fusion
  69.6 11.7 %collective-permute-done.1 = bf16[128,2048]{1,0:T(8,128)(2,1)S(1)} collective-permute-done((bf16[128,2048]{1,0:T(8,128)(2,1)}, bf16[128,2048]{1,0:T(8,128)(2,1)S(1)}, u32[]{:S(2)}, u32[]{:S(2)}) %collective-permute-start.1) | collective-permute-done | bytes 524320 | tf_op jit(solution)/shard_map/ppermute | solution.py:29
  81.4 5.0 %collective-permute-done.2 = bf16[128,2048]{1,0:T(8,128)(2,1)S(1)} collective-permute-done((bf16[128,2048]{1,0:T(8,128)(2,1)}, bf16[128,2048]{1,0:T(8,128)(2,1)S(1)}, u32[]{:S(2)}, u32[]{:S(2)}) %collective-permute-start.2) | collective-permute-done | bytes 524320 | tf_op jit(solution)/shard_map/ppermute | solution.py:29
  86.4 0.8 copy-done.8
  87.1 1.9 pad_maximum_fusion.2
  89.1 3.4 %pad_maximum_fusion = bf16[4,128,4096]{2,1,0:T(8,128)(2,1)} fusion(bf16[1,128,4096]{2,1,0:T(8,128)(2,1)} %bitcast.7, bf16[1,128,4096]{2,1,0:T(8,128)(2,1)} %bitcast.6, bf16[1,128,4096]{2,1,0:T(8,128)(2,1)S(1)} %bitcast.225, bf16[1,128,4096]{2,1,0:T(8,128)(2,1)S(1)} %bitcast.224), kind=kLoop, calls=%fused_computation.1 | loop fusion | flops 6291456 | bytes 8388608 | tf_op jit(solution)/shard_map/stack | solution.py:30
  92.5 5.8 %fusion.27 = bf16[512,512]{1,0:T(8,128)(2,1)S(1)} fusion(bf16[512,4096]{1,0:T(8,128)(2,1)} %bitcast.206, bf16[4096,512]{1,0:T(8,128)(2,1)} %all-gather.7.cloned.1.call-done, bf16[512]{0:T(512)(128)(2,1)S(1)} %fusion.104), kind=kOutput, calls=%fused_computation.54 | convolution fusion | flops 2148007936 | bytes 8913920 | tf_op jit(solution)/shard_map/dot_general | solution.py:70
  98.6 1.2 collective-permute-start.10
  99.8 1.1 collective-permute-start.11
  101.0 0.7 convert_reduce_fusion
  101.7 1.7 collective-permute-start.18
  103.5 0.3 collective-permute-start.19
  103.8 20.8 %collective-permute-done.18 = f32[]{:T(128)} collective-permute-done((f32[]{:T(128)}, f32[]{:T(128)}, u32[]{:S(2)}, u32[]{:S(2)}) %collective-permute-start.18) | collective-permute-done | bytes 36 | tf_op jit(solution)/shard_map/ppermute | solution.py:84
  127.3 2.0 convolution_convert_fusion.1
  129.5 2.1 fusion
  131.6 1.6 concatenate.30
  133.2 1.3 copy-done.3
  134.7 0.9 collective-permute-start.12
  135.7 1.0 collective-permute-start.13
  136.6 1.0 collective-permute-start.14
  137.6 1.3 dynamic-slice_bitcast_fusion.3
  139.0 0.7 collective-permute-start.16
  139.7 34.4 %collective-permute-done.15 = bf16[4,64,384]{2,1,0:T(8,128)(2,1)S(1)} collective-permute-done((bf16[4,64,384]{2,1,0:T(8,128)(2,1)S(1)}, bf16[4,64,384]{2,1,0:T(8,128)(2,1)S(1)}, u32[]{:S(2)}, u32[]{:S(2)}) %collective-permute-start.15) | collective-permute-done | bytes 196640 | tf_op jit(solution)/shard_map/ppermute | solution.py:100
  174.2 3.0 %collective-permute-done.16 = bf16[4,64,384]{2,1,0:T(8,128)(2,1)S(1)} collective-permute-done((bf16[4,64,384]{2,1,0:T(8,128)(2,1)S(1)}, bf16[4,64,384]{2,1,0:T(8,128)(2,1)S(1)}, u32[]{:S(2)}, u32[]{:S(2)}) %collective-permute-start.16) | collective-permute-done | bytes 196640 | tf_op jit(solution)/shard_map/ppermute | solution.py:100
  177.2 1.6 collective-permute-done.17
  179.0 3.0 %pad_maximum_fusion.1 = bf16[4,1024,384]{2,1,0:T(8,128)(2,1)} fusion(bf16[1,1024,384]{2,1,0:T(8,128)(2,1)} %bitcast.22, bf16[1,1024,384]{2,1,0:T(8,128)(2,1)} %bitcast.21, bf16[1,1024,384]{2,1,0:T(8,128)(2,1)S(1)} %bitcast.226, bf16[1,1024,384]{2,1,0:T(8,128)(2,1)S(1)} %bitcast.208), kind=kLoop, calls=%fused_computation.16 | loop fusion | flops 4718592 | bytes 6291456 | tf_op jit(solution)/shard_map/stack | solution.py:30
  182.0 1.1 slice.206
  183.3 0.3 fusion.73
  184.0 0.8 pad_maximum_fusion.4
  184.8 0.9 collective-permute-start.21
  185.8 1.4 collective-permute-start.22
  187.7 1.4 slice.88
  189.8 0.7 fusion.107
  190.4 13.1 %collective-permute-done.21 = bf16[1024,384]{1,0:T(8,128)(2,1)S(1)} collective-permute-done((bf16[1024,384]{1,0:T(8,128)(2,1)S(1)}, bf16[1024,384]{1,0:T(8,128)(2,1)S(1)}, u32[]{:S(2)}, u32[]{:S(2)}) %collective-permute-start.21) | collective-permute-done | bytes 786464 | tf_op jit(solution)/shard_map/ppermute | solution.py:29
  203.5 2.9 %collective-permute-done.22 = bf16[1024,384]{1,0:T(8,128)(2,1)} collective-permute-done((bf16[1024,384]{1,0:T(8,128)(2,1)S(1)}, bf16[1024,384]{1,0:T(8,128)(2,1)}, u32[]{:S(2)}, u32[]{:S(2)}) %collective-permute-start.22) | collective-permute-done | bytes 786464 | tf_op jit(solution)/shard_map/ppermute | solution.py:29
  206.3 13.5 %collective-permute-done.23 = bf16[1024,384]{1,0:T(8,128)(2,1)} collective-permute-done((bf16[1024,384]{1,0:T(8,128)(2,1)S(1)}, bf16[1024,384]{1,0:T(8,128)(2,1)}, u32[]{:S(2)}, u32[]{:S(2)}) %collective-permute-start.23) | collective-permute-done | bytes 786464 | tf_op jit(solution)/shard_map/ppermute | solution.py:29
  219.9 3.1 %maximum_maximum_fusion = bf16[4,2048,384]{2,1,0:T(8,128)(2,1)S(1)} fusion(bf16[1,1024,384]{2,1,0:T(8,128)(2,1)} %bitcast.36, bf16[1,1024,384]{2,1,0:T(8,128)(2,1)} %bitcast.35, bf16[1,1024,384]{2,1,0:T(8,128)(2,1)S(1)} %bitcast.227, bf16[1,1024,384]{2,1,0:T(8,128)(2,1)S(1)} %bitcast.207, bf16[4,1024,384]{2,1,0:T(8,128)(2,1)S(1)} %copy-done.2), kind=kLoop, calls=%fused_computation | loop fusion | flops 31457280 | bytes 12582912 | tf_op jit(solution)/shard_map/concatenate | solution.py:111
  223.0 1.9 fusion.35
  224.9 1.8 fusion.36
  226.7 1.8 fusion.37
  228.5 1.8 fusion.38
  230.3 1.8 fusion.39
  232.2 1.8 fusion.40
  234.2 2.1 fusion.14
  236.3 5.1 %fusion.26 = f32[4,384]{1,0:T(4,128)S(1)} fusion(f32[4,192,384]{2,1,0:T(8,128)S(1)} %bitcast.217, bf16[4,2048,384]{2,1,0:T(8,128)(2,1)} %copy-done, f32[]{:T(128)} %bitcast.54, bf16[192,4096]{1,0:T(8,128)(2,1)S(1)} %bitcast.211), kind=kOutput, calls=%fused_computation.53 | convolution fusion | flops 1210513920 | bytes 9050116 | tf_op jit(solution)/shard_map/ij,sjt->sit/dot_general | solution.py:120
  241.4 2.0 fusion.25
  243.4 2.0 fusion.24
  245.5 2.0 fusion.23
  247.4 2.1 fusion.22
  249.5 2.1 fusion.21
  251.8 2.4 collective-permute-start.24
  254.1 1.4 collective-permute-start.25
  256.2 1.6 collective-permute-done.25
  257.8 0.8 collective-permute-done.26
  258.6 0.6 fusion.103
  (91 shorter events, 2.6 us)
Async XLA Ops:
  6.5 86.0 %all-gather.7.cloned.1.call-start = ((), (), s32[]{:S(2)}) async-start(), calls=%async_computation.2 | async-start | bytes 5242880 | tf_op jit(solution)/shard_map/all_gather | solution.py:65
  7.3 120.1 %all-gather.5.cloned.1.call-start = ((), (), s32[]{:S(2)}) async-start(), calls=%async_computation.1 | async-start | bytes 1310720 | tf_op jit(solution)/shard_map/all_gather | solution.py:64
  7.3 61.5 %collective-permute-start = (bf16[128,2048]{1,0:T(8,128)(2,1)}, bf16[128,2048]{1,0:T(8,128)(2,1)S(1)}, u32[]{:S(2)}, u32[]{:S(2)}) collective-permute-start(bf16[128,2048]{1,0:T(8,128)(2,1)} %param.10), channel_id=1, source_target_pairs={{0,1},{1,2},{2,3},{3,0},{4,5},{5,6},{6,7},{7,4},{8,9},{9,10},{10,1... | collective-permute-start | bytes 1572872 | tf_op jit(solution)/shard_map/ppermute | solution.py:29
  7.8 81.2 %collective-permute-start.3 = (bf16[128,4096]{1,0:T(8,128)(2,1)}, bf16[128,4096]{1,0:T(8,128)(2,1)S(1)}, u32[]{:S(2)}, u32[]{:S(2)}) collective-permute-start(bf16[128,4096]{1,0:T(8,128)(2,1)} %param.11), channel_id=1, source_target_pairs={{0,1},{1,2},{2,3},{3,0},{4,5},{5,6},{6,7},{7,4},{8,9},{9,10},{10,1... | collective-permute-start | bytes 3145736 | tf_op jit(solution)/shard_map/ppermute | solution.py:29
  10.4 78.6 %collective-permute-start.4 = (bf16[128,4096]{1,0:T(8,128)(2,1)}, bf16[128,4096]{1,0:T(8,128)(2,1)}, u32[]{:S(2)}, u32[]{:S(2)}) collective-permute-start(bf16[128,4096]{1,0:T(8,128)(2,1)} %param.11), channel_id=1, source_target_pairs={{0,2},{1,3},{2,0},{3,1},{4,6},{5,7},{6,4},{7,5},{8,10},{9,11},{10,... | collective-permute-start | bytes 3145736 | tf_op jit(solution)/shard_map/ppermute | solution.py:29
  10.5 78.6 %collective-permute-start.5 = (bf16[128,4096]{1,0:T(8,128)(2,1)}, bf16[128,4096]{1,0:T(8,128)(2,1)}, u32[]{:S(2)}, u32[]{:S(2)}) collective-permute-start(bf16[128,4096]{1,0:T(8,128)(2,1)} %param.11), channel_id=1, source_target_pairs={{0,3},{1,0},{2,1},{3,2},{4,7},{5,4},{6,5},{7,6},{8,11},{9,8},{10,9... | collective-permute-start | bytes 3145736 | tf_op jit(solution)/shard_map/ppermute | solution.py:29
  11.9 47.3 %collective-permute-start.7 = (s32[128]{0:T(128)}, s32[128]{0:T(128)S(1)}, u32[]{:S(2)}, u32[]{:S(2)}) collective-permute-start(s32[128]{0:T(128)} %param.12), channel_id=1, source_target_pairs={{0,2},{1,3},{2,0},{3,1},{4,6},{5,7},{6,4},{7,5},{8,10},{9,11},{10,... | collective-permute-start | bytes 1544 | tf_op jit(solution)/shard_map/ppermute | solution.py:29
  59.2 6.1 %collective-permute-start.8 = (s32[128]{0:T(128)}, s32[128]{0:T(128)S(1)}, u32[]{:S(2)}, u32[]{:S(2)}) collective-permute-start(s32[128]{0:T(128)} %param.12), channel_id=1, source_target_pairs={{0,3},{1,0},{2,1},{3,2},{4,7},{5,4},{6,5},{7,6},{8,11},{9,8},{10,9... | collective-permute-start | bytes 1544 | tf_op jit(solution)/shard_map/ppermute | solution.py:29
  65.3 3.4 %collective-permute-start.6 = (s32[128]{0:T(128)}, s32[128]{0:T(128)S(1)}, u32[]{:S(2)}, u32[]{:S(2)}) collective-permute-start(s32[128]{0:T(128)} %param.12), channel_id=1, source_target_pairs={{0,1},{1,2},{2,3},{3,0},{4,5},{5,6},{6,7},{7,4},{8,9},{9,10},{10,1... | collective-permute-start | bytes 1544 | tf_op jit(solution)/shard_map/ppermute | solution.py:29
  68.8 12.6 %collective-permute-start.1 = (bf16[128,2048]{1,0:T(8,128)(2,1)}, bf16[128,2048]{1,0:T(8,128)(2,1)S(1)}, u32[]{:S(2)}, u32[]{:S(2)}) collective-permute-start(bf16[128,2048]{1,0:T(8,128)(2,1)} %param.10), channel_id=1, source_target_pairs={{0,2},{1,3},{2,0},{3,1},{4,6},{5,7},{6,4},{7,5},{8,10},{9,11},{10,... | collective-permute-start | bytes 1572872 | tf_op jit(solution)/shard_map/ppermute | solution.py:29
  68.8 17.6 %copy-start.6 = (bf16[128,2048]{1,0:T(8,128)(2,1)}, bf16[128,2048]{1,0:T(8,128)(2,1)S(1)}, u32[]{:S(2)}) copy-start(bf16[128,2048]{1,0:T(8,128)(2,1)S(1)} %collective-permute-done) | copy-start | bytes 1572868
  68.8 17.6 %collective-permute-start.2 = (bf16[128,2048]{1,0:T(8,128)(2,1)}, bf16[128,2048]{1,0:T(8,128)(2,1)S(1)}, u32[]{:S(2)}, u32[]{:S(2)}) collective-permute-start(bf16[128,2048]{1,0:T(8,128)(2,1)} %param.10), channel_id=1, source_target_pairs={{0,3},{1,0},{2,1},{3,2},{4,7},{5,4},{6,5},{7,6},{8,11},{9,8},{10,9... | collective-permute-start | bytes 1572872 | tf_op jit(solution)/shard_map/ppermute | solution.py:29
  68.9 113.1 %reduce-scatter.2.cloned.1.call-start = ((), (), s32[]{:S(2)}) async-start(), calls=%async_computation.3 | async-start | bytes 2785280 | tf_op jit(solution)/shard_map/reduce_scatter | solution.py:86
  81.4 5.0 %copy-start.7 = (bf16[128,2048]{1,0:T(8,128)(2,1)}, bf16[128,2048]{1,0:T(8,128)(2,1)S(1)}, u32[]{:S(2)}) copy-start(bf16[128,2048]{1,0:T(8,128)(2,1)S(1)} %collective-permute-done.1) | copy-start | bytes 1572868
  86.3 0.8 copy-start.8
  87.1 1.9 copy-start.5
  98.3 2.7 %copy-start.4 = (bf16[64,2048]{1,0:T(8,128)(2,1)S(1)}, bf16[64,2048]{1,0:T(8,128)(2,1)}, u32[]{:S(2)}) copy-start(bf16[64,2048]{1,0:T(8,128)(2,1)} %param.15) | copy-start | bytes 786436
  98.6 30.8 %collective-permute-start.10 = (bf16[512,512]{1,0:T(8,128)(2,1)S(1)}, bf16[512,512]{1,0:T(8,128)(2,1)}, u32[]{:S(2)}, u32[]{:S(2)}) collective-permute-start(bf16[512,512]{1,0:T(8,128)(2,1)S(1)} %bitcast.230), channel_id=1, source_target_pairs={{0,2},{1,3},{2,0},{3,1},{4,6},{5,7},{6,4},{7,5},{8,10},{9,11},{10,... | collective-permute-start | bytes 1572872 | tf_op jit(solution)/shard_map/ppermute | solution.py:29
  99.8 29.6 %collective-permute-start.11 = (bf16[512,512]{1,0:T(8,128)(2,1)S(1)}, bf16[512,512]{1,0:T(8,128)(2,1)}, u32[]{:S(2)}, u32[]{:S(2)}) collective-permute-start(bf16[512,512]{1,0:T(8,128)(2,1)S(1)} %bitcast.231), channel_id=1, source_target_pairs={{0,3},{1,0},{2,1},{3,2},{4,7},{5,4},{6,5},{7,6},{8,11},{9,8},{10,9... | collective-permute-start | bytes 1572872 | tf_op jit(solution)/shard_map/ppermute | solution.py:29
  100.9 28.5 %collective-permute-start.9 = (bf16[512,512]{1,0:T(8,128)(2,1)S(1)}, bf16[512,512]{1,0:T(8,128)(2,1)}, u32[]{:S(2)}, u32[]{:S(2)}) collective-permute-start(bf16[512,512]{1,0:T(8,128)(2,1)S(1)} %bitcast.232), channel_id=1, source_target_pairs={{0,1},{1,2},{2,3},{3,0},{4,5},{5,6},{6,7},{7,4},{8,9},{9,10},{10,1... | collective-permute-start | bytes 1572872 | tf_op jit(solution)/shard_map/ppermute | solution.py:29
  101.7 22.9 %collective-permute-start.18 = (f32[]{:T(128)}, f32[]{:T(128)}, u32[]{:S(2)}, u32[]{:S(2)}) collective-permute-start(f32[]{:T(128)} %convert_reduce_fusion), channel_id=1, source_target_pairs={{0,1},{1,2},{2,3},{3,0},{4,5},{5,6},{6,7},{7,4},{8,9},{9,10},{10,1... | collective-permute-start | bytes 20 | tf_op jit(solution)/shard_map/ppermute | solution.py:84
  103.5 22.5 %collective-permute-start.19 = (f32[]{:T(128)}, f32[]{:T(128)}, u32[]{:S(2)}, u32[]{:S(2)}) collective-permute-start(f32[]{:T(128)} %convert_reduce_fusion), channel_id=1, source_target_pairs={{0,2},{1,3},{2,0},{3,1},{4,6},{5,7},{6,4},{7,5},{8,10},{9,11},{10,... | collective-permute-start | bytes 20 | tf_op jit(solution)/shard_map/ppermute | solution.py:84
  124.6 2.1 collective-permute-start.20
  133.2 1.4 copy-start.3
  133.2 100.9 %all-gather.9.cloned.1.call-start = ((), (), s32[]{:S(2)}) async-start(), calls=%async_computation.4 | async-start | bytes 2621440 | tf_op jit(solution)/shard_map/all_gather | solution.py:126
  134.7 44.2 %collective-permute-start.12 = (bf16[1024,384]{1,0:T(8,128)(2,1)S(1)}, bf16[1024,384]{1,0:T(8,128)(2,1)S(1)}, u32[]{:S(2)}, u32[]{:S(2)}) collective-permute-start(bf16[1024,384]{1,0:T(8,128)(2,1)S(1)} %get-tuple-element.17), channel_id=1, source_target_pairs={{0,1},{1,2},{2,3},{3,0},{4,5},{5,6},{6,7},{7,4},{8,9},{9,10},{10,1... | collective-permute-start | bytes 2359304 | tf_op jit(solution)/shard_map/ppermute | solution.py:29
  135.7 43.3 %collective-permute-start.13 = (bf16[1024,384]{1,0:T(8,128)(2,1)S(1)}, bf16[1024,384]{1,0:T(8,128)(2,1)}, u32[]{:S(2)}, u32[]{:S(2)}) collective-permute-start(bf16[1024,384]{1,0:T(8,128)(2,1)S(1)} %get-tuple-element.17), channel_id=1, source_target_pairs={{0,2},{1,3},{2,0},{3,1},{4,6},{5,7},{6,4},{7,5},{8,10},{9,11},{10,... | collective-permute-start | bytes 2359304 | tf_op jit(solution)/shard_map/ppermute | solution.py:29
  136.6 42.3 %collective-permute-start.14 = (bf16[1024,384]{1,0:T(8,128)(2,1)S(1)}, bf16[1024,384]{1,0:T(8,128)(2,1)}, u32[]{:S(2)}, u32[]{:S(2)}) collective-permute-start(bf16[1024,384]{1,0:T(8,128)(2,1)S(1)} %get-tuple-element.17), channel_id=1, source_target_pairs={{0,3},{1,0},{2,1},{3,2},{4,7},{5,4},{6,5},{7,6},{8,11},{9,8},{10,9... | collective-permute-start | bytes 2359304 | tf_op jit(solution)/shard_map/ppermute | solution.py:29
  139.0 35.2 %collective-permute-start.15 = (bf16[4,64,384]{2,1,0:T(8,128)(2,1)S(1)}, bf16[4,64,384]{2,1,0:T(8,128)(2,1)S(1)}, u32[]{:S(2)}, u32[]{:S(2)}) collective-permute-start(bf16[4,64,384]{2,1,0:T(8,128)(2,1)S(1)} %get-tuple-element.28), channel_id=1, source_target_pairs={{0,1},{1,2},{2,3},{3,0},{4,5},{5,6},{6,7},{7,4},{8,9},{9,10},{10,1... | collective-permute-start | bytes 589832 | tf_op jit(solution)/shard_map/ppermute | solution.py:100
  139.0 38.2 %collective-permute-start.16 = (bf16[4,64,384]{2,1,0:T(8,128)(2,1)S(1)}, bf16[4,64,384]{2,1,0:T(8,128)(2,1)S(1)}, u32[]{:S(2)}, u32[]{:S(2)}) collective-permute-start(bf16[4,64,384]{2,1,0:T(8,128)(2,1)S(1)} %get-tuple-element.27), channel_id=1, source_target_pairs={{0,2},{1,3},{2,0},{3,1},{4,6},{5,7},{6,4},{7,5},{8,10},{9,11},{10,... | collective-permute-start | bytes 589832 | tf_op jit(solution)/shard_map/ppermute | solution.py:100
  174.2 4.6 %collective-permute-start.17 = (bf16[4,64,384]{2,1,0:T(8,128)(2,1)S(1)}, bf16[4,64,384]{2,1,0:T(8,128)(2,1)S(1)}, u32[]{:S(2)}, u32[]{:S(2)}) collective-permute-start(bf16[4,64,384]{2,1,0:T(8,128)(2,1)S(1)} %get-tuple-element.26), channel_id=1, source_target_pairs={{0,3},{1,0},{2,1},{3,2},{4,7},{5,4},{6,5},{7,6},{8,11},{9,8},{10,9... | collective-permute-start | bytes 589832 | tf_op jit(solution)/shard_map/ppermute | solution.py:100
  184.8 18.6 %collective-permute-start.21 = (bf16[1024,384]{1,0:T(8,128)(2,1)S(1)}, bf16[1024,384]{1,0:T(8,128)(2,1)S(1)}, u32[]{:S(2)}, u32[]{:S(2)}) collective-permute-start(bf16[1024,384]{1,0:T(8,128)(2,1)S(1)} %get-tuple-element.21), channel_id=1, source_target_pairs={{0,1},{1,2},{2,3},{3,0},{4,5},{5,6},{6,7},{7,4},{8,9},{9,10},{10,1... | collective-permute-start | bytes 2359304 | tf_op jit(solution)/shard_map/ppermute | solution.py:29
  185.8 20.6 %collective-permute-start.22 = (bf16[1024,384]{1,0:T(8,128)(2,1)S(1)}, bf16[1024,384]{1,0:T(8,128)(2,1)}, u32[]{:S(2)}, u32[]{:S(2)}) collective-permute-start(bf16[1024,384]{1,0:T(8,128)(2,1)S(1)} %get-tuple-element.21), channel_id=1, source_target_pairs={{0,2},{1,3},{2,0},{3,1},{4,6},{5,7},{6,4},{7,5},{8,10},{9,11},{10,... | collective-permute-start | bytes 2359304 | tf_op jit(solution)/shard_map/ppermute | solution.py:29
  187.2 32.7 %collective-permute-start.23 = (bf16[1024,384]{1,0:T(8,128)(2,1)S(1)}, bf16[1024,384]{1,0:T(8,128)(2,1)}, u32[]{:S(2)}, u32[]{:S(2)}) collective-permute-start(bf16[1024,384]{1,0:T(8,128)(2,1)S(1)} %get-tuple-element.21), channel_id=1, source_target_pairs={{0,3},{1,0},{2,1},{3,2},{4,7},{5,4},{6,5},{7,6},{8,11},{9,8},{10,9... | collective-permute-start | bytes 2359304 | tf_op jit(solution)/shard_map/ppermute | solution.py:29
  187.4 2.4 copy-start.10
  187.4 32.5 %copy-start.2 = (bf16[4,1024,384]{2,1,0:T(8,128)(2,1)S(1)}, bf16[4,1024,384]{2,1,0:T(8,128)(2,1)}, u32[]{:S(2)}) copy-start(bf16[4,1024,384]{2,1,0:T(8,128)(2,1)} %pad_maximum_fusion.1) | copy-start | bytes 9437188
  219.9 3.1 %copy-start.1 = (bf16[64,4096]{1,0:T(8,128)(2,1)S(1)}, bf16[64,4096]{1,0:T(8,128)(2,1)}, u32[]{:S(2)}) copy-start(bf16[64,4096]{1,0:T(8,128)(2,1)} %pad_maximum_fusion.4) | copy-start | bytes 1572868
  222.9 9.2 %copy-start = (bf16[4,2048,384]{2,1,0:T(8,128)(2,1)}, bf16[4,2048,384]{2,1,0:T(8,128)(2,1)S(1)}, u32[]{:S(2)}) copy-start(bf16[4,2048,384]{2,1,0:T(8,128)(2,1)S(1)} %maximum_maximum_fusion) | copy-start | bytes 18874372
  234.1 7.2 %slice-start = ((s8[6291456]{0:T(1024)(128)(4,1)}), s8[4194304]{0:T(1024)(128)(4,1)S(1)}, s32[]{:S(2)}) async-start(s8[6291456]{0:T(1024)(128)(4,1)} %bitcast.204), calls=%async_computation.5 | async-start | bytes 8388608
  236.3 5.1 %slice-start.1 = ((s8[6291456]{0:T(1024)(128)(4,1)}), s8[2097152]{0:T(1024)(128)(4,1)S(1)}, s32[]{:S(2)}) async-start(s8[6291456]{0:T(1024)(128)(4,1)} %bitcast.204), calls=%async_computation.6 | async-start | bytes 4194304
  249.5 6.0 %copy-start.9 = (s32[384]{0:T(512)S(1)}, s32[384]{0:T(512)}, u32[]{:S(2)}) copy-start(s32[384]{0:T(512)} %param.19) | copy-start | bytes 4612
  251.8 4.4 %collective-permute-start.24 = (f32[6,384]{1,0:T(8,128)S(1)}, f32[6,384]{1,0:T(8,128)S(1)}, u32[]{:S(2)}, u32[]{:S(2)}) collective-permute-start(f32[6,384]{1,0:T(8,128)S(1)} %get-tuple-element.29), channel_id=1, source_target_pairs={{0,3},{1,0},{2,1},{3,2},{4,7},{5,4},{6,5},{7,6},{8,11},{9,8},{10,9... | collective-permute-start | bytes 27656 | tf_op jit(solution)/shard_map/ppermute | solution.py:133
  254.1 3.7 %collective-permute-start.25 = (f32[6,384]{1,0:T(8,128)S(1)}, f32[6,384]{1,0:T(8,128)S(1)}, u32[]{:S(2)}, u32[]{:S(2)}) collective-permute-start(f32[6,384]{1,0:T(8,128)S(1)} %get-tuple-element.31), channel_id=1, source_target_pairs={{0,2},{1,3},{2,0},{3,1},{4,6},{5,7},{6,4},{7,5},{8,10},{9,11},{10,... | collective-permute-start | bytes 27656 | tf_op jit(solution)/shard_map/ppermute | solution.py:133
  255.5 3.1 %collective-permute-start.26 = (f32[6,384]{1,0:T(8,128)S(1)}, f32[6,384]{1,0:T(8,128)S(1)}, u32[]{:S(2)}, u32[]{:S(2)}) collective-permute-start(f32[6,384]{1,0:T(8,128)S(1)} %get-tuple-element.30), channel_id=1, source_target_pairs={{0,1},{1,2},{2,3},{3,0},{4,5},{5,6},{6,7},{7,4},{8,9},{9,10},{10,1... | collective-permute-start | bytes 27656 | tf_op jit(solution)/shard_map/ppermute | solution.py:133
Sparse Core Ops, SparseCore 0:
  8.9 83.2 all-gather.6
  93.8 26.0 all-gather.4
  133.3 47.1 reduce-scatter.1
  187.3 46.6 all-gather.8
